TPU v7x, 32 devices: a whole 2x2x4 slice. The times are simulated.
32 devices in a mesh: dp: 8 (over y, x, core), space: 4 (over z).
Axes of the slice: x: 2, y: 2, z: 4, core: 2. Of those that a mesh axis runs over, the one named last changes fastest.
Arguments:
- volume: bfloat16 [8, 32, 8, 16, 128], P('dp', None, 'space')
- out_grad: bfloat16 [8, 32, 8, 16, 128], P('dp', None, 'space'), may hold values from -0.016479492 to 0.016479492
- kernel: bfloat16 [32, 864], replicated, may hold values from -0.21875 to 0.21875
- sample_idx: int32 [8, 4096], P('dp', 'space'), may hold values from 0 to 4095
- a_inverse: float32 [864, 864], P('space')
- g_inverse: float32 [32, 32], replicated
Outputs:
- conv_out: bfloat16 [8, 32, 8, 16, 128], P('dp', None, 'space')
- a_factor: float32 [864, 864], P('dp', 'space')
- g_factor: float32 [32, 32], replicated
- pre_grad: float32 [32, 864], replicated
Inputs may be any that keep to these rules, and one draw needn't show every extreme that they name: `sample_idx`: column s of a sample's row names a cell of slab s // 1024, as the number z * 16 * 128 + y * 128 + x counted within that slab of 2 planes.
All inputs are finite; a program needn't handle non-finite values.
Results may differ from a plain program's by a relative error of at most 0.0085.
Values may be sent and summed in bfloat16 or wider, within the bound.
No kernel may reach another device: no remote copies, remote signals or barrier semaphores. Data moves between devices by JAX's collectives and lax.ppermute only.
A program may use at most 128 MiB of HBM per device.

v0:
```python
import jax
import jax.numpy as jnp
from jax import lax
from jax.sharding import PartitionSpec as P


def padded_2(cells, sides, width):
    for axis, dim in sides:
        count = lax.axis_size(axis)
        ends = count - 1
        head = lax.slice_in_dim(cells, 0, width, axis=dim)
        tail = lax.slice_in_dim(cells, cells.shape[dim] - width, cells.shape[dim], axis=dim)
        cells = jnp.concatenate(
            [
                lax.ppermute(tail, axis, [(i, (i + 1) % count) for i in range(ends)]),
                cells,
                lax.ppermute(head, axis, [((i + 1) % count, i) for i in range(ends)]),
            ],
            axis=dim,
        )
    return cells


def on_device(volume, out_grad, kernel, sample_idx, a_inverse, g_inverse):
    highest = lax.Precision.HIGHEST
    channels = volume.shape[1]
    planes = volume.shape[2]
    y_cells = volume.shape[3]
    x_cells = volume.shape[4]
    block = padded_2(volume, (("space", 2),), 1)
    padded = jnp.pad(block[0], ((0, 0), (0, 0), (1, 1), (1, 1)))
    grad_flat = out_grad[0].reshape(channels, -1)
    kernel_taps = kernel.reshape(channels, channels, 3, 3, 3)
    forward = jnp.zeros((channels, planes * y_cells * x_cells), jnp.float32)
    grad_parts = []
    for z_off in range(3):
        for y_off in range(3):
            shifted = jnp.stack(
                [
                    padded[
                        :, z_off : z_off + planes, y_off : y_off + y_cells, x_off : x_off + x_cells
                    ]
                    for x_off in range(3)
                ],
                axis=1,
            )
            shifted = shifted.reshape(channels * 3, -1)
            kernel_cols = kernel_taps[:, :, z_off, y_off, :].reshape(channels, channels * 3)
            forward = forward + jnp.dot(kernel_cols, shifted, preferred_element_type=jnp.float32)
            grad_parts.append(
                jnp.einsum(
                    "ok,ck->oc", grad_flat, shifted, preferred_element_type=jnp.float32
                ).reshape(channels, channels, 3)
            )
    grad_w = jnp.stack(grad_parts, axis=2).reshape(channels, channels * 27)
    conv_out = forward.astype(jnp.bfloat16).reshape(1, channels, planes, y_cells, x_cells)
    g_part = jnp.einsum("ok,pk->op", grad_flat, grad_flat, preferred_element_type=jnp.float32)
    cell_ids = sample_idx[0]
    z_pos = cell_ids // (y_cells * x_cells)
    y_pos = cell_ids // x_cells % y_cells
    x_pos = cell_ids % x_cells
    offsets = jnp.arange(27, dtype=jnp.int32)
    gathered = padded[
        :,
        z_pos[:, None] + offsets[None, :] // 9,
        y_pos[:, None] + offsets[None, :] // 3 % 3,
        x_pos[:, None] + offsets[None, :] % 3,
    ]
    patches = jnp.transpose(gathered, (1, 0, 2)).reshape(cell_ids.shape[0], channels * 27)
    total_samples = sample_idx.shape[1] * lax.axis_size("space") * lax.axis_size("dp")
    a_part = jnp.einsum(
        "sp,sq->pq", patches, patches, preferred_element_type=jnp.float32
    ) / jnp.float32(total_samples)
    tile_sum = lax.psum_scatter(
        a_part.astype(jnp.bfloat16), "space", scatter_dimension=1, tiled=True
    )
    a_factor = lax.psum_scatter(tile_sum, "dp", scatter_dimension=0, tiled=True).astype(jnp.float32)
    grad_sum, g_factor = lax.psum((grad_w, g_part), ("dp", "space"))
    left = jnp.dot(g_inverse, grad_sum, precision=highest)
    full_inverse = lax.all_gather(a_inverse, "space", axis=0, tiled=True)
    pre_grad = jnp.dot(left, full_inverse, precision=highest)
    return (conv_out, a_factor, g_factor, pre_grad)


def solution(mesh):
    placed = (
        P("dp", None, "space", None, None),
        P("dp", None, "space", None, None),
        P(),
        P("dp", "space"),
        P("space", None),
        P(),
    )
    return jax.shard_map(
        on_device,
        mesh=mesh,
        in_specs=placed,
        out_specs=(P("dp", None, "space", None, None), P("dp", "space"), P(), P()),
        check_vma=False,
    )
```

profile of v0, /device:TPU:0, one launch (start us, length us, event | category | flops | bytes accessed | tf_op | source)
XLA Modules:
  0.0 758.8 jit_solution(1612512045983143140)
XLA Ops:
  9.1 4.9 collective-permute-start
  18.1 2.8 collective-permute-done.1
  22.3 12.4 %slice_bitcast_fusion.3 = (bf16[32,1,2,16,128]{0,2,4,3,1:T(2,128)(2,1)}, bf16[32,1,2,16,128]{0,2,4,3,1:T(2,128)(2,1)}, bf16[32,1,2,16,128]{0,2,4,3,1:T(2,128)(2,...) fusion(bf16[32,4,16,128]{0,1,3,2:T(4,128)(2,1)S(1)} %bitcast.197), kind=kLoop, calls=%fused_computation.28 | loop fusion | bytes 4980736 | tf_op jit(solution)/shard_map/stack | solution.py:38
  34.7 17.3 %slice_bitcast_fusion.4 = (bf16[32,1,2,16,128]{0,2,4,3,1:T(2,128)(2,1)}, bf16[32,1,2,16,128]{0,2,4,3,1:T(2,128)(2,1)}, bf16[32,1,2,16,128]{0,2,4,3,1:T(2,128)(2,...) fusion(bf16[32,4,16,128]{0,1,3,2:T(4,128)(2,1)S(1)} %bitcast.198), kind=kLoop, calls=%fused_computation.29 | loop fusion | bytes 5767168 | tf_op jit(solution)/shard_map/stack | solution.py:38
  52.0 14.2 %slice_bitcast_fusion.5 = (bf16[32,1,2,16,128]{0,2,4,3,1:T(2,128)(2,1)}, bf16[32,1,2,16,128]{0,2,4,3,1:T(2,128)(2,1)}, bf16[32,1,2,16,128]{0,2,4,3,1:T(2,128)(2,...) fusion(bf16[32,4,16,128]{0,1,3,2:T(4,128)(2,1)S(1)} %bitcast.199), kind=kLoop, calls=%fused_computation.30 | loop fusion | bytes 5767168 | tf_op jit(solution)/shard_map/stack | solution.py:38
  66.2 2.7 pad.4
  68.9 294.0 %gather_fusion = bf16[27648,32]{1,0:T(8,128)(2,1)} fusion(bf16[32,4,18,130]{0,1,3,2:T(4,128)(2,1)S(1)} %pad.4, s32[27648]{0:T(1024)S(1)} %reshape.365), kind=kCustom, calls=%fused_computation | custom fusion | bytes 3870720 | tf_op jit(solution)/shard_map/gather | solution.py:63
  362.9 5.4 copy.71
  368.3 22.7 %reshape.368 = bf16[1024,27,32]{1,0,2:T(8,128)(2,1)} reshape(bf16[27648,32]{0,1:T(8,128)(2,1)S(1)} %copy.71) | data formatting | bytes 3538944 | tf_op jit(solution)/shard_map/gather | solution.py:63
  391.1 7.1 copy.72
  398.2 11.5 %reshape.362 = bf16[1024,864]{0,1:T(8,128)(2,1)} reshape(bf16[1024,32,27]{0,2,1:T(8,128)(2,1)S(1)} %copy.72) | data formatting | bytes 3538944 | tf_op jit(solution)/shard_map/reshape | solution.py:69
  409.6 5.2 multiply_convert_fusion
  439.7 2.4 copy.57
  447.7 2.4 copy.70
  453.8 2.4 copy.48
  456.3 2.4 copy.69
  459.0 2.4 copy.68
  467.3 2.4 copy.43
  469.8 2.4 copy.44
  472.2 2.4 copy.45
  476.6 2.2 reshape.351
  481.1 2.4 copy.47
  483.5 2.4 copy.49
  492.4 2.4 copy.50
  494.8 2.4 copy.51
  497.3 2.4 copy.52
  506.2 2.4 copy.66
  510.5 2.2 reshape.359
  527.8 44.4 %psum.14 = f32[32,32]{1,0:T(8,128)} all-reduce(f32[32,32]{1,0:T(8,128)S(1)} %convolution_bitcast_fusion.9), channel_id=1, replica_groups=mesh['dp'=8,'space'=4] {'dp','space'}, use_global_device_ids=true, to_apply=%region_2.3 | all-reduce | flops 1024 | bytes 8192 | tf_op jit(solution)/shard_map/psum | solution.py:78
  577.4 109.9 %all-reduce.6.cloned.1.call-done = f32[32,864]{0,1:T(8,128)} async-done(((f32[32,864]{0,1:T(8,128)}), f32[32,864]{0,1:T(8,128)}) %all-reduce.6.cloned.1.call-update) | async-done | bytes 110608 | tf_op jit(solution)/shard_map/psum | solution.py:78
  688.9 56.3 %all-reduce.8.cloned.1.call-done = bf16[864,216]{0,1:T(8,128)(2,1)} async-done(((bf16[864,216]{0,1:T(8,128)(2,1)}), bf16[864,216]{0,1:T(8,128)(2,1)}) %all-reduce.8.cloned.1.call-update) | async-done | bytes 373264
  746.8 4.1 fusion.20
  (144 shorter events, 88.4 us)
Async XLA Ops:
  8.0 679.3 %copy-start = (f32[32,32]{1,0:T(8,128)S(1)}, f32[32,32]{1,0:T(8,128)}, u32[]{:S(2)}) copy-start(f32[32,32]{1,0:T(8,128)} %param.11) | copy-start | bytes 12292
  8.0 12.9 %copy-start.10 = (bf16[1,32,2,16,128]{4,3,2,1,0:T(8,128)(2,1)S(1)}, bf16[1,32,2,16,128]{4,3,2,1,0:T(8,128)(2,1)}, u32[]{:S(2)}) copy-start(bf16[1,32,2,16,128]{4,3,2,1,0:T(8,128)(2,1)} %param.6) | copy-start | bytes 786436
  8.0 507.8 %reduce-scatter.5.cloned.1.call-start = ((), (), s32[]{:S(2)}) async-start(), calls=%async_computation.4 | async-start | bytes 1935360
  9.1 9.0 %collective-permute-start = (bf16[1,32,1,16,128]{4,3,2,1,0:T(8,128)(2,1)S(1)}, bf16[1,32,1,16,128]{4,3,2,1,0:T(8,128)(2,1)S(1)}, u32[]{:S(2)}, u32[]{:S(2)}) collective-permute-start(bf16[1,32,1,16,128]{4,3,2,1,0:T(8,128)(2,1)S(1)} %get-tuple-element.40), channel_id=1, source_target_pairs={{0,1},{1,2},{2,3},{4,5},{5,6},{6,7},{8,9},{9,10},{10,11},{12,13},{... | collective-permute-start | bytes 393224 | tf_op jit(solution)/shard_map/ppermute | solution.py:15
  14.0 6.9 collective-permute-start.1
  22.3 29.7 %copy-start.1 = (bf16[1,32,4,16,128]{1,2,4,3,0:T(4,128)(2,1)}, bf16[1,32,4,16,128]{1,2,4,3,0:T(4,128)(2,1)S(1)}, u32[]{:S(2)}) copy-start(bf16[1,32,4,16,128]{1,2,4,3,0:T(4,128)(2,1)S(1)} %copy.42) | copy-start | bytes 1572868
  414.8 2.0 copy-start.8
  414.8 2.7 copy-start.7
  414.9 272.5 %all-reduce.6.cloned.1.call-start = ((), (), s32[]{:S(2)}) async-start(), calls=%async_computation.1 | async-start | bytes 884736 | tf_op jit(solution)/shard_map/psum | solution.py:78
  419.2 5.2 copy-start.9
  510.5 3.9 copy-start.11
  510.5 3.9 copy-start.12
  510.5 4.0 copy-start.13
  514.4 2.7 copy-start.14
  515.8 229.4 %all-reduce.8.cloned.1.call-start = ((), (), s32[]{:S(2)}) async-start(), calls=%async_computation.3 | async-start | bytes 774144
  515.8 57.9 %copy-start.3 = (bf16[96,4096]{1,0:T(8,128)(2,1)S(1)}, bf16[96,4096]{1,0:T(8,128)(2,1)}, u32[]{:S(2)}) copy-start(bf16[96,4096]{1,0:T(8,128)(2,1)} %reshape.353) | copy-start | bytes 2359300
  516.4 230.5 %all-gather.2.cloned.1.call-start = ((), (), s32[]{:S(2)}) async-start(), calls=%async_computation.2 | async-start | bytes 3870720 | tf_op jit(solution)/shard_map/all_gather | solution.py:80
  572.2 1.8 copy-start.5
  573.7 1.1 copy-start.2
  574.9 1.1 copy-start.4
  575.2 1.2 copy-start.6
Sparse Core Ops, SparseCore 0:
  415.0 35.0 reduce-scatter.4
  518.8 64.9 all-gather.1
Sparse Core Ops, SparseCore 1:
  515.8 171.4 all-reduce.5
  690.6 54.6 all-reduce.7
where the time goes:
time: 765 us; the launch traced here: 759 us
  local copies, waits for them, and re-layouts  476 us (62%)
  waiting for transfers between devices  170 us (22%)
  blocking collectives  44.4 us (6%)
  matrix products  26.2 us (3%)
  other arithmetic  18.1 us (2%)
  between operations  17.1 us (2%)
    gather x3, local copies, waits for them, and re-layouts, on_device(): padded[:, z_pos[:, None] + offsets[None, :] // 9, y_pos[:, None] + offset...  322 us
    psum x1, waiting for transfers between devices, on_device(): grad_sum, g_factor = lax.psum((grad_w, g_part), ('dp', 'space'))  110 us
    another operation x30, local copies, waits for them, and re-layouts, on_device(): jnp.stack([padded[:, z_off:z_off + planes, y_off:y_off + y_cells, x_off:x...  98.5 us
    unnamed x6, waiting for transfers between devices  57.6 us
    psum x1, blocking collectives, on_device(): grad_sum, g_factor = lax.psum((grad_w, g_part), ('dp', 'space'))  44.4 us
    reshape x9, local copies, waits for them, and re-layouts, on_device(): shifted = shifted.reshape(channels * 3, -1)  16.3 us
  transfers between devices with their start and end apart: 6, of which 3 were waited for; matrix products, arithmetic and copies ran while one was open for 16% of the time, Pallas kernels for 0%

commit v1 on v0

v1 whole, which is shorter than its diff:
```python
import jax
import jax.numpy as jnp
from jax import lax
from jax.sharding import PartitionSpec as P


def padded_2(cells, sides, width):
    for axis, dim in sides:
        count = lax.axis_size(axis)
        ends = count - 1
        head = lax.slice_in_dim(cells, 0, width, axis=dim)
        tail = lax.slice_in_dim(cells, cells.shape[dim] - width, cells.shape[dim], axis=dim)
        cells = jnp.concatenate(
            [
                lax.ppermute(tail, axis, [(i, (i + 1) % count) for i in range(ends)]),
                cells,
                lax.ppermute(head, axis, [((i + 1) % count, i) for i in range(ends)]),
            ],
            axis=dim,
        )
    return cells


def on_device(volume, out_grad, kernel, sample_idx, a_inverse, g_inverse):
    highest = lax.Precision.HIGHEST
    f32 = jnp.float32
    channels = volume.shape[1]
    planes = volume.shape[2]
    y_cells = volume.shape[3]
    x_cells = volume.shape[4]
    cells = planes * y_cells * x_cells
    patch = kernel.shape[1]
    n_dp = lax.axis_size("dp")
    n_sp = lax.axis_size("space")
    contract_cells = (((1,), (1,)), ((), ()))

    block = padded_2(volume, (("space", 2),), 1)
    padded = jnp.pad(block[0], ((0, 0), (0, 0), (1, 1), (1, 1)))
    taps = [
        padded[:, dz : dz + planes, dy : dy + y_cells, dx : dx + x_cells]
        for dz in range(3)
        for dy in range(3)
        for dx in range(3)
    ]
    patches_t = jnp.stack(taps, axis=1).reshape(patch, cells)
    grad_flat = out_grad[0].reshape(channels, cells)

    forward = jnp.dot(kernel, patches_t, preferred_element_type=f32)
    conv_out = forward.astype(jnp.bfloat16).reshape(1, channels, planes, y_cells, x_cells)
    grad_w = lax.dot_general(grad_flat, patches_t, contract_cells, preferred_element_type=f32)
    g_part = lax.dot_general(grad_flat, grad_flat, contract_cells, preferred_element_type=f32)

    cell_ids = sample_idx[0]
    counts = jnp.sum(
        (cell_ids[:, None] == jnp.arange(cells, dtype=jnp.int32)[None, :]).astype(f32), axis=0
    )
    weighted = patches_t.astype(f32) * counts[None, :]
    high = weighted.astype(jnp.bfloat16)
    low = (weighted - high.astype(f32)).astype(jnp.bfloat16)
    total_samples = sample_idx.shape[1] * n_sp * n_dp
    a_part = (
        lax.dot_general(high, patches_t, contract_cells, preferred_element_type=f32)
        + lax.dot_general(low, patches_t, contract_cells, preferred_element_type=f32)
    ) / jnp.float32(total_samples)
    rows = patch // n_dp
    cols = patch // n_sp
    a_blocks = (
        a_part.astype(jnp.bfloat16)
        .reshape(n_dp, rows, n_sp, cols)
        .transpose(0, 2, 1, 3)
        .reshape(n_dp * n_sp, rows, cols)
    )
    a_factor = lax.psum_scatter(a_blocks, ("dp", "space"), scatter_dimension=0, tiled=True)
    a_factor = a_factor.reshape(rows, cols).astype(f32)

    both = lax.psum(jnp.concatenate([grad_w, g_part], axis=1), ("dp", "space"))
    grad_sum = both[:, :patch]
    g_factor = both[:, patch:]
    left = jnp.dot(g_inverse, grad_sum, precision=highest)
    own_rows = a_inverse.shape[0]
    left_rows = lax.dynamic_slice_in_dim(left, lax.axis_index("space") * own_rows, own_rows, axis=1)
    pre_grad = lax.psum(jnp.dot(left_rows, a_inverse, precision=highest), "space")
    return (conv_out, a_factor, g_factor, pre_grad)


def solution(mesh):
    placed = (
        P("dp", None, "space", None, None),
        P("dp", None, "space", None, None),
        P(),
        P("dp", "space"),
        P("space", None),
        P(),
    )
    return jax.shard_map(
        on_device,
        mesh=mesh,
        in_specs=placed,
        out_specs=(P("dp", None, "space", None, None), P("dp", "space"), P(), P()),
        check_vma=False,
    )
```

time: 765 us -> 375 us (0.49)
  local copies, waits for them, and re-layouts: 476 us -> 71.4 us
  waiting for transfers between devices: 170 us -> 224 us
  blocking collectives: 44.4 us -> 0 us
  matrix products: 26.2 us -> 39.4 us
    gather x3 -> x0, local copies, waits for them, and re-layouts: 322 us -> none  [on_device(): padded[:, z_pos[:, None] + offsets[None, :] // 9, y_pos[:, None] + offset...]
    another operation x51 -> x3, local copies, waits for them, and re-layouts: 107 us -> 5.85 us  [the longest x2 4.78 us: on_device(): patches_t = jnp.stack(taps, axis=1).reshape(patch, cells)]
    psum x1 -> x0, blocking collectives: 44.4 us -> none  [on_device(): grad_sum, g_factor = lax.psum((grad_w, g_part), ('dp', 'space'))]
    convert_element_type x0 -> x4, local copies, waits for them, and re-layouts: none -> 37.4 us  [the longest x2 18.8 us: on_device(): high = weighted.astype(jnp.bfloat16)]
    unnamed x6 -> x4, waiting for transfers between devices: 57.6 us -> 92 us
    psum x1 -> x2, waiting for transfers between devices: 110 us -> 132 us  [the longest x1 97.5 us: on_device(): both = lax.psum(jnp.concatenate([grad_w, g_part], axis=1), ('dp', 'space'))]
    another operation x9 -> x0, other arithmetic: 15.1 us -> none  [on_device(): jnp.stack([padded[:, z_off:z_off + planes, y_off:y_off + y_cells, x_off:x...]
    reshape x12 -> x2, local copies, waits for them, and re-layouts: 29.9 us -> 16.2 us  [the longest x1 11.6 us: on_device(): patches_t = jnp.stack(taps, axis=1).reshape(patch, cells)]
  transfers between devices with their start and end apart: 6 -> 5, of which waited for: 3 -> 3; matrix products, arithmetic and copies ran while one was open for 16% -> 10% of each run, Pallas kernels for 0% -> 0%
where the time goes in v1:
time: 375 us; the launch traced here: 374 us
  waiting for transfers between devices  224 us (60%)
  local copies, waits for them, and re-layouts  71.4 us (19%)
  matrix products  39.4 us (11%)
  other arithmetic  18.6 us (5%)
  between operations  14 us (4%)
  starting transfers between devices  6.35 us (2%)
    psum x1, waiting for transfers between devices, on_device(): both = lax.psum(jnp.concatenate([grad_w, g_part], axis=1), ('dp', 'space'))  97.5 us
    unnamed x4, waiting for transfers between devices  92 us
    psum x1, waiting for transfers between devices, on_device(): lax.psum(jnp.dot(left_rows, a_inverse, precision=highest), 'space')  34.7 us
    convert_element_type x2, local copies, waits for them, and re-layouts, on_device(): high = weighted.astype(jnp.bfloat16)  18.8 us
    convert_element_type x2, local copies, waits for them, and re-layouts, on_device(): low = (weighted - high.astype(f32)).astype(jnp.bfloat16)  18.6 us
    dot_general x1, matrix products, on_device(): lax.dot_general(low, patches_t, contract_cells, preferred_element_type=f32)  13.3 us
    dot_general x1, matrix products, on_device(): lax.dot_general(high, patches_t, contract_cells, preferred_element_type=f32)  12.9 us
    convert_element_type x1, other arithmetic, on_device(): low = (weighted - high.astype(f32)).astype(jnp.bfloat16)  12 us
  transfers between devices with their start and end apart: 5, of which 3 were waited for; matrix products, arithmetic and copies ran while one was open for 10% of the time, Pallas kernels for 0%

profile of v1, /device:TPU:0, one launch (start us, length us, event | category | flops | bytes accessed | tf_op | source)
XLA Modules:
  0.0 373.9 jit_solution(7109457592317233880)
XLA Ops:
  7.2 1.1 fusion.59
  8.3 4.9 %collective-permute-start = (bf16[1,32,1,16,128]{4,3,2,1,0:T(8,128)(2,1)S(1)}, bf16[1,32,1,16,128]{4,3,2,1,0:T(8,128)(2,1)S(1)}, u32[]{:S(2)}, u32[]{:S(2)}) collective-permute-start(bf16[1,32,1,16,128]{4,3,2,1,0:T(8,128)(2,1)S(1)} %get-tuple-element.6), channel_id=1, source_target_pairs={{0,1},{1,2},{2,3},{4,5},{5,6},{6,7},{8,9},{9,10},{10,11},{12,13},{... | collective-permute-start | bytes 393224 | tf_op jit(solution)/shard_map/ppermute | solution.py:15
  13.2 1.3 collective-permute-start.1
  14.5 3.4 convert_reduce_fusion
  17.9 1.1 reshape_squeeze.3
  19.0 1.3 convolution_bitcast_fusion.1
  20.3 1.0 maximum_bitcast_fusion
  24.4 0.2 fusion.39
  25.6 4.6 %copy.25 = bf16[32,27,2,16,128]{4,3,2,1,0:T(8,128)(2,1)} copy(bf16[32,27,2,16,128]{4,3,2,0,1:T(8,128)(2,1)S(1)} %fusion.49) | data formatting | bytes 14155776 | tf_op jit(solution)/shard_map/stack | solution.py:45
  30.2 0.7 copy-done.1
  30.8 12.0 %subtract_convert_fusion = (bf16[32,27,2,16,128]{4,3,2,0,1:T(8,128)(2,1)}, bf16[32,27,2,16,128]{4,3,2,0,1:T(8,128)(2,1)}) fusion(bf16[32,27,2,16,128]{4,3,2,0,1:T(8,128)(2,1)} %copy-done.1, f32[2,16,128]{2,1,0:T(8,128)S(1)} %bitcast.151), kind=kLoop, calls=%fused_computation.2 | loop fusion | flops 21233664 | bytes 21250048 | tf_op jit(solution)/shard_map/convert_element_type | solution.py:59
  42.9 7.1 %copy.26 = bf16[32,27,2,16,128]{4,3,2,1,0:T(8,128)(2,1)} copy(bf16[32,27,2,16,128]{4,3,2,0,1:T(8,128)(2,1)} %get-tuple-element.5) | data formatting | bytes 14155776 | tf_op jit(solution)/shard_map/convert_element_type | solution.py:58
  50.0 11.6 %convert_element_type.83 = bf16[864,4096]{1,0:T(8,128)(2,1)} reshape(bf16[32,27,2,16,128]{4,3,2,1,0:T(8,128)(2,1)} %copy.26) | data formatting | bytes 14155776 | tf_op jit(solution)/shard_map/convert_element_type | solution.py:58
  61.6 11.6 %reshape.94 = bf16[864,4096]{1,0:T(8,128)(2,1)} reshape(bf16[32,27,2,16,128]{4,3,2,1,0:T(8,128)(2,1)} %copy.25) | data formatting | bytes 14155776 | tf_op jit(solution)/shard_map/reshape | solution.py:45
  73.2 7.1 %copy.27 = bf16[32,27,2,16,128]{4,3,2,1,0:T(8,128)(2,1)} copy(bf16[32,27,2,16,128]{4,3,2,0,1:T(8,128)(2,1)} %get-tuple-element.4) | data formatting | bytes 14155776 | tf_op jit(solution)/shard_map/convert_element_type | solution.py:59
  80.3 11.6 %convert_element_type.86 = bf16[864,4096]{1,0:T(8,128)(2,1)} reshape(bf16[32,27,2,16,128]{4,3,2,1,0:T(8,128)(2,1)} %copy.27) | data formatting | bytes 14155776 | tf_op jit(solution)/shard_map/convert_element_type | solution.py:59
  91.9 12.9 %fusion.60 = f32[864,864]{1,0:T(8,128)} fusion(bf16[864,4096]{1,0:T(8,128)(2,1)} %convert_element_type.83, bf16[864,4096]{1,0:T(8,128)(2,1)} %reshape.94), kind=kOutput, calls=%fused_computation.98 | convolution fusion | flops 6115295232 | bytes 17141760 | tf_op jit(solution)/shard_map/dot_general | solution.py:62
  104.8 5.1 %convolution_bitcast_fusion = f32[32,864]{1,0:T(8,128)S(1)} fusion(bf16[864,4096]{1,0:T(8,128)(2,1)} %reshape.94, bf16[32,4096]{1,0:T(8,128)(2,1)S(1)} %reshape_squeeze.3), kind=kOutput, calls=%fused_computation.32 | convolution fusion | flops 226492416 | bytes 7450624 | tf_op jit(solution)/shard_map/dot_general | solution.py:50
  109.9 0.7 pad_maximum_fusion
  110.7 13.3 %multiply_convert_fusion = bf16[864,864]{1,0:T(8,128)(2,1)} fusion(f32[864,864]{1,0:T(8,128)} %fusion.60, bf16[864,4096]{1,0:T(8,128)(2,1)} %convert_element_type.86, bf16[864,4096]{1,0:T(8,128)(2,1)} %reshape.94), kind=kOutput, calls=%fused_computation.30 | convolution fusion | flops 6117534720 | bytes 18634752 | tf_op jit(solution)/shard_map/dot_general | solution.py:63
  124.0 4.6 %reshape.96 = bf16[8,108,4,216]{3,2,1,0:T(4,128)(2,1)S(1)} reshape(bf16[864,864]{1,0:T(8,128)(2,1)} %multiply_convert_fusion) | data formatting | bytes 2985984 | tf_op jit(solution)/shard_map/reshape | solution.py:69
  128.6 2.6 copy.28
  131.2 4.4 %fusion.1 = bf16[4,8,32,128]{3,1,2,0:T(8,128)(2,1)S(1)} fusion(bf16[32,864]{1,0:T(8,128)(2,1)S(1)} %copy-done.2, bf16[864,4096]{1,0:T(8,128)(2,1)} %reshape.94), kind=kOutput, calls=%fused_computation.31 | convolution fusion | flops 226623488 | bytes 7395328 | tf_op jit(solution)/shard_map/dot_general | solution.py:48
  135.6 0.8 copy.32
  136.3 97.5 %all-reduce.5.cloned.1.call-done = f32[32,896]{1,0:T(8,128)} async-done(((f32[32,896]{1,0:T(8,128)}), f32[32,896]{1,0:T(8,128)}) %all-reduce.5.cloned.1.call-update) | async-done | bytes 114704 | tf_op jit(solution)/shard_map/psum | solution.py:76
  233.8 1.1 fusion.54
  235.0 1.3 fusion.56
  236.3 1.4 slice.130
  237.7 92.0 %reduce-scatter.4.cloned.1.call-done = bf16[1,108,216]{1,2,0:T(8,128)(2,1)} async-done(((bf16[32,108,216]{1,2,0:T(8,128)(2,1)}), bf16[1,108,216]{1,2,0:T(8,128)(2,1)}) %reduce-scatter.4.cloned.1.call-update) | async-done | bytes 46672
  329.7 1.5 bitcast_convert_fusion
  331.2 34.7 %all-reduce.7.cloned.1.call-done = f32[32,864]{1,0:T(8,128)} async-done(((f32[32,864]{1,0:T(8,128)}), f32[32,864]{1,0:T(8,128)}) %all-reduce.7.cloned.1.call-update) | async-done | bytes 110608 | tf_op jit(solution)/shard_map/psum | solution.py:82
  365.9 1.6 copy.63
  (41 shorter events, 4.1 us)
Async XLA Ops:
  7.2 227.8 %copy-start = (f32[216,864]{1,0:T(8,128)S(1)}, f32[216,864]{1,0:T(8,128)}, u32[]{:S(2)}) copy-start(f32[216,864]{1,0:T(8,128)} %param.10) | copy-start | bytes 2239492
  7.2 226.7 %all-reduce.5.cloned.1.call-start = ((), (), s32[]{:S(2)}) async-start(), calls=%async_computation.1 | async-start | bytes 229376 | tf_op jit(solution)/shard_map/psum | solution.py:76
  8.3 12.0 %collective-permute-start = (bf16[1,32,1,16,128]{4,3,2,1,0:T(8,128)(2,1)S(1)}, bf16[1,32,1,16,128]{4,3,2,1,0:T(8,128)(2,1)S(1)}, u32[]{:S(2)}, u32[]{:S(2)}) collective-permute-start(bf16[1,32,1,16,128]{4,3,2,1,0:T(8,128)(2,1)S(1)} %get-tuple-element.6), channel_id=1, source_target_pairs={{0,1},{1,2},{2,3},{4,5},{5,6},{6,7},{8,9},{9,10},{10,11},{12,13},{... | collective-permute-start | bytes 393224 | tf_op jit(solution)/shard_map/ppermute | solution.py:15
  13.2 7.0 %collective-permute-start.1 = (bf16[1,32,1,16,128]{4,3,2,1,0:T(8,128)(2,1)S(1)}, bf16[1,32,1,16,128]{4,3,2,1,0:T(8,128)(2,1)S(1)}, u32[]{:S(2)}, u32[]{:S(2)}) collective-permute-start(bf16[1,32,1,16,128]{4,3,2,1,0:T(8,128)(2,1)S(1)} %get-tuple-element.7), channel_id=1, source_target_pairs={{1,0},{2,1},{3,2},{5,4},{6,5},{7,6},{9,8},{10,9},{11,10},{13,12},{... | collective-permute-start | bytes 393224 | tf_op jit(solution)/shard_map/ppermute | solution.py:17
  25.6 5.3 %copy-start.1 = (bf16[32,27,2,16,128]{4,3,2,0,1:T(8,128)(2,1)}, bf16[32,27,2,16,128]{4,3,2,0,1:T(8,128)(2,1)S(1)}, u32[]{:S(2)}) copy-start(bf16[32,27,2,16,128]{4,3,2,0,1:T(8,128)(2,1)S(1)} %fusion.49) | copy-start | bytes 21233668
  110.7 219.0 %reduce-scatter.4.cloned.1.call-start = ((), (), s32[]{:S(2)}) async-start(), calls=%async_computation.3 | async-start | bytes 1824768
  124.0 7.2 %copy-start.2 = (bf16[32,864]{1,0:T(8,128)(2,1)S(1)}, bf16[32,864]{1,0:T(8,128)(2,1)}, u32[]{:S(2)}) copy-start(bf16[32,864]{1,0:T(8,128)(2,1)} %param.8) | copy-start | bytes 165892
  128.5 105.3 %copy-start.3 = (f32[32,32]{1,0:T(8,128)S(1)}, f32[32,32]{1,0:T(8,128)}, u32[]{:S(2)}) copy-start(f32[32,32]{1,0:T(8,128)} %param.11) | copy-start | bytes 12292
  131.1 234.7 %all-reduce.7.cloned.1.call-start = ((), (), s32[]{:S(2)}) async-start(), calls=%async_computation.2 | async-start | bytes 229376 | tf_op jit(solution)/shard_map/psum | solution.py:82
Sparse Core Ops, SparseCore 0:
  110.8 123.0 all-reduce.4
  239.2 90.4 reduce-scatter.3
  332.7 33.1 all-reduce.6

commit v2 on v1

--- a/solution.py
+++ b/solution.py
@@ -21,6 +21,45 @@
     return cells
 
 
+def partner(axis, step):
+    return [(i, i ^ step) for i in range(lax.axis_size(axis))]
+
+
+def butterfly_sum(x, axes):
+    for axis in axes:
+        step = 1
+        while step < lax.axis_size(axis):
+            x = x + lax.ppermute(x, axis, partner(axis, step))
+            step *= 2
+    return x
+
+
+def halving_scatter(blocks, axis, dim):
+    me = lax.axis_index(axis)
+    step = 1
+    while step < lax.axis_size(axis):
+        shape = blocks.shape
+        split = blocks.reshape(shape[:dim] + (shape[dim] // 2, 2) + shape[dim + 1 :])
+        bit = (me // step) % 2
+        keep = lax.dynamic_index_in_dim(split, bit, axis=dim + 1, keepdims=False)
+        send = lax.dynamic_index_in_dim(split, 1 - bit, axis=dim + 1, keepdims=False)
+        got = lax.ppermute(send.astype(jnp.bfloat16), axis, partner(axis, step))
+        blocks = keep + got.astype(jnp.float32)
+        step *= 2
+    return blocks
+
+
+def doubling_gather(x, axis):
+    me = lax.axis_index(axis)
+    step = 1
+    while step < lax.axis_size(axis):
+        other = lax.ppermute(x, axis, partner(axis, step))
+        first = (me // step) % 2 == 0
+        x = jnp.where(first, jnp.concatenate([x, other]), jnp.concatenate([other, x]))
+        step *= 2
+    return x
+
+
 def on_device(volume, out_grad, kernel, sample_idx, a_inverse, g_inverse):
     highest = lax.Precision.HIGHEST
     f32 = jnp.float32
@@ -30,9 +69,12 @@
     x_cells = volume.shape[4]
     cells = planes * y_cells * x_cells
     patch = kernel.shape[1]
+    n_taps = patch // channels
     n_dp = lax.axis_size("dp")
     n_sp = lax.axis_size("space")
     contract_cells = (((1,), (1,)), ((), ()))
+
+    full_inverse = doubling_gather(a_inverse, "space")
 
     block = padded_2(volume, (("space", 2),), 1)
     padded = jnp.pad(block[0], ((0, 0), (0, 0), (1, 1), (1, 1)))
@@ -42,13 +84,21 @@
         for dy in range(3)
         for dx in range(3)
     ]
-    patches_t = jnp.stack(taps, axis=1).reshape(patch, cells)
+    patches_t = jnp.stack(taps, axis=0).reshape(patch, cells)
     grad_flat = out_grad[0].reshape(channels, cells)
+    kernel_perm = kernel.reshape(channels, channels, n_taps).transpose(0, 2, 1).reshape(channels, patch)
 
-    forward = jnp.dot(kernel, patches_t, preferred_element_type=f32)
+    grad_perm = lax.dot_general(grad_flat, patches_t, contract_cells, preferred_element_type=f32)
+    grad_w = grad_perm.reshape(channels, n_taps, channels).transpose(0, 2, 1).reshape(channels, patch)
+    g_part = lax.dot_general(grad_flat, grad_flat, contract_cells, preferred_element_type=f32)
+    both = butterfly_sum(jnp.concatenate([grad_w, g_part], axis=1), ("dp", "space"))
+    grad_sum = both[:, :patch]
+    g_factor = both[:, patch:]
+    left = jnp.dot(g_inverse, grad_sum, precision=highest)
+    pre_grad = jnp.dot(left, full_inverse, precision=highest)
+
+    forward = jnp.dot(kernel_perm, patches_t, preferred_element_type=f32)
     conv_out = forward.astype(jnp.bfloat16).reshape(1, channels, planes, y_cells, x_cells)
-    grad_w = lax.dot_general(grad_flat, patches_t, contract_cells, preferred_element_type=f32)
-    g_part = lax.dot_general(grad_flat, grad_flat, contract_cells, preferred_element_type=f32)
 
     cell_ids = sample_idx[0]
     counts = jnp.sum(
@@ -58,28 +108,17 @@
     high = weighted.astype(jnp.bfloat16)
     low = (weighted - high.astype(f32)).astype(jnp.bfloat16)
     total_samples = sample_idx.shape[1] * n_sp * n_dp
-    a_part = (
+    a_perm = (
         lax.dot_general(high, patches_t, contract_cells, preferred_element_type=f32)
         + lax.dot_general(low, patches_t, contract_cells, preferred_element_type=f32)
     ) / jnp.float32(total_samples)
+    a_part = (
+        a_perm.reshape(n_taps, channels, n_taps, channels).transpose(1, 0, 3, 2).reshape(patch, patch)
+    )
     rows = patch // n_dp
     cols = patch // n_sp
-    a_blocks = (
-        a_part.astype(jnp.bfloat16)
-        .reshape(n_dp, rows, n_sp, cols)
-        .transpose(0, 2, 1, 3)
-        .reshape(n_dp * n_sp, rows, cols)
-    )
-    a_factor = lax.psum_scatter(a_blocks, ("dp", "space"), scatter_dimension=0, tiled=True)
-    a_factor = a_factor.reshape(rows, cols).astype(f32)
-
-    both = lax.psum(jnp.concatenate([grad_w, g_part], axis=1), ("dp", "space"))
-    grad_sum = both[:, :patch]
-    g_factor = both[:, patch:]
-    left = jnp.dot(g_inverse, grad_sum, precision=highest)
-    own_rows = a_inverse.shape[0]
-    left_rows = lax.dynamic_slice_in_dim(left, lax.axis_index("space") * own_rows, own_rows, axis=1)
-    pre_grad = lax.psum(jnp.dot(left_rows, a_inverse, precision=highest), "space")
+    a_rows = halving_scatter(a_part.reshape(n_dp, rows, patch), "dp", 0)
+    a_factor = halving_scatter(a_rows.reshape(rows, n_sp, cols), "space", 1).reshape(rows, cols)
     return (conv_out, a_factor, g_factor, pre_grad)
 
 

time: 375 us -> 268 us (0.71)
  waiting for transfers between devices: 224 us -> 77 us
  local copies, waits for them, and re-layouts: 71.4 us -> 108 us
  starting transfers between devices: 6.35 us -> 21.7 us
  between operations: 14 us -> 0.91 us
    psum x2 -> x0, waiting for transfers between devices: 132 us -> none  [the longest x1 97.5 us: on_device(): both = lax.psum(jnp.concatenate([grad_w, g_part], axis=1), ('dp', 'space'))]
    unnamed x4 -> x0, waiting for transfers between devices: 92 us -> none
    ppermute x0 -> x12, waiting for transfers between devices: none -> 74.9 us  [the longest x5 42.4 us: butterfly_sum(): x = x + lax.ppermute(x, axis, partner(axis, step))]
    unnamed x36 -> x39, local copies, waits for them, and re-layouts: 6.94 us -> 23.5 us
    transpose x1 -> x3, local copies, waits for them, and re-layouts: 2.55 us -> 18.3 us  [the longest x1 15.9 us: on_device(): a_perm.reshape(n_taps, channels, n_taps, channels).transpose(1, 0, 3, 2)]
    ppermute x0 -> x12, starting transfers between devices: none -> 15.4 us  [the longest x5 7.94 us: halving_scatter(): got = lax.ppermute(send.astype(jnp.bfloat16), axis, partner(axis, step))]
    reshape x2 -> x6, local copies, waits for them, and re-layouts: 16.2 us -> 25.3 us  [the longest x1 11.6 us: on_device(): patches_t = jnp.stack(taps, axis=0).reshape(patch, cells)]
    another operation x2, local copies, waits for them, and re-layouts: 4.78 us -> 13.6 us  [the longest x1 12.8 us: halving_scatter(): split = blocks.reshape(shape[:dim] + (shape[dim] // 2, 2) + shape[dim + 1:])]
  transfers between devices with their start and end apart: 5 -> 14, of which waited for: 3 -> 7; matrix products, arithmetic and copies ran while one was open for 10% -> 11% of each run, Pallas kernels for 0% -> 0%
where the time goes in v2:
time: 268 us; the launch traced here: 266 us
  local copies, waits for them, and re-layouts  108 us (40%)
  waiting for transfers between devices  77 us (29%)
  matrix products  36.4 us (14%)
  other arithmetic  21.8 us (8%)
  starting transfers between devices  21.7 us (8%)
    ppermute x5, waiting for transfers between devices, butterfly_sum(): x = x + lax.ppermute(x, axis, partner(axis, step))  42.4 us
    ppermute x5, waiting for transfers between devices, halving_scatter(): got = lax.ppermute(send.astype(jnp.bfloat16), axis, partner(axis, step))  32.5 us
    unnamed x39, local copies, waits for them, and re-layouts  23.5 us
    transpose x1, local copies, waits for them, and re-layouts, on_device(): a_perm.reshape(n_taps, channels, n_taps, channels).transpose(1, 0, 3, 2)  15.9 us
    another operation x1, local copies, waits for them, and re-layouts, halving_scatter(): split = blocks.reshape(shape[:dim] + (shape[dim] // 2, 2) + shape[dim + 1:])  12.8 us
    convert_element_type x1, other arithmetic, on_device(): low = (weighted - high.astype(f32)).astype(jnp.bfloat16)  12 us
    convert_element_type x1, local copies, waits for them, and re-layouts, on_device(): high = weighted.astype(jnp.bfloat16)  11.7 us
    reshape x1, local copies, waits for them, and re-layouts, on_device(): patches_t = jnp.stack(taps, axis=0).reshape(patch, cells)  11.6 us
  transfers between devices with their start and end apart: 14, of which 7 were waited for; matrix products, arithmetic and copies ran while one was open for 11% of the time, Pallas kernels for 0%

profile of v2, /device:TPU:0, one launch (start us, length us, event | category | flops | bytes accessed | tf_op | source)
XLA Modules:
  0.0 266.2 jit_solution(3165617046899434170)
XLA Ops:
  1.6 4.9 %collective-permute-start = (bf16[1,32,1,16,128]{4,3,2,1,0:T(8,128)(2,1)S(1)}, bf16[1,32,1,16,128]{4,3,2,1,0:T(8,128)(2,1)S(1)}, u32[]{:S(2)}, u32[]{:S(2)}) collective-permute-start(bf16[1,32,1,16,128]{4,3,2,1,0:T(8,128)(2,1)S(1)} %get-tuple-element.6), channel_id=1, source_target_pairs={{0,1},{1,2},{2,3},{4,5},{5,6},{6,7},{8,9},{9,10},{10,11},{12,13},{... | collective-permute-start | bytes 393224 | tf_op jit(solution)/shard_map/ppermute | solution.py:15
  6.6 1.3 collective-permute-start.1
  7.9 3.4 %convert_reduce_fusion = f32[4096]{0:T(1024)S(1)} fusion(s32[1024]{0:T(1024)} %bitcast.175), kind=kLoop, calls=%fused_computation | loop fusion | flops 12578816 | bytes 20480 | tf_op jit(solution)/shard_map/reduce_sum | solution.py:104
  11.3 2.2 collective-permute-done.1
  36.8 11.6 %reshape.123 = bf16[864,4096]{1,0:T(8,128)(2,1)} reshape(bf16[27,32,2,16,128]{4,3,2,1,0:T(8,128)(2,1)} %fusion.58) | data formatting | bytes 14155776 | tf_op jit(solution)/shard_map/reshape | solution.py:87
  48.4 12.0 %subtract_convert_fusion = (bf16[27,32,2,16,128]{4,3,2,1,0:T(8,128)(2,1)}, bf16[27,32,2,16,128]{4,3,2,1,0:T(8,128)(2,1)}) fusion(bf16[27,32,2,16,128]{4,3,2,1,0:T(8,128)(2,1)} %fusion.58, f32[2,16,128]{2,1,0:T(8,128)S(1)} %bitcast.174), kind=kLoop, calls=%fused_computation.2 | loop fusion | flops 21233664 | bytes 21250048 | tf_op jit(solution)/shard_map/convert_element_type | solution.py:109
  60.4 11.6 %convert_element_type.120 = bf16[864,4096]{1,0:T(8,128)(2,1)} reshape(bf16[27,32,2,16,128]{4,3,2,1,0:T(8,128)(2,1)} %get-tuple-element.4) | data formatting | bytes 14155776 | tf_op jit(solution)/shard_map/convert_element_type | solution.py:109
  72.0 11.7 %convert_element_type.117 = bf16[864,4096]{1,0:T(8,128)(2,1)} reshape(bf16[27,32,2,16,128]{4,3,2,1,0:T(8,128)(2,1)} %get-tuple-element.5) | data formatting | bytes 14155776 | tf_op jit(solution)/shard_map/convert_element_type | solution.py:108
  83.7 11.2 %fusion.68 = f32[864,864]{1,0:T(8,128)S(1)} fusion(bf16[864,4096]{1,0:T(8,128)(2,1)} %convert_element_type.117, bf16[864,4096]{1,0:T(8,128)(2,1)} %reshape.123), kind=kOutput, calls=%fused_computation.117 | convolution fusion | flops 6115295232 | bytes 17141760 | tf_op jit(solution)/shard_map/dot_general | solution.py:112
  95.0 9.2 %add_multiply_fusion = f32[864,864]{1,0:T(8,128)} fusion(f32[864,864]{1,0:T(8,128)S(1)} %fusion.68, bf16[864,4096]{1,0:T(8,128)(2,1)S(1)} %copy-done.1, bf16[864,4096]{1,0:T(8,128)(2,1)S(1)} %bitcast.164), kind=kOutput, calls=%fused_computation.37 | convolution fusion | flops 6116788224 | bytes 20127744 | tf_op jit(solution)/shard_map/dot_general | solution.py:113
  104.1 9.7 %reshape.127 = f32[27,32,27,32]{3,2,1,0:T(8,128)} reshape(f32[864,864]{1,0:T(8,128)} %add_multiply_fusion) | data formatting | bytes 5971968 | tf_op jit(solution)/shard_map/reshape | solution.py:116
  113.8 15.9 %copy.35 = f32[32,27,32,27]{3,2,1,0:T(8,128)} copy(f32[32,27,32,27]{2,3,0,1:T(8,128)} %bitcast.165) | data formatting | bytes 5971968 | tf_op jit(solution)/shard_map/transpose | solution.py:116
  129.7 12.8 %reshape_reshape_reshape.3 = f32[4,2,108,864]{3,2,1,0:T(8,128)S(1)} reshape(f32[32,27,32,27]{3,2,1,0:T(8,128)} %copy.35) | data formatting | bytes 5971968 | tf_op jit(solution)/shard_map/reshape;reshape;reshape | solution.py:42
  143.8 1.6 collective-permute-start.12
  146.4 1.3 convolution_bitcast_fusion.1
  147.7 5.8 %convolution_bitcast_fusion = f32[32,864]{1,0:T(8,128)} fusion(bf16[864,4096]{1,0:T(8,128)(2,1)} %reshape.123, bf16[32,4096]{1,0:T(8,128)(2,1)S(1)} %reshape_squeeze.3), kind=kOutput, calls=%fused_computation.43 | convolution fusion | flops 226492416 | bytes 7450624 | tf_op jit(solution)/shard_map/dot_general | solution.py:91
  153.5 1.9 reshape.130
  155.4 2.1 copy.39
  157.5 1.3 reshape.131
  161.6 1.6 collective-permute-start.3
  163.8 11.8 %collective-permute-done.8 = f32[32,896]{1,0:T(8,128)S(1)} collective-permute-done((f32[32,896]{1,0:T(8,128)S(1)}, f32[32,896]{1,0:T(8,128)S(1)}, u32[]{:S(2)}, u32[]{:S(2)}) %collective-permute-start.8) | collective-permute-done | bytes 114720 | tf_op jit(solution)/shard_map/ppermute | solution.py:32
  175.6 1.6 collective-permute-start.9
  177.2 3.3 %collective-permute-done.9 = f32[32,896]{1,0:T(8,128)S(1)} collective-permute-done((f32[32,896]{1,0:T(8,128)S(1)}, f32[32,896]{1,0:T(8,128)S(1)}, u32[]{:S(2)}, u32[]{:S(2)}) %collective-permute-start.9) | collective-permute-done | bytes 114720 | tf_op jit(solution)/shard_map/ppermute | solution.py:32
  182.3 1.6 collective-permute-start.4
  185.4 2.4 collective-permute-start.11
  187.7 2.0 maximum_select_fusion.2
  190.8 1.3 collective-permute-start.5
  192.1 4.3 %fusion.8 = bf16[4,8,32,128]{3,1,2,0:T(8,128)(2,1)S(1)} fusion(bf16[32,864]{1,0:T(8,128)(2,1)S(1)} %reshape.125, bf16[864,4096]{1,0:T(8,128)(2,1)} %reshape.123), kind=kOutput, calls=%fused_computation.42 | convolution fusion | flops 226623488 | bytes 7395328 | tf_op jit(solution)/shard_map/dot_general | solution.py:100
  197.2 27.0 %collective-permute-done.11 = f32[32,896]{1,0:T(8,128)S(1)} collective-permute-done((f32[32,896]{1,0:T(8,128)S(1)}, f32[32,896]{1,0:T(8,128)S(1)}, u32[]{:S(2)}, u32[]{:S(2)}) %collective-permute-start.11) | collective-permute-done | bytes 114720 | tf_op jit(solution)/shard_map/ppermute | solution.py:32
  224.7 3.4 %collective-permute-start.6 = (bf16[108,1,216]{0,2,1:T(8,128)(2,1)S(1)}, bf16[108,1,216]{0,2,1:T(8,128)(2,1)S(1)}, u32[]{:S(2)}, u32[]{:S(2)}) collective-permute-start(bf16[108,1,216]{0,2,1:T(8,128)(2,1)S(1)} %dynamic-slice_convert_fusion.4), channel_id=1, source_target_pairs={{0,2},{1,3},{2,0},{3,1},{4,6},{5,7},{6,4},{7,5},{8,10},{9,11},{10,... | collective-permute-start | bytes 139976 | tf_op jit(solution)/shard_map/ppermute | solution.py:46
  229.1 32.0 %collective-permute-done.6 = bf16[108,1,216]{0,2,1:T(8,128)(2,1)S(1)} collective-permute-done((bf16[108,1,216]{0,2,1:T(8,128)(2,1)S(1)}, bf16[108,1,216]{0,2,1:T(8,128)(2,1)S(1)}, u32[]{:S(2)}, u32[]{:S(2)}) %collective-permute-start.6) | collective-permute-done | bytes 46688 | tf_op jit(solution)/shard_map/ppermute | solution.py:46
  261.7 4.4 %fusion.1 = f32[32,864]{1,0:T(8,128)} fusion(f32[864,32]{0,1:T(8,128)S(1)} %fusion.63, f32[432,864]{1,0:T(8,128)} %collective-permute-done.13, f32[432,864]{1,0:T(8,128)S(1)} %maximum_select_fusion.2, pred[]{:T(512)S(6)} %eq.33), kind=kOutput, calls=%fused_computation.31 | convolution fusion | flops 288893952 | bytes 3207169 | tf_op jit(solution)/shard_map/dot_general | solution.py:98
  (81 shorter events, 37.2 us)
Async XLA Ops:
  0.6 227.5 %copy-start = (f32[32,32]{1,0:T(8,128)S(1)}, f32[32,32]{1,0:T(8,128)}, u32[]{:S(2)}) copy-start(f32[32,32]{1,0:T(8,128)} %param.11) | copy-start | bytes 12292
  1.6 9.6 %collective-permute-start = (bf16[1,32,1,16,128]{4,3,2,1,0:T(8,128)(2,1)S(1)}, bf16[1,32,1,16,128]{4,3,2,1,0:T(8,128)(2,1)S(1)}, u32[]{:S(2)}, u32[]{:S(2)}) collective-permute-start(bf16[1,32,1,16,128]{4,3,2,1,0:T(8,128)(2,1)S(1)} %get-tuple-element.6), channel_id=1, source_target_pairs={{0,1},{1,2},{2,3},{4,5},{5,6},{6,7},{8,9},{9,10},{10,11},{12,13},{... | collective-permute-start | bytes 393224 | tf_op jit(solution)/shard_map/ppermute | solution.py:15
  6.6 6.9 %collective-permute-start.1 = (bf16[1,32,1,16,128]{4,3,2,1,0:T(8,128)(2,1)S(1)}, bf16[1,32,1,16,128]{4,3,2,1,0:T(8,128)(2,1)S(1)}, u32[]{:S(2)}, u32[]{:S(2)}) collective-permute-start(bf16[1,32,1,16,128]{4,3,2,1,0:T(8,128)(2,1)S(1)} %get-tuple-element.7), channel_id=1, source_target_pairs={{1,0},{2,1},{3,2},{5,4},{6,5},{7,6},{9,8},{10,9},{11,10},{13,12},{... | collective-permute-start | bytes 393224 | tf_op jit(solution)/shard_map/ppermute | solution.py:17
  72.0 23.0 %slice-start = ((s8[7077888]{0:T(1024)(128)(4,1)}), s8[2883584]{0:T(1024)(128)(4,1)S(1)}, s32[]{:S(2)}) async-start(s8[7077888]{0:T(1024)(128)(4,1)} %bitcast.163), calls=%async_computation | async-start | bytes 5767168
  83.7 11.2 %slice-start.1 = ((s8[7077888]{0:T(1024)(128)(4,1)}), s8[4194304]{0:T(1024)(128)(4,1)S(1)}, s32[]{:S(2)}) async-start(s8[7077888]{0:T(1024)(128)(4,1)} %bitcast.163), calls=%async_computation.1 | async-start | bytes 8388608
  83.7 11.2 %copy-start.1 = (bf16[864,4096]{1,0:T(8,128)(2,1)S(1)}, bf16[864,4096]{1,0:T(8,128)(2,1)}, u32[]{:S(2)}) copy-start(bf16[864,4096]{1,0:T(8,128)(2,1)} %convert_element_type.120) | copy-start | bytes 21233668
  143.8 15.3 %collective-permute-start.2 = (bf16[4,108,864]{2,0,1:T(4,128)(2,1)}, bf16[4,108,864]{2,0,1:T(4,128)(2,1)}, u32[]{:S(2)}, u32[]{:S(2)}) collective-permute-start(bf16[4,108,864]{2,0,1:T(4,128)(2,1)} %copy.36), channel_id=1, source_target_pairs={{0,4},{4,0},{8,12},{12,8},{16,20},{20,16},{24,28},{28,24},{1,5},{5... | collective-permute-start | bytes 2239496 | tf_op jit(solution)/shard_map/ppermute | solution.py:46
  143.8 44.0 %collective-permute-start.12 = (f32[216,864]{1,0:T(8,128)}, f32[216,864]{1,0:T(8,128)}, u32[]{:S(2)}, u32[]{:S(2)}) collective-permute-start(f32[216,864]{1,0:T(8,128)} %param.10), channel_id=1, source_target_pairs={{0,1},{1,0},{2,3},{3,2},{4,5},{5,4},{6,7},{7,6},{8,9},{9,8},{10,11... | collective-permute-start | bytes 2239496 | tf_op jit(solution)/shard_map/ppermute | solution.py:56
  153.5 30.4 %copy-start.3 = (bf16[32,864]{1,0:T(8,128)(2,1)S(1)}, bf16[32,864]{1,0:T(8,128)(2,1)}, u32[]{:S(2)}) copy-start(bf16[32,864]{1,0:T(8,128)(2,1)} %param.8) | copy-start | bytes 165892
  158.9 4.3 %collective-permute-start.7 = (f32[32,896]{1,0:T(8,128)S(1)}, f32[32,896]{1,0:T(8,128)S(1)}, u32[]{:S(2)}, u32[]{:S(2)}) collective-permute-start(f32[32,896]{1,0:T(8,128)S(1)} %pad_maximum_fusion), channel_id=1, source_target_pairs={{0,4},{4,0},{8,12},{12,8},{16,20},{20,16},{24,28},{28,24},{1,5},{5... | collective-permute-start | bytes 344072 | tf_op jit(solution)/shard_map/ppermute | solution.py:32
  160.4 1.2 copy-start.2
  161.6 19.4 %collective-permute-start.3 = (bf16[2,108,864]{2,1,0:T(8,128)(2,1)S(1)}, bf16[2,108,864]{2,1,0:T(8,128)(2,1)S(1)}, u32[]{:S(2)}, u32[]{:S(2)}) collective-permute-start(bf16[2,108,864]{2,1,0:T(8,128)(2,1)S(1)} %fusion.10), channel_id=1, source_target_pairs={{0,8},{4,12},{8,0},{12,4},{16,24},{20,28},{24,16},{28,20},{1,9},{5... | collective-permute-start | bytes 1119752 | tf_op jit(solution)/shard_map/ppermute | solution.py:46
  163.2 12.4 %collective-permute-start.8 = (f32[32,896]{1,0:T(8,128)S(1)}, f32[32,896]{1,0:T(8,128)S(1)}, u32[]{:S(2)}, u32[]{:S(2)}) collective-permute-start(f32[32,896]{1,0:T(8,128)S(1)} %fusion.79), channel_id=1, source_target_pairs={{0,8},{4,12},{8,0},{12,4},{16,24},{20,28},{24,16},{28,20},{1,9},{5... | collective-permute-start | bytes 344072 | tf_op jit(solution)/shard_map/ppermute | solution.py:32
  175.6 4.9 %collective-permute-start.9 = (f32[32,896]{1,0:T(8,128)S(1)}, f32[32,896]{1,0:T(8,128)S(1)}, u32[]{:S(2)}, u32[]{:S(2)}) collective-permute-start(f32[32,896]{1,0:T(8,128)S(1)} %add.120), channel_id=1, source_target_pairs={{0,16},{4,20},{8,24},{12,28},{16,0},{20,4},{24,8},{28,12},{1,17},{... | collective-permute-start | bytes 344072 | tf_op jit(solution)/shard_map/ppermute | solution.py:32
  180.5 4.9 %collective-permute-start.10 = (f32[32,896]{1,0:T(8,128)S(1)}, f32[32,896]{1,0:T(8,128)S(1)}, u32[]{:S(2)}, u32[]{:S(2)}) collective-permute-start(f32[32,896]{1,0:T(8,128)S(1)} %add.121), channel_id=1, source_target_pairs={{0,1},{1,0},{2,3},{3,2},{4,5},{5,4},{6,7},{7,6},{8,9},{9,8},{10,11... | collective-permute-start | bytes 344072 | tf_op jit(solution)/shard_map/ppermute | solution.py:32
  182.3 8.2 %collective-permute-start.4 = (bf16[1,108,864]{2,1,0:T(8,128)(2,1)S(1)}, bf16[1,108,864]{2,1,0:T(8,128)(2,1)S(1)}, u32[]{:S(2)}, u32[]{:S(2)}) collective-permute-start(bf16[1,108,864]{2,1,0:T(8,128)(2,1)S(1)} %dynamic-slice_convert_fusion.2), channel_id=1, source_target_pairs={{0,16},{4,20},{8,24},{12,28},{16,0},{20,4},{24,8},{28,12},{1,17},{... | collective-permute-start | bytes 559880 | tf_op jit(solution)/shard_map/ppermute | solution.py:46
  185.4 38.8 %collective-permute-start.11 = (f32[32,896]{1,0:T(8,128)S(1)}, f32[32,896]{1,0:T(8,128)S(1)}, u32[]{:S(2)}, u32[]{:S(2)}) collective-permute-start(f32[32,896]{1,0:T(8,128)S(1)} %add.122), channel_id=1, source_target_pairs={{0,2},{1,3},{2,0},{3,1},{4,6},{5,7},{6,4},{7,5},{8,10},{9,11},{10,... | collective-permute-start | bytes 344072 | tf_op jit(solution)/shard_map/ppermute | solution.py:32
  189.8 71.9 %collective-permute-start.13 = (f32[432,864]{1,0:T(8,128)S(1)}, f32[432,864]{1,0:T(8,128)}, u32[]{:S(2)}, u32[]{:S(2)}) collective-permute-start(f32[432,864]{1,0:T(8,128)S(1)} %maximum_select_fusion.2), channel_id=1, source_target_pairs={{0,2},{1,3},{2,0},{3,1},{4,6},{5,7},{6,4},{7,5},{8,10},{9,11},{10,... | collective-permute-start | bytes 4478984 | tf_op jit(solution)/shard_map/ppermute | solution.py:56
  190.8 33.9 %collective-permute-start.5 = (bf16[108,2,216]{0,2,1:T(8,128)(2,1)S(1)}, bf16[108,2,216]{0,2,1:T(8,128)(2,1)S(1)}, u32[]{:S(2)}, u32[]{:S(2)}) collective-permute-start(bf16[108,2,216]{0,2,1:T(8,128)(2,1)S(1)} %fusion.65), channel_id=1, source_target_pairs={{0,1},{1,0},{2,3},{3,2},{4,5},{5,4},{6,7},{7,6},{8,9},{9,8},{10,11... | collective-permute-start | bytes 279944 | tf_op jit(solution)/shard_map/ppermute | solution.py:46
  224.7 36.4 %collective-permute-start.6 = (bf16[108,1,216]{0,2,1:T(8,128)(2,1)S(1)}, bf16[108,1,216]{0,2,1:T(8,128)(2,1)S(1)}, u32[]{:S(2)}, u32[]{:S(2)}) collective-permute-start(bf16[108,1,216]{0,2,1:T(8,128)(2,1)S(1)} %dynamic-slice_convert_fusion.4), channel_id=1, source_target_pairs={{0,2},{1,3},{2,0},{3,1},{4,6},{5,7},{6,4},{7,5},{8,10},{9,11},{10,... | collective-permute-start | bytes 139976 | tf_op jit(solution)/shard_map/ppermute | solution.py:46

commit v3 on v2

--- a/solution.py
+++ b/solution.py
@@ -1,3 +1,5 @@
+import math
+
 import jax
 import jax.numpy as jnp
 from jax import lax
@@ -72,24 +74,34 @@
     n_taps = patch // channels
     n_dp = lax.axis_size("dp")
     n_sp = lax.axis_size("space")
+    row_ch = channels // n_dp
+    col_ch = channels // n_sp
+    grain = math.gcd(row_ch, col_ch)
+    n_grains = channels // grain
     contract_cells = (((1,), (1,)), ((), ()))
 
-    full_inverse = doubling_gather(a_inverse, "space")
+    full_inverse = lax.all_gather(a_inverse, "space", axis=0, tiled=True)
 
     block = padded_2(volume, (("space", 2),), 1)
     padded = jnp.pad(block[0], ((0, 0), (0, 0), (1, 1), (1, 1)))
+    grains = padded.reshape((n_grains, grain) + padded.shape[1:])
     taps = [
-        padded[:, dz : dz + planes, dy : dy + y_cells, dx : dx + x_cells]
+        grains[:, :, dz : dz + planes, dy : dy + y_cells, dx : dx + x_cells]
         for dz in range(3)
         for dy in range(3)
         for dx in range(3)
     ]
-    patches_t = jnp.stack(taps, axis=0).reshape(patch, cells)
+    patches_t = jnp.stack(taps, axis=1).reshape(patch, cells)
+    patches_t = lax.optimization_barrier(patches_t)
     grad_flat = out_grad[0].reshape(channels, cells)
-    kernel_perm = kernel.reshape(channels, channels, n_taps).transpose(0, 2, 1).reshape(channels, patch)
+    kernel_perm = (
+        kernel.reshape(channels, n_grains, grain, n_taps).transpose(0, 1, 3, 2).reshape(channels, patch)
+    )
 
     grad_perm = lax.dot_general(grad_flat, patches_t, contract_cells, preferred_element_type=f32)
-    grad_w = grad_perm.reshape(channels, n_taps, channels).transpose(0, 2, 1).reshape(channels, patch)
+    grad_w = (
+        grad_perm.reshape(channels, n_grains, n_taps, grain).transpose(0, 1, 3, 2).reshape(channels, patch)
+    )
     g_part = lax.dot_general(grad_flat, grad_flat, contract_cells, preferred_element_type=f32)
     both = butterfly_sum(jnp.concatenate([grad_w, g_part], axis=1), ("dp", "space"))
     grad_sum = both[:, :patch]
@@ -112,13 +124,21 @@
         lax.dot_general(high, patches_t, contract_cells, preferred_element_type=f32)
         + lax.dot_general(low, patches_t, contract_cells, preferred_element_type=f32)
     ) / jnp.float32(total_samples)
-    a_part = (
-        a_perm.reshape(n_taps, channels, n_taps, channels).transpose(1, 0, 3, 2).reshape(patch, patch)
-    )
     rows = patch // n_dp
     cols = patch // n_sp
-    a_rows = halving_scatter(a_part.reshape(n_dp, rows, patch), "dp", 0)
-    a_factor = halving_scatter(a_rows.reshape(rows, n_sp, cols), "space", 1).reshape(rows, cols)
+    a_blocks = (
+        a_perm.astype(jnp.bfloat16)
+        .reshape(n_dp, rows, n_sp, cols)
+        .transpose(0, 2, 1, 3)
+        .reshape(n_dp * n_sp, rows, cols)
+    )
+    got = lax.all_to_all(a_blocks, ("dp", "space"), 0, 0, tiled=True)
+    a_own = jnp.sum(got.astype(f32), axis=0)
+    a_factor = (
+        a_own.reshape(row_ch // grain, n_taps, grain, col_ch // grain, n_taps, grain)
+        .transpose(0, 2, 1, 3, 5, 4)
+        .reshape(rows, cols)
+    )
     return (conv_out, a_factor, g_factor, pre_grad)
 
 

time: 268 us -> 154 us (0.57)
  local copies, waits for them, and re-layouts: 108 us -> 53.4 us
  waiting for transfers between devices: 77 us -> 26.6 us
  other arithmetic: 21.8 us -> 5.58 us
  between operations: 0.91 us -> 14.2 us
  matrix products: 36.4 us -> 33.3 us
    ppermute x7 -> x0, waiting for transfers between devices: 32.5 us -> none  [the longest x5 32.5 us: halving_scatter(): got = lax.ppermute(send.astype(jnp.bfloat16), axis, partner(axis, step))]
    convert_element_type x8 -> x0, local copies, waits for them, and re-layouts: 24.7 us -> none  [the longest x1 11.7 us: on_device(): high = weighted.astype(jnp.bfloat16)]
    ppermute x5, waiting for transfers between devices: 42.4 us -> 24.4 us  [butterfly_sum(): x = x + lax.ppermute(x, axis, partner(axis, step))]
    transpose x3, local copies, waits for them, and re-layouts: 18.3 us -> 3.42 us  [the longest x1 2.4 us: on_device(): a_factor = a_own.reshape(row_ch // grain, n_taps, grain, col_ch // grain,...]
    another operation x2 -> x1, local copies, waits for them, and re-layouts: 13.6 us -> 0.98 us  [on_device(): patches_t = jnp.stack(taps, axis=1).reshape(patch, cells)]
    convert_element_type x1 -> x0, other arithmetic: 12 us -> none  [on_device(): low = (weighted - high.astype(f32)).astype(jnp.bfloat16)]
    ppermute x7 -> x0, starting transfers between devices: 10.2 us -> none  [the longest x5 7.94 us: halving_scatter(): got = lax.ppermute(send.astype(jnp.bfloat16), axis, partner(axis, step))]
    all_to_all x0 -> x1, starting transfers between devices: none -> 5.11 us  [on_device(): got = lax.all_to_all(a_blocks, ('dp', 'space'), 0, 0, tiled=True)]
  transfers between devices with their start and end apart: 14 -> 9, of which waited for: 7 -> 6; matrix products, arithmetic and copies ran while one was open for 11% -> 57% of each run, Pallas kernels for 0% -> 0%
where the time goes in v3:
time: 154 us; the launch traced here: 153 us
  local copies, waits for them, and re-layouts  53.4 us (35%)
  matrix products  33.3 us (22%)
  waiting for transfers between devices  26.6 us (17%)
  starting transfers between devices  20.2 us (13%)
  between operations  14.2 us (9%)
  other arithmetic  5.58 us (4%)
    ppermute x5, waiting for transfers between devices, butterfly_sum(): x = x + lax.ppermute(x, axis, partner(axis, step))  24.4 us
    unnamed x35, local copies, waits for them, and re-layouts  23.5 us
    reshape x1, local copies, waits for them, and re-layouts, on_device(): patches_t = jnp.stack(taps, axis=1).reshape(patch, cells)  11.6 us
    dot_general x1, matrix products, on_device(): lax.dot_general(high, patches_t, contract_cells, preferred_element_type=f32)  11 us
    ppermute x5, starting transfers between devices, butterfly_sum(): x = x + lax.ppermute(x, axis, partner(axis, step))  8.84 us
    dot_general x1, matrix products, on_device(): lax.dot_general(low, patches_t, contract_cells, preferred_element_type=f32)  7.55 us
    dot_general x1, matrix products, on_device(): lax.dot_general(grad_flat, patches_t, contract_cells, preferred_element_t...  5.13 us
    all_to_all x1, starting transfers between devices, on_device(): got = lax.all_to_all(a_blocks, ('dp', 'space'), 0, 0, tiled=True)  5.11 us
  transfers between devices with their start and end apart: 9, of which 6 were waited for; matrix products, arithmetic and copies ran while one was open for 57% of the time, Pallas kernels for 0%

profile of v3, /device:TPU:0, one launch (start us, length us, event | category | flops | bytes accessed | tf_op | source)
XLA Modules:
  0.0 153.3 jit_solution(4314968996669419487)
XLA Ops:
  7.2 1.0 fusion.37
  8.2 4.9 %collective-permute-start = (bf16[1,32,1,16,128]{4,3,2,1,0:T(8,128)(2,1)S(1)}, bf16[1,32,1,16,128]{4,3,2,1,0:T(8,128)(2,1)S(1)}, u32[]{:S(2)}, u32[]{:S(2)}) collective-permute-start(bf16[1,32,1,16,128]{4,3,2,1,0:T(8,128)(2,1)S(1)} %get-tuple-element.4), channel_id=1, source_target_pairs={{0,1},{1,2},{2,3},{4,5},{5,6},{6,7},{8,9},{9,10},{10,11},{12,13},{... | collective-permute-start | bytes 393224 | tf_op jit(solution)/shard_map/ppermute | solution.py:17
  13.2 1.3 collective-permute-start.1
  14.5 3.4 %convert_reduce_fusion = f32[4096]{0:T(1024)S(1)} fusion(s32[1024]{0:T(1024)} %bitcast.235), kind=kLoop, calls=%fused_computation | loop fusion | flops 12578816 | bytes 20480 | tf_op jit(solution)/shard_map/reduce_sum | solution.py:116
  17.9 2.2 %collective-permute-done.1 = bf16[1,32,1,16,128]{4,3,2,1,0:T(8,128)(2,1)S(1)} collective-permute-done((bf16[1,32,1,16,128]{4,3,2,1,0:T(8,128)(2,1)S(1)}, bf16[1,32,1,16,128]{4,3,2,1,0:T(8,128)(2,1)S(1)}, u32[]{:S(2)}, u32[]{:S(2)}) %collective-permute-start.1) | collective-permute-done | bytes 131104 | tf_op jit(solution)/shard_map/ppermute | solution.py:19
  20.0 1.0 maximum_bitcast_fusion
  25.2 1.0 fusion.29
  26.2 1.0 fusion.28
  36.8 1.0 fusion.16
  44.7 1.0 fusion.7
  45.6 11.6 %reshape.48 = bf16[864,4096]{1,0:T(8,128)(2,1)} reshape(bf16[8,27,4,2,16,128]{5,4,3,2,1,0:T(8,128)(2,1)} %fusion.7) | data formatting | bytes 14155776 | tf_op jit(solution)/shard_map/reshape | solution.py:94
  57.3 11.0 %fusion.1 = f32[864,864]{1,0:T(8,128)S(1)} fusion(bf16[864,4096]{1,0:T(8,128)(2,1)} %reshape.48, f32[4096]{0:T(1024)S(1)} %convert_reduce_fusion), kind=kOutput, calls=%fused_computation.5 | convolution fusion | flops 6125912064 | bytes 10080256 | tf_op jit(solution)/shard_map/dot_general | solution.py:124
  68.3 7.5 %multiply_convert_fusion = bf16[864,864]{1,0:T(8,128)(2,1)S(1)} fusion(f32[864,864]{1,0:T(8,128)S(1)} %fusion.1, bf16[864,4096]{1,0:T(8,128)(2,1)S(1)} %copy-done.1, f32[4096]{0:T(1024)S(1)} %convert_reduce_fusion), kind=kOutput, calls=%fused_computation.11 | convolution fusion | flops 6138768384 | bytes 11573248 | tf_op jit(solution)/shard_map/dot_general | solution.py:125
  75.8 1.6 %reshape.52 = bf16[8,108,4,216]{3,2,1,0:T(4,128)(2,1)S(1)} reshape(bf16[864,864]{1,0:T(8,128)(2,1)S(1)} %multiply_convert_fusion) | data formatting | bytes 2985984 | tf_op jit(solution)/shard_map/reshape | solution.py:131
  77.4 2.5 %copy.105 = bf16[8,108,4,216]{1,3,2,0:T(8,128)(2,1)} copy(bf16[8,108,4,216]{3,2,1,0:T(4,128)(2,1)S(1)} %reshape.52) | data formatting | bytes 2985984 | tf_op jit(solution)/shard_map/reshape | solution.py:131
  79.9 5.1 %all-to-all-start = ((bf16[32,108,216]{1,2,0:T(8,128)(2,1)}), bf16[32,108,216]{1,2,0:T(8,128)(2,1)S(1)}, u32[]{:S(2)}, u32[]{:S(2)}) async-start(bf16[32,108,216]{1,2,0:T(8,128)(2,1)} %bitcast.60), calls=%async_computation | async-start | bytes 3538944 | tf_op jit(solution)/shard_map/all_to_all | solution.py:135
  85.4 5.1 %convolution_bitcast_fusion = f32[32,864]{1,0:T(8,128)S(1)} fusion(bf16[864,4096]{1,0:T(8,128)(2,1)} %reshape.48, bf16[32,4096]{1,0:T(8,128)(2,1)S(1)} %reshape_squeeze.3), kind=kOutput, calls=%fused_computation.13 | convolution fusion | flops 226492416 | bytes 7450624 | tf_op jit(solution)/shard_map/dot_general | solution.py:101
  92.0 1.3 collective-permute-done.2
  93.3 1.6 %collective-permute-start.3 = (f32[32,896]{1,0:T(8,128)S(1)}, f32[32,896]{1,0:T(8,128)S(1)}, u32[]{:S(2)}, u32[]{:S(2)}) collective-permute-start(f32[32,896]{1,0:T(8,128)S(1)} %fusion.48), channel_id=1, source_target_pairs={{0,8},{4,12},{8,0},{12,4},{16,24},{20,28},{24,16},{28,20},{1,9},{5... | collective-permute-start | bytes 344072 | tf_op jit(solution)/shard_map/ppermute | solution.py:34
  94.9 6.5 %collective-permute-done.3 = f32[32,896]{1,0:T(8,128)S(1)} collective-permute-done((f32[32,896]{1,0:T(8,128)S(1)}, f32[32,896]{1,0:T(8,128)S(1)}, u32[]{:S(2)}, u32[]{:S(2)}) %collective-permute-start.3) | collective-permute-done | bytes 114720 | tf_op jit(solution)/shard_map/ppermute | solution.py:34
  101.5 1.5 collective-permute-start.4
  102.9 3.9 %collective-permute-done.4 = f32[32,896]{1,0:T(8,128)S(1)} collective-permute-done((f32[32,896]{1,0:T(8,128)S(1)}, f32[32,896]{1,0:T(8,128)S(1)}, u32[]{:S(2)}, u32[]{:S(2)}) %collective-permute-start.4) | collective-permute-done | bytes 114720 | tf_op jit(solution)/shard_map/ppermute | solution.py:34
  106.9 1.2 collective-permute-start.5
  109.1 7.4 %collective-permute-done.5 = f32[32,896]{1,0:T(8,128)S(1)} collective-permute-done((f32[32,896]{1,0:T(8,128)S(1)}, f32[32,896]{1,0:T(8,128)S(1)}, u32[]{:S(2)}, u32[]{:S(2)}) %collective-permute-start.5) | collective-permute-done | bytes 114720 | tf_op jit(solution)/shard_map/ppermute | solution.py:34
  116.5 4.6 %collective-permute-start.6 = (f32[32,896]{1,0:T(8,128)S(1)}, f32[32,896]{1,0:T(8,128)S(1)}, u32[]{:S(2)}, u32[]{:S(2)}) collective-permute-start(f32[32,896]{1,0:T(8,128)S(1)} %add.24), channel_id=1, source_target_pairs={{0,2},{1,3},{2,0},{3,1},{4,6},{5,7},{6,4},{7,5},{8,10},{9,11},{10,... | collective-permute-start | bytes 344072 | tf_op jit(solution)/shard_map/ppermute | solution.py:34
  121.1 4.3 %fusion.6 = bf16[4,8,32,128]{3,1,2,0:T(8,128)(2,1)S(1)} fusion(bf16[864,4096]{1,0:T(8,128)(2,1)} %reshape.48, bf16[32,864]{0,1:T(8,128)(2,1)S(1)} %bitcast.232), kind=kOutput, calls=%fused_computation.12 | convolution fusion | flops 226623488 | bytes 7395328 | tf_op jit(solution)/shard_map/dot_general | solution.py:112
  126.1 5.3 %collective-permute-done.6 = f32[32,896]{1,0:T(8,128)S(1)} collective-permute-done((f32[32,896]{1,0:T(8,128)S(1)}, f32[32,896]{1,0:T(8,128)S(1)}, u32[]{:S(2)}, u32[]{:S(2)}) %collective-permute-start.6) | collective-permute-done | bytes 114720 | tf_op jit(solution)/shard_map/ppermute | solution.py:34
  133.0 1.0 convert_reduce_fusion.1
  134.0 3.9 %reshape.54 = f32[1,27,4,2,27,4]{2,1,5,4,3,0:T(8,128)S(1)} reshape(f32[108,216]{0,1:T(8,128)} %convert_reduce_fusion.1) | data formatting | bytes 186624 | tf_op jit(solution)/shard_map/reshape | solution.py:138
  138.0 2.4 %copy.106 = f32[1,4,27,2,4,27]{2,1,5,4,3,0:T(4,128)} copy(f32[1,4,27,2,4,27]{1,2,4,5,3,0:T(8,128)S(1)} %bitcast.229) | data formatting | bytes 186624 | tf_op jit(solution)/shard_map/transpose | solution.py:139
  140.3 1.9 %reshape.55 = f32[108,216]{0,1:T(8,128)} reshape(f32[1,4,27,2,4,27]{2,1,5,4,3,0:T(4,128)} %copy.106) | data formatting | bytes 186624 | tf_op jit(solution)/shard_map/reshape | solution.py:140
  142.2 4.2 %fusion.38 = f32[32,864]{1,0:T(8,128)} fusion(f32[864,32]{0,1:T(8,128)} %fusion.35, f32[864,864]{1,0:T(8,128)} %all-gather.2.cloned.1.call-done), kind=kOutput, calls=%fused_computation.75 | convolution fusion | flops 286654464 | bytes 3207168 | tf_op jit(solution)/shard_map/dot_general | solution.py:110
  (54 shorter events, 26.0 us)
Async XLA Ops:
  7.2 125.0 %copy-start = (f32[32,32]{1,0:T(8,128)S(1)}, f32[32,32]{1,0:T(8,128)}, u32[]{:S(2)}) copy-start(f32[32,32]{1,0:T(8,128)} %param.11) | copy-start | bytes 12292
  7.2 135.0 %all-gather.2.cloned.1.call-start = ((), (), s32[]{:S(2)}) async-start(), calls=%async_computation.1 | async-start | bytes 3870720 | tf_op jit(solution)/shard_map/all_gather | solution.py:83
  8.2 9.6 %collective-permute-start = (bf16[1,32,1,16,128]{4,3,2,1,0:T(8,128)(2,1)S(1)}, bf16[1,32,1,16,128]{4,3,2,1,0:T(8,128)(2,1)S(1)}, u32[]{:S(2)}, u32[]{:S(2)}) collective-permute-start(bf16[1,32,1,16,128]{4,3,2,1,0:T(8,128)(2,1)S(1)} %get-tuple-element.4), channel_id=1, source_target_pairs={{0,1},{1,2},{2,3},{4,5},{5,6},{6,7},{8,9},{9,10},{10,11},{12,13},{... | collective-permute-start | bytes 393224 | tf_op jit(solution)/shard_map/ppermute | solution.py:17
  13.2 6.9 %collective-permute-start.1 = (bf16[1,32,1,16,128]{4,3,2,1,0:T(8,128)(2,1)S(1)}, bf16[1,32,1,16,128]{4,3,2,1,0:T(8,128)(2,1)S(1)}, u32[]{:S(2)}, u32[]{:S(2)}) collective-permute-start(bf16[1,32,1,16,128]{4,3,2,1,0:T(8,128)(2,1)S(1)} %get-tuple-element.5), channel_id=1, source_target_pairs={{1,0},{2,1},{3,2},{5,4},{6,5},{7,6},{9,8},{10,9},{11,10},{13,12},{... | collective-permute-start | bytes 393224 | tf_op jit(solution)/shard_map/ppermute | solution.py:19
  57.3 11.0 %copy-start.1 = (bf16[864,4096]{1,0:T(8,128)(2,1)S(1)}, bf16[864,4096]{1,0:T(8,128)(2,1)}, u32[]{:S(2)}) copy-start(bf16[864,4096]{1,0:T(8,128)(2,1)} %reshape.48) | copy-start | bytes 21233668
  77.4 7.7 %copy-start.2 = (bf16[1,32,2,16,128]{4,3,2,1,0:T(8,128)(2,1)S(1)}, bf16[1,32,2,16,128]{4,3,2,1,0:T(8,128)(2,1)}, u32[]{:S(2)}) copy-start(bf16[1,32,2,16,128]{4,3,2,1,0:T(8,128)(2,1)} %param.7) | copy-start | bytes 786436
  79.9 53.1 %all-to-all-start = ((bf16[32,108,216]{1,2,0:T(8,128)(2,1)}), bf16[32,108,216]{1,2,0:T(8,128)(2,1)S(1)}, u32[]{:S(2)}, u32[]{:S(2)}) async-start(bf16[32,108,216]{1,2,0:T(8,128)(2,1)} %bitcast.60), calls=%async_computation | async-start | bytes 3538944 | tf_op jit(solution)/shard_map/all_to_all | solution.py:135
  85.1 23.0 %copy-start.3 = (bf16[32,864]{1,0:T(8,128)(2,1)S(1)}, bf16[32,864]{1,0:T(8,128)(2,1)}, u32[]{:S(2)}) copy-start(bf16[32,864]{1,0:T(8,128)(2,1)} %param.8) | copy-start | bytes 165892
  91.9 1.3 collective-permute-start.2
  93.3 8.1 %collective-permute-start.3 = (f32[32,896]{1,0:T(8,128)S(1)}, f32[32,896]{1,0:T(8,128)S(1)}, u32[]{:S(2)}, u32[]{:S(2)}) collective-permute-start(f32[32,896]{1,0:T(8,128)S(1)} %fusion.48), channel_id=1, source_target_pairs={{0,8},{4,12},{8,0},{12,4},{16,24},{20,28},{24,16},{28,20},{1,9},{5... | collective-permute-start | bytes 344072 | tf_op jit(solution)/shard_map/ppermute | solution.py:34
  101.5 5.4 %collective-permute-start.4 = (f32[32,896]{1,0:T(8,128)S(1)}, f32[32,896]{1,0:T(8,128)S(1)}, u32[]{:S(2)}, u32[]{:S(2)}) collective-permute-start(f32[32,896]{1,0:T(8,128)S(1)} %add.22), channel_id=1, source_target_pairs={{0,16},{4,20},{8,24},{12,28},{16,0},{20,4},{24,8},{28,12},{1,17},{... | collective-permute-start | bytes 344072 | tf_op jit(solution)/shard_map/ppermute | solution.py:34
  106.9 9.6 %collective-permute-start.5 = (f32[32,896]{1,0:T(8,128)S(1)}, f32[32,896]{1,0:T(8,128)S(1)}, u32[]{:S(2)}, u32[]{:S(2)}) collective-permute-start(f32[32,896]{1,0:T(8,128)S(1)} %add.23), channel_id=1, source_target_pairs={{0,1},{1,0},{2,3},{3,2},{4,5},{5,4},{6,7},{7,6},{8,9},{9,8},{10,11... | collective-permute-start | bytes 344072 | tf_op jit(solution)/shard_map/ppermute | solution.py:34
  116.5 14.9 %collective-permute-start.6 = (f32[32,896]{1,0:T(8,128)S(1)}, f32[32,896]{1,0:T(8,128)S(1)}, u32[]{:S(2)}, u32[]{:S(2)}) collective-permute-start(f32[32,896]{1,0:T(8,128)S(1)} %add.24), channel_id=1, source_target_pairs={{0,2},{1,3},{2,0},{3,1},{4,6},{5,7},{6,4},{7,5},{8,10},{9,11},{10,... | collective-permute-start | bytes 344072 | tf_op jit(solution)/shard_map/ppermute | solution.py:34
Sparse Core Ops, SparseCore 0:
  14.6 64.9 all-gather.1

commit v4 on v3

--- a/solution.py
+++ b/solution.py
@@ -62,6 +62,13 @@
     return x
 
 
+def block_order(n_grains, n_taps, grain):
+    size = n_grains * n_taps * grain
+    old = jnp.arange(size, dtype=jnp.int32)
+    new = ((old // (n_taps * grain)) * grain + old % grain) * n_taps + (old // grain) % n_taps
+    return (jnp.arange(size, dtype=jnp.int32)[:, None] == new[None, :]).astype(jnp.float32)
+
+
 def on_device(volume, out_grad, kernel, sample_idx, a_inverse, g_inverse):
     highest = lax.Precision.HIGHEST
     f32 = jnp.float32
@@ -80,7 +87,9 @@
     n_grains = channels // grain
     contract_cells = (((1,), (1,)), ((), ()))
 
-    full_inverse = lax.all_gather(a_inverse, "space", axis=0, tiled=True)
+    own = a_inverse.shape[0] // grain // n_taps
+    own_rows = a_inverse.reshape(own, grain, n_taps, patch).transpose(0, 2, 1, 3).reshape(-1, patch)
+    inverse_rows = lax.all_gather(own_rows, "space", axis=0, tiled=True)
 
     block = padded_2(volume, (("space", 2),), 1)
     padded = jnp.pad(block[0], ((0, 0), (0, 0), (1, 1), (1, 1)))
@@ -92,22 +101,20 @@
         for dx in range(3)
     ]
     patches_t = jnp.stack(taps, axis=1).reshape(patch, cells)
-    patches_t = lax.optimization_barrier(patches_t)
     grad_flat = out_grad[0].reshape(channels, cells)
     kernel_perm = (
         kernel.reshape(channels, n_grains, grain, n_taps).transpose(0, 1, 3, 2).reshape(channels, patch)
     )
 
     grad_perm = lax.dot_general(grad_flat, patches_t, contract_cells, preferred_element_type=f32)
-    grad_w = (
-        grad_perm.reshape(channels, n_grains, n_taps, grain).transpose(0, 1, 3, 2).reshape(channels, patch)
-    )
     g_part = lax.dot_general(grad_flat, grad_flat, contract_cells, preferred_element_type=f32)
-    both = butterfly_sum(jnp.concatenate([grad_w, g_part], axis=1), ("dp", "space"))
+    terms = jnp.concatenate([grad_perm, g_part], axis=1)
+    terms, patches_t = lax.optimization_barrier((terms, patches_t))
+    both = butterfly_sum(terms, ("dp", "space"))
     grad_sum = both[:, :patch]
     g_factor = both[:, patch:]
     left = jnp.dot(g_inverse, grad_sum, precision=highest)
-    pre_grad = jnp.dot(left, full_inverse, precision=highest)
+    pre_grad = jnp.dot(left, inverse_rows, precision=highest)
 
     forward = jnp.dot(kernel_perm, patches_t, preferred_element_type=f32)
     conv_out = forward.astype(jnp.bfloat16).reshape(1, channels, planes, y_cells, x_cells)
@@ -134,10 +141,10 @@
     )
     got = lax.all_to_all(a_blocks, ("dp", "space"), 0, 0, tiled=True)
     a_own = jnp.sum(got.astype(f32), axis=0)
-    a_factor = (
-        a_own.reshape(row_ch // grain, n_taps, grain, col_ch // grain, n_taps, grain)
-        .transpose(0, 2, 1, 3, 5, 4)
-        .reshape(rows, cols)
+    a_factor = jnp.dot(
+        jnp.dot(block_order(row_ch // grain, n_taps, grain), a_own, precision=highest),
+        block_order(col_ch // grain, n_taps, grain).T,
+        precision=highest,
     )
     return (conv_out, a_factor, g_factor, pre_grad)
 

time: 154 us -> 152 us (0.987)
  local copies, waits for them, and re-layouts: 53.4 us -> 47.7 us
  waiting for transfers between devices: 26.6 us -> 32.3 us
  other arithmetic: 5.58 us -> 3.97 us
  matrix products: 33.3 us -> 31.7 us
    ppermute x5, waiting for transfers between devices: 24.4 us -> 32.2 us  [butterfly_sum(): x = x + lax.ppermute(x, axis, partner(axis, step))]
    reshape x3 -> x2, local copies, waits for them, and re-layouts: 6.3 us -> 2.38 us  [on_device(): a_inverse.reshape(own, grain, n_taps, patch).transpose(0, 2, 1, 3)]
    dot_general x1, matrix products: 11 us -> 7.49 us  [on_device(): lax.dot_general(high, patches_t, contract_cells, preferred_element_type=f32)]
    transpose x2 -> x1, local copies, waits for them, and re-layouts: 2.99 us -> 0.5 us  [on_device(): a_inverse.reshape(own, grain, n_taps, patch).transpose(0, 2, 1, 3)]
    ppermute x1, waiting for transfers between devices: 2.17 us -> 0.01 us  [padded_2(): lax.ppermute(head, axis, [((i + 1) % count, i) for i in range(ends)])]
    all_to_all x1, starting transfers between devices: 5.11 us -> 6.94 us  [on_device(): got = lax.all_to_all(a_blocks, ('dp', 'space'), 0, 0, tiled=True)]
    dot_general x1 -> x3, matrix products: 4.19 us -> 5.28 us  [the longest x1 4.12 us: on_device(): pre_grad = jnp.dot(left, inverse_rows, precision=highest)]
  transfers between devices with their start and end apart: 9 -> 9, of which waited for: 6 -> 5; matrix products, arithmetic and copies ran while one was open for 57% -> 52% of each run, Pallas kernels for 0% -> 0%
where the time goes in v4:
time: 152 us; the launch traced here: 151 us
  local copies, waits for them, and re-layouts  47.7 us (31%)
  waiting for transfers between devices  32.3 us (21%)
  matrix products  31.7 us (21%)
  starting transfers between devices  21.3 us (14%)
  between operations  14.2 us (9%)
  other arithmetic  3.97 us (3%)
    ppermute x5, waiting for transfers between devices, butterfly_sum(): x = x + lax.ppermute(x, axis, partner(axis, step))  32.2 us
    unnamed x35, local copies, waits for them, and re-layouts  23.5 us
    reshape x1, local copies, waits for them, and re-layouts, on_device(): patches_t = jnp.stack(taps, axis=1).reshape(patch, cells)  11.6 us
    ppermute x5, starting transfers between devices, butterfly_sum(): x = x + lax.ppermute(x, axis, partner(axis, step))  8.12 us
    dot_general x1, matrix products, on_device(): lax.dot_general(low, patches_t, contract_cells, preferred_element_type=f32)  7.8 us
    dot_general x1, matrix products, on_device(): lax.dot_general(high, patches_t, contract_cells, preferred_element_type=f32)  7.49 us
    all_to_all x1, starting transfers between devices, on_device(): got = lax.all_to_all(a_blocks, ('dp', 'space'), 0, 0, tiled=True)  6.94 us
    dot_general x1, matrix products, on_device(): lax.dot_general(grad_flat, patches_t, contract_cells, preferred_element_t...  5.27 us
  transfers between devices with their start and end apart: 9, of which 5 were waited for; matrix products, arithmetic and copies ran while one was open for 52% of the time, Pallas kernels for 0%

profile of v4, /device:TPU:0, one launch (start us, length us, event | category | flops | bytes accessed | tf_op | source)
XLA Modules:
  0.0 151.2 jit_solution(14418855451594103225)
XLA Ops:
  7.2 1.0 fusion.54
  8.3 4.9 %collective-permute-start = (bf16[1,32,1,16,128]{4,3,2,1,0:T(8,128)(2,1)S(1)}, bf16[1,32,1,16,128]{4,3,2,1,0:T(8,128)(2,1)S(1)}, u32[]{:S(2)}, u32[]{:S(2)}) collective-permute-start(bf16[1,32,1,16,128]{4,3,2,1,0:T(8,128)(2,1)S(1)} %get-tuple-element.8), channel_id=1, source_target_pairs={{0,1},{1,2},{2,3},{4,5},{5,6},{6,7},{8,9},{9,10},{10,11},{12,13},{... | collective-permute-start | bytes 393224 | tf_op jit(solution)/shard_map/ppermute | solution.py:17
  13.2 1.3 collective-permute-start.1
  14.5 1.2 reshape.124
  16.3 1.1 reshape.125
  17.4 3.4 %convert_reduce_fusion = f32[4096]{0:T(1024)S(1)} fusion(s32[1024]{0:T(1024)} %bitcast.229), kind=kLoop, calls=%fused_computation | loop fusion | flops 12578816 | bytes 20480 | tf_op jit(solution)/shard_map/reduce_sum | solution.py:123
  20.8 1.1 reshape_squeeze.3
  21.9 1.3 convolution_bitcast_fusion.1
  27.4 1.0 fusion.29
  28.4 1.0 fusion.28
  31.1 1.0 fusion.25
  35.3 1.0 fusion.20
  39.0 1.0 fusion.16
  44.2 1.0 fusion.10
  46.9 1.0 fusion.7
  47.8 11.6 %reshape.117 = bf16[864,4096]{1,0:T(8,128)(2,1)} reshape(bf16[8,27,4,2,16,128]{5,4,3,2,1,0:T(8,128)(2,1)} %fusion.7) | data formatting | bytes 14155776 | tf_op jit(solution)/shard_map/reshape | solution.py:103
  59.5 5.3 %convolution_bitcast_fusion = f32[32,864]{1,0:T(8,128)S(1)} fusion(bf16[864,4096]{1,0:T(8,128)(2,1)} %reshape.117, bf16[32,4096]{1,0:T(8,128)(2,1)S(1)} %reshape_squeeze.3), kind=kOutput, calls=%fused_computation.13 | convolution fusion | flops 226492416 | bytes 7450624 | tf_op jit(solution)/shard_map/dot_general | solution.py:109
  64.8 7.5 %fusion.1 = f32[864,864]{1,0:T(8,128)S(1)} fusion(bf16[864,4096]{1,0:T(8,128)(2,1)S(1)} %copy-done.1, f32[4096]{0:T(1024)S(1)} %convert_reduce_fusion), kind=kOutput, calls=%fused_computation.5 | convolution fusion | flops 6125912064 | bytes 10080256 | tf_op jit(solution)/shard_map/dot_general | solution.py:131
  72.3 7.8 %multiply_convert_fusion = bf16[864,864]{1,0:T(8,128)(2,1)S(1)} fusion(f32[864,864]{1,0:T(8,128)S(1)} %fusion.1, bf16[864,4096]{1,0:T(8,128)(2,1)S(1)} %copy-done.1, f32[4096]{0:T(1024)S(1)} %convert_reduce_fusion), kind=kOutput, calls=%fused_computation.11 | convolution fusion | flops 6138768384 | bytes 11573248 | tf_op jit(solution)/shard_map/dot_general | solution.py:132
  80.1 1.6 %reshape.122 = bf16[8,108,4,216]{3,2,1,0:T(4,128)(2,1)S(1)} reshape(bf16[864,864]{1,0:T(8,128)(2,1)S(1)} %multiply_convert_fusion) | data formatting | bytes 2985984 | tf_op jit(solution)/shard_map/reshape | solution.py:138
  81.7 2.5 %copy.103 = bf16[8,108,4,216]{1,3,2,0:T(8,128)(2,1)} copy(bf16[8,108,4,216]{3,2,1,0:T(4,128)(2,1)S(1)} %reshape.122) | data formatting | bytes 2985984 | tf_op jit(solution)/shard_map/reshape | solution.py:138
  84.2 6.9 %all-to-all-start = ((bf16[32,108,216]{1,2,0:T(8,128)(2,1)}), bf16[32,108,216]{1,2,0:T(8,128)(2,1)S(1)}, u32[]{:S(2)}, u32[]{:S(2)}) async-start(bf16[32,108,216]{1,2,0:T(8,128)(2,1)} %bitcast.64), calls=%async_computation | async-start | bytes 3538944 | tf_op jit(solution)/shard_map/all_to_all | solution.py:142
  91.5 1.1 collective-permute-done.2
  92.6 1.8 %collective-permute-start.3 = (f32[32,896]{1,0:T(8,128)S(1)}, f32[32,896]{1,0:T(8,128)S(1)}, u32[]{:S(2)}, u32[]{:S(2)}) collective-permute-start(f32[32,896]{1,0:T(8,128)S(1)} %add.113), channel_id=1, source_target_pairs={{0,8},{4,12},{8,0},{12,4},{16,24},{20,28},{24,16},{28,20},{1,9},{5... | collective-permute-start | bytes 344072 | tf_op jit(solution)/shard_map/ppermute | solution.py:34
  94.4 13.4 %collective-permute-done.3 = f32[32,896]{1,0:T(8,128)S(1)} collective-permute-done((f32[32,896]{1,0:T(8,128)S(1)}, f32[32,896]{1,0:T(8,128)S(1)}, u32[]{:S(2)}, u32[]{:S(2)}) %collective-permute-start.3) | collective-permute-done | bytes 114720 | tf_op jit(solution)/shard_map/ppermute | solution.py:34
  107.8 1.5 collective-permute-start.4
  109.3 3.9 %collective-permute-done.4 = f32[32,896]{1,0:T(8,128)S(1)} collective-permute-done((f32[32,896]{1,0:T(8,128)S(1)}, f32[32,896]{1,0:T(8,128)S(1)}, u32[]{:S(2)}, u32[]{:S(2)}) %collective-permute-start.4) | collective-permute-done | bytes 114720 | tf_op jit(solution)/shard_map/ppermute | solution.py:34
  114.4 8.6 %collective-permute-done.5 = f32[32,896]{1,0:T(8,128)S(1)} collective-permute-done((f32[32,896]{1,0:T(8,128)S(1)}, f32[32,896]{1,0:T(8,128)S(1)}, u32[]{:S(2)}, u32[]{:S(2)}) %collective-permute-start.5) | collective-permute-done | bytes 114720 | tf_op jit(solution)/shard_map/ppermute | solution.py:34
  123.0 4.4 %collective-permute-start.6 = (f32[32,896]{1,0:T(8,128)S(1)}, f32[32,896]{1,0:T(8,128)S(1)}, u32[]{:S(2)}, u32[]{:S(2)}) collective-permute-start(f32[32,896]{1,0:T(8,128)S(1)} %add.116), channel_id=1, source_target_pairs={{0,2},{1,3},{2,0},{3,1},{4,6},{5,7},{6,4},{7,5},{8,10},{9,11},{10,... | collective-permute-start | bytes 344072 | tf_op jit(solution)/shard_map/ppermute | solution.py:34
  127.4 4.3 %fusion.6 = bf16[4,8,32,128]{3,1,2,0:T(8,128)(2,1)S(1)} fusion(bf16[864,4096]{1,0:T(8,128)(2,1)} %reshape.117, bf16[32,864]{0,1:T(8,128)(2,1)S(1)} %bitcast.226), kind=kOutput, calls=%fused_computation.12 | convolution fusion | flops 226623488 | bytes 7395328 | tf_op jit(solution)/shard_map/dot_general | solution.py:119
  132.5 5.3 %collective-permute-done.6 = f32[32,896]{1,0:T(8,128)S(1)} collective-permute-done((f32[32,896]{1,0:T(8,128)S(1)}, f32[32,896]{1,0:T(8,128)S(1)}, u32[]{:S(2)}, u32[]{:S(2)}) %collective-permute-start.6) | collective-permute-done | bytes 114720 | tf_op jit(solution)/shard_map/ppermute | solution.py:34
  140.3 4.1 %fusion.55 = f32[32,864]{1,0:T(8,128)} fusion(f32[864,32]{0,1:T(8,128)S(1)} %fusion.36, f32[864,864]{1,0:T(8,128)} %all-gather.2.cloned.1.call-done), kind=kOutput, calls=%fused_computation.111 | convolution fusion | flops 286654464 | bytes 3207168 | tf_op jit(solution)/shard_map/dot_general | solution.py:117
  (55 shorter events, 23.2 us)
Async XLA Ops:
  7.2 131.3 %copy-start = (f32[32,32]{1,0:T(8,128)S(1)}, f32[32,32]{1,0:T(8,128)}, u32[]{:S(2)}) copy-start(f32[32,32]{1,0:T(8,128)} %param.11) | copy-start | bytes 12292
  7.2 16.0 %copy-start.2 = (bf16[1,32,2,16,128]{4,3,2,1,0:T(8,128)(2,1)S(1)}, bf16[1,32,2,16,128]{4,3,2,1,0:T(8,128)(2,1)}, u32[]{:S(2)}) copy-start(bf16[1,32,2,16,128]{4,3,2,1,0:T(8,128)(2,1)} %param.6) | copy-start | bytes 786436
  7.2 133.1 %all-gather.2.cloned.1.call-start = ((), (), s32[]{:S(2)}) async-start(), calls=%async_computation.1 | async-start | bytes 3870720 | tf_op jit(solution)/shard_map/all_gather | solution.py:92
  8.3 14.9 %collective-permute-start = (bf16[1,32,1,16,128]{4,3,2,1,0:T(8,128)(2,1)S(1)}, bf16[1,32,1,16,128]{4,3,2,1,0:T(8,128)(2,1)S(1)}, u32[]{:S(2)}, u32[]{:S(2)}) collective-permute-start(bf16[1,32,1,16,128]{4,3,2,1,0:T(8,128)(2,1)S(1)} %get-tuple-element.8), channel_id=1, source_target_pairs={{0,1},{1,2},{2,3},{4,5},{5,6},{6,7},{8,9},{9,10},{10,11},{12,13},{... | collective-permute-start | bytes 393224 | tf_op jit(solution)/shard_map/ppermute | solution.py:17
  13.2 9.9 %collective-permute-start.1 = (bf16[1,32,1,16,128]{4,3,2,1,0:T(8,128)(2,1)S(1)}, bf16[1,32,1,16,128]{4,3,2,1,0:T(8,128)(2,1)S(1)}, u32[]{:S(2)}, u32[]{:S(2)}) collective-permute-start(bf16[1,32,1,16,128]{4,3,2,1,0:T(8,128)(2,1)S(1)} %get-tuple-element.9), channel_id=1, source_target_pairs={{1,0},{2,1},{3,2},{5,4},{6,5},{7,6},{9,8},{10,9},{11,10},{13,12},{... | collective-permute-start | bytes 393224 | tf_op jit(solution)/shard_map/ppermute | solution.py:19
  59.5 5.4 %copy-start.1 = (bf16[864,4096]{1,0:T(8,128)(2,1)S(1)}, bf16[864,4096]{1,0:T(8,128)(2,1)}, u32[]{:S(2)}) copy-start(bf16[864,4096]{1,0:T(8,128)(2,1)} %reshape.117) | copy-start | bytes 21233668
  80.1 33.2 %copy-start.3 = (bf16[32,864]{1,0:T(8,128)(2,1)S(1)}, bf16[32,864]{1,0:T(8,128)(2,1)}, u32[]{:S(2)}) copy-start(bf16[32,864]{1,0:T(8,128)(2,1)} %param.8) | copy-start | bytes 165892
  84.2 54.5 %all-to-all-start = ((bf16[32,108,216]{1,2,0:T(8,128)(2,1)}), bf16[32,108,216]{1,2,0:T(8,128)(2,1)S(1)}, u32[]{:S(2)}, u32[]{:S(2)}) async-start(bf16[32,108,216]{1,2,0:T(8,128)(2,1)} %bitcast.64), calls=%async_computation | async-start | bytes 3538944 | tf_op jit(solution)/shard_map/all_to_all | solution.py:142
  91.2 1.4 collective-permute-start.2
  92.6 15.2 %collective-permute-start.3 = (f32[32,896]{1,0:T(8,128)S(1)}, f32[32,896]{1,0:T(8,128)S(1)}, u32[]{:S(2)}, u32[]{:S(2)}) collective-permute-start(f32[32,896]{1,0:T(8,128)S(1)} %add.113), channel_id=1, source_target_pairs={{0,8},{4,12},{8,0},{12,4},{16,24},{20,28},{24,16},{28,20},{1,9},{5... | collective-permute-start | bytes 344072 | tf_op jit(solution)/shard_map/ppermute | solution.py:34
  107.8 5.4 %collective-permute-start.4 = (f32[32,896]{1,0:T(8,128)S(1)}, f32[32,896]{1,0:T(8,128)S(1)}, u32[]{:S(2)}, u32[]{:S(2)}) collective-permute-start(f32[32,896]{1,0:T(8,128)S(1)} %add.114), channel_id=1, source_target_pairs={{0,16},{4,20},{8,24},{12,28},{16,0},{20,4},{24,8},{28,12},{1,17},{... | collective-permute-start | bytes 344072 | tf_op jit(solution)/shard_map/ppermute | solution.py:34
  113.2 9.8 %collective-permute-start.5 = (f32[32,896]{1,0:T(8,128)S(1)}, f32[32,896]{1,0:T(8,128)S(1)}, u32[]{:S(2)}, u32[]{:S(2)}) collective-permute-start(f32[32,896]{1,0:T(8,128)S(1)} %add.115), channel_id=1, source_target_pairs={{0,1},{1,0},{2,3},{3,2},{4,5},{5,4},{6,7},{7,6},{8,9},{9,8},{10,11... | collective-permute-start | bytes 344072 | tf_op jit(solution)/shard_map/ppermute | solution.py:34
  123.0 14.7 %collective-permute-start.6 = (f32[32,896]{1,0:T(8,128)S(1)}, f32[32,896]{1,0:T(8,128)S(1)}, u32[]{:S(2)}, u32[]{:S(2)}) collective-permute-start(f32[32,896]{1,0:T(8,128)S(1)} %add.116), channel_id=1, source_target_pairs={{0,2},{1,3},{2,0},{3,1},{4,6},{5,7},{6,4},{7,5},{8,10},{9,11},{10,... | collective-permute-start | bytes 344072 | tf_op jit(solution)/shard_map/ppermute | solution.py:34
Sparse Core Ops, SparseCore 0:
  17.5 64.9 all-gather.1

commit v5 on v4

--- a/solution.py
+++ b/solution.py
@@ -62,6 +62,16 @@
     return x
 
 
+def exchange_sum(x, axes, n):
+    width = x.shape[1]
+    piece = -(-width // n)
+    x = jnp.pad(x, ((0, 0), (0, piece * n - width)))
+    parts = x.reshape(x.shape[0], n, piece).transpose(1, 0, 2)
+    mine = jnp.sum(lax.all_to_all(parts, axes, 0, 0, tiled=True), axis=0)
+    back = lax.all_to_all(jnp.broadcast_to(mine[None], (n,) + mine.shape), axes, 0, 0, tiled=True)
+    return back.transpose(1, 0, 2).reshape(x.shape[0], n * piece)[:, :width]
+
+
 def block_order(n_grains, n_taps, grain):
     size = n_grains * n_taps * grain
     old = jnp.arange(size, dtype=jnp.int32)
@@ -89,7 +99,9 @@
 
     own = a_inverse.shape[0] // grain // n_taps
     own_rows = a_inverse.reshape(own, grain, n_taps, patch).transpose(0, 2, 1, 3).reshape(-1, patch)
-    inverse_rows = lax.all_gather(own_rows, "space", axis=0, tiled=True)
+    inverse_rows = lax.all_to_all(
+        jnp.broadcast_to(own_rows[None], (n_sp,) + own_rows.shape), "space", 0, 0, tiled=True
+    ).reshape(patch, patch)
 
     block = padded_2(volume, (("space", 2),), 1)
     padded = jnp.pad(block[0], ((0, 0), (0, 0), (1, 1), (1, 1)))
@@ -110,7 +122,7 @@
     g_part = lax.dot_general(grad_flat, grad_flat, contract_cells, preferred_element_type=f32)
     terms = jnp.concatenate([grad_perm, g_part], axis=1)
     terms, patches_t = lax.optimization_barrier((terms, patches_t))
-    both = butterfly_sum(terms, ("dp", "space"))
+    both = exchange_sum(terms, ("dp", "space"), n_dp * n_sp)
     grad_sum = both[:, :patch]
     g_factor = both[:, patch:]
     left = jnp.dot(g_inverse, grad_sum, precision=highest)

time: 152 us -> 233 us (1.53)
  waiting for transfers between devices: 32.3 us -> 92.2 us
  between operations: 14.2 us -> 0.88 us
  local copies, waits for them, and re-layouts: 47.7 us -> 58.4 us
  matrix products: 31.7 us -> 41.5 us
  starting transfers between devices: 21.3 us -> 29.7 us
  other arithmetic: 3.97 us -> 9.11 us
    all_to_all x0 -> x3, waiting for transfers between devices: none -> 53.1 us  [the longest x1 53.1 us: on_device(): lax.all_to_all(jnp.broadcast_to(own_rows[None], (n_sp,) + own_rows.shape)...]
    all_to_all x1, waiting for transfers between devices: 0.01 us -> 39.1 us  [on_device(): got = lax.all_to_all(a_blocks, ('dp', 'space'), 0, 0, tiled=True)]
    ppermute x5 -> x0, waiting for transfers between devices: 32.2 us -> none  [butterfly_sum(): x = x + lax.ppermute(x, axis, partner(axis, step))]
    all_to_all x0 -> x3, starting transfers between devices: none -> 17.7 us  [the longest x1 7.1 us: exchange_sum(): mine = jnp.sum(lax.all_to_all(parts, axes, 0, 0, tiled=True), axis=0)]
    ppermute x5 -> x0, starting transfers between devices: 8.12 us -> none  [butterfly_sum(): x = x + lax.ppermute(x, axis, partner(axis, step))]
    dot_general x1, matrix products: 7.49 us -> 13.7 us  [on_device(): lax.dot_general(high, patches_t, contract_cells, preferred_element_type=f32)]
    dot_general x1, matrix products: 7.8 us -> 13.5 us  [on_device(): lax.dot_general(low, patches_t, contract_cells, preferred_element_type=f32)]
    unnamed x35 -> x39, local copies, waits for them, and re-layouts: 23.5 us -> 28.5 us
  transfers between devices with their start and end apart: 9 -> 6, of which waited for: 5 -> 2; matrix products, arithmetic and copies ran while one was open for 52% -> 24% of each run, Pallas kernels for 0% -> 0%
where the time goes in v5:
time: 233 us; the launch traced here: 232 us
  waiting for transfers between devices  92.2 us (40%)
  local copies, waits for them, and re-layouts  58.4 us (25%)
  matrix products  41.5 us (18%)
  starting transfers between devices  29.7 us (13%)
  other arithmetic  9.11 us (4%)
    all_to_all x1, waiting for transfers between devices, on_device(): lax.all_to_all(jnp.broadcast_to(own_rows[None], (n_sp,) + own_rows.shape)...  53.1 us
    all_to_all x1, waiting for transfers between devices, on_device(): got = lax.all_to_all(a_blocks, ('dp', 'space'), 0, 0, tiled=True)  39.1 us
    unnamed x39, local copies, waits for them, and re-layouts  28.5 us
    dot_general x1, matrix products, on_device(): lax.dot_general(high, patches_t, contract_cells, preferred_element_type=f32)  13.7 us
    dot_general x1, matrix products, on_device(): lax.dot_general(low, patches_t, contract_cells, preferred_element_type=f32)  13.5 us
    reshape x1, local copies, waits for them, and re-layouts, on_device(): patches_t = jnp.stack(taps, axis=1).reshape(patch, cells)  11.6 us
    all_to_all x1, starting transfers between devices, exchange_sum(): mine = jnp.sum(lax.all_to_all(parts, axes, 0, 0, tiled=True), axis=0)  7.1 us
    all_to_all x1, starting transfers between devices, exchange_sum(): lax.all_to_all(jnp.broadcast_to(mine[None], (n,) + mine.shape), axes, 0,...  5.78 us
  transfers between devices with their start and end apart: 6, of which 2 were waited for; matrix products, arithmetic and copies ran while one was open for 24% of the time, Pallas kernels for 0%

profile of v5, /device:TPU:0, one launch (start us, length us, event | category | flops | bytes accessed | tf_op | source)
XLA Modules:
  0.0 231.8 jit_solution(14031144157042935503)
XLA Ops:
  1.6 4.9 %collective-permute-start = (bf16[1,32,1,16,128]{4,3,2,1,0:T(8,128)(2,1)S(1)}, bf16[1,32,1,16,128]{4,3,2,1,0:T(8,128)(2,1)S(1)}, u32[]{:S(2)}, u32[]{:S(2)}) collective-permute-start(bf16[1,32,1,16,128]{4,3,2,1,0:T(8,128)(2,1)S(1)} %get-tuple-element.8), channel_id=1, source_target_pairs={{0,1},{1,2},{2,3},{4,5},{5,6},{6,7},{8,9},{9,10},{10,11},{12,13},{... | collective-permute-start | bytes 393224 | tf_op jit(solution)/shard_map/ppermute | solution.py:17
  6.6 1.3 collective-permute-start.1
  7.9 3.4 %convert_reduce_fusion = f32[4096]{0:T(1024)S(1)} fusion(s32[1024]{0:T(1024)} %bitcast.235), kind=kLoop, calls=%fused_computation | loop fusion | flops 12578816 | bytes 20480 | tf_op jit(solution)/shard_map/reduce_sum | solution.py:135
  11.2 1.1 reshape_squeeze.3
  12.3 1.3 convolution_bitcast_fusion.1
  13.7 1.0 maximum_bitcast_fusion
  27.9 1.0 fusion.19
  29.8 1.0 fusion.17
  30.8 1.0 fusion.16
  39.8 11.6 %reshape.125 = bf16[864,4096]{1,0:T(8,128)(2,1)} reshape(bf16[8,27,4,2,16,128]{5,4,3,2,1,0:T(8,128)(2,1)} %fusion.7) | data formatting | bytes 14155776 | tf_op jit(solution)/shard_map/reshape | solution.py:115
  51.4 5.1 %convolution_bitcast_fusion = f32[32,864]{1,0:T(8,128)S(1)} fusion(bf16[864,4096]{1,0:T(8,128)(2,1)} %reshape.125, bf16[32,4096]{1,0:T(8,128)(2,1)S(1)} %reshape_squeeze.3), kind=kOutput, calls=%fused_computation.13 | convolution fusion | flops 226492416 | bytes 7450624 | tf_op jit(solution)/shard_map/dot_general | solution.py:121
  57.5 1.2 reshape.137
  58.7 7.1 %all-to-all-start.1 = ((f32[32,1,896]{2,1,0:T(1,128)}), f32[32,1,896]{2,1,0:T(1,128)S(1)}, u32[]{:S(2)}, u32[]{:S(2)}) async-start(f32[32,1,896]{2,1,0:T(1,128)} %reshape.137), calls=%async_computation.1 | async-start | bytes 229376 | tf_op jit(solution)/shard_map/all_to_all | solution.py:70
  65.8 13.7 %fusion.1 = f32[864,864]{1,0:T(8,128)} fusion(bf16[864,4096]{1,0:T(8,128)(2,1)} %reshape.125, f32[4096]{0:T(1024)S(1)} %convert_reduce_fusion), kind=kOutput, calls=%fused_computation.5 | convolution fusion | flops 6125912064 | bytes 10080256 | tf_op jit(solution)/shard_map/dot_general | solution.py:143
  81.6 1.2 reshape.139
  82.8 5.8 %all-to-all-start.2 = ((f32[32,1,896]{2,1,0:T(1,128)}), f32[32,1,896]{2,1,0:T(1,128)}, u32[]{:S(2)}, u32[]{:S(2)}) async-start(f32[32,1,896]{2,1,0:T(1,128)} %reshape.139), calls=%async_computation.2 | async-start | bytes 229376 | tf_op jit(solution)/shard_map/all_to_all | solution.py:71
  88.6 13.5 %multiply_convert_fusion = bf16[864,864]{1,0:T(8,128)(2,1)S(1)} fusion(f32[864,864]{1,0:T(8,128)} %fusion.1, bf16[864,4096]{1,0:T(8,128)(2,1)} %reshape.125, f32[4096]{0:T(1024)S(1)} %convert_reduce_fusion), kind=kOutput, calls=%fused_computation.11 | convolution fusion | flops 6138768384 | bytes 11573248 | tf_op jit(solution)/shard_map/dot_general | solution.py:144
  102.1 1.6 reshape.130
  103.6 2.6 %copy.105 = bf16[8,108,4,216]{1,3,2,0:T(8,128)(2,1)} copy(bf16[8,108,4,216]{3,2,1,0:T(4,128)(2,1)S(1)} %reshape.130) | data formatting | bytes 2985984 | tf_op jit(solution)/shard_map/reshape | solution.py:150
  106.2 5.8 %all-to-all-start = ((bf16[32,108,216]{1,2,0:T(8,128)(2,1)}), bf16[32,108,216]{1,2,0:T(8,128)(2,1)S(1)}, u32[]{:S(2)}, u32[]{:S(2)}) async-start(bf16[32,108,216]{1,2,0:T(8,128)(2,1)} %bitcast.64), calls=%async_computation | async-start | bytes 3538944 | tf_op jit(solution)/shard_map/all_to_all | solution.py:154
  112.9 39.1 %all-to-all-done = bf16[32,108,216]{1,2,0:T(8,128)(2,1)S(1)} async-done(((bf16[32,108,216]{1,2,0:T(8,128)(2,1)}), bf16[32,108,216]{1,2,0:T(8,128)(2,1)S(1)}, u32[]{:S(2)}, u32[]{:S(2)}) %all-to-all-start) | async-done | bytes 1493024 | tf_op jit(solution)/shard_map/all_to_all | solution.py:154
  152.0 2.0 broadcast_in_dim.8
  154.2 4.8 %all-to-all-start.3 = ((f32[4,216,864]{2,1,0:T(8,128)}), f32[4,216,864]{2,1,0:T(8,128)S(1)}, u32[]{:S(2)}, u32[]{:S(2)}) async-start(f32[4,216,864]{2,1,0:T(8,128)} %broadcast_in_dim.8), calls=%async_computation.3 | async-start | bytes 6193152 | tf_op jit(solution)/shard_map/all_to_all | solution.py:102
  159.7 1.1 copy.104
  160.8 4.3 %fusion.6 = bf16[4,8,32,128]{3,1,2,0:T(8,128)(2,1)S(1)} fusion(bf16[864,4096]{1,0:T(8,128)(2,1)} %reshape.125, bf16[32,864]{0,1:T(8,128)(2,1)} %bitcast.232), kind=kOutput, calls=%fused_computation.12 | convolution fusion | flops 226623488 | bytes 7395328 | tf_op jit(solution)/shard_map/dot_general | solution.py:131
  165.9 1.8 reduce.1
  167.7 1.4 reshape.140
  169.1 2.2 copy.107
  171.2 1.3 reshape.133
  173.5 1.8 convert_reduce_fusion.1
  176.5 53.1 %all-to-all-done.3 = f32[4,216,864]{2,1,0:T(8,128)S(1)} async-done(((f32[4,216,864]{2,1,0:T(8,128)}), f32[4,216,864]{2,1,0:T(8,128)S(1)}, u32[]{:S(2)}, u32[]{:S(2)}) %all-to-all-start.3) | async-done | bytes 2986016 | tf_op jit(solution)/shard_map/all_to_all | solution.py:102
  229.6 2.2 fusion.55
  (57 shorter events, 30.7 us)
Async XLA Ops:
  0.6 172.6 %copy-start = (f32[32,32]{1,0:T(8,128)S(1)}, f32[32,32]{1,0:T(8,128)}, u32[]{:S(2)}) copy-start(f32[32,32]{1,0:T(8,128)} %param.11) | copy-start | bytes 12292
  1.6 12.0 %collective-permute-start = (bf16[1,32,1,16,128]{4,3,2,1,0:T(8,128)(2,1)S(1)}, bf16[1,32,1,16,128]{4,3,2,1,0:T(8,128)(2,1)S(1)}, u32[]{:S(2)}, u32[]{:S(2)}) collective-permute-start(bf16[1,32,1,16,128]{4,3,2,1,0:T(8,128)(2,1)S(1)} %get-tuple-element.8), channel_id=1, source_target_pairs={{0,1},{1,2},{2,3},{4,5},{5,6},{6,7},{8,9},{9,10},{10,11},{12,13},{... | collective-permute-start | bytes 393224 | tf_op jit(solution)/shard_map/ppermute | solution.py:17
  6.6 7.1 %collective-permute-start.1 = (bf16[1,32,1,16,128]{4,3,2,1,0:T(8,128)(2,1)S(1)}, bf16[1,32,1,16,128]{4,3,2,1,0:T(8,128)(2,1)S(1)}, u32[]{:S(2)}, u32[]{:S(2)}) collective-permute-start(bf16[1,32,1,16,128]{4,3,2,1,0:T(8,128)(2,1)S(1)} %get-tuple-element.9), channel_id=1, source_target_pairs={{1,0},{2,1},{3,2},{5,4},{6,5},{7,6},{9,8},{10,9},{11,10},{13,12},{... | collective-permute-start | bytes 393224 | tf_op jit(solution)/shard_map/ppermute | solution.py:19
  58.7 20.8 %all-to-all-start.1 = ((f32[32,1,896]{2,1,0:T(1,128)}), f32[32,1,896]{2,1,0:T(1,128)S(1)}, u32[]{:S(2)}, u32[]{:S(2)}) async-start(f32[32,1,896]{2,1,0:T(1,128)} %reshape.137), calls=%async_computation.1 | async-start | bytes 229376 | tf_op jit(solution)/shard_map/all_to_all | solution.py:70
  82.8 23.4 %all-to-all-start.2 = ((f32[32,1,896]{2,1,0:T(1,128)}), f32[32,1,896]{2,1,0:T(1,128)}, u32[]{:S(2)}, u32[]{:S(2)}) async-start(f32[32,1,896]{2,1,0:T(1,128)} %reshape.139), calls=%async_computation.2 | async-start | bytes 229376 | tf_op jit(solution)/shard_map/all_to_all | solution.py:71
  103.6 8.4 %copy-start.2 = (f32[216,864]{1,0:T(8,128)S(1)}, f32[216,864]{1,0:T(8,128)}, u32[]{:S(2)}) copy-start(f32[216,864]{1,0:T(8,128)} %param.10) | copy-start | bytes 2239492
  106.2 45.8 %all-to-all-start = ((bf16[32,108,216]{1,2,0:T(8,128)(2,1)}), bf16[32,108,216]{1,2,0:T(8,128)(2,1)S(1)}, u32[]{:S(2)}, u32[]{:S(2)}) async-start(bf16[32,108,216]{1,2,0:T(8,128)(2,1)} %bitcast.64), calls=%async_computation | async-start | bytes 3538944 | tf_op jit(solution)/shard_map/all_to_all | solution.py:154
  112.0 47.0 %copy-start.3 = (bf16[32,864]{1,0:T(8,128)(2,1)S(1)}, bf16[32,864]{1,0:T(8,128)(2,1)}, u32[]{:S(2)}) copy-start(bf16[32,864]{1,0:T(8,128)(2,1)} %param.8) | copy-start | bytes 165892
  152.0 2.2 copy-start.1
  154.2 75.4 %all-to-all-start.3 = ((f32[4,216,864]{2,1,0:T(8,128)}), f32[4,216,864]{2,1,0:T(8,128)S(1)}, u32[]{:S(2)}, u32[]{:S(2)}) async-start(f32[4,216,864]{2,1,0:T(8,128)} %broadcast_in_dim.8), calls=%async_computation.3 | async-start | bytes 6193152 | tf_op jit(solution)/shard_map/all_to_all | solution.py:102

commit v6 on v4

--- a/solution.py
+++ b/solution.py
@@ -62,6 +62,13 @@
     return x
 
 
+def tap_order(channels, n_taps):
+    size = channels * n_taps
+    new = jnp.arange(size, dtype=jnp.int32)
+    old = (new % n_taps) * channels + new // n_taps
+    return (old[:, None] == jnp.arange(size, dtype=jnp.int32)[None, :]).astype(jnp.bfloat16)
+
+
 def block_order(n_grains, n_taps, grain):
     size = n_grains * n_taps * grain
     old = jnp.arange(size, dtype=jnp.int32)
@@ -87,34 +94,32 @@
     n_grains = channels // grain
     contract_cells = (((1,), (1,)), ((), ()))
 
-    own = a_inverse.shape[0] // grain // n_taps
-    own_rows = a_inverse.reshape(own, grain, n_taps, patch).transpose(0, 2, 1, 3).reshape(-1, patch)
-    inverse_rows = lax.all_gather(own_rows, "space", axis=0, tiled=True)
+    full_inverse = lax.all_gather(a_inverse, "space", axis=0, tiled=True)
 
     block = padded_2(volume, (("space", 2),), 1)
     padded = jnp.pad(block[0], ((0, 0), (0, 0), (1, 1), (1, 1)))
-    grains = padded.reshape((n_grains, grain) + padded.shape[1:])
+    slab = jnp.transpose(padded, (1, 2, 0, 3))
     taps = [
-        grains[:, :, dz : dz + planes, dy : dy + y_cells, dx : dx + x_cells]
+        slab[dz : dz + planes, dy : dy + y_cells, :, dx : dx + x_cells]
         for dz in range(3)
         for dy in range(3)
         for dx in range(3)
     ]
-    patches_t = jnp.stack(taps, axis=1).reshape(patch, cells)
+    patches_t = jnp.stack(taps, axis=0).transpose(0, 3, 1, 2, 4).reshape(patch, cells)
     grad_flat = out_grad[0].reshape(channels, cells)
-    kernel_perm = (
-        kernel.reshape(channels, n_grains, grain, n_taps).transpose(0, 1, 3, 2).reshape(channels, patch)
-    )
+    kernel_perm = kernel.reshape(channels, channels, n_taps).transpose(0, 2, 1).reshape(channels, patch)
 
     grad_perm = lax.dot_general(grad_flat, patches_t, contract_cells, preferred_element_type=f32)
     g_part = lax.dot_general(grad_flat, grad_flat, contract_cells, preferred_element_type=f32)
     terms = jnp.concatenate([grad_perm, g_part], axis=1)
     terms, patches_t = lax.optimization_barrier((terms, patches_t))
     both = butterfly_sum(terms, ("dp", "space"))
-    grad_sum = both[:, :patch]
+    grad_sum = (
+        both[:, :patch].reshape(channels, n_taps, channels).transpose(0, 2, 1).reshape(channels, patch)
+    )
     g_factor = both[:, patch:]
     left = jnp.dot(g_inverse, grad_sum, precision=highest)
-    pre_grad = jnp.dot(left, inverse_rows, precision=highest)
+    pre_grad = jnp.dot(left, full_inverse, precision=highest)
 
     forward = jnp.dot(kernel_perm, patches_t, preferred_element_type=f32)
     conv_out = forward.astype(jnp.bfloat16).reshape(1, channels, planes, y_cells, x_cells)
@@ -131,21 +136,19 @@
         lax.dot_general(high, patches_t, contract_cells, preferred_element_type=f32)
         + lax.dot_general(low, patches_t, contract_cells, preferred_element_type=f32)
     ) / jnp.float32(total_samples)
+    order = tap_order(channels, n_taps)
+    a_rows = jnp.dot(order, a_perm.astype(jnp.bfloat16), preferred_element_type=f32)
+    a_orig = lax.dot_general(
+        a_rows.astype(jnp.bfloat16), order, contract_cells, preferred_element_type=f32
+    ).astype(jnp.bfloat16)
     rows = patch // n_dp
     cols = patch // n_sp
     a_blocks = (
-        a_perm.astype(jnp.bfloat16)
-        .reshape(n_dp, rows, n_sp, cols)
-        .transpose(0, 2, 1, 3)
-        .reshape(n_dp * n_sp, rows, cols)
+        a_orig.reshape(n_dp, rows, n_sp, cols).transpose(0, 2, 1, 3).reshape(n_dp * n_sp, rows, cols)
     )
+    a_blocks, pre_grad, g_factor = lax.optimization_barrier((a_blocks, pre_grad, g_factor))
     got = lax.all_to_all(a_blocks, ("dp", "space"), 0, 0, tiled=True)
-    a_own = jnp.sum(got.astype(f32), axis=0)
-    a_factor = jnp.dot(
-        jnp.dot(block_order(row_ch // grain, n_taps, grain), a_own, precision=highest),
-        block_order(col_ch // grain, n_taps, grain).T,
-        precision=highest,
-    )
+    a_factor = jnp.sum(got.astype(f32), axis=0)
     return (conv_out, a_factor, g_factor, pre_grad)
 
 

time: 152 us -> 172 us (1.13)
  waiting for transfers between devices: 32.3 us -> 67.1 us
  local copies, waits for them, and re-layouts: 47.7 us -> 30.2 us
  starting transfers between devices: 21.3 us -> 14.4 us
  matrix products: 31.7 us -> 38.5 us
  other arithmetic: 3.97 us -> 5.86 us
    all_to_all x1, waiting for transfers between devices: 0.01 us -> 33.8 us  [on_device(): got = lax.all_to_all(a_blocks, ('dp', 'space'), 0, 0, tiled=True)]
    ppermute x5, waiting for transfers between devices: 32.2 us -> 15.9 us  [butterfly_sum(): x = x + lax.ppermute(x, axis, partner(axis, step))]
    unnamed x35 -> x39, local copies, waits for them, and re-layouts: 23.5 us -> 8.68 us
    all_gather x1, waiting for transfers between devices: 0.01 us -> 14.2 us  [on_device(): full_inverse = lax.all_gather(a_inverse, 'space', axis=0, tiled=True)]
    dot_general x1, matrix products: 7.49 us -> 12.1 us  [on_device(): lax.dot_general(high, patches_t, contract_cells, preferred_element_type=f32)]
    all_to_all x1, starting transfers between devices: 6.94 us -> 3.21 us  [on_device(): got = lax.all_to_all(a_blocks, ('dp', 'space'), 0, 0, tiled=True)]
    ppermute x5, starting transfers between devices: 8.12 us -> 4.92 us  [butterfly_sum(): x = x + lax.ppermute(x, axis, partner(axis, step))]
    ppermute x1, waiting for transfers between devices: 0.01 us -> 3.19 us  [padded_2(): lax.ppermute(head, axis, [((i + 1) % count, i) for i in range(ends)])]
  transfers between devices with their start and end apart: 9 -> 9, of which waited for: 5 -> 7; matrix products, arithmetic and copies ran while one was open for 52% -> 24% of each run, Pallas kernels for 0% -> 0%
where the time goes in v6:
time: 172 us; the launch traced here: 170 us
  waiting for transfers between devices  67.1 us (39%)
  matrix products  38.5 us (22%)
  local copies, waits for them, and re-layouts  30.2 us (18%)
  starting transfers between devices  14.4 us (8%)
  between operations  14.3 us (8%)
  other arithmetic  5.86 us (3%)
    all_to_all x1, waiting for transfers between devices, on_device(): got = lax.all_to_all(a_blocks, ('dp', 'space'), 0, 0, tiled=True)  33.8 us
    ppermute x5, waiting for transfers between devices, butterfly_sum(): x = x + lax.ppermute(x, axis, partner(axis, step))  15.9 us
    all_gather x1, waiting for transfers between devices, on_device(): full_inverse = lax.all_gather(a_inverse, 'space', axis=0, tiled=True)  14.2 us
    dot_general x1, matrix products, on_device(): lax.dot_general(high, patches_t, contract_cells, preferred_element_type=f32)  12.1 us
    reshape x1, local copies, waits for them, and re-layouts, on_device(): jnp.stack(taps, axis=0).transpose(0, 3, 1, 2, 4).reshape(patch, cells)  11.6 us
    unnamed x39, local copies, waits for them, and re-layouts  8.68 us
    dot_general x1, matrix products, on_device(): lax.dot_general(low, patches_t, contract_cells, preferred_element_type=f32)  7.55 us
    dot_general x1, matrix products, on_device(): lax.dot_general(grad_flat, patches_t, contract_cells, preferred_element_t...  5.13 us
  transfers between devices with their start and end apart: 9, of which 7 were waited for; matrix products, arithmetic and copies ran while one was open for 24% of the time, Pallas kernels for 0%

profile of v6, /device:TPU:0, one launch (start us, length us, event | category | flops | bytes accessed | tf_op | source)
XLA Modules:
  0.0 170.3 jit_solution(3779458327086587398)
XLA Ops:
  7.2 1.0 fusion.50
  8.2 4.9 %collective-permute-start = (bf16[1,32,1,16,128]{4,3,2,1,0:T(8,128)(2,1)S(1)}, bf16[1,32,1,16,128]{4,3,2,1,0:T(8,128)(2,1)S(1)}, u32[]{:S(2)}, u32[]{:S(2)}) collective-permute-start(bf16[1,32,1,16,128]{4,3,2,1,0:T(8,128)(2,1)S(1)} %get-tuple-element.14), channel_id=1, source_target_pairs={{0,1},{1,2},{2,3},{4,5},{5,6},{6,7},{8,9},{9,10},{10,11},{12,13},{... | collective-permute-start | bytes 393224 | tf_op jit(solution)/shard_map/ppermute | solution.py:17
  13.2 1.3 collective-permute-start.1
  14.5 1.1 reshape_squeeze.3
  15.5 1.3 convolution_bitcast_fusion.1
  16.8 3.2 %collective-permute-done.1 = bf16[1,32,1,16,128]{4,3,2,1,0:T(8,128)(2,1)S(1)} collective-permute-done((bf16[1,32,1,16,128]{4,3,2,1,0:T(8,128)(2,1)S(1)}, bf16[1,32,1,16,128]{4,3,2,1,0:T(8,128)(2,1)S(1)}, u32[]{:S(2)}, u32[]{:S(2)}) %collective-permute-start.1) | collective-permute-done | bytes 131104 | tf_op jit(solution)/shard_map/ppermute | solution.py:19
  20.0 1.0 maximum_bitcast_fusion
  21.0 0.9 pad_bitcast_fusion
  27.3 2.9 %copy-done.1 = bf16[27,2,16,32,128]{4,2,1,3,0:T(8,128)(2,1)} copy-done((bf16[27,2,16,32,128]{4,2,1,3,0:T(8,128)(2,1)}, bf16[27,2,16,32,128]{4,2,1,3,0:T(8,128)(2,1)S(1)}, u32[]{:S(2)}) %copy-start.1) | copy-done | bytes 7077912
  30.2 11.6 %reshape.57 = bf16[864,4096]{1,0:T(8,128)(2,1)} reshape(bf16[27,32,2,16,128]{4,3,2,1,0:T(8,128)(2,1)} %bitcast.149) | data formatting | bytes 14155776 | tf_op jit(solution)/shard_map/reshape | solution.py:108
  41.8 5.1 %convolution_bitcast_fusion = f32[32,864]{1,0:T(8,128)S(1)} fusion(bf16[864,4096]{1,0:T(8,128)(2,1)} %reshape.57, bf16[32,4096]{1,0:T(8,128)(2,1)S(1)} %reshape_squeeze.3), kind=kOutput, calls=%fused_computation.21 | convolution fusion | flops 226492416 | bytes 7450624 | tf_op jit(solution)/shard_map/dot_general | solution.py:112
  47.1 1.3 collective-permute-done.2
  48.4 1.6 collective-permute-start.3
  49.9 2.8 %convert_reduce_fusion = f32[4096]{0:T(1024)S(1)} fusion(s32[1024]{0:T(1024)S(1)} %bitcast.155), kind=kLoop, calls=%fused_computation | loop fusion | flops 12578816 | bytes 20480 | tf_op jit(solution)/shard_map/reduce_sum | solution.py:128
  52.7 0.9 collective-permute-done.3
  53.7 1.6 collective-permute-start.4
  55.3 12.1 %fusion.1 = f32[864,864]{1,0:T(8,128)S(1)} fusion(bf16[864,4096]{1,0:T(8,128)(2,1)} %reshape.57, f32[4096]{0:T(1024)S(1)} %convert_reduce_fusion), kind=kOutput, calls=%fused_computation.5 | convolution fusion | flops 6125912064 | bytes 10080256 | tf_op jit(solution)/shard_map/dot_general | solution.py:136
  67.4 1.7 collective-permute-start.5
  69.1 7.5 %multiply_convert_fusion = bf16[864,864]{1,0:T(8,128)(2,1)S(1)} fusion(f32[864,864]{1,0:T(8,128)S(1)} %fusion.1, bf16[864,4096]{1,0:T(8,128)(2,1)S(1)} %bitcast.148, f32[4096]{0:T(1024)S(1)} %convert_reduce_fusion), kind=kOutput, calls=%fused_computation.11 | convolution fusion | flops 6138768384 | bytes 11573248 | tf_op jit(solution)/shard_map/dot_general | solution.py:137
  76.7 7.2 %collective-permute-done.5 = f32[32,896]{1,0:T(8,128)S(1)} collective-permute-done((f32[32,896]{1,0:T(8,128)S(1)}, f32[32,896]{1,0:T(8,128)S(1)}, u32[]{:S(2)}, u32[]{:S(2)}) %collective-permute-start.5) | collective-permute-done | bytes 114720 | tf_op jit(solution)/shard_map/ppermute | solution.py:34
  84.0 3.8 %fusion.9 = bf16[864,864]{1,0:T(8,128)(2,1)S(1)} fusion(s32[864]{0:T(1024)S(1)} %fusion.47, bf16[864,864]{1,0:T(8,128)(2,1)S(1)} %multiply_convert_fusion), kind=kOutput, calls=%fused_computation.16 | convolution fusion | flops 2582876160 | bytes 2989440 | tf_op jit(solution)/shard_map/dot_general | solution.py:141
  87.7 1.6 reshape.62
  89.3 2.5 %copy.20 = bf16[8,108,4,216]{1,3,2,0:T(8,128)(2,1)} copy(bf16[8,108,4,216]{3,2,1,0:T(4,128)(2,1)S(1)} %reshape.62) | data formatting | bytes 2985984 | tf_op jit(solution)/shard_map/reshape | solution.py:147
  91.9 6.5 %collective-permute-done.6 = f32[32,896]{1,0:T(8,128)} collective-permute-done((f32[32,896]{1,0:T(8,128)S(1)}, f32[32,896]{1,0:T(8,128)}, u32[]{:S(2)}, u32[]{:S(2)}) %collective-permute-start.6) | collective-permute-done | bytes 114720 | tf_op jit(solution)/shard_map/ppermute | solution.py:34
  98.4 0.9 add.53
  100.9 14.2 %all-gather.2.cloned.1.call-done = f32[864,864]{1,0:T(8,128)} async-done(((f32[216,864]{1,0:T(8,128)}), f32[864,864]{1,0:T(8,128)}) %all-gather.2.cloned.1.call-update) | async-done | bytes 2986000 | tf_op jit(solution)/shard_map/all_gather | solution.py:97
  115.1 4.1 %fusion.52 = f32[32,864]{1,0:T(8,128)} fusion(f32[864,32]{0,1:T(8,128)S(1)} %fusion.51, f32[864,864]{1,0:T(8,128)} %all-gather.2.cloned.1.call-done), kind=kOutput, calls=%fused_computation.95 | convolution fusion | flops 286654464 | bytes 3207168 | tf_op jit(solution)/shard_map/dot_general | solution.py:122
  119.3 3.2 %all-to-all-start = ((bf16[32,108,216]{1,2,0:T(8,128)(2,1)}), bf16[32,108,216]{1,2,0:T(8,128)(2,1)S(1)}, u32[]{:S(2)}, u32[]{:S(2)}) async-start(bf16[32,108,216]{1,2,0:T(8,128)(2,1)} %bitcast.38), calls=%async_computation | async-start | bytes 3538944 | tf_op jit(solution)/shard_map/all_to_all | solution.py:150
  123.6 4.3 %fusion.12 = bf16[4,8,32,128]{3,1,2,0:T(8,128)(2,1)S(1)} fusion(bf16[32,864]{1,0:T(8,128)(2,1)S(1)} %reshape.60, bf16[864,4096]{1,0:T(8,128)(2,1)} %reshape.57), kind=kOutput, calls=%fused_computation.20 | convolution fusion | flops 226623488 | bytes 7395328 | tf_op jit(solution)/shard_map/dot_general | solution.py:124
  128.0 0.8 copy.23
  128.7 33.8 %all-to-all-done = bf16[32,108,216]{1,2,0:T(8,128)(2,1)S(1)} async-done(((bf16[32,108,216]{1,2,0:T(8,128)(2,1)}), bf16[32,108,216]{1,2,0:T(8,128)(2,1)S(1)}, u32[]{:S(2)}, u32[]{:S(2)}) %all-to-all-start) | async-done | bytes 1493024 | tf_op jit(solution)/shard_map/all_to_all | solution.py:150
  162.5 1.0 convert_reduce_fusion.1
  (59 shorter events, 8.4 us)
Async XLA Ops:
  7.2 93.5 %copy-start = (f32[32,32]{1,0:T(8,128)S(1)}, f32[32,32]{1,0:T(8,128)}, u32[]{:S(2)}) copy-start(f32[32,32]{1,0:T(8,128)} %param.11) | copy-start | bytes 12292
  7.2 108.0 %all-gather.2.cloned.1.call-start = ((), (), s32[]{:S(2)}) async-start(), calls=%async_computation.1 | async-start | bytes 3870720 | tf_op jit(solution)/shard_map/all_gather | solution.py:97
  8.2 8.6 %collective-permute-start = (bf16[1,32,1,16,128]{4,3,2,1,0:T(8,128)(2,1)S(1)}, bf16[1,32,1,16,128]{4,3,2,1,0:T(8,128)(2,1)S(1)}, u32[]{:S(2)}, u32[]{:S(2)}) collective-permute-start(bf16[1,32,1,16,128]{4,3,2,1,0:T(8,128)(2,1)S(1)} %get-tuple-element.14), channel_id=1, source_target_pairs={{0,1},{1,2},{2,3},{4,5},{5,6},{6,7},{8,9},{9,10},{10,11},{12,13},{... | collective-permute-start | bytes 393224 | tf_op jit(solution)/shard_map/ppermute | solution.py:17
  13.2 6.9 %collective-permute-start.1 = (bf16[1,32,1,16,128]{4,3,2,1,0:T(8,128)(2,1)S(1)}, bf16[1,32,1,16,128]{4,3,2,1,0:T(8,128)(2,1)S(1)}, u32[]{:S(2)}, u32[]{:S(2)}) collective-permute-start(bf16[1,32,1,16,128]{4,3,2,1,0:T(8,128)(2,1)S(1)} %get-tuple-element.15), channel_id=1, source_target_pairs={{1,0},{2,1},{3,2},{5,4},{6,5},{7,6},{9,8},{10,9},{11,10},{13,12},{... | collective-permute-start | bytes 393224 | tf_op jit(solution)/shard_map/ppermute | solution.py:19
  27.2 2.9 %copy-start.1 = (bf16[27,2,16,32,128]{4,2,1,3,0:T(8,128)(2,1)}, bf16[27,2,16,32,128]{4,2,1,3,0:T(8,128)(2,1)S(1)}, u32[]{:S(2)}) copy-start(bf16[27,2,16,32,128]{4,2,1,3,0:T(8,128)(2,1)S(1)} %fusion.13) | copy-start | bytes 21233668
  41.8 8.1 %copy-start.3 = (s32[1,1024]{1,0:T(1,128)S(1)}, s32[1,1024]{1,0:T(1,128)}, u32[]{:S(2)}) copy-start(s32[1,1024]{1,0:T(1,128)} %param.9) | copy-start | bytes 12292
  47.0 1.3 collective-permute-start.2
  48.4 5.3 %collective-permute-start.3 = (f32[32,896]{1,0:T(8,128)S(1)}, f32[32,896]{1,0:T(8,128)S(1)}, u32[]{:S(2)}, u32[]{:S(2)}) collective-permute-start(f32[32,896]{1,0:T(8,128)S(1)} %add.49), channel_id=1, source_target_pairs={{0,8},{4,12},{8,0},{12,4},{16,24},{20,28},{24,16},{28,20},{1,9},{5... | collective-permute-start | bytes 344072 | tf_op jit(solution)/shard_map/ppermute | solution.py:34
  53.6 15.5 %slice-start = ((s8[7077888]{0:T(1024)(128)(4,1)}), s8[4194304]{0:T(1024)(128)(4,1)S(1)}, s32[]{:S(2)}) async-start(s8[7077888]{0:T(1024)(128)(4,1)} %bitcast.147), calls=%async_computation.2 | async-start | bytes 8388608
  53.7 15.4 %slice-start.1 = ((s8[7077888]{0:T(1024)(128)(4,1)}), s8[2883584]{0:T(1024)(128)(4,1)S(1)}, s32[]{:S(2)}) async-start(s8[7077888]{0:T(1024)(128)(4,1)} %bitcast.147), calls=%async_computation.3 | async-start | bytes 5767168
  53.7 13.7 %collective-permute-start.4 = (f32[32,896]{1,0:T(8,128)S(1)}, f32[32,896]{1,0:T(8,128)S(1)}, u32[]{:S(2)}, u32[]{:S(2)}) collective-permute-start(f32[32,896]{1,0:T(8,128)S(1)} %add.50), channel_id=1, source_target_pairs={{0,16},{4,20},{8,24},{12,28},{16,0},{20,4},{24,8},{28,12},{1,17},{... | collective-permute-start | bytes 344072 | tf_op jit(solution)/shard_map/ppermute | solution.py:34
  67.4 16.5 %collective-permute-start.5 = (f32[32,896]{1,0:T(8,128)S(1)}, f32[32,896]{1,0:T(8,128)S(1)}, u32[]{:S(2)}, u32[]{:S(2)}) collective-permute-start(f32[32,896]{1,0:T(8,128)S(1)} %add.51), channel_id=1, source_target_pairs={{0,1},{1,0},{2,3},{3,2},{4,5},{5,4},{6,7},{7,6},{8,9},{9,8},{10,11... | collective-permute-start | bytes 344072 | tf_op jit(solution)/shard_map/ppermute | solution.py:34
  83.9 14.5 %collective-permute-start.6 = (f32[32,896]{1,0:T(8,128)S(1)}, f32[32,896]{1,0:T(8,128)}, u32[]{:S(2)}, u32[]{:S(2)}) collective-permute-start(f32[32,896]{1,0:T(8,128)S(1)} %add.52), channel_id=1, source_target_pairs={{0,2},{1,3},{2,0},{3,1},{4,6},{5,7},{6,4},{7,5},{8,10},{9,11},{10,... | collective-permute-start | bytes 344072 | tf_op jit(solution)/shard_map/ppermute | solution.py:34
  89.3 33.2 %copy-start.2 = (bf16[32,864]{1,0:T(8,128)(2,1)S(1)}, bf16[32,864]{1,0:T(8,128)(2,1)}, u32[]{:S(2)}) copy-start(bf16[32,864]{1,0:T(8,128)(2,1)} %param.8) | copy-start | bytes 165892
  119.3 43.2 %all-to-all-start = ((bf16[32,108,216]{1,2,0:T(8,128)(2,1)}), bf16[32,108,216]{1,2,0:T(8,128)(2,1)S(1)}, u32[]{:S(2)}, u32[]{:S(2)}) async-start(bf16[32,108,216]{1,2,0:T(8,128)(2,1)} %bitcast.38), calls=%async_computation | async-start | bytes 3538944 | tf_op jit(solution)/shard_map/all_to_all | solution.py:150
Sparse Core Ops, SparseCore 0:
  47.2 67.8 all-gather.1

commit v7 on v6

--- a/solution.py
+++ b/solution.py
@@ -146,7 +146,6 @@
     a_blocks = (
         a_orig.reshape(n_dp, rows, n_sp, cols).transpose(0, 2, 1, 3).reshape(n_dp * n_sp, rows, cols)
     )
-    a_blocks, pre_grad, g_factor = lax.optimization_barrier((a_blocks, pre_grad, g_factor))
     got = lax.all_to_all(a_blocks, ("dp", "space"), 0, 0, tiled=True)
     a_factor = jnp.sum(got.astype(f32), axis=0)
     return (conv_out, a_factor, g_factor, pre_grad)

time: 172 us -> 139 us (0.81)
  waiting for transfers between devices: 67.1 us -> 32.2 us
  starting transfers between devices: 14.4 us -> 21.3 us
  matrix products: 38.5 us -> 34.3 us
    all_to_all x1, waiting for transfers between devices: 33.8 us -> 0.01 us  [on_device(): got = lax.all_to_all(a_blocks, ('dp', 'space'), 0, 0, tiled=True)]
    ppermute x5, waiting for transfers between devices: 15.9 us -> 32.1 us  [butterfly_sum(): x = x + lax.ppermute(x, axis, partner(axis, step))]
    all_gather x1, waiting for transfers between devices: 14.2 us -> 0.01 us  [on_device(): full_inverse = lax.all_gather(a_inverse, 'space', axis=0, tiled=True)]
    dot_general x1, matrix products: 12.1 us -> 7.49 us  [on_device(): lax.dot_general(high, patches_t, contract_cells, preferred_element_type=f32)]
    all_to_all x1, starting transfers between devices: 3.21 us -> 6.93 us  [on_device(): got = lax.all_to_all(a_blocks, ('dp', 'space'), 0, 0, tiled=True)]
    ppermute x5, starting transfers between devices: 4.92 us -> 8.12 us  [butterfly_sum(): x = x + lax.ppermute(x, axis, partner(axis, step))]
    ppermute x1, waiting for transfers between devices: 3.19 us -> 0.01 us  [padded_2(): lax.ppermute(head, axis, [((i + 1) % count, i) for i in range(ends)])]
    unnamed x39 -> x35, local copies, waits for them, and re-layouts: 8.68 us -> 8.66 us
  transfers between devices with their start and end apart: 9 -> 9, of which waited for: 7 -> 5; matrix products, arithmetic and copies ran while one was open for 24% -> 45% of each run, Pallas kernels for 0% -> 0%
where the time goes in v7:
time: 139 us; the launch traced here: 138 us
  matrix products  34.3 us (25%)
  waiting for transfers between devices  32.2 us (23%)
  local copies, waits for them, and re-layouts  30.2 us (22%)
  starting transfers between devices  21.3 us (15%)
  between operations  14.3 us (10%)
  other arithmetic  5.55 us (4%)
    ppermute x5, waiting for transfers between devices, butterfly_sum(): x = x + lax.ppermute(x, axis, partner(axis, step))  32.1 us
    reshape x1, local copies, waits for them, and re-layouts, on_device(): jnp.stack(taps, axis=0).transpose(0, 3, 1, 2, 4).reshape(patch, cells)  11.6 us
    unnamed x35, local copies, waits for them, and re-layouts  8.66 us
    ppermute x5, starting transfers between devices, butterfly_sum(): x = x + lax.ppermute(x, axis, partner(axis, step))  8.12 us
    dot_general x1, matrix products, on_device(): lax.dot_general(low, patches_t, contract_cells, preferred_element_type=f32)  7.8 us
    dot_general x1, matrix products, on_device(): lax.dot_general(high, patches_t, contract_cells, preferred_element_type=f32)  7.49 us
    all_to_all x1, starting transfers between devices, on_device(): got = lax.all_to_all(a_blocks, ('dp', 'space'), 0, 0, tiled=True)  6.93 us
    dot_general x1, matrix products, on_device(): lax.dot_general(grad_flat, patches_t, contract_cells, preferred_element_t...  5.33 us
  transfers between devices with their start and end apart: 9, of which 5 were waited for; matrix products, arithmetic and copies ran while one was open for 45% of the time, Pallas kernels for 0%

profile of v7, /device:TPU:0, one launch (start us, length us, event | category | flops | bytes accessed | tf_op | source)
XLA Modules:
  0.0 137.8 jit_solution(163711167494180145)
XLA Ops:
  7.2 1.0 fusion.50
  8.2 4.9 %collective-permute-start = (bf16[1,32,1,16,128]{4,3,2,1,0:T(8,128)(2,1)S(1)}, bf16[1,32,1,16,128]{4,3,2,1,0:T(8,128)(2,1)S(1)}, u32[]{:S(2)}, u32[]{:S(2)}) collective-permute-start(bf16[1,32,1,16,128]{4,3,2,1,0:T(8,128)(2,1)S(1)} %get-tuple-element.8), channel_id=1, source_target_pairs={{0,1},{1,2},{2,3},{4,5},{5,6},{6,7},{8,9},{9,10},{10,11},{12,13},{... | collective-permute-start | bytes 393224 | tf_op jit(solution)/shard_map/ppermute | solution.py:17
  13.2 1.3 collective-permute-start.1
  14.5 3.4 %convert_reduce_fusion = f32[4096]{0:T(1024)S(1)} fusion(s32[1024]{0:T(1024)} %bitcast.153), kind=kLoop, calls=%fused_computation | loop fusion | flops 12578816 | bytes 20480 | tf_op jit(solution)/shard_map/reduce_sum | solution.py:128
  17.9 1.1 reshape_squeeze.3
  18.9 1.3 convolution_bitcast_fusion.1
  20.2 1.0 maximum_bitcast_fusion
  21.3 0.9 pad_bitcast_fusion
  27.5 2.9 %copy-done.2 = bf16[27,2,16,32,128]{4,2,1,3,0:T(8,128)(2,1)} copy-done((bf16[27,2,16,32,128]{4,2,1,3,0:T(8,128)(2,1)}, bf16[27,2,16,32,128]{4,2,1,3,0:T(8,128)(2,1)S(1)}, u32[]{:S(2)}) %copy-start.2) | copy-done | bytes 7077912
  30.4 11.6 %reshape.57 = bf16[864,4096]{1,0:T(8,128)(2,1)} reshape(bf16[27,32,2,16,128]{4,3,2,1,0:T(8,128)(2,1)} %bitcast.147) | data formatting | bytes 14155776 | tf_op jit(solution)/shard_map/reshape | solution.py:108
  42.0 5.3 %convolution_bitcast_fusion = f32[32,864]{1,0:T(8,128)S(1)} fusion(bf16[864,4096]{1,0:T(8,128)(2,1)} %reshape.57, bf16[32,4096]{1,0:T(8,128)(2,1)S(1)} %reshape_squeeze.3), kind=kOutput, calls=%fused_computation.21 | convolution fusion | flops 226492416 | bytes 7450624 | tf_op jit(solution)/shard_map/dot_general | solution.py:112
  47.4 7.5 %fusion.1 = f32[864,864]{1,0:T(8,128)S(1)} fusion(bf16[864,4096]{1,0:T(8,128)(2,1)S(1)} %copy-done.1, f32[4096]{0:T(1024)S(1)} %convert_reduce_fusion), kind=kOutput, calls=%fused_computation.5 | convolution fusion | flops 6125912064 | bytes 10080256 | tf_op jit(solution)/shard_map/dot_general | solution.py:136
  54.9 7.8 %multiply_convert_fusion = bf16[864,864]{1,0:T(8,128)(2,1)S(1)} fusion(f32[864,864]{1,0:T(8,128)S(1)} %fusion.1, bf16[864,4096]{1,0:T(8,128)(2,1)S(1)} %copy-done.1, f32[4096]{0:T(1024)S(1)} %convert_reduce_fusion), kind=kOutput, calls=%fused_computation.11 | convolution fusion | flops 6138768384 | bytes 11573248 | tf_op jit(solution)/shard_map/dot_general | solution.py:137
  62.7 3.8 %fusion.9 = bf16[864,864]{1,0:T(8,128)(2,1)S(1)} fusion(s32[864]{0:T(1024)S(1)} %fusion.47, bf16[864,864]{1,0:T(8,128)(2,1)S(1)} %multiply_convert_fusion), kind=kOutput, calls=%fused_computation.16 | convolution fusion | flops 2582876160 | bytes 2989440 | tf_op jit(solution)/shard_map/dot_general | solution.py:141
  66.5 1.6 %reshape.62 = bf16[8,108,4,216]{3,2,1,0:T(4,128)(2,1)S(1)} reshape(bf16[864,864]{1,0:T(8,128)(2,1)S(1)} %fusion.9) | data formatting | bytes 2985984 | tf_op jit(solution)/shard_map/reshape | solution.py:147
  68.1 2.5 %copy.20 = bf16[8,108,4,216]{1,3,2,0:T(8,128)(2,1)} copy(bf16[8,108,4,216]{3,2,1,0:T(4,128)(2,1)S(1)} %reshape.62) | data formatting | bytes 2985984 | tf_op jit(solution)/shard_map/reshape | solution.py:147
  70.6 6.9 %all-to-all-start = ((bf16[32,108,216]{1,2,0:T(8,128)(2,1)}), bf16[32,108,216]{1,2,0:T(8,128)(2,1)S(1)}, u32[]{:S(2)}, u32[]{:S(2)}) async-start(bf16[32,108,216]{1,2,0:T(8,128)(2,1)} %bitcast.38), calls=%async_computation | async-start | bytes 3538944 | tf_op jit(solution)/shard_map/all_to_all | solution.py:149
  77.6 0.3 collective-permute-start.2
  77.9 1.1 collective-permute-done.2
  79.0 1.8 %collective-permute-start.3 = (f32[32,896]{1,0:T(8,128)S(1)}, f32[32,896]{1,0:T(8,128)S(1)}, u32[]{:S(2)}, u32[]{:S(2)}) collective-permute-start(f32[32,896]{1,0:T(8,128)S(1)} %add.49), channel_id=1, source_target_pairs={{0,8},{4,12},{8,0},{12,4},{16,24},{20,28},{24,16},{28,20},{1,9},{5... | collective-permute-start | bytes 344072 | tf_op jit(solution)/shard_map/ppermute | solution.py:34
  80.8 13.4 %collective-permute-done.3 = f32[32,896]{1,0:T(8,128)S(1)} collective-permute-done((f32[32,896]{1,0:T(8,128)S(1)}, f32[32,896]{1,0:T(8,128)S(1)}, u32[]{:S(2)}, u32[]{:S(2)}) %collective-permute-start.3) | collective-permute-done | bytes 114720 | tf_op jit(solution)/shard_map/ppermute | solution.py:34
  94.2 1.5 %collective-permute-start.4 = (f32[32,896]{1,0:T(8,128)S(1)}, f32[32,896]{1,0:T(8,128)S(1)}, u32[]{:S(2)}, u32[]{:S(2)}) collective-permute-start(f32[32,896]{1,0:T(8,128)S(1)} %add.50), channel_id=1, source_target_pairs={{0,16},{4,20},{8,24},{12,28},{16,0},{20,4},{24,8},{28,12},{1,17},{... | collective-permute-start | bytes 344072 | tf_op jit(solution)/shard_map/ppermute | solution.py:34
  95.7 3.9 %collective-permute-done.4 = f32[32,896]{1,0:T(8,128)S(1)} collective-permute-done((f32[32,896]{1,0:T(8,128)S(1)}, f32[32,896]{1,0:T(8,128)S(1)}, u32[]{:S(2)}, u32[]{:S(2)}) %collective-permute-start.4) | collective-permute-done | bytes 114720 | tf_op jit(solution)/shard_map/ppermute | solution.py:34
  99.7 0.6 reshape.59
  100.9 8.5 %collective-permute-done.5 = f32[32,896]{1,0:T(8,128)S(1)} collective-permute-done((f32[32,896]{1,0:T(8,128)S(1)}, f32[32,896]{1,0:T(8,128)S(1)}, u32[]{:S(2)}, u32[]{:S(2)}) %collective-permute-start.5) | collective-permute-done | bytes 114720 | tf_op jit(solution)/shard_map/ppermute | solution.py:34
  109.4 4.4 %collective-permute-start.6 = (f32[32,896]{1,0:T(8,128)S(1)}, f32[32,896]{1,0:T(8,128)S(1)}, u32[]{:S(2)}, u32[]{:S(2)}) collective-permute-start(f32[32,896]{1,0:T(8,128)S(1)} %add.52), channel_id=1, source_target_pairs={{0,2},{1,3},{2,0},{3,1},{4,6},{5,7},{6,4},{7,5},{8,10},{9,11},{10,... | collective-permute-start | bytes 344072 | tf_op jit(solution)/shard_map/ppermute | solution.py:34
  113.8 4.3 %fusion.12 = bf16[4,8,32,128]{3,1,2,0:T(8,128)(2,1)S(1)} fusion(bf16[32,864]{1,0:T(8,128)(2,1)S(1)} %reshape.60, bf16[864,4096]{1,0:T(8,128)(2,1)} %reshape.57), kind=kOutput, calls=%fused_computation.20 | convolution fusion | flops 226623488 | bytes 7395328 | tf_op jit(solution)/shard_map/dot_general | solution.py:124
  118.1 0.8 copy.23
  118.9 5.3 %collective-permute-done.6 = f32[32,896]{1,0:T(8,128)S(1)} collective-permute-done((f32[32,896]{1,0:T(8,128)S(1)}, f32[32,896]{1,0:T(8,128)S(1)}, u32[]{:S(2)}, u32[]{:S(2)}) %collective-permute-start.6) | collective-permute-done | bytes 114720 | tf_op jit(solution)/shard_map/ppermute | solution.py:34
  124.2 0.7 slice.151
  125.8 1.0 convert_reduce_fusion.1
  126.8 4.1 %fusion.52 = f32[32,864]{1,0:T(8,128)} fusion(f32[864,32]{0,1:T(8,128)S(1)} %fusion.51, f32[864,864]{1,0:T(8,128)} %all-gather.2.cloned.1.call-done), kind=kOutput, calls=%fused_computation.95 | convolution fusion | flops 286654464 | bytes 3207168 | tf_op jit(solution)/shard_map/dot_general | solution.py:122
  (54 shorter events, 7.1 us)
Async XLA Ops:
  7.2 118.4 %copy-start = (f32[32,32]{1,0:T(8,128)S(1)}, f32[32,32]{1,0:T(8,128)}, u32[]{:S(2)}) copy-start(f32[32,32]{1,0:T(8,128)} %param.11) | copy-start | bytes 12292
  7.2 119.7 %all-gather.2.cloned.1.call-start = ((), (), s32[]{:S(2)}) async-start(), calls=%async_computation.1 | async-start | bytes 3870720 | tf_op jit(solution)/shard_map/all_gather | solution.py:97
  8.2 12.0 %collective-permute-start = (bf16[1,32,1,16,128]{4,3,2,1,0:T(8,128)(2,1)S(1)}, bf16[1,32,1,16,128]{4,3,2,1,0:T(8,128)(2,1)S(1)}, u32[]{:S(2)}, u32[]{:S(2)}) collective-permute-start(bf16[1,32,1,16,128]{4,3,2,1,0:T(8,128)(2,1)S(1)} %get-tuple-element.8), channel_id=1, source_target_pairs={{0,1},{1,2},{2,3},{4,5},{5,6},{6,7},{8,9},{9,10},{10,11},{12,13},{... | collective-permute-start | bytes 393224 | tf_op jit(solution)/shard_map/ppermute | solution.py:17
  13.2 7.1 %collective-permute-start.1 = (bf16[1,32,1,16,128]{4,3,2,1,0:T(8,128)(2,1)S(1)}, bf16[1,32,1,16,128]{4,3,2,1,0:T(8,128)(2,1)S(1)}, u32[]{:S(2)}, u32[]{:S(2)}) collective-permute-start(bf16[1,32,1,16,128]{4,3,2,1,0:T(8,128)(2,1)S(1)} %get-tuple-element.9), channel_id=1, source_target_pairs={{1,0},{2,1},{3,2},{5,4},{6,5},{7,6},{9,8},{10,9},{11,10},{13,12},{... | collective-permute-start | bytes 393224 | tf_op jit(solution)/shard_map/ppermute | solution.py:19
  27.5 2.9 %copy-start.2 = (bf16[27,2,16,32,128]{4,2,1,3,0:T(8,128)(2,1)}, bf16[27,2,16,32,128]{4,2,1,3,0:T(8,128)(2,1)S(1)}, u32[]{:S(2)}) copy-start(bf16[27,2,16,32,128]{4,2,1,3,0:T(8,128)(2,1)S(1)} %fusion.13) | copy-start | bytes 21233668
  42.0 5.4 %copy-start.1 = (bf16[864,4096]{1,0:T(8,128)(2,1)S(1)}, bf16[864,4096]{1,0:T(8,128)(2,1)}, u32[]{:S(2)}) copy-start(bf16[864,4096]{1,0:T(8,128)(2,1)} %reshape.57) | copy-start | bytes 21233668
  66.5 33.2 %copy-start.3 = (bf16[32,864]{1,0:T(8,128)(2,1)S(1)}, bf16[32,864]{1,0:T(8,128)(2,1)}, u32[]{:S(2)}) copy-start(bf16[32,864]{1,0:T(8,128)(2,1)} %param.8) | copy-start | bytes 165892
  70.6 55.2 %all-to-all-start = ((bf16[32,108,216]{1,2,0:T(8,128)(2,1)}), bf16[32,108,216]{1,2,0:T(8,128)(2,1)S(1)}, u32[]{:S(2)}, u32[]{:S(2)}) async-start(bf16[32,108,216]{1,2,0:T(8,128)(2,1)} %bitcast.38), calls=%async_computation | async-start | bytes 3538944 | tf_op jit(solution)/shard_map/all_to_all | solution.py:149
  77.6 1.4 %collective-permute-start.2 = (f32[32,896]{1,0:T(8,128)S(1)}, f32[32,896]{1,0:T(8,128)S(1)}, u32[]{:S(2)}, u32[]{:S(2)}) collective-permute-start(f32[32,896]{1,0:T(8,128)S(1)} %pad_maximum_fusion), channel_id=1, source_target_pairs={{0,4},{4,0},{8,12},{12,8},{16,20},{20,16},{24,28},{28,24},{1,5},{5... | collective-permute-start | bytes 344072 | tf_op jit(solution)/shard_map/ppermute | solution.py:34
  79.0 15.2 %collective-permute-start.3 = (f32[32,896]{1,0:T(8,128)S(1)}, f32[32,896]{1,0:T(8,128)S(1)}, u32[]{:S(2)}, u32[]{:S(2)}) collective-permute-start(f32[32,896]{1,0:T(8,128)S(1)} %add.49), channel_id=1, source_target_pairs={{0,8},{4,12},{8,0},{12,4},{16,24},{20,28},{24,16},{28,20},{1,9},{5... | collective-permute-start | bytes 344072 | tf_op jit(solution)/shard_map/ppermute | solution.py:34
  94.2 5.4 %collective-permute-start.4 = (f32[32,896]{1,0:T(8,128)S(1)}, f32[32,896]{1,0:T(8,128)S(1)}, u32[]{:S(2)}, u32[]{:S(2)}) collective-permute-start(f32[32,896]{1,0:T(8,128)S(1)} %add.50), channel_id=1, source_target_pairs={{0,16},{4,20},{8,24},{12,28},{16,0},{20,4},{24,8},{28,12},{1,17},{... | collective-permute-start | bytes 344072 | tf_op jit(solution)/shard_map/ppermute | solution.py:34
  99.6 9.8 %collective-permute-start.5 = (f32[32,896]{1,0:T(8,128)S(1)}, f32[32,896]{1,0:T(8,128)S(1)}, u32[]{:S(2)}, u32[]{:S(2)}) collective-permute-start(f32[32,896]{1,0:T(8,128)S(1)} %add.51), channel_id=1, source_target_pairs={{0,1},{1,0},{2,3},{3,2},{4,5},{5,4},{6,7},{7,6},{8,9},{9,8},{10,11... | collective-permute-start | bytes 344072 | tf_op jit(solution)/shard_map/ppermute | solution.py:34
  109.4 14.7 %collective-permute-start.6 = (f32[32,896]{1,0:T(8,128)S(1)}, f32[32,896]{1,0:T(8,128)S(1)}, u32[]{:S(2)}, u32[]{:S(2)}) collective-permute-start(f32[32,896]{1,0:T(8,128)S(1)} %add.52), channel_id=1, source_target_pairs={{0,2},{1,3},{2,0},{3,1},{4,6},{5,7},{6,4},{7,5},{8,10},{9,11},{10,... | collective-permute-start | bytes 344072 | tf_op jit(solution)/shard_map/ppermute | solution.py:34
Sparse Core Ops, SparseCore 0:
  14.6 64.9 all-gather.1

commit v8 on v7

--- a/solution.py
+++ b/solution.py
@@ -3,6 +3,7 @@
 import jax
 import jax.numpy as jnp
 from jax import lax
+from jax.experimental import pallas as pl
 from jax.sharding import PartitionSpec as P
 
 
@@ -62,6 +63,29 @@
     return x
 
 
+def patch_matrix(slab, planes, y_cells, x_cells):
+    channels = slab.shape[2]
+    cells = planes * y_cells * x_cells
+    shifted = jnp.stack([slab[:, :, :, dx : dx + x_cells] for dx in range(3)])
+
+    def body(src_ref, out_ref):
+        tap = pl.program_id(0)
+        dz = tap // 9
+        dy = (tap // 3) % 3
+        dx = tap % 3
+        for z in range(planes):
+            for y in range(y_cells):
+                out_ref[:, pl.ds((z * y_cells + y) * x_cells, x_cells)] = src_ref[dx, z + dz, y + dy]
+
+    return pl.pallas_call(
+        body,
+        grid=(27,),
+        in_specs=[pl.BlockSpec(shifted.shape, lambda tap: (0, 0, 0, 0, 0))],
+        out_specs=pl.BlockSpec((channels, cells), lambda tap: (tap, 0)),
+        out_shape=jax.ShapeDtypeStruct((27 * channels, cells), slab.dtype),
+    )(shifted)
+
+
 def tap_order(channels, n_taps):
     size = channels * n_taps
     new = jnp.arange(size, dtype=jnp.int32)
@@ -99,13 +123,7 @@
     block = padded_2(volume, (("space", 2),), 1)
     padded = jnp.pad(block[0], ((0, 0), (0, 0), (1, 1), (1, 1)))
     slab = jnp.transpose(padded, (1, 2, 0, 3))
-    taps = [
-        slab[dz : dz + planes, dy : dy + y_cells, :, dx : dx + x_cells]
-        for dz in range(3)
-        for dy in range(3)
-        for dx in range(3)
-    ]
-    patches_t = jnp.stack(taps, axis=0).transpose(0, 3, 1, 2, 4).reshape(patch, cells)
+    patches_t = patch_matrix(slab, planes, y_cells, x_cells)
     grad_flat = out_grad[0].reshape(channels, cells)
     kernel_perm = kernel.reshape(channels, channels, n_taps).transpose(0, 2, 1).reshape(channels, patch)
 

time: 139 us -> 136 us (0.978)
  local copies, waits for them, and re-layouts: 30.2 us -> 10.4 us
  Pallas kernels: 0 us -> 12.1 us
  waiting for transfers between devices: 32.2 us -> 35.1 us
  matrix products: 34.3 us -> 36.6 us
    pallas_call x0 -> x1, Pallas kernels: none -> 12.1 us  [patch_matrix(): pl.pallas_call(body, grid=(27,), in_specs=[pl.BlockSpec(shifted.shape, la...]
    reshape x1 -> x0, local copies, waits for them, and re-layouts: 11.6 us -> none  [on_device(): jnp.stack(taps, axis=0).transpose(0, 3, 1, 2, 4).reshape(patch, cells)]
    unnamed x35 -> x8, local copies, waits for them, and re-layouts: 8.66 us -> 1.83 us
    ppermute x5, waiting for transfers between devices: 32.1 us -> 35.1 us  [butterfly_sum(): x = x + lax.ppermute(x, axis, partner(axis, step))]
    another operation x0 -> x1, other arithmetic: none -> 1.4 us  [patch_matrix(): shifted = jnp.stack([slab[:, :, :, dx:dx + x_cells] for dx in range(3)])]
    dot_general x1, matrix products: 3.76 us -> 5.16 us  [on_device(): lax.dot_general(a_rows.astype(jnp.bfloat16), order, contract_cells, prefe...]
  transfers between devices with their start and end apart: 9 -> 9, of which waited for: 5 -> 5; matrix products, arithmetic and copies ran while one was open for 45% -> 35% of each run, Pallas kernels for 0% -> 9%
where the time goes in v8:
time: 136 us
  matrix products  36.6 us (27%)
  waiting for transfers between devices  35.1 us (26%)
  starting transfers between devices  21.5 us (16%)
  between operations  14.2 us (10%)
  Pallas kernels  12.1 us (9%)
  local copies, waits for them, and re-layouts  10.4 us (8%)
  other arithmetic  6 us (4%)
    ppermute x5, waiting for transfers between devices, butterfly_sum(): x = x + lax.ppermute(x, axis, partner(axis, step))  35.1 us
    pallas_call x1, Pallas kernels, patch_matrix(): pl.pallas_call(body, grid=(27,), in_specs=[pl.BlockSpec(shifted.shape, la...  12.1 us
    dot_general x1, matrix products, on_device(): lax.dot_general(low, patches_t, contract_cells, preferred_element_type=f32)  8.7 us
    ppermute x5, starting transfers between devices, butterfly_sum(): x = x + lax.ppermute(x, axis, partner(axis, step))  8.34 us
    dot_general x1, matrix products, on_device(): lax.dot_general(high, patches_t, contract_cells, preferred_element_type=f32)  7.5 us
    all_to_all x1, starting transfers between devices, on_device(): got = lax.all_to_all(a_blocks, ('dp', 'space'), 0, 0, tiled=True)  6.92 us
    dot_general x1, matrix products, on_device(): lax.dot_general(grad_flat, patches_t, contract_cells, preferred_element_t...  5.3 us
    dot_general x1, matrix products, on_device(): lax.dot_general(a_rows.astype(jnp.bfloat16), order, contract_cells, prefe...  5.16 us
  transfers between devices with their start and end apart: 9, of which 5 were waited for; matrix products, arithmetic and copies ran while one was open for 35% of the time, Pallas kernels for 9%

profile of v8, /device:TPU:0, one launch (start us, length us, event | category | flops | bytes accessed | tf_op | source)
XLA Modules:
  0.0 135.9 jit_solution(13166953625508025917)
XLA Ops:
  7.2 1.1 copy.23
  8.3 4.9 %collective-permute-start = (bf16[1,32,1,16,128]{4,1,3,2,0:T(8,128)(2,1)S(1)}, bf16[1,32,1,16,128]{4,1,3,2,0:T(8,128)(2,1)S(1)}, u32[]{:S(2)}, u32[]{:S(2)}) collective-permute-start(bf16[1,32,1,16,128]{4,1,3,2,0:T(8,128)(2,1)S(1)} %get-tuple-element.11), channel_id=1, source_target_pairs={{0,1},{1,2},{2,3},{4,5},{5,6},{6,7},{8,9},{9,10},{10,11},{12,13},{... | collective-permute-start | bytes 393224 | tf_op jit(solution)/shard_map/ppermute | solution.py:18
  13.3 1.3 collective-permute-start.1
  14.6 3.4 %convert_reduce_fusion = f32[4096]{0:T(1024)S(1)} fusion(s32[1024]{0:T(1024)} %bitcast.47), kind=kLoop, calls=%fused_computation | loop fusion | flops 12578816 | bytes 20480 | tf_op jit(solution)/shard_map/reduce_sum | solution.py:146
  17.9 1.1 reshape_squeeze.3
  19.0 1.3 convolution_bitcast_fusion.1
  20.4 0.4 pad_bitcast_fusion
  20.8 0.4 slice_bitcast_fusion.2
  21.3 1.4 %pad_maximum_fusion.src_ref = bf16[3,4,18,32,128]{4,3,2,1,0:T(8,128)(2,1)} fusion(bf16[1,4,18,32,128]{4,3,2,1,0:T(8,128)(2,1)S(1)} %get-tuple-element.9, bf16[1,4,18,32,128]{4,3,2,1,0:T(8,128)(2,1)S(1)} %get-tuple-element.10, bf16[1,4,18,32,128]{4,3,2,1,0:T(8,128)(2,1)S(1)} %get-tuple-element.8), kind=kLoop, calls=%fused_computation.15 | loop fusion | flops 1769472 | bytes 3538944 | tf_op jit(solution)/shard_map/stack | solution.py:69
  22.7 12.1 %shard_map.93 = bf16[864,4096]{1,0:T(8,128)(2,1)} custom-call(bf16[3,4,18,32,128]{4,3,2,1,0:T(8,128)(2,1)} %pad_maximum_fusion.src_ref), custom_call_target="tpu_custom_call" | custom-call | tf_op jit(solution)/shard_map/pallas_call | solution.py:80
  34.7 5.3 %convolution_bitcast_fusion = f32[32,864]{1,0:T(8,128)S(1)} fusion(bf16[864,4096]{1,0:T(8,128)(2,1)} %shard_map.93, bf16[32,4096]{1,0:T(8,128)(2,1)S(1)} %reshape_squeeze.3), kind=kOutput, calls=%fused_computation.22 | convolution fusion | flops 226492416 | bytes 7450624 | tf_op jit(solution)/shard_map/dot_general | solution.py:130
  40.1 7.5 %fusion.1 = f32[864,864]{1,0:T(8,128)S(1)} fusion(bf16[864,4096]{1,0:T(8,128)(2,1)S(1)} %copy-done.1, f32[4096]{0:T(1024)S(1)} %convert_reduce_fusion), kind=kOutput, calls=%fused_computation.5 | convolution fusion | flops 6125912064 | bytes 10080256 | tf_op jit(solution)/shard_map/dot_general | solution.py:154
  47.6 8.7 %multiply_convert_fusion = bf16[864,864]{1,0:T(8,128)(2,1)} fusion(f32[864,864]{1,0:T(8,128)S(1)} %fusion.1, bf16[864,4096]{1,0:T(8,128)(2,1)S(1)} %copy-done.1, f32[4096]{0:T(1024)S(1)} %convert_reduce_fusion), kind=kOutput, calls=%fused_computation.11 | convolution fusion | flops 6138768384 | bytes 11573248 | tf_op jit(solution)/shard_map/dot_general | solution.py:155
  56.3 5.2 %fusion.9 = bf16[864,864]{1,0:T(8,128)(2,1)S(1)} fusion(s32[864]{0:T(1024)S(1)} %fusion.20, bf16[864,864]{1,0:T(8,128)(2,1)} %multiply_convert_fusion), kind=kOutput, calls=%fused_computation.17 | convolution fusion | flops 2582876160 | bytes 2989440 | tf_op jit(solution)/shard_map/dot_general | solution.py:159
  61.5 1.6 %reshape.58 = bf16[8,108,4,216]{3,2,1,0:T(4,128)(2,1)S(1)} reshape(bf16[864,864]{1,0:T(8,128)(2,1)S(1)} %fusion.9) | data formatting | bytes 2985984 | tf_op jit(solution)/shard_map/reshape | solution.py:165
  63.1 2.5 %copy.29 = bf16[8,108,4,216]{1,3,2,0:T(8,128)(2,1)} copy(bf16[8,108,4,216]{3,2,1,0:T(4,128)(2,1)S(1)} %reshape.58) | data formatting | bytes 2985984 | tf_op jit(solution)/shard_map/reshape | solution.py:165
  65.6 6.9 %all-to-all-start = ((bf16[32,108,216]{1,2,0:T(8,128)(2,1)}), bf16[32,108,216]{1,2,0:T(8,128)(2,1)S(1)}, u32[]{:S(2)}, u32[]{:S(2)}) async-start(bf16[32,108,216]{1,2,0:T(8,128)(2,1)} %bitcast.13), calls=%async_computation | async-start | bytes 3538944 | tf_op jit(solution)/shard_map/all_to_all | solution.py:167
  72.5 0.3 collective-permute-start.2
  72.9 1.1 collective-permute-done.2
  73.9 1.8 %collective-permute-start.3 = (f32[32,896]{1,0:T(8,128)S(1)}, f32[32,896]{1,0:T(8,128)S(1)}, u32[]{:S(2)}, u32[]{:S(2)}) collective-permute-start(f32[32,896]{1,0:T(8,128)S(1)} %add.49), channel_id=1, source_target_pairs={{0,8},{4,12},{8,0},{12,4},{16,24},{20,28},{24,16},{28,20},{1,9},{5... | collective-permute-start | bytes 344072 | tf_op jit(solution)/shard_map/ppermute | solution.py:35
  75.8 11.6 %collective-permute-done.3 = f32[32,896]{1,0:T(8,128)S(1)} collective-permute-done((f32[32,896]{1,0:T(8,128)S(1)}, f32[32,896]{1,0:T(8,128)S(1)}, u32[]{:S(2)}, u32[]{:S(2)}) %collective-permute-start.3) | collective-permute-done | bytes 114720 | tf_op jit(solution)/shard_map/ppermute | solution.py:35
  87.4 1.5 %collective-permute-start.4 = (f32[32,896]{1,0:T(8,128)S(1)}, f32[32,896]{1,0:T(8,128)S(1)}, u32[]{:S(2)}, u32[]{:S(2)}) collective-permute-start(f32[32,896]{1,0:T(8,128)S(1)} %add.50), channel_id=1, source_target_pairs={{0,16},{4,20},{8,24},{12,28},{16,0},{20,4},{24,8},{28,12},{1,17},{... | collective-permute-start | bytes 344072 | tf_op jit(solution)/shard_map/ppermute | solution.py:35
  88.9 4.7 %collective-permute-done.4 = f32[32,896]{1,0:T(8,128)S(1)} collective-permute-done((f32[32,896]{1,0:T(8,128)S(1)}, f32[32,896]{1,0:T(8,128)S(1)}, u32[]{:S(2)}, u32[]{:S(2)}) %collective-permute-start.4) | collective-permute-done | bytes 114720 | tf_op jit(solution)/shard_map/ppermute | solution.py:35
  93.8 0.6 reshape.55
  95.0 12.1 %collective-permute-done.5 = f32[32,896]{1,0:T(8,128)S(1)} collective-permute-done((f32[32,896]{1,0:T(8,128)S(1)}, f32[32,896]{1,0:T(8,128)S(1)}, u32[]{:S(2)}, u32[]{:S(2)}) %collective-permute-start.5) | collective-permute-done | bytes 114720 | tf_op jit(solution)/shard_map/ppermute | solution.py:35
  107.1 4.5 %collective-permute-start.6 = (f32[32,896]{1,0:T(8,128)S(1)}, f32[32,896]{1,0:T(8,128)S(1)}, u32[]{:S(2)}, u32[]{:S(2)}) collective-permute-start(f32[32,896]{1,0:T(8,128)S(1)} %add.52), channel_id=1, source_target_pairs={{0,2},{1,3},{2,0},{3,1},{4,6},{5,7},{6,4},{7,5},{8,10},{9,11},{10,... | collective-permute-start | bytes 344072 | tf_op jit(solution)/shard_map/ppermute | solution.py:35
  111.6 4.3 %fusion.12 = bf16[4,8,32,128]{3,1,2,0:T(8,128)(2,1)S(1)} fusion(bf16[32,864]{1,0:T(8,128)(2,1)S(1)} %reshape.56, bf16[864,4096]{1,0:T(8,128)(2,1)} %shard_map.93), kind=kOutput, calls=%fused_computation.21 | convolution fusion | flops 226623488 | bytes 7395328 | tf_op jit(solution)/shard_map/dot_general | solution.py:142
  115.9 0.8 copy.32
  116.7 5.6 %collective-permute-done.6 = f32[32,896]{1,0:T(8,128)S(1)} collective-permute-done((f32[32,896]{1,0:T(8,128)S(1)}, f32[32,896]{1,0:T(8,128)S(1)}, u32[]{:S(2)}, u32[]{:S(2)}) %collective-permute-start.6) | collective-permute-done | bytes 114720 | tf_op jit(solution)/shard_map/ppermute | solution.py:35
  122.3 0.7 slice.33
  124.0 1.0 convert_reduce_fusion.1
  125.0 4.1 %fusion.25 = f32[32,864]{1,0:T(8,128)} fusion(f32[864,32]{0,1:T(8,128)S(1)} %fusion.24, f32[864,864]{1,0:T(8,128)} %all-gather.2.cloned.1.call-done), kind=kOutput, calls=%fused_computation.45 | convolution fusion | flops 286654464 | bytes 3207168 | tf_op jit(solution)/shard_map/dot_general | solution.py:140
  (28 shorter events, 2.0 us)
Async XLA Ops:
  7.2 116.5 %copy-start = (f32[32,32]{1,0:T(8,128)S(1)}, f32[32,32]{1,0:T(8,128)}, u32[]{:S(2)}) copy-start(f32[32,32]{1,0:T(8,128)} %param.11) | copy-start | bytes 12292
  7.2 117.8 %all-gather.2.cloned.1.call-start = ((), (), s32[]{:S(2)}) async-start(), calls=%async_computation.1 | async-start | bytes 3870720 | tf_op jit(solution)/shard_map/all_gather | solution.py:121
  8.3 12.0 %collective-permute-start = (bf16[1,32,1,16,128]{4,1,3,2,0:T(8,128)(2,1)S(1)}, bf16[1,32,1,16,128]{4,1,3,2,0:T(8,128)(2,1)S(1)}, u32[]{:S(2)}, u32[]{:S(2)}) collective-permute-start(bf16[1,32,1,16,128]{4,1,3,2,0:T(8,128)(2,1)S(1)} %get-tuple-element.11), channel_id=1, source_target_pairs={{0,1},{1,2},{2,3},{4,5},{5,6},{6,7},{8,9},{9,10},{10,11},{12,13},{... | collective-permute-start | bytes 393224 | tf_op jit(solution)/shard_map/ppermute | solution.py:18
  13.3 7.1 %collective-permute-start.1 = (bf16[1,32,1,16,128]{4,1,3,2,0:T(8,128)(2,1)S(1)}, bf16[1,32,1,16,128]{4,1,3,2,0:T(8,128)(2,1)S(1)}, u32[]{:S(2)}, u32[]{:S(2)}) collective-permute-start(bf16[1,32,1,16,128]{4,1,3,2,0:T(8,128)(2,1)S(1)} %get-tuple-element.12), channel_id=1, source_target_pairs={{1,0},{2,1},{3,2},{5,4},{6,5},{7,6},{9,8},{10,9},{11,10},{13,12},{... | collective-permute-start | bytes 393224 | tf_op jit(solution)/shard_map/ppermute | solution.py:20
  34.7 5.4 %copy-start.1 = (bf16[864,4096]{1,0:T(8,128)(2,1)S(1)}, bf16[864,4096]{1,0:T(8,128)(2,1)}, u32[]{:S(2)}) copy-start(bf16[864,4096]{1,0:T(8,128)(2,1)} %shard_map.93) | copy-start | bytes 21233668
  65.6 28.2 %copy-start.2 = (bf16[32,864]{1,0:T(8,128)(2,1)S(1)}, bf16[32,864]{1,0:T(8,128)(2,1)}, u32[]{:S(2)}) copy-start(bf16[32,864]{1,0:T(8,128)(2,1)} %param.8) | copy-start | bytes 165892
  65.6 58.3 %all-to-all-start = ((bf16[32,108,216]{1,2,0:T(8,128)(2,1)}), bf16[32,108,216]{1,2,0:T(8,128)(2,1)S(1)}, u32[]{:S(2)}, u32[]{:S(2)}) async-start(bf16[32,108,216]{1,2,0:T(8,128)(2,1)} %bitcast.13), calls=%async_computation | async-start | bytes 3538944 | tf_op jit(solution)/shard_map/all_to_all | solution.py:167
  72.5 1.4 %collective-permute-start.2 = (f32[32,896]{1,0:T(8,128)S(1)}, f32[32,896]{1,0:T(8,128)S(1)}, u32[]{:S(2)}, u32[]{:S(2)}) collective-permute-start(f32[32,896]{1,0:T(8,128)S(1)} %pad_maximum_fusion.1), channel_id=1, source_target_pairs={{0,4},{4,0},{8,12},{12,8},{16,20},{20,16},{24,28},{28,24},{1,5},{5... | collective-permute-start | bytes 344072 | tf_op jit(solution)/shard_map/ppermute | solution.py:35
  73.9 13.4 %collective-permute-start.3 = (f32[32,896]{1,0:T(8,128)S(1)}, f32[32,896]{1,0:T(8,128)S(1)}, u32[]{:S(2)}, u32[]{:S(2)}) collective-permute-start(f32[32,896]{1,0:T(8,128)S(1)} %add.49), channel_id=1, source_target_pairs={{0,8},{4,12},{8,0},{12,4},{16,24},{20,28},{24,16},{28,20},{1,9},{5... | collective-permute-start | bytes 344072 | tf_op jit(solution)/shard_map/ppermute | solution.py:35
  87.4 6.3 %collective-permute-start.4 = (f32[32,896]{1,0:T(8,128)S(1)}, f32[32,896]{1,0:T(8,128)S(1)}, u32[]{:S(2)}, u32[]{:S(2)}) collective-permute-start(f32[32,896]{1,0:T(8,128)S(1)} %add.50), channel_id=1, source_target_pairs={{0,16},{4,20},{8,24},{12,28},{16,0},{20,4},{24,8},{28,12},{1,17},{... | collective-permute-start | bytes 344072 | tf_op jit(solution)/shard_map/ppermute | solution.py:35
  93.7 13.4 %collective-permute-start.5 = (f32[32,896]{1,0:T(8,128)S(1)}, f32[32,896]{1,0:T(8,128)S(1)}, u32[]{:S(2)}, u32[]{:S(2)}) collective-permute-start(f32[32,896]{1,0:T(8,128)S(1)} %add.51), channel_id=1, source_target_pairs={{0,1},{1,0},{2,3},{3,2},{4,5},{5,4},{6,7},{7,6},{8,9},{9,8},{10,11... | collective-permute-start | bytes 344072 | tf_op jit(solution)/shard_map/ppermute | solution.py:35
  107.1 15.2 %collective-permute-start.6 = (f32[32,896]{1,0:T(8,128)S(1)}, f32[32,896]{1,0:T(8,128)S(1)}, u32[]{:S(2)}, u32[]{:S(2)}) collective-permute-start(f32[32,896]{1,0:T(8,128)S(1)} %add.52), channel_id=1, source_target_pairs={{0,2},{1,3},{2,0},{3,1},{4,6},{5,7},{6,4},{7,5},{8,10},{9,11},{10,... | collective-permute-start | bytes 344072 | tf_op jit(solution)/shard_map/ppermute | solution.py:35
Sparse Core Ops, SparseCore 0:
  14.7 69.0 all-gather.1

commit v9 on v8

--- a/solution.py
+++ b/solution.py
@@ -30,10 +30,19 @@
 
 def butterfly_sum(x, axes):
     for axis in axes:
-        step = 1
-        while step < lax.axis_size(axis):
-            x = x + lax.ppermute(x, axis, partner(axis, step))
-            step *= 2
+        size = lax.axis_size(axis)
+        low = 1
+        while low < size:
+            high = low * 2
+            got = lax.ppermute(x, axis, partner(axis, low))
+            if high < size:
+                pair = lax.ppermute(x, axis, partner(axis, high))
+                other = lax.ppermute(x, axis, partner(axis, low + high))
+                x = (x + got) + (pair + other)
+                low = high * 2
+            else:
+                x = x + got
+                low = high
     return x
 
 

time: 136 us -> 139 us (1.022)
  starting transfers between devices: 21.5 us -> 23.5 us
    ppermute x5 -> x7, starting transfers between devices: 8.34 us -> 10.3 us  [the longest x2 8.35 us: butterfly_sum(): pair = lax.ppermute(x, axis, partner(axis, high))]
    ppermute x5 -> x7, waiting for transfers between devices: 35.1 us -> 35.5 us  [the longest x2 28.3 us: butterfly_sum(): pair = lax.ppermute(x, axis, partner(axis, high))]
  transfers between devices with their start and end apart: 9 -> 11, of which waited for: 5 -> 4; matrix products, arithmetic and copies ran while one was open for 35% -> 35% of each run, Pallas kernels for 9% -> 9%
where the time goes in v9:
time: 139 us; the launch traced here: 138 us
  matrix products  36.6 us (26%)
  waiting for transfers between devices  35.6 us (26%)
  starting transfers between devices  23.5 us (17%)
  between operations  14.2 us (10%)
  Pallas kernels  12.1 us (9%)
  local copies, waits for them, and re-layouts  10.4 us (7%)
  other arithmetic  5.99 us (4%)
    ppermute x2, waiting for transfers between devices, butterfly_sum(): pair = lax.ppermute(x, axis, partner(axis, high))  28.3 us
    pallas_call x1, Pallas kernels, patch_matrix(): pl.pallas_call(body, grid=(27,), in_specs=[pl.BlockSpec(shifted.shape, la...  12.1 us
    dot_general x1, matrix products, on_device(): lax.dot_general(low, patches_t, contract_cells, preferred_element_type=f32)  8.71 us
    ppermute x2, starting transfers between devices, butterfly_sum(): pair = lax.ppermute(x, axis, partner(axis, high))  8.35 us
    dot_general x1, matrix products, on_device(): lax.dot_general(high, patches_t, contract_cells, preferred_element_type=f32)  7.5 us
    all_to_all x1, starting transfers between devices, on_device(): got = lax.all_to_all(a_blocks, ('dp', 'space'), 0, 0, tiled=True)  6.92 us
    dot_general x1, matrix products, on_device(): lax.dot_general(grad_flat, patches_t, contract_cells, preferred_element_t...  5.31 us
    dot_general x1, matrix products, on_device(): lax.dot_general(a_rows.astype(jnp.bfloat16), order, contract_cells, prefe...  5.16 us
  transfers between devices with their start and end apart: 11, of which 4 were waited for; matrix products, arithmetic and copies ran while one was open for 35% of the time, Pallas kernels for 9%

profile of v9, /device:TPU:0, one launch (start us, length us, event | category | flops | bytes accessed | tf_op | source)
XLA Modules:
  0.0 138.4 jit_solution(11295721022724542871)
XLA Ops:
  7.2 1.1 copy.23
  8.3 4.9 %collective-permute-start = (bf16[1,32,1,16,128]{4,1,3,2,0:T(8,128)(2,1)S(1)}, bf16[1,32,1,16,128]{4,1,3,2,0:T(8,128)(2,1)S(1)}, u32[]{:S(2)}, u32[]{:S(2)}) collective-permute-start(bf16[1,32,1,16,128]{4,1,3,2,0:T(8,128)(2,1)S(1)} %get-tuple-element.11), channel_id=1, source_target_pairs={{0,1},{1,2},{2,3},{4,5},{5,6},{6,7},{8,9},{9,10},{10,11},{12,13},{... | collective-permute-start | bytes 393224 | tf_op jit(solution)/shard_map/ppermute | solution.py:18
  13.3 1.3 collective-permute-start.1
  14.6 3.4 %convert_reduce_fusion = f32[4096]{0:T(1024)S(1)} fusion(s32[1024]{0:T(1024)} %bitcast.47), kind=kLoop, calls=%fused_computation | loop fusion | flops 12578816 | bytes 20480 | tf_op jit(solution)/shard_map/reduce_sum | solution.py:155
  17.9 1.1 reshape_squeeze.3
  19.0 1.3 convolution_bitcast_fusion.1
  20.4 0.4 pad_bitcast_fusion
  20.8 0.4 slice_bitcast_fusion.2
  21.3 1.4 %pad_maximum_fusion.src_ref = bf16[3,4,18,32,128]{4,3,2,1,0:T(8,128)(2,1)} fusion(bf16[1,4,18,32,128]{4,3,2,1,0:T(8,128)(2,1)S(1)} %get-tuple-element.9, bf16[1,4,18,32,128]{4,3,2,1,0:T(8,128)(2,1)S(1)} %get-tuple-element.10, bf16[1,4,18,32,128]{4,3,2,1,0:T(8,128)(2,1)S(1)} %get-tuple-element.8), kind=kLoop, calls=%fused_computation.15 | loop fusion | flops 1769472 | bytes 3538944 | tf_op jit(solution)/shard_map/stack | solution.py:78
  22.7 12.1 %shard_map.93 = bf16[864,4096]{1,0:T(8,128)(2,1)} custom-call(bf16[3,4,18,32,128]{4,3,2,1,0:T(8,128)(2,1)} %pad_maximum_fusion.src_ref), custom_call_target="tpu_custom_call" | custom-call | tf_op jit(solution)/shard_map/pallas_call | solution.py:89
  34.8 5.3 %convolution_bitcast_fusion = f32[32,864]{1,0:T(8,128)S(1)} fusion(bf16[864,4096]{1,0:T(8,128)(2,1)} %shard_map.93, bf16[32,4096]{1,0:T(8,128)(2,1)S(1)} %reshape_squeeze.3), kind=kOutput, calls=%fused_computation.22 | convolution fusion | flops 226492416 | bytes 7450624 | tf_op jit(solution)/shard_map/dot_general | solution.py:139
  40.2 7.5 %fusion.1 = f32[864,864]{1,0:T(8,128)S(1)} fusion(bf16[864,4096]{1,0:T(8,128)(2,1)S(1)} %copy-done.1, f32[4096]{0:T(1024)S(1)} %convert_reduce_fusion), kind=kOutput, calls=%fused_computation.5 | convolution fusion | flops 6125912064 | bytes 10080256 | tf_op jit(solution)/shard_map/dot_general | solution.py:163
  47.7 8.7 %multiply_convert_fusion = bf16[864,864]{1,0:T(8,128)(2,1)} fusion(f32[864,864]{1,0:T(8,128)S(1)} %fusion.1, bf16[864,4096]{1,0:T(8,128)(2,1)S(1)} %copy-done.1, f32[4096]{0:T(1024)S(1)} %convert_reduce_fusion), kind=kOutput, calls=%fused_computation.11 | convolution fusion | flops 6138768384 | bytes 11573248 | tf_op jit(solution)/shard_map/dot_general | solution.py:164
  56.4 5.2 %fusion.9 = bf16[864,864]{1,0:T(8,128)(2,1)S(1)} fusion(s32[864]{0:T(1024)S(1)} %fusion.20, bf16[864,864]{1,0:T(8,128)(2,1)} %multiply_convert_fusion), kind=kOutput, calls=%fused_computation.17 | convolution fusion | flops 2582876160 | bytes 2989440 | tf_op jit(solution)/shard_map/dot_general | solution.py:168
  61.6 1.6 %reshape.58 = bf16[8,108,4,216]{3,2,1,0:T(4,128)(2,1)S(1)} reshape(bf16[864,864]{1,0:T(8,128)(2,1)S(1)} %fusion.9) | data formatting | bytes 2985984 | tf_op jit(solution)/shard_map/reshape | solution.py:174
  63.1 2.5 %copy.29 = bf16[8,108,4,216]{1,3,2,0:T(8,128)(2,1)} copy(bf16[8,108,4,216]{3,2,1,0:T(4,128)(2,1)S(1)} %reshape.58) | data formatting | bytes 2985984 | tf_op jit(solution)/shard_map/reshape | solution.py:174
  65.7 6.9 %all-to-all-start = ((bf16[32,108,216]{1,2,0:T(8,128)(2,1)}), bf16[32,108,216]{1,2,0:T(8,128)(2,1)S(1)}, u32[]{:S(2)}, u32[]{:S(2)}) async-start(bf16[32,108,216]{1,2,0:T(8,128)(2,1)} %bitcast.13), calls=%async_computation | async-start | bytes 3538944 | tf_op jit(solution)/shard_map/all_to_all | solution.py:176
  72.6 0.3 collective-permute-start.2
  72.9 1.7 %collective-permute-start.3 = (f32[32,896]{1,0:T(8,128)S(1)}, f32[32,896]{1,0:T(8,128)S(1)}, u32[]{:S(2)}, u32[]{:S(2)}) collective-permute-start(f32[32,896]{1,0:T(8,128)S(1)} %pad_maximum_fusion.1), channel_id=1, source_target_pairs={{0,8},{4,12},{8,0},{12,4},{16,24},{20,28},{24,16},{28,20},{1,9},{5... | collective-permute-start | bytes 344072 | tf_op jit(solution)/shard_map/ppermute | solution.py:39
  74.6 13.3 %collective-permute-done.3 = f32[32,896]{1,0:T(8,128)S(1)} collective-permute-done((f32[32,896]{1,0:T(8,128)S(1)}, f32[32,896]{1,0:T(8,128)S(1)}, u32[]{:S(2)}, u32[]{:S(2)}) %collective-permute-start.3) | collective-permute-done | bytes 114720 | tf_op jit(solution)/shard_map/ppermute | solution.py:39
  87.9 3.2 %collective-permute-done.4 = f32[32,896]{1,0:T(8,128)S(1)} collective-permute-done((f32[32,896]{1,0:T(8,128)S(1)}, f32[32,896]{1,0:T(8,128)S(1)}, u32[]{:S(2)}, u32[]{:S(2)}) %collective-permute-start.4) | collective-permute-done | bytes 114720 | tf_op jit(solution)/shard_map/ppermute | solution.py:40
  91.2 1.5 %collective-permute-start.5 = (f32[32,896]{1,0:T(8,128)S(1)}, f32[32,896]{1,0:T(8,128)S(1)}, u32[]{:S(2)}, u32[]{:S(2)}) collective-permute-start(f32[32,896]{1,0:T(8,128)S(1)} %add_add_fusion.1), channel_id=1, source_target_pairs={{0,16},{4,20},{8,24},{12,28},{16,0},{20,4},{24,8},{28,12},{1,17},{... | collective-permute-start | bytes 344072 | tf_op jit(solution)/shard_map/ppermute | solution.py:37
  92.7 0.6 reshape.55
  93.3 0.3 copy.28
  93.9 4.0 %collective-permute-done.5 = f32[32,896]{1,0:T(8,128)S(1)} collective-permute-done((f32[32,896]{1,0:T(8,128)S(1)}, f32[32,896]{1,0:T(8,128)S(1)}, u32[]{:S(2)}, u32[]{:S(2)}) %collective-permute-start.5) | collective-permute-done | bytes 114720 | tf_op jit(solution)/shard_map/ppermute | solution.py:37
  98.0 6.7 %collective-permute-start.7 = (f32[32,896]{1,0:T(8,128)S(1)}, f32[32,896]{1,0:T(8,128)S(1)}, u32[]{:S(2)}, u32[]{:S(2)}) collective-permute-start(f32[32,896]{1,0:T(8,128)S(1)} %add.58), channel_id=1, source_target_pairs={{0,2},{1,3},{2,0},{3,1},{4,6},{5,7},{6,4},{7,5},{8,10},{9,11},{10,... | collective-permute-start | bytes 344072 | tf_op jit(solution)/shard_map/ppermute | solution.py:39
  104.7 4.3 %fusion.12 = bf16[4,8,32,128]{3,1,2,0:T(8,128)(2,1)S(1)} fusion(bf16[32,864]{1,0:T(8,128)(2,1)S(1)} %reshape.56, bf16[864,4096]{1,0:T(8,128)(2,1)} %shard_map.93), kind=kOutput, calls=%fused_computation.21 | convolution fusion | flops 226623488 | bytes 7395328 | tf_op jit(solution)/shard_map/dot_general | solution.py:151
  109.0 0.8 copy.32
  109.8 15.0 %collective-permute-done.7 = f32[32,896]{1,0:T(8,128)S(1)} collective-permute-done((f32[32,896]{1,0:T(8,128)S(1)}, f32[32,896]{1,0:T(8,128)S(1)}, u32[]{:S(2)}, u32[]{:S(2)}) %collective-permute-start.7) | collective-permute-done | bytes 114720 | tf_op jit(solution)/shard_map/ppermute | solution.py:39
  124.8 0.7 slice.33
  126.4 1.0 convert_reduce_fusion.1
  127.4 4.1 %fusion.25 = f32[32,864]{1,0:T(8,128)} fusion(f32[864,32]{0,1:T(8,128)S(1)} %fusion.24, f32[864,864]{1,0:T(8,128)} %all-gather.2.cloned.1.call-done), kind=kOutput, calls=%fused_computation.47 | convolution fusion | flops 286654464 | bytes 3207168 | tf_op jit(solution)/shard_map/dot_general | solution.py:149
  (30 shorter events, 1.6 us)
Async XLA Ops:
  7.2 119.0 %copy-start = (f32[32,32]{1,0:T(8,128)S(1)}, f32[32,32]{1,0:T(8,128)}, u32[]{:S(2)}) copy-start(f32[32,32]{1,0:T(8,128)} %param.11) | copy-start | bytes 12292
  7.2 120.3 %all-gather.2.cloned.1.call-start = ((), (), s32[]{:S(2)}) async-start(), calls=%async_computation.1 | async-start | bytes 3870720 | tf_op jit(solution)/shard_map/all_gather | solution.py:130
  8.3 12.0 %collective-permute-start = (bf16[1,32,1,16,128]{4,1,3,2,0:T(8,128)(2,1)S(1)}, bf16[1,32,1,16,128]{4,1,3,2,0:T(8,128)(2,1)S(1)}, u32[]{:S(2)}, u32[]{:S(2)}) collective-permute-start(bf16[1,32,1,16,128]{4,1,3,2,0:T(8,128)(2,1)S(1)} %get-tuple-element.11), channel_id=1, source_target_pairs={{0,1},{1,2},{2,3},{4,5},{5,6},{6,7},{8,9},{9,10},{10,11},{12,13},{... | collective-permute-start | bytes 393224 | tf_op jit(solution)/shard_map/ppermute | solution.py:18
  13.3 7.1 %collective-permute-start.1 = (bf16[1,32,1,16,128]{4,1,3,2,0:T(8,128)(2,1)S(1)}, bf16[1,32,1,16,128]{4,1,3,2,0:T(8,128)(2,1)S(1)}, u32[]{:S(2)}, u32[]{:S(2)}) collective-permute-start(bf16[1,32,1,16,128]{4,1,3,2,0:T(8,128)(2,1)S(1)} %get-tuple-element.12), channel_id=1, source_target_pairs={{1,0},{2,1},{3,2},{5,4},{6,5},{7,6},{9,8},{10,9},{11,10},{13,12},{... | collective-permute-start | bytes 393224 | tf_op jit(solution)/shard_map/ppermute | solution.py:20
  34.8 5.4 %copy-start.1 = (bf16[864,4096]{1,0:T(8,128)(2,1)S(1)}, bf16[864,4096]{1,0:T(8,128)(2,1)}, u32[]{:S(2)}) copy-start(bf16[864,4096]{1,0:T(8,128)(2,1)} %shard_map.93) | copy-start | bytes 21233668
  63.1 29.6 %copy-start.2 = (bf16[32,864]{1,0:T(8,128)(2,1)S(1)}, bf16[32,864]{1,0:T(8,128)(2,1)}, u32[]{:S(2)}) copy-start(bf16[32,864]{1,0:T(8,128)(2,1)} %param.8) | copy-start | bytes 165892
  65.7 60.8 %all-to-all-start = ((bf16[32,108,216]{1,2,0:T(8,128)(2,1)}), bf16[32,108,216]{1,2,0:T(8,128)(2,1)S(1)}, u32[]{:S(2)}, u32[]{:S(2)}) async-start(bf16[32,108,216]{1,2,0:T(8,128)(2,1)} %bitcast.13), calls=%async_computation | async-start | bytes 3538944 | tf_op jit(solution)/shard_map/all_to_all | solution.py:176
  72.6 2.0 %collective-permute-start.2 = (f32[32,896]{1,0:T(8,128)S(1)}, f32[32,896]{1,0:T(8,128)S(1)}, u32[]{:S(2)}, u32[]{:S(2)}) collective-permute-start(f32[32,896]{1,0:T(8,128)S(1)} %pad_maximum_fusion.1), channel_id=1, source_target_pairs={{0,4},{4,0},{8,12},{12,8},{16,20},{20,16},{24,28},{28,24},{1,5},{5... | collective-permute-start | bytes 344072 | tf_op jit(solution)/shard_map/ppermute | solution.py:37
  72.9 15.0 %collective-permute-start.3 = (f32[32,896]{1,0:T(8,128)S(1)}, f32[32,896]{1,0:T(8,128)S(1)}, u32[]{:S(2)}, u32[]{:S(2)}) collective-permute-start(f32[32,896]{1,0:T(8,128)S(1)} %pad_maximum_fusion.1), channel_id=1, source_target_pairs={{0,8},{4,12},{8,0},{12,4},{16,24},{20,28},{24,16},{28,20},{1,9},{5... | collective-permute-start | bytes 344072 | tf_op jit(solution)/shard_map/ppermute | solution.py:39
  74.6 16.6 %collective-permute-start.4 = (f32[32,896]{1,0:T(8,128)S(1)}, f32[32,896]{1,0:T(8,128)S(1)}, u32[]{:S(2)}, u32[]{:S(2)}) collective-permute-start(f32[32,896]{1,0:T(8,128)S(1)} %pad_maximum_fusion.1), channel_id=1, source_target_pairs={{0,12},{4,8},{8,4},{12,0},{16,28},{20,24},{24,20},{28,16},{1,13},{... | collective-permute-start | bytes 344072 | tf_op jit(solution)/shard_map/ppermute | solution.py:40
  91.2 6.8 %collective-permute-start.5 = (f32[32,896]{1,0:T(8,128)S(1)}, f32[32,896]{1,0:T(8,128)S(1)}, u32[]{:S(2)}, u32[]{:S(2)}) collective-permute-start(f32[32,896]{1,0:T(8,128)S(1)} %add_add_fusion.1), channel_id=1, source_target_pairs={{0,16},{4,20},{8,24},{12,28},{16,0},{20,4},{24,8},{28,12},{1,17},{... | collective-permute-start | bytes 344072 | tf_op jit(solution)/shard_map/ppermute | solution.py:37
  97.9 11.8 %collective-permute-start.6 = (f32[32,896]{1,0:T(8,128)S(1)}, f32[32,896]{1,0:T(8,128)S(1)}, u32[]{:S(2)}, u32[]{:S(2)}) collective-permute-start(f32[32,896]{1,0:T(8,128)S(1)} %add.58), channel_id=1, source_target_pairs={{0,1},{1,0},{2,3},{3,2},{4,5},{5,4},{6,7},{7,6},{8,9},{9,8},{10,11... | collective-permute-start | bytes 344072 | tf_op jit(solution)/shard_map/ppermute | solution.py:37
  98.0 26.7 %collective-permute-start.7 = (f32[32,896]{1,0:T(8,128)S(1)}, f32[32,896]{1,0:T(8,128)S(1)}, u32[]{:S(2)}, u32[]{:S(2)}) collective-permute-start(f32[32,896]{1,0:T(8,128)S(1)} %add.58), channel_id=1, source_target_pairs={{0,2},{1,3},{2,0},{3,1},{4,6},{5,7},{6,4},{7,5},{8,10},{9,11},{10,... | collective-permute-start | bytes 344072 | tf_op jit(solution)/shard_map/ppermute | solution.py:39
  104.7 20.0 %collective-permute-start.8 = (f32[32,896]{1,0:T(8,128)S(1)}, f32[32,896]{1,0:T(8,128)S(1)}, u32[]{:S(2)}, u32[]{:S(2)}) collective-permute-start(f32[32,896]{1,0:T(8,128)S(1)} %add.58), channel_id=1, source_target_pairs={{0,3},{1,2},{2,1},{3,0},{4,7},{5,6},{6,5},{7,4},{8,11},{9,10},{10,... | collective-permute-start | bytes 344072 | tf_op jit(solution)/shard_map/ppermute | solution.py:40
Sparse Core Ops, SparseCore 0:
  14.7 69.0 all-gather.1

commit v10 on v9

--- a/solution.py
+++ b/solution.py
@@ -167,14 +167,11 @@
     a_rows = jnp.dot(order, a_perm.astype(jnp.bfloat16), preferred_element_type=f32)
     a_orig = lax.dot_general(
         a_rows.astype(jnp.bfloat16), order, contract_cells, preferred_element_type=f32
-    ).astype(jnp.bfloat16)
+    )
     rows = patch // n_dp
     cols = patch // n_sp
-    a_blocks = (
-        a_orig.reshape(n_dp, rows, n_sp, cols).transpose(0, 2, 1, 3).reshape(n_dp * n_sp, rows, cols)
-    )
-    got = lax.all_to_all(a_blocks, ("dp", "space"), 0, 0, tiled=True)
-    a_factor = jnp.sum(got.astype(f32), axis=0)
+    a_rows = halving_scatter(a_orig.reshape(n_dp, rows, patch), "dp", 0)
+    a_factor = halving_scatter(a_rows.reshape(rows, n_sp, cols), "space", 1).reshape(rows, cols)
     return (conv_out, a_factor, g_factor, pre_grad)
 
 

time: 139 us -> 127 us (0.914)
  waiting for transfers between devices: 35.6 us -> 25.1 us
  starting transfers between devices: 23.5 us -> 19.6 us
  other arithmetic: 5.99 us -> 8.22 us
    ppermute x2, waiting for transfers between devices: 28.3 us -> 14.9 us  [butterfly_sum(): pair = lax.ppermute(x, axis, partner(axis, high))]
    ppermute x0 -> x5, waiting for transfers between devices: none -> 7.35 us  [halving_scatter(): got = lax.ppermute(send.astype(jnp.bfloat16), axis, partner(axis, step))]
    all_to_all x1 -> x0, starting transfers between devices: 6.92 us -> none  [on_device(): got = lax.all_to_all(a_blocks, ('dp', 'space'), 0, 0, tiled=True)]
    ppermute x2, starting transfers between devices: 8.35 us -> 2.73 us  [butterfly_sum(): pair = lax.ppermute(x, axis, partner(axis, high))]
    ppermute x0 -> x5, starting transfers between devices: none -> 4.99 us  [halving_scatter(): got = lax.ppermute(send.astype(jnp.bfloat16), axis, partner(axis, step))]
    reshape x2 -> x0, local copies, waits for them, and re-layouts: 4.08 us -> none  [on_device(): a_orig.reshape(n_dp, rows, n_sp, cols).transpose(0, 2, 1, 3)]
    add x0 -> x4, other arithmetic: none -> 2.56 us  [halving_scatter(): blocks = keep + got.astype(jnp.float32)]
    ppermute x3, waiting for transfers between devices: 4.02 us -> 1.54 us  [butterfly_sum(): got = lax.ppermute(x, axis, partner(axis, low))]
  transfers between devices with their start and end apart: 11 -> 15, of which waited for: 4 -> 7; matrix products, arithmetic and copies ran while one was open for 35% -> 39% of each run, Pallas kernels for 9% -> 10%
where the time goes in v10:
time: 127 us
  matrix products  36.1 us (28%)
  waiting for transfers between devices  25.1 us (20%)
  starting transfers between devices  19.6 us (15%)
  between operations  14.3 us (11%)
  Pallas kernels  12.1 us (10%)
  local copies, waits for them, and re-layouts  11.1 us (9%)
  other arithmetic  8.22 us (6%)
    ppermute x2, waiting for transfers between devices, butterfly_sum(): pair = lax.ppermute(x, axis, partner(axis, high))  14.9 us
    pallas_call x1, Pallas kernels, patch_matrix(): pl.pallas_call(body, grid=(27,), in_specs=[pl.BlockSpec(shifted.shape, la...  12.1 us
    dot_general x1, matrix products, on_device(): lax.dot_general(low, patches_t, contract_cells, preferred_element_type=f32)  7.8 us
    dot_general x1, matrix products, on_device(): lax.dot_general(high, patches_t, contract_cells, preferred_element_type=f32)  7.49 us
    ppermute x5, waiting for transfers between devices, halving_scatter(): got = lax.ppermute(send.astype(jnp.bfloat16), axis, partner(axis, step))  7.35 us
    ppermute x1, starting transfers between devices, padded_2(): lax.ppermute(tail, axis, [(i, (i + 1) % count) for i in range(ends)])  5.56 us
    dot_general x1, matrix products, on_device(): lax.dot_general(a_rows.astype(jnp.bfloat16), order, contract_cells, prefe...  5.49 us
    dot_general x1, matrix products, on_device(): lax.dot_general(grad_flat, patches_t, contract_cells, preferred_element_t...  5.28 us
  transfers between devices with their start and end apart: 15, of which 7 were waited for; matrix products, arithmetic and copies ran while one was open for 39% of the time, Pallas kernels for 10%

profile of v10, /device:TPU:0, one launch (start us, length us, event | category | flops | bytes accessed | tf_op | source)
XLA Modules:
  0.0 126.5 jit_solution(7647552568154056833)
XLA Ops:
  7.2 1.1 copy.42
  8.3 1.3 %collective-permute-start.1 = (bf16[1,32,1,16,128]{4,1,3,2,0:T(8,128)(2,1)S(1)}, bf16[1,32,1,16,128]{4,1,3,2,0:T(8,128)(2,1)S(1)}, u32[]{:S(2)}, u32[]{:S(2)}) collective-permute-start(bf16[1,32,1,16,128]{4,1,3,2,0:T(8,128)(2,1)S(1)} %get-tuple-element.12), channel_id=1, source_target_pairs={{1,0},{2,1},{3,2},{5,4},{6,5},{7,6},{9,8},{10,9},{11,10},{13,12},{... | collective-permute-start | bytes 393224 | tf_op jit(solution)/shard_map/ppermute | solution.py:20
  9.6 5.6 %collective-permute-start = (bf16[1,32,1,16,128]{4,1,3,2,0:T(8,128)(2,1)S(1)}, bf16[1,32,1,16,128]{4,1,3,2,0:T(8,128)(2,1)S(1)}, u32[]{:S(2)}, u32[]{:S(2)}) collective-permute-start(bf16[1,32,1,16,128]{4,1,3,2,0:T(8,128)(2,1)S(1)} %get-tuple-element.11), channel_id=1, source_target_pairs={{0,1},{1,2},{2,3},{4,5},{5,6},{6,7},{8,9},{9,10},{10,11},{12,13},{... | collective-permute-start | bytes 393224 | tf_op jit(solution)/shard_map/ppermute | solution.py:18
  15.2 3.4 %convert_reduce_fusion = f32[4096]{0:T(1024)S(1)} fusion(s32[1024]{0:T(1024)} %bitcast.64), kind=kLoop, calls=%fused_computation | loop fusion | flops 12578816 | bytes 20480 | tf_op jit(solution)/shard_map/reduce_sum | solution.py:155
  18.6 1.1 reshape_squeeze.3
  19.7 1.3 %convolution_bitcast_fusion.1 = f32[32,32]{1,0:T(8,128)S(1)} fusion(bf16[32,2,16,128]{3,2,1,0:T(8,128)(2,1)} %bitcast.62), kind=kOutput, calls=%fused_computation.23 | convolution fusion | flops 8388608 | bytes 266240 | tf_op jit(solution)/shard_map/dot_general | solution.py:140
  22.0 1.4 %pad_maximum_fusion.src_ref = bf16[3,4,18,32,128]{4,3,2,1,0:T(8,128)(2,1)} fusion(bf16[1,4,18,32,128]{4,3,2,1,0:T(8,128)(2,1)S(1)} %get-tuple-element.9, bf16[1,4,18,32,128]{4,3,2,1,0:T(8,128)(2,1)S(1)} %get-tuple-element.10, bf16[1,4,18,32,128]{4,3,2,1,0:T(8,128)(2,1)S(1)} %get-tuple-element.8), kind=kLoop, calls=%fused_computation.14 | loop fusion | flops 1769472 | bytes 3538944 | tf_op jit(solution)/shard_map/stack | solution.py:78
  23.4 12.1 %shard_map.93 = bf16[864,4096]{1,0:T(8,128)(2,1)} custom-call(bf16[3,4,18,32,128]{4,3,2,1,0:T(8,128)(2,1)} %pad_maximum_fusion.src_ref), custom_call_target="tpu_custom_call" | custom-call | tf_op jit(solution)/shard_map/pallas_call | solution.py:89
  35.5 5.3 %convolution_bitcast_fusion = f32[32,864]{1,0:T(8,128)S(1)} fusion(bf16[864,4096]{1,0:T(8,128)(2,1)} %shard_map.93, bf16[32,4096]{1,0:T(8,128)(2,1)S(1)} %reshape_squeeze.3), kind=kOutput, calls=%fused_computation.22 | convolution fusion | flops 226492416 | bytes 7450624 | tf_op jit(solution)/shard_map/dot_general | solution.py:139
  40.9 7.5 %fusion.1 = f32[864,864]{1,0:T(8,128)S(1)} fusion(bf16[864,4096]{1,0:T(8,128)(2,1)S(1)} %copy-done.1, f32[4096]{0:T(1024)S(1)} %convert_reduce_fusion), kind=kOutput, calls=%fused_computation.5 | convolution fusion | flops 6125912064 | bytes 10080256 | tf_op jit(solution)/shard_map/dot_general | solution.py:163
  48.4 7.8 %multiply_convert_fusion = bf16[864,864]{1,0:T(8,128)(2,1)S(1)} fusion(f32[864,864]{1,0:T(8,128)S(1)} %fusion.1, bf16[864,4096]{1,0:T(8,128)(2,1)S(1)} %copy-done.1, f32[4096]{0:T(1024)S(1)} %convert_reduce_fusion), kind=kOutput, calls=%fused_computation.10 | convolution fusion | flops 6138768384 | bytes 11573248 | tf_op jit(solution)/shard_map/dot_general | solution.py:164
  56.2 5.5 %fusion.6 = f32[864,864]{1,0:T(8,128)} fusion(s32[864]{0:T(1024)S(1)} %fusion.22, bf16[864,864]{1,0:T(8,128)(2,1)S(1)} %multiply_convert_fusion), kind=kOutput, calls=%fused_computation.12 | convolution fusion | flops 2582129664 | bytes 4482432 | tf_op jit(solution)/shard_map/dot_general | solution.py:168
  61.7 2.0 %reshape_reshape.6 = f32[4,2,108,864]{3,2,1,0:T(8,128)S(1)} reshape(f32[864,864]{1,0:T(8,128)} %fusion.6) | data formatting | bytes 5971968 | tf_op jit(solution)/shard_map/reshape;reshape | solution.py:54
  63.8 1.2 copy.48
  65.0 2.6 %collective-permute-done.2 = bf16[4,108,864]{2,0,1:T(4,128)(2,1)} collective-permute-done((bf16[4,108,864]{2,0,1:T(4,128)(2,1)}, bf16[4,108,864]{2,0,1:T(4,128)(2,1)}, u32[]{:S(2)}, u32[]{:S(2)}) %collective-permute-start.2) | collective-permute-done | bytes 746528 | tf_op jit(solution)/shard_map/ppermute | solution.py:58
  67.6 1.3 %bitcast_add_fusion = f32[4,108,864]{2,1,0:T(8,128)S(1)} fusion(f32[4,2,108,864]{3,2,1,0:T(8,128)S(1)} %reshape_reshape.6, s32[]{:T(128)S(6)} %select_n.96, bf16[4,108,864]{2,0,1:T(4,128)(2,1)} %collective-permute-done.2), kind=kLoop, calls=%fused_computation.16 | loop fusion | flops 746496 | bytes 3732484 | tf_op jit(solution)/shard_map/add | solution.py:59
  68.9 1.1 copy-done.2
  70.1 2.0 %collective-permute-start.3 = (bf16[2,108,864]{2,1,0:T(8,128)(2,1)S(1)}, bf16[2,108,864]{2,1,0:T(8,128)(2,1)S(1)}, u32[]{:S(2)}, u32[]{:S(2)}) collective-permute-start(bf16[2,108,864]{2,1,0:T(8,128)(2,1)S(1)} %fusion.13), channel_id=1, source_target_pairs={{0,8},{4,12},{8,0},{12,4},{16,24},{20,28},{24,16},{28,20},{1,9},{5... | collective-permute-start | bytes 1119752 | tf_op jit(solution)/shard_map/ppermute | solution.py:58
  72.2 1.1 collective-permute-start.9
  73.3 0.9 collective-permute-start.7
  75.5 9.3 %collective-permute-done.8 = f32[32,896]{1,0:T(8,128)S(1)} collective-permute-done((f32[32,896]{1,0:T(8,128)S(1)}, f32[32,896]{1,0:T(8,128)S(1)}, u32[]{:S(2)}, u32[]{:S(2)}) %collective-permute-start.8) | collective-permute-done | bytes 114720 | tf_op jit(solution)/shard_map/ppermute | solution.py:39
  84.7 1.3 %collective-permute-done.9 = f32[32,896]{1,0:T(8,128)S(1)} collective-permute-done((f32[32,896]{1,0:T(8,128)S(1)}, f32[32,896]{1,0:T(8,128)S(1)}, u32[]{:S(2)}, u32[]{:S(2)}) %collective-permute-start.9) | collective-permute-done | bytes 114720 | tf_op jit(solution)/shard_map/ppermute | solution.py:40
  86.1 1.6 %collective-permute-start.10 = (f32[32,896]{1,0:T(8,128)S(1)}, f32[32,896]{1,0:T(8,128)S(1)}, u32[]{:S(2)}, u32[]{:S(2)}) collective-permute-start(f32[32,896]{1,0:T(8,128)S(1)} %add_add_fusion.1), channel_id=1, source_target_pairs={{0,16},{4,20},{8,24},{12,28},{16,0},{20,4},{24,8},{28,12},{1,17},{... | collective-permute-start | bytes 344072 | tf_op jit(solution)/shard_map/ppermute | solution.py:37
  87.7 1.2 bitcast_add_fusion.1
  89.5 4.3 %fusion.11 = bf16[4,8,32,128]{3,1,2,0:T(8,128)(2,1)S(1)} fusion(bf16[32,864]{1,0:T(8,128)(2,1)S(1)} %reshape.73, bf16[864,4096]{1,0:T(8,128)(2,1)} %shard_map.93), kind=kOutput, calls=%fused_computation.21 | convolution fusion | flops 226623488 | bytes 7395328 | tf_op jit(solution)/shard_map/dot_general | solution.py:151
  94.6 2.6 %collective-permute-start.12 = (f32[32,896]{1,0:T(8,128)S(1)}, f32[32,896]{1,0:T(8,128)S(1)}, u32[]{:S(2)}, u32[]{:S(2)}) collective-permute-start(f32[32,896]{1,0:T(8,128)S(1)} %add.154), channel_id=1, source_target_pairs={{0,2},{1,3},{2,0},{3,1},{4,6},{5,7},{6,4},{7,5},{8,10},{9,11},{10,... | collective-permute-start | bytes 344072 | tf_op jit(solution)/shard_map/ppermute | solution.py:39
  97.2 1.3 %collective-permute-start.13 = (f32[32,896]{1,0:T(8,128)S(1)}, f32[32,896]{1,0:T(8,128)S(1)}, u32[]{:S(2)}, u32[]{:S(2)}) collective-permute-start(f32[32,896]{1,0:T(8,128)S(1)} %add.154), channel_id=1, source_target_pairs={{0,3},{1,2},{2,1},{3,0},{4,7},{5,6},{6,5},{7,4},{8,11},{9,10},{10,... | collective-permute-start | bytes 344072 | tf_op jit(solution)/shard_map/ppermute | solution.py:40
  98.8 2.1 %collective-permute-start.5 = (bf16[108,2,216]{0,2,1:T(8,128)(2,1)S(1)}, bf16[108,2,216]{0,2,1:T(8,128)(2,1)S(1)}, u32[]{:S(2)}, u32[]{:S(2)}) collective-permute-start(bf16[108,2,216]{0,2,1:T(8,128)(2,1)S(1)} %fusion.15), channel_id=1, source_target_pairs={{0,1},{1,0},{2,3},{3,2},{4,5},{5,4},{6,7},{7,6},{8,9},{9,8},{10,11... | collective-permute-start | bytes 279944 | tf_op jit(solution)/shard_map/ppermute | solution.py:58
  100.9 5.6 %collective-permute-done.12 = f32[32,896]{1,0:T(8,128)S(1)} collective-permute-done((f32[32,896]{1,0:T(8,128)S(1)}, f32[32,896]{1,0:T(8,128)S(1)}, u32[]{:S(2)}, u32[]{:S(2)}) %collective-permute-start.12) | collective-permute-done | bytes 114720 | tf_op jit(solution)/shard_map/ppermute | solution.py:39
  106.6 1.5 %collective-permute-done.11 = f32[32,896]{1,0:T(8,128)S(1)} collective-permute-done((f32[32,896]{1,0:T(8,128)S(1)}, f32[32,896]{1,0:T(8,128)S(1)}, u32[]{:S(2)}, u32[]{:S(2)}) %collective-permute-start.11) | collective-permute-done | bytes 114720 | tf_op jit(solution)/shard_map/ppermute | solution.py:37
  110.6 4.3 %collective-permute-done.6 = bf16[108,1,216]{0,2,1:T(8,128)(2,1)S(1)} collective-permute-done((bf16[108,1,216]{0,2,1:T(8,128)(2,1)S(1)}, bf16[108,1,216]{0,2,1:T(8,128)(2,1)S(1)}, u32[]{:S(2)}, u32[]{:S(2)}) %collective-permute-start.6) | collective-permute-done | bytes 46688 | tf_op jit(solution)/shard_map/ppermute | solution.py:58
  115.6 4.1 %fusion.27 = f32[32,864]{1,0:T(8,128)} fusion(f32[864,32]{0,1:T(8,128)S(1)} %fusion.26, f32[864,864]{1,0:T(8,128)} %all-gather.2.cloned.1.call-done), kind=kOutput, calls=%fused_computation.58 | convolution fusion | flops 286654464 | bytes 3207168 | tf_op jit(solution)/shard_map/dot_general | solution.py:149
  (50 shorter events, 7.3 us)
Async XLA Ops:
  7.2 102.5 %copy-start = (f32[32,32]{1,0:T(8,128)S(1)}, f32[32,32]{1,0:T(8,128)}, u32[]{:S(2)}) copy-start(f32[32,32]{1,0:T(8,128)} %param.11) | copy-start | bytes 12292
  7.2 108.4 %all-gather.2.cloned.1.call-start = ((), (), s32[]{:S(2)}) async-start(), calls=%async_computation | async-start | bytes 3870720 | tf_op jit(solution)/shard_map/all_gather | solution.py:130
  8.3 12.7 %collective-permute-start.1 = (bf16[1,32,1,16,128]{4,1,3,2,0:T(8,128)(2,1)S(1)}, bf16[1,32,1,16,128]{4,1,3,2,0:T(8,128)(2,1)S(1)}, u32[]{:S(2)}, u32[]{:S(2)}) collective-permute-start(bf16[1,32,1,16,128]{4,1,3,2,0:T(8,128)(2,1)S(1)} %get-tuple-element.12), channel_id=1, source_target_pairs={{1,0},{2,1},{3,2},{5,4},{6,5},{7,6},{9,8},{10,9},{11,10},{13,12},{... | collective-permute-start | bytes 393224 | tf_op jit(solution)/shard_map/ppermute | solution.py:20
  9.6 11.4 %collective-permute-start = (bf16[1,32,1,16,128]{4,1,3,2,0:T(8,128)(2,1)S(1)}, bf16[1,32,1,16,128]{4,1,3,2,0:T(8,128)(2,1)S(1)}, u32[]{:S(2)}, u32[]{:S(2)}) collective-permute-start(bf16[1,32,1,16,128]{4,1,3,2,0:T(8,128)(2,1)S(1)} %get-tuple-element.11), channel_id=1, source_target_pairs={{0,1},{1,2},{2,3},{4,5},{5,6},{6,7},{8,9},{9,10},{10,11},{12,13},{... | collective-permute-start | bytes 393224 | tf_op jit(solution)/shard_map/ppermute | solution.py:18
  35.5 5.4 %copy-start.1 = (bf16[864,4096]{1,0:T(8,128)(2,1)S(1)}, bf16[864,4096]{1,0:T(8,128)(2,1)}, u32[]{:S(2)}) copy-start(bf16[864,4096]{1,0:T(8,128)(2,1)} %shard_map.93) | copy-start | bytes 21233668
  63.8 10.4 %copy-start.3 = (bf16[32,864]{1,0:T(8,128)(2,1)S(1)}, bf16[32,864]{1,0:T(8,128)(2,1)}, u32[]{:S(2)}) copy-start(bf16[32,864]{1,0:T(8,128)(2,1)} %param.8) | copy-start | bytes 165892
  65.0 2.6 %collective-permute-start.2 = (bf16[4,108,864]{2,0,1:T(4,128)(2,1)}, bf16[4,108,864]{2,0,1:T(4,128)(2,1)}, u32[]{:S(2)}, u32[]{:S(2)}) collective-permute-start(bf16[4,108,864]{2,0,1:T(4,128)(2,1)} %copy.48), channel_id=1, source_target_pairs={{0,4},{4,0},{8,12},{12,8},{16,20},{20,16},{24,28},{28,24},{1,5},{5... | collective-permute-start | bytes 2239496 | tf_op jit(solution)/shard_map/ppermute | solution.py:58
  68.9 1.2 copy-start.2
  70.1 17.6 %collective-permute-start.3 = (bf16[2,108,864]{2,1,0:T(8,128)(2,1)S(1)}, bf16[2,108,864]{2,1,0:T(8,128)(2,1)S(1)}, u32[]{:S(2)}, u32[]{:S(2)}) collective-permute-start(bf16[2,108,864]{2,1,0:T(8,128)(2,1)S(1)} %fusion.13), channel_id=1, source_target_pairs={{0,8},{4,12},{8,0},{12,4},{16,24},{20,28},{24,16},{28,20},{1,9},{5... | collective-permute-start | bytes 1119752 | tf_op jit(solution)/shard_map/ppermute | solution.py:58
  72.1 12.6 %collective-permute-start.8 = (f32[32,896]{1,0:T(8,128)S(1)}, f32[32,896]{1,0:T(8,128)S(1)}, u32[]{:S(2)}, u32[]{:S(2)}) collective-permute-start(f32[32,896]{1,0:T(8,128)S(1)} %pad_maximum_fusion.1), channel_id=1, source_target_pairs={{0,8},{4,12},{8,0},{12,4},{16,24},{20,28},{24,16},{28,20},{1,9},{5... | collective-permute-start | bytes 344072 | tf_op jit(solution)/shard_map/ppermute | solution.py:39
  72.2 13.8 %collective-permute-start.9 = (f32[32,896]{1,0:T(8,128)S(1)}, f32[32,896]{1,0:T(8,128)S(1)}, u32[]{:S(2)}, u32[]{:S(2)}) collective-permute-start(f32[32,896]{1,0:T(8,128)S(1)} %pad_maximum_fusion.1), channel_id=1, source_target_pairs={{0,12},{4,8},{8,4},{12,0},{16,28},{20,24},{24,20},{28,16},{1,13},{... | collective-permute-start | bytes 344072 | tf_op jit(solution)/shard_map/ppermute | solution.py:40
  73.3 12.7 %collective-permute-start.7 = (f32[32,896]{1,0:T(8,128)S(1)}, f32[32,896]{1,0:T(8,128)S(1)}, u32[]{:S(2)}, u32[]{:S(2)}) collective-permute-start(f32[32,896]{1,0:T(8,128)S(1)} %pad_maximum_fusion.1), channel_id=1, source_target_pairs={{0,4},{4,0},{8,12},{12,8},{16,20},{20,16},{24,28},{28,24},{1,5},{5... | collective-permute-start | bytes 344072 | tf_op jit(solution)/shard_map/ppermute | solution.py:37
  86.1 8.5 %collective-permute-start.10 = (f32[32,896]{1,0:T(8,128)S(1)}, f32[32,896]{1,0:T(8,128)S(1)}, u32[]{:S(2)}, u32[]{:S(2)}) collective-permute-start(f32[32,896]{1,0:T(8,128)S(1)} %add_add_fusion.1), channel_id=1, source_target_pairs={{0,16},{4,20},{8,24},{12,28},{16,0},{20,4},{24,8},{28,12},{1,17},{... | collective-permute-start | bytes 344072 | tf_op jit(solution)/shard_map/ppermute | solution.py:37
  89.0 9.6 %collective-permute-start.4 = (bf16[1,108,864]{2,1,0:T(8,128)(2,1)S(1)}, bf16[1,108,864]{2,1,0:T(8,128)(2,1)S(1)}, u32[]{:S(2)}, u32[]{:S(2)}) collective-permute-start(bf16[1,108,864]{2,1,0:T(8,128)(2,1)S(1)} %dynamic-slice_convert_fusion.2), channel_id=1, source_target_pairs={{0,16},{4,20},{8,24},{12,28},{16,0},{20,4},{24,8},{28,12},{1,17},{... | collective-permute-start | bytes 559880 | tf_op jit(solution)/shard_map/ppermute | solution.py:58
  94.6 11.9 %collective-permute-start.12 = (f32[32,896]{1,0:T(8,128)S(1)}, f32[32,896]{1,0:T(8,128)S(1)}, u32[]{:S(2)}, u32[]{:S(2)}) collective-permute-start(f32[32,896]{1,0:T(8,128)S(1)} %add.154), channel_id=1, source_target_pairs={{0,2},{1,3},{2,0},{3,1},{4,6},{5,7},{6,4},{7,5},{8,10},{9,11},{10,... | collective-permute-start | bytes 344072 | tf_op jit(solution)/shard_map/ppermute | solution.py:39
  97.2 9.3 %collective-permute-start.13 = (f32[32,896]{1,0:T(8,128)S(1)}, f32[32,896]{1,0:T(8,128)S(1)}, u32[]{:S(2)}, u32[]{:S(2)}) collective-permute-start(f32[32,896]{1,0:T(8,128)S(1)} %add.154), channel_id=1, source_target_pairs={{0,3},{1,2},{2,1},{3,0},{4,7},{5,6},{6,5},{7,4},{8,11},{9,10},{10,... | collective-permute-start | bytes 344072 | tf_op jit(solution)/shard_map/ppermute | solution.py:40
  98.6 9.5 %collective-permute-start.11 = (f32[32,896]{1,0:T(8,128)S(1)}, f32[32,896]{1,0:T(8,128)S(1)}, u32[]{:S(2)}, u32[]{:S(2)}) collective-permute-start(f32[32,896]{1,0:T(8,128)S(1)} %add.154), channel_id=1, source_target_pairs={{0,1},{1,0},{2,3},{3,2},{4,5},{5,4},{6,7},{7,6},{8,9},{9,8},{10,11... | collective-permute-start | bytes 344072 | tf_op jit(solution)/shard_map/ppermute | solution.py:37
  98.8 10.4 %collective-permute-start.5 = (bf16[108,2,216]{0,2,1:T(8,128)(2,1)S(1)}, bf16[108,2,216]{0,2,1:T(8,128)(2,1)S(1)}, u32[]{:S(2)}, u32[]{:S(2)}) collective-permute-start(bf16[108,2,216]{0,2,1:T(8,128)(2,1)S(1)} %fusion.15), channel_id=1, source_target_pairs={{0,1},{1,0},{2,3},{3,2},{4,5},{5,4},{6,7},{7,6},{8,9},{9,8},{10,11... | collective-permute-start | bytes 279944 | tf_op jit(solution)/shard_map/ppermute | solution.py:58
  109.3 5.6 %collective-permute-start.6 = (bf16[108,1,216]{0,2,1:T(8,128)(2,1)S(1)}, bf16[108,1,216]{0,2,1:T(8,128)(2,1)S(1)}, u32[]{:S(2)}, u32[]{:S(2)}) collective-permute-start(bf16[108,1,216]{0,2,1:T(8,128)(2,1)S(1)} %dynamic-slice_convert_fusion.4), channel_id=1, source_target_pairs={{0,2},{1,3},{2,0},{3,1},{4,6},{5,7},{6,4},{7,5},{8,10},{9,11},{10,... | collective-permute-start | bytes 139976 | tf_op jit(solution)/shard_map/ppermute | solution.py:58
Sparse Core Ops, SparseCore 0:
  15.3 63.3 all-gather.1

commit v11 on v10

--- a/solution.py
+++ b/solution.py
@@ -46,7 +46,7 @@
     return x
 
 
-def halving_scatter(blocks, axis, dim):
+def halving_scatter(blocks, axis, dim, wire=jnp.bfloat16):
     me = lax.axis_index(axis)
     step = 1
     while step < lax.axis_size(axis):
@@ -55,7 +55,7 @@
         bit = (me // step) % 2
         keep = lax.dynamic_index_in_dim(split, bit, axis=dim + 1, keepdims=False)
         send = lax.dynamic_index_in_dim(split, 1 - bit, axis=dim + 1, keepdims=False)
-        got = lax.ppermute(send.astype(jnp.bfloat16), axis, partner(axis, step))
+        got = lax.ppermute(send.astype(wire), axis, partner(axis, step))
         blocks = keep + got.astype(jnp.float32)
         step *= 2
     return blocks
@@ -127,8 +127,6 @@
     n_grains = channels // grain
     contract_cells = (((1,), (1,)), ((), ()))
 
-    full_inverse = lax.all_gather(a_inverse, "space", axis=0, tiled=True)
-
     block = padded_2(volume, (("space", 2),), 1)
     padded = jnp.pad(block[0], ((0, 0), (0, 0), (1, 1), (1, 1)))
     slab = jnp.transpose(padded, (1, 2, 0, 3))
@@ -140,13 +138,18 @@
     g_part = lax.dot_general(grad_flat, grad_flat, contract_cells, preferred_element_type=f32)
     terms = jnp.concatenate([grad_perm, g_part], axis=1)
     terms, patches_t = lax.optimization_barrier((terms, patches_t))
-    both = butterfly_sum(terms, ("dp", "space"))
-    grad_sum = (
-        both[:, :patch].reshape(channels, n_taps, channels).transpose(0, 2, 1).reshape(channels, patch)
+    plane = butterfly_sum(terms, ("dp",))
+    grad_plane = (
+        plane[:, :patch].reshape(channels, n_taps, channels).transpose(0, 2, 1).reshape(channels, patch)
     )
+    own_cols = halving_scatter(
+        grad_plane.reshape(channels, n_sp, patch // n_sp), "space", 1, wire=f32
+    ).reshape(channels, patch // n_sp)
+    left = jnp.dot(g_inverse, own_cols, precision=highest)
+    partial = jnp.dot(left, a_inverse, precision=highest)
+    both = butterfly_sum(jnp.concatenate([partial, plane[:, patch:]], axis=1), ("space",))
+    pre_grad = both[:, :patch]
     g_factor = both[:, patch:]
-    left = jnp.dot(g_inverse, grad_sum, precision=highest)
-    pre_grad = jnp.dot(left, full_inverse, precision=highest)
 
     forward = jnp.dot(kernel_perm, patches_t, preferred_element_type=f32)
     conv_out = forward.astype(jnp.bfloat16).reshape(1, channels, planes, y_cells, x_cells)

time: 127 us -> 111 us (0.87)
  between operations: 14.3 us -> 1.1 us
  waiting for transfers between devices: 25.1 us -> 21.1 us
  starting transfers between devices: 19.6 us -> 22.5 us
  other arithmetic: 8.22 us -> 6.25 us
  local copies, waits for them, and re-layouts: 11.1 us -> 12.9 us
  matrix products: 36.1 us -> 34.8 us
    ppermute x2, waiting for transfers between devices: 14.9 us -> 3.1 us  [butterfly_sum(): pair = lax.ppermute(x, axis, partner(axis, high))]
    ppermute x5 -> x7, waiting for transfers between devices: 7.35 us -> 16 us  [halving_scatter(): got = lax.ppermute(send.astype(wire), axis, partner(axis, step))]
    dot_general x2, matrix products: 4.36 us -> 0.76 us  [the longest x1 0.6 us: on_device(): partial = jnp.dot(left, a_inverse, precision=highest)]
    ppermute x5 -> x7, starting transfers between devices: 4.99 us -> 7.94 us  [halving_scatter(): got = lax.ppermute(send.astype(wire), axis, partner(axis, step))]
    add x4 -> x6, other arithmetic: 2.56 us -> 0.38 us  [halving_scatter(): blocks = keep + got.astype(jnp.float32)]
    another operation x1 -> x2, local copies, waits for them, and re-layouts: 2.04 us -> 3.54 us  [halving_scatter(): split = blocks.reshape(shape[:dim] + (shape[dim] // 2, 2) + shape[dim + 1:])]
    dot_general x1, matrix products: 5.49 us -> 6.88 us  [on_device(): lax.dot_general(a_rows.astype(jnp.bfloat16), order, contract_cells, prefe...]
    ppermute x2, waiting for transfers between devices: 1.3 us -> 0.01 us  [butterfly_sum(): other = lax.ppermute(x, axis, partner(axis, low + high))]
  transfers between devices with their start and end apart: 15 -> 16, of which waited for: 7 -> 8; matrix products, arithmetic and copies ran while one was open for 39% -> 40% of each run, Pallas kernels for 10% -> 0%
where the time goes in v11:
time: 111 us; the launch traced here: 110 us
  matrix products  34.8 us (31%)
  starting transfers between devices  22.5 us (20%)
  waiting for transfers between devices  21.1 us (19%)
  local copies, waits for them, and re-layouts  12.9 us (12%)
  Pallas kernels  11.9 us (11%)
  other arithmetic  6.25 us (6%)
    ppermute x7, waiting for transfers between devices, halving_scatter(): got = lax.ppermute(send.astype(wire), axis, partner(axis, step))  16 us
    pallas_call x1, Pallas kernels, patch_matrix(): pl.pallas_call(body, grid=(27,), in_specs=[pl.BlockSpec(shifted.shape, la...  11.9 us
    dot_general x1, matrix products, on_device(): lax.dot_general(low, patches_t, contract_cells, preferred_element_type=f32)  8.76 us
    ppermute x7, starting transfers between devices, halving_scatter(): got = lax.ppermute(send.astype(wire), axis, partner(axis, step))  7.94 us
    dot_general x1, matrix products, on_device(): lax.dot_general(high, patches_t, contract_cells, preferred_element_type=f32)  7.48 us
    dot_general x1, matrix products, on_device(): lax.dot_general(a_rows.astype(jnp.bfloat16), order, contract_cells, prefe...  6.88 us
    ppermute x1, starting transfers between devices, padded_2(): lax.ppermute(tail, axis, [(i, (i + 1) % count) for i in range(ends)])  5.56 us
    dot_general x1, matrix products, on_device(): lax.dot_general(grad_flat, patches_t, contract_cells, preferred_element_t...  5.26 us
  transfers between devices with their start and end apart: 16, of which 8 were waited for; matrix products, arithmetic and copies ran while one was open for 40% of the time, Pallas kernels for 0%

profile of v11, /device:TPU:0, one launch (start us, length us, event | category | flops | bytes accessed | tf_op | source)
XLA Modules:
  0.0 110.4 jit_solution(16330423232709009776)
XLA Ops:
  0.6 1.1 %copy.42 = bf16[1,32,2,16,128]{4,1,3,2,0:T(8,128)(2,1)S(1)} copy(bf16[1,32,2,16,128]{4,3,2,1,0:T(8,128)(2,1)} %param.6) | data formatting | bytes 524288 | tf_op args[0]
  1.8 1.3 %collective-permute-start.1 = (bf16[1,32,1,16,128]{4,1,3,2,0:T(8,128)(2,1)S(1)}, bf16[1,32,1,16,128]{4,1,3,2,0:T(8,128)(2,1)S(1)}, u32[]{:S(2)}, u32[]{:S(2)}) collective-permute-start(bf16[1,32,1,16,128]{4,1,3,2,0:T(8,128)(2,1)S(1)} %get-tuple-element.12), channel_id=1, source_target_pairs={{1,0},{2,1},{3,2},{5,4},{6,5},{7,6},{9,8},{10,9},{11,10},{13,12},{... | collective-permute-start | bytes 393224 | tf_op jit(solution)/shard_map/ppermute | solution.py:20
  3.1 5.6 %collective-permute-start = (bf16[1,32,1,16,128]{4,1,3,2,0:T(8,128)(2,1)S(1)}, bf16[1,32,1,16,128]{4,1,3,2,0:T(8,128)(2,1)S(1)}, u32[]{:S(2)}, u32[]{:S(2)}) collective-permute-start(bf16[1,32,1,16,128]{4,1,3,2,0:T(8,128)(2,1)S(1)} %get-tuple-element.11), channel_id=1, source_target_pairs={{0,1},{1,2},{2,3},{4,5},{5,6},{6,7},{8,9},{9,10},{10,11},{12,13},{... | collective-permute-start | bytes 393224 | tf_op jit(solution)/shard_map/ppermute | solution.py:18
  8.8 3.4 %convert_reduce_fusion = f32[4096]{0:T(1024)S(1)} fusion(s32[1024]{0:T(1024)} %bitcast.74), kind=kLoop, calls=%fused_computation | loop fusion | flops 12578816 | bytes 20480 | tf_op jit(solution)/shard_map/reduce_sum | solution.py:158
  12.2 1.4 %reshape.77 = bf16[32,32,27]{2,1,0:T(8,128)(2,1)S(1)} reshape(bf16[32,864]{1,0:T(8,128)(2,1)} %param.8) | data formatting | bytes 110592 | tf_op jit(solution)/shard_map/reshape | solution.py:135
  14.2 1.1 reshape_squeeze.3
  15.3 1.3 %convolution_bitcast_fusion.1 = f32[32,32]{1,0:T(8,128)S(1)} fusion(bf16[32,2,16,128]{3,2,1,0:T(8,128)(2,1)} %bitcast.70), kind=kOutput, calls=%fused_computation.23 | convolution fusion | flops 8388608 | bytes 266240 | tf_op jit(solution)/shard_map/dot_general | solution.py:138
  17.5 1.5 %pad_maximum_fusion.src_ref = bf16[3,4,18,32,128]{4,3,2,1,0:T(8,128)(2,1)} fusion(bf16[1,4,18,32,128]{4,3,2,1,0:T(8,128)(2,1)S(1)} %get-tuple-element.9, bf16[1,4,18,32,128]{4,3,2,1,0:T(8,128)(2,1)S(1)} %get-tuple-element.10, bf16[1,4,18,32,128]{4,3,2,1,0:T(8,128)(2,1)S(1)} %get-tuple-element.8), kind=kLoop, calls=%fused_computation.14 | loop fusion | flops 1769472 | bytes 3538944 | tf_op jit(solution)/shard_map/stack | solution.py:78
  19.0 11.9 %shard_map.93 = bf16[864,4096]{1,0:T(8,128)(2,1)} custom-call(bf16[3,4,18,32,128]{4,3,2,1,0:T(8,128)(2,1)} %pad_maximum_fusion.src_ref), custom_call_target="tpu_custom_call" | custom-call | tf_op jit(solution)/shard_map/pallas_call | solution.py:89
  30.9 5.3 %convolution_bitcast_fusion = f32[32,864]{1,0:T(8,128)S(1)} fusion(bf16[864,4096]{1,0:T(8,128)(2,1)} %shard_map.93, bf16[32,4096]{1,0:T(8,128)(2,1)S(1)} %reshape_squeeze.3), kind=kOutput, calls=%fused_computation.22 | convolution fusion | flops 226492416 | bytes 7450624 | tf_op jit(solution)/shard_map/dot_general | solution.py:137
  36.3 1.9 %collective-permute-start.8 = (f32[32,896]{1,0:T(8,128)S(1)}, f32[32,896]{1,0:T(8,128)S(1)}, u32[]{:S(2)}, u32[]{:S(2)}) collective-permute-start(f32[32,896]{1,0:T(8,128)S(1)} %pad_maximum_fusion.1), channel_id=1, source_target_pairs={{0,8},{4,12},{8,0},{12,4},{16,24},{20,28},{24,16},{28,20},{1,9},{5... | collective-permute-start | bytes 344072 | tf_op jit(solution)/shard_map/ppermute | solution.py:39
  38.5 7.5 %fusion.1 = f32[864,864]{1,0:T(8,128)S(1)} fusion(bf16[864,4096]{1,0:T(8,128)(2,1)S(1)} %copy-done.1, f32[4096]{0:T(1024)S(1)} %convert_reduce_fusion), kind=kOutput, calls=%fused_computation.5 | convolution fusion | flops 6125912064 | bytes 10080256 | tf_op jit(solution)/shard_map/dot_general | solution.py:166
  45.9 8.8 %multiply_convert_fusion = bf16[864,864]{1,0:T(8,128)(2,1)} fusion(f32[864,864]{1,0:T(8,128)S(1)} %fusion.1, bf16[864,4096]{1,0:T(8,128)(2,1)S(1)} %copy-done.1, f32[4096]{0:T(1024)S(1)} %convert_reduce_fusion), kind=kOutput, calls=%fused_computation.10 | convolution fusion | flops 6138768384 | bytes 11573248 | tf_op jit(solution)/shard_map/dot_general | solution.py:167
  54.7 6.9 %fusion.6 = f32[864,864]{1,0:T(8,128)} fusion(s32[864]{0:T(1024)S(1)} %fusion.25, bf16[864,864]{1,0:T(8,128)(2,1)} %multiply_convert_fusion), kind=kOutput, calls=%fused_computation.12 | convolution fusion | flops 2582129664 | bytes 4482432 | tf_op jit(solution)/shard_map/dot_general | solution.py:171
  61.6 3.3 %reshape_reshape.6 = f32[4,2,108,864]{3,2,1,0:T(8,128)} reshape(f32[864,864]{1,0:T(8,128)} %fusion.6) | data formatting | bytes 5971968 | tf_op jit(solution)/shard_map/reshape;reshape | solution.py:54
  64.9 2.0 %collective-permute-start.10 = (f32[32,896]{1,0:T(8,128)S(1)}, f32[32,896]{1,0:T(8,128)S(1)}, u32[]{:S(2)}, u32[]{:S(2)}) collective-permute-start(f32[32,896]{1,0:T(8,128)S(1)} %add_add_fusion.1), channel_id=1, source_target_pairs={{0,16},{4,20},{8,24},{12,28},{16,0},{20,4},{24,8},{28,12},{1,17},{... | collective-permute-start | bytes 344072 | tf_op jit(solution)/shard_map/ppermute | solution.py:37
  66.9 1.5 %fusion.12 = bf16[4,108,864]{2,1,0:T(8,128)(2,1)S(1)} fusion(f32[4,2,108,864]{3,2,1,0:T(8,128)} %reshape_reshape.6, s32[]{:T(128)S(6)} %select_n.109), kind=kLoop, calls=%fused_computation.24 | loop fusion | bytes 1492996 | tf_op jit(solution)/shard_map/convert_element_type | solution.py:58
  68.8 1.5 %collective-permute-done.10 = f32[32,896]{1,0:T(8,128)S(1)} collective-permute-done((f32[32,896]{1,0:T(8,128)S(1)}, f32[32,896]{1,0:T(8,128)S(1)}, u32[]{:S(2)}, u32[]{:S(2)}) %collective-permute-start.10) | collective-permute-done | bytes 114720 | tf_op jit(solution)/shard_map/ppermute | solution.py:37
  71.2 1.8 %collective-permute-start.11 = (f32[32,2,216]{2,1,0:T(2,128)S(1)}, f32[32,2,216]{2,1,0:T(2,128)S(1)}, u32[]{:S(2)}, u32[]{:S(2)}) collective-permute-start(f32[32,2,216]{2,1,0:T(2,128)S(1)} %bitcast.73), channel_id=1, source_target_pairs={{0,1},{1,0},{2,3},{3,2},{4,5},{5,4},{6,7},{7,6},{8,9},{9,8},{10,11... | collective-permute-start | bytes 165896 | tf_op jit(solution)/shard_map/ppermute | solution.py:58
  73.0 4.3 %fusion.11 = bf16[4,8,32,128]{3,1,2,0:T(8,128)(2,1)S(1)} fusion(bf16[32,864]{1,0:T(8,128)(2,1)S(1)} %reshape.78, bf16[864,4096]{1,0:T(8,128)(2,1)} %shard_map.93), kind=kOutput, calls=%fused_computation.21 | convolution fusion | flops 226623488 | bytes 7395328 | tf_op jit(solution)/shard_map/dot_general | solution.py:154
  78.3 1.2 %collective-permute-start.12 = (f32[32,1,216]{2,1,0:T(1,128)S(1)}, f32[32,1,216]{2,1,0:T(1,128)S(1)}, u32[]{:S(2)}, u32[]{:S(2)}) collective-permute-start(f32[32,1,216]{2,1,0:T(1,128)S(1)} %constant_dynamic-slice_fusion), channel_id=1, source_target_pairs={{0,2},{1,3},{2,0},{3,1},{4,6},{5,7},{6,4},{7,5},{8,10},{9,11},{10,... | collective-permute-start | bytes 82952 | tf_op jit(solution)/shard_map/ppermute | solution.py:58
  79.7 1.6 %collective-permute-start.3 = (bf16[2,108,864]{2,1,0:T(8,128)(2,1)S(1)}, bf16[2,108,864]{2,1,0:T(8,128)(2,1)S(1)}, u32[]{:S(2)}, u32[]{:S(2)}) collective-permute-start(bf16[2,108,864]{2,1,0:T(8,128)(2,1)S(1)} %fusion.13), channel_id=1, source_target_pairs={{0,8},{4,12},{8,0},{12,4},{16,24},{20,28},{24,16},{28,20},{1,9},{5... | collective-permute-start | bytes 1119752 | tf_op jit(solution)/shard_map/ppermute | solution.py:58
  81.3 2.2 %collective-permute-done.12 = f32[32,1,216]{2,1,0:T(1,128)S(1)} collective-permute-done((f32[32,1,216]{2,1,0:T(1,128)S(1)}, f32[32,1,216]{2,1,0:T(1,128)S(1)}, u32[]{:S(2)}, u32[]{:S(2)}) %collective-permute-start.12) | collective-permute-done | bytes 27680 | tf_op jit(solution)/shard_map/ppermute | solution.py:58
  83.7 6.2 %collective-permute-done.3 = bf16[2,108,864]{2,1,0:T(8,128)(2,1)S(1)} collective-permute-done((bf16[2,108,864]{2,1,0:T(8,128)(2,1)S(1)}, bf16[2,108,864]{2,1,0:T(8,128)(2,1)S(1)}, u32[]{:S(2)}, u32[]{:S(2)}) %collective-permute-start.3) | collective-permute-done | bytes 373280 | tf_op jit(solution)/shard_map/ppermute | solution.py:58
  90.0 1.6 %collective-permute-start.4 = (bf16[1,108,864]{2,1,0:T(8,128)(2,1)S(1)}, bf16[1,108,864]{2,1,0:T(8,128)(2,1)S(1)}, u32[]{:S(2)}, u32[]{:S(2)}) collective-permute-start(bf16[1,108,864]{2,1,0:T(8,128)(2,1)S(1)} %dynamic-slice_convert_fusion.2), channel_id=1, source_target_pairs={{0,16},{4,20},{8,24},{12,28},{16,0},{20,4},{24,8},{28,12},{1,17},{... | collective-permute-start | bytes 559880 | tf_op jit(solution)/shard_map/ppermute | solution.py:58
  92.2 3.6 %collective-permute-done.4 = bf16[1,108,864]{2,1,0:T(8,128)(2,1)S(1)} collective-permute-done((bf16[1,108,864]{2,1,0:T(8,128)(2,1)S(1)}, bf16[1,108,864]{2,1,0:T(8,128)(2,1)S(1)}, u32[]{:S(2)}, u32[]{:S(2)}) %collective-permute-start.4) | collective-permute-done | bytes 186656 | tf_op jit(solution)/shard_map/ppermute | solution.py:58
  96.0 1.6 %collective-permute-start.5 = (bf16[108,2,216]{0,2,1:T(8,128)(2,1)S(1)}, bf16[108,2,216]{0,2,1:T(8,128)(2,1)S(1)}, u32[]{:S(2)}, u32[]{:S(2)}) collective-permute-start(bf16[108,2,216]{0,2,1:T(8,128)(2,1)S(1)} %fusion.15), channel_id=1, source_target_pairs={{0,1},{1,0},{2,3},{3,2},{4,5},{5,4},{6,7},{7,6},{8,9},{9,8},{10,11... | collective-permute-start | bytes 279944 | tf_op jit(solution)/shard_map/ppermute | solution.py:58
  97.8 0.8 collective-permute-start.14
  98.6 2.0 %collective-permute-start.15 = (f32[32,896]{1,0:T(8,128)S(1)}, f32[32,896]{1,0:T(8,128)S(1)}, u32[]{:S(2)}, u32[]{:S(2)}) collective-permute-start(f32[32,896]{1,0:T(8,128)S(1)} %pad_maximum_fusion.2), channel_id=1, source_target_pairs={{0,3},{1,2},{2,1},{3,0},{4,7},{5,6},{6,5},{7,4},{8,11},{9,10},{10,... | collective-permute-start | bytes 344072 | tf_op jit(solution)/shard_map/ppermute | solution.py:40
  101.3 2.9 %collective-permute-done.5 = bf16[108,2,216]{0,2,1:T(8,128)(2,1)S(1)} collective-permute-done((bf16[108,2,216]{0,2,1:T(8,128)(2,1)S(1)}, bf16[108,2,216]{0,2,1:T(8,128)(2,1)S(1)}, u32[]{:S(2)}, u32[]{:S(2)}) %collective-permute-start.5) | collective-permute-done | bytes 93344 | tf_op jit(solution)/shard_map/ppermute | solution.py:58
  104.3 3.1 %collective-permute-done.14 = f32[32,896]{1,0:T(8,128)S(1)} collective-permute-done((f32[32,896]{1,0:T(8,128)S(1)}, f32[32,896]{1,0:T(8,128)S(1)}, u32[]{:S(2)}, u32[]{:S(2)}) %collective-permute-start.14) | collective-permute-done | bytes 114720 | tf_op jit(solution)/shard_map/ppermute | solution.py:39
  108.6 1.1 %collective-permute-done.6 = bf16[108,1,216]{0,2,1:T(8,128)(2,1)S(1)} collective-permute-done((bf16[108,1,216]{0,2,1:T(8,128)(2,1)S(1)}, bf16[108,1,216]{0,2,1:T(8,128)(2,1)S(1)}, u32[]{:S(2)}, u32[]{:S(2)}) %collective-permute-start.6) | collective-permute-done | bytes 46688 | tf_op jit(solution)/shard_map/ppermute | solution.py:58
  (60 shorter events, 8.1 us)
Async XLA Ops:
  0.6 90.9 %copy-start = (f32[216,864]{1,0:T(8,128)S(1)}, f32[216,864]{1,0:T(8,128)}, u32[]{:S(2)}) copy-start(f32[216,864]{1,0:T(8,128)} %param.10) | copy-start | bytes 2239492
  1.8 14.8 %collective-permute-start.1 = (bf16[1,32,1,16,128]{4,1,3,2,0:T(8,128)(2,1)S(1)}, bf16[1,32,1,16,128]{4,1,3,2,0:T(8,128)(2,1)S(1)}, u32[]{:S(2)}, u32[]{:S(2)}) collective-permute-start(bf16[1,32,1,16,128]{4,1,3,2,0:T(8,128)(2,1)S(1)} %get-tuple-element.12), channel_id=1, source_target_pairs={{1,0},{2,1},{3,2},{5,4},{6,5},{7,6},{9,8},{10,9},{11,10},{13,12},{... | collective-permute-start | bytes 393224 | tf_op jit(solution)/shard_map/ppermute | solution.py:20
  3.1 13.5 %collective-permute-start = (bf16[1,32,1,16,128]{4,1,3,2,0:T(8,128)(2,1)S(1)}, bf16[1,32,1,16,128]{4,1,3,2,0:T(8,128)(2,1)S(1)}, u32[]{:S(2)}, u32[]{:S(2)}) collective-permute-start(bf16[1,32,1,16,128]{4,1,3,2,0:T(8,128)(2,1)S(1)} %get-tuple-element.11), channel_id=1, source_target_pairs={{0,1},{1,2},{2,3},{4,5},{5,6},{6,7},{8,9},{9,10},{10,11},{12,13},{... | collective-permute-start | bytes 393224 | tf_op jit(solution)/shard_map/ppermute | solution.py:18
  30.9 7.5 %copy-start.1 = (bf16[864,4096]{1,0:T(8,128)(2,1)S(1)}, bf16[864,4096]{1,0:T(8,128)(2,1)}, u32[]{:S(2)}) copy-start(bf16[864,4096]{1,0:T(8,128)(2,1)} %shard_map.93) | copy-start | bytes 21233668
  36.3 28.6 %collective-permute-start.8 = (f32[32,896]{1,0:T(8,128)S(1)}, f32[32,896]{1,0:T(8,128)S(1)}, u32[]{:S(2)}, u32[]{:S(2)}) collective-permute-start(f32[32,896]{1,0:T(8,128)S(1)} %pad_maximum_fusion.1), channel_id=1, source_target_pairs={{0,8},{4,12},{8,0},{12,4},{16,24},{20,28},{24,16},{28,20},{1,9},{5... | collective-permute-start | bytes 344072 | tf_op jit(solution)/shard_map/ppermute | solution.py:39
  38.2 26.6 %collective-permute-start.9 = (f32[32,896]{1,0:T(8,128)S(1)}, f32[32,896]{1,0:T(8,128)S(1)}, u32[]{:S(2)}, u32[]{:S(2)}) collective-permute-start(f32[32,896]{1,0:T(8,128)S(1)} %pad_maximum_fusion.1), channel_id=1, source_target_pairs={{0,12},{4,8},{8,4},{12,0},{16,28},{20,24},{24,20},{28,16},{1,13},{... | collective-permute-start | bytes 344072 | tf_op jit(solution)/shard_map/ppermute | solution.py:40
  38.2 26.6 %collective-permute-start.7 = (f32[32,896]{1,0:T(8,128)S(1)}, f32[32,896]{1,0:T(8,128)S(1)}, u32[]{:S(2)}, u32[]{:S(2)}) collective-permute-start(f32[32,896]{1,0:T(8,128)S(1)} %pad_maximum_fusion.1), channel_id=1, source_target_pairs={{0,4},{4,0},{8,12},{12,8},{16,20},{20,16},{24,28},{28,24},{1,5},{5... | collective-permute-start | bytes 344072 | tf_op jit(solution)/shard_map/ppermute | solution.py:37
  64.9 5.4 %collective-permute-start.10 = (f32[32,896]{1,0:T(8,128)S(1)}, f32[32,896]{1,0:T(8,128)S(1)}, u32[]{:S(2)}, u32[]{:S(2)}) collective-permute-start(f32[32,896]{1,0:T(8,128)S(1)} %add_add_fusion.1), channel_id=1, source_target_pairs={{0,16},{4,20},{8,24},{12,28},{16,0},{20,4},{24,8},{28,12},{1,17},{... | collective-permute-start | bytes 344072 | tf_op jit(solution)/shard_map/ppermute | solution.py:37
  68.8 10.8 %collective-permute-start.2 = (bf16[4,108,864]{2,0,1:T(4,128)(2,1)S(1)}, bf16[4,108,864]{2,0,1:T(4,128)(2,1)S(1)}, u32[]{:S(2)}, u32[]{:S(2)}) collective-permute-start(bf16[4,108,864]{2,0,1:T(4,128)(2,1)S(1)} %copy.48), channel_id=1, source_target_pairs={{0,4},{4,0},{8,12},{12,8},{16,20},{20,16},{24,28},{28,24},{1,5},{5... | collective-permute-start | bytes 2239496 | tf_op jit(solution)/shard_map/ppermute | solution.py:58
  71.2 8.3 %copy-start.2 = (f32[4,2,108,864]{3,2,1,0:T(8,128)S(1)}, f32[4,2,108,864]{3,2,1,0:T(8,128)}, u32[]{:S(2)}) copy-start(f32[4,2,108,864]{3,2,1,0:T(8,128)} %reshape_reshape.6) | copy-start | bytes 8957956
  71.2 6.9 %collective-permute-start.11 = (f32[32,2,216]{2,1,0:T(2,128)S(1)}, f32[32,2,216]{2,1,0:T(2,128)S(1)}, u32[]{:S(2)}, u32[]{:S(2)}) collective-permute-start(f32[32,2,216]{2,1,0:T(2,128)S(1)} %bitcast.73), channel_id=1, source_target_pairs={{0,1},{1,0},{2,3},{3,2},{4,5},{5,4},{6,7},{7,6},{8,9},{9,8},{10,11... | collective-permute-start | bytes 165896 | tf_op jit(solution)/shard_map/ppermute | solution.py:58
  77.3 6.2 %copy-start.4 = (f32[32,32]{1,0:T(8,128)S(1)}, f32[32,32]{1,0:T(8,128)}, u32[]{:S(2)}) copy-start(f32[32,32]{1,0:T(8,128)} %param.11) | copy-start | bytes 12292
  78.3 5.2 %collective-permute-start.12 = (f32[32,1,216]{2,1,0:T(1,128)S(1)}, f32[32,1,216]{2,1,0:T(1,128)S(1)}, u32[]{:S(2)}, u32[]{:S(2)}) collective-permute-start(f32[32,1,216]{2,1,0:T(1,128)S(1)} %constant_dynamic-slice_fusion), channel_id=1, source_target_pairs={{0,2},{1,3},{2,0},{3,1},{4,6},{5,7},{6,4},{7,5},{8,10},{9,11},{10,... | collective-permute-start | bytes 82952 | tf_op jit(solution)/shard_map/ppermute | solution.py:58
  79.7 10.1 %collective-permute-start.3 = (bf16[2,108,864]{2,1,0:T(8,128)(2,1)S(1)}, bf16[2,108,864]{2,1,0:T(8,128)(2,1)S(1)}, u32[]{:S(2)}, u32[]{:S(2)}) collective-permute-start(bf16[2,108,864]{2,1,0:T(8,128)(2,1)S(1)} %fusion.13), channel_id=1, source_target_pairs={{0,8},{4,12},{8,0},{12,4},{16,24},{20,28},{24,16},{28,20},{1,9},{5... | collective-permute-start | bytes 1119752 | tf_op jit(solution)/shard_map/ppermute | solution.py:58
  90.0 5.8 %collective-permute-start.4 = (bf16[1,108,864]{2,1,0:T(8,128)(2,1)S(1)}, bf16[1,108,864]{2,1,0:T(8,128)(2,1)S(1)}, u32[]{:S(2)}, u32[]{:S(2)}) collective-permute-start(bf16[1,108,864]{2,1,0:T(8,128)(2,1)S(1)} %dynamic-slice_convert_fusion.2), channel_id=1, source_target_pairs={{0,16},{4,20},{8,24},{12,28},{16,0},{20,4},{24,8},{28,12},{1,17},{... | collective-permute-start | bytes 559880 | tf_op jit(solution)/shard_map/ppermute | solution.py:58
  96.0 8.1 %collective-permute-start.5 = (bf16[108,2,216]{0,2,1:T(8,128)(2,1)S(1)}, bf16[108,2,216]{0,2,1:T(8,128)(2,1)S(1)}, u32[]{:S(2)}, u32[]{:S(2)}) collective-permute-start(bf16[108,2,216]{0,2,1:T(8,128)(2,1)S(1)} %fusion.15), channel_id=1, source_target_pairs={{0,1},{1,0},{2,3},{3,2},{4,5},{5,4},{6,7},{7,6},{8,9},{9,8},{10,11... | collective-permute-start | bytes 279944 | tf_op jit(solution)/shard_map/ppermute | solution.py:58
  97.8 9.7 %collective-permute-start.14 = (f32[32,896]{1,0:T(8,128)S(1)}, f32[32,896]{1,0:T(8,128)S(1)}, u32[]{:S(2)}, u32[]{:S(2)}) collective-permute-start(f32[32,896]{1,0:T(8,128)S(1)} %pad_maximum_fusion.2), channel_id=1, source_target_pairs={{0,2},{1,3},{2,0},{3,1},{4,6},{5,7},{6,4},{7,5},{8,10},{9,11},{10,... | collective-permute-start | bytes 344072 | tf_op jit(solution)/shard_map/ppermute | solution.py:39
  98.6 8.9 %collective-permute-start.15 = (f32[32,896]{1,0:T(8,128)S(1)}, f32[32,896]{1,0:T(8,128)S(1)}, u32[]{:S(2)}, u32[]{:S(2)}) collective-permute-start(f32[32,896]{1,0:T(8,128)S(1)} %pad_maximum_fusion.2), channel_id=1, source_target_pairs={{0,3},{1,2},{2,1},{3,0},{4,7},{5,6},{6,5},{7,4},{8,11},{9,10},{10,... | collective-permute-start | bytes 344072 | tf_op jit(solution)/shard_map/ppermute | solution.py:40
  100.6 7.3 %collective-permute-start.13 = (f32[32,896]{1,0:T(8,128)S(1)}, f32[32,896]{1,0:T(8,128)S(1)}, u32[]{:S(2)}, u32[]{:S(2)}) collective-permute-start(f32[32,896]{1,0:T(8,128)S(1)} %pad_maximum_fusion.2), channel_id=1, source_target_pairs={{0,1},{1,0},{2,3},{3,2},{4,5},{5,4},{6,7},{7,6},{8,9},{9,8},{10,11... | collective-permute-start | bytes 344072 | tf_op jit(solution)/shard_map/ppermute | solution.py:37
  104.2 5.5 %collective-permute-start.6 = (bf16[108,1,216]{0,2,1:T(8,128)(2,1)S(1)}, bf16[108,1,216]{0,2,1:T(8,128)(2,1)S(1)}, u32[]{:S(2)}, u32[]{:S(2)}) collective-permute-start(bf16[108,1,216]{0,2,1:T(8,128)(2,1)S(1)} %dynamic-slice_convert_fusion.4), channel_id=1, source_target_pairs={{0,2},{1,3},{2,0},{3,1},{4,6},{5,7},{6,4},{7,5},{8,10},{9,11},{10,... | collective-permute-start | bytes 139976 | tf_op jit(solution)/shard_map/ppermute | solution.py:58
  107.9 2.5 %copy-start.3 = (f32[32,896]{1,0:T(8,128)}, f32[32,896]{1,0:T(8,128)S(1)}, u32[]{:S(2)}) copy-start(f32[32,896]{1,0:T(8,128)S(1)} %add_add_fusion) | copy-start | bytes 344068

commit v12 on v11

--- a/solution.py
+++ b/solution.py
@@ -78,19 +78,21 @@
     shifted = jnp.stack([slab[:, :, :, dx : dx + x_cells] for dx in range(3)])
 
     def body(src_ref, out_ref):
-        tap = pl.program_id(0)
-        dz = tap // 9
-        dy = (tap // 3) % 3
-        dx = tap % 3
-        for z in range(planes):
-            for y in range(y_cells):
-                out_ref[:, pl.ds((z * y_cells + y) * x_cells, x_cells)] = src_ref[dx, z + dz, y + dy]
+        dz = pl.program_id(0)
+        for dy in range(3):
+            for dx in range(3):
+                row = (dy * 3 + dx) * channels
+                for z in range(planes):
+                    for y in range(y_cells):
+                        out_ref[pl.ds(row, channels), pl.ds((z * y_cells + y) * x_cells, x_cells)] = (
+                            src_ref[dx, z + dz, y + dy]
+                        )
 
     return pl.pallas_call(
         body,
-        grid=(27,),
-        in_specs=[pl.BlockSpec(shifted.shape, lambda tap: (0, 0, 0, 0, 0))],
-        out_specs=pl.BlockSpec((channels, cells), lambda tap: (tap, 0)),
+        grid=(3,),
+        in_specs=[pl.BlockSpec(shifted.shape, lambda dz: (0, 0, 0, 0, 0))],
+        out_specs=pl.BlockSpec((9 * channels, cells), lambda dz: (dz, 0)),
         out_shape=jax.ShapeDtypeStruct((27 * channels, cells), slab.dtype),
     )(shifted)
 
@@ -151,26 +153,24 @@
     pre_grad = both[:, :patch]
     g_factor = both[:, patch:]
 
-    forward = jnp.dot(kernel_perm, patches_t, preferred_element_type=f32)
-    conv_out = forward.astype(jnp.bfloat16).reshape(1, channels, planes, y_cells, x_cells)
 
     cell_ids = sample_idx[0]
     counts = jnp.sum(
         (cell_ids[:, None] == jnp.arange(cells, dtype=jnp.int32)[None, :]).astype(f32), axis=0
     )
-    weighted = patches_t.astype(f32) * counts[None, :]
-    high = weighted.astype(jnp.bfloat16)
-    low = (weighted - high.astype(f32)).astype(jnp.bfloat16)
+    weighted = (patches_t.astype(f32) * counts[None, :]).astype(jnp.bfloat16)
     total_samples = sample_idx.shape[1] * n_sp * n_dp
-    a_perm = (
-        lax.dot_general(high, patches_t, contract_cells, preferred_element_type=f32)
-        + lax.dot_general(low, patches_t, contract_cells, preferred_element_type=f32)
+    a_perm = lax.dot_general(
+        weighted, patches_t, contract_cells, preferred_element_type=f32
     ) / jnp.float32(total_samples)
     order = tap_order(channels, n_taps)
     a_rows = jnp.dot(order, a_perm.astype(jnp.bfloat16), preferred_element_type=f32)
     a_orig = lax.dot_general(
         a_rows.astype(jnp.bfloat16), order, contract_cells, preferred_element_type=f32
     )
+    a_orig, kernel_perm = lax.optimization_barrier((a_orig, kernel_perm))
+    forward = jnp.dot(kernel_perm, patches_t, preferred_element_type=f32)
+    conv_out = forward.astype(jnp.bfloat16).reshape(1, channels, planes, y_cells, x_cells)
     rows = patch // n_dp
     cols = patch // n_sp
     a_rows = halving_scatter(a_orig.reshape(n_dp, rows, patch), "dp", 0)

time: 111 us -> 102 us (0.919)
  Pallas kernels: 11.9 us -> 5.16 us
  matrix products: 34.8 us -> 32.2 us
    pallas_call x1, Pallas kernels: 11.9 us -> 5.16 us  [patch_matrix(): pl.pallas_call(body, grid=(3,), in_specs=[pl.BlockSpec(shifted.shape, lam...]
    dot_general x1, matrix products: 6.88 us -> 5.18 us  [on_device(): lax.dot_general(a_rows.astype(jnp.bfloat16), order, contract_cells, prefe...]
    dot_general x2 -> x1, matrix products: 16.2 us -> 15.5 us  [on_device(): jnp.dot(order, a_perm.astype(jnp.bfloat16), preferred_element_type=f32)]
  transfers between devices with their start and end apart: 16 -> 16, of which waited for: 8 -> 8; matrix products, arithmetic and copies ran while one was open for 40% -> 41% of each run, Pallas kernels for 0% -> 0%
where the time goes in v12:
time: 102 us; the launch traced here: 101 us
  matrix products  32.2 us (32%)
  starting transfers between devices  22.5 us (22%)
  waiting for transfers between devices  21.1 us (21%)
  local copies, waits for them, and re-layouts  12.9 us (13%)
  other arithmetic  6.26 us (6%)
  Pallas kernels  5.16 us (5%)
  between operations  1.1 us (1%)
    ppermute x7, waiting for transfers between devices, halving_scatter(): got = lax.ppermute(send.astype(wire), axis, partner(axis, step))  16 us
    dot_general x1, matrix products, on_device(): jnp.dot(order, a_perm.astype(jnp.bfloat16), preferred_element_type=f32)  15.5 us
    ppermute x7, starting transfers between devices, halving_scatter(): got = lax.ppermute(send.astype(wire), axis, partner(axis, step))  7.95 us
    ppermute x1, starting transfers between devices, padded_2(): lax.ppermute(tail, axis, [(i, (i + 1) % count) for i in range(ends)])  5.56 us
    dot_general x1, matrix products, on_device(): lax.dot_general(a_rows.astype(jnp.bfloat16), order, contract_cells, prefe...  5.18 us
    pallas_call x1, Pallas kernels, patch_matrix(): pl.pallas_call(body, grid=(3,), in_specs=[pl.BlockSpec(shifted.shape, lam...  5.16 us
    dot_general x1, matrix products, on_device(): lax.dot_general(grad_flat, patches_t, contract_cells, preferred_element_t...  5.12 us
    dot_general x1, matrix products, on_device(): forward = jnp.dot(kernel_perm, patches_t, preferred_element_type=f32)  4.33 us
  transfers between devices with their start and end apart: 16, of which 8 were waited for; matrix products, arithmetic and copies ran while one was open for 41% of the time, Pallas kernels for 0%

profile of v12, /device:TPU:0, one launch (start us, length us, event | category | flops | bytes accessed | tf_op | source)
XLA Modules:
  0.0 101.1 jit_solution(9877593943949311114)
XLA Ops:
  0.6 1.1 %copy.42 = bf16[1,32,2,16,128]{4,1,3,2,0:T(8,128)(2,1)S(1)} copy(bf16[1,32,2,16,128]{4,3,2,1,0:T(8,128)(2,1)} %param.6) | data formatting | bytes 524288 | tf_op args[0]
  1.8 1.3 %collective-permute-start.1 = (bf16[1,32,1,16,128]{4,1,3,2,0:T(8,128)(2,1)S(1)}, bf16[1,32,1,16,128]{4,1,3,2,0:T(8,128)(2,1)S(1)}, u32[]{:S(2)}, u32[]{:S(2)}) collective-permute-start(bf16[1,32,1,16,128]{4,1,3,2,0:T(8,128)(2,1)S(1)} %get-tuple-element.16), channel_id=1, source_target_pairs={{1,0},{2,1},{3,2},{5,4},{6,5},{7,6},{9,8},{10,9},{11,10},{13,12},{... | collective-permute-start | bytes 393224 | tf_op jit(solution)/shard_map/ppermute | solution.py:20
  3.1 5.6 %collective-permute-start = (bf16[1,32,1,16,128]{4,1,3,2,0:T(8,128)(2,1)S(1)}, bf16[1,32,1,16,128]{4,1,3,2,0:T(8,128)(2,1)S(1)}, u32[]{:S(2)}, u32[]{:S(2)}) collective-permute-start(bf16[1,32,1,16,128]{4,1,3,2,0:T(8,128)(2,1)S(1)} %get-tuple-element.15), channel_id=1, source_target_pairs={{0,1},{1,2},{2,3},{4,5},{5,6},{6,7},{8,9},{9,10},{10,11},{12,13},{... | collective-permute-start | bytes 393224 | tf_op jit(solution)/shard_map/ppermute | solution.py:18
  8.8 3.4 %convert_reduce_fusion = f32[4096]{0:T(1024)S(1)} fusion(s32[1024]{0:T(1024)} %bitcast.72), kind=kLoop, calls=%fused_computation | loop fusion | flops 12578816 | bytes 20480 | tf_op jit(solution)/shard_map/reduce_sum | solution.py:158
  12.2 1.1 %reshape_squeeze.3 = bf16[32,4096]{1,0:T(8,128)(2,1)S(1)} reshape(bf16[1,32,2,16,128]{4,3,2,1,0:T(8,128)(2,1)} %param.7) | data formatting | bytes 524288 | tf_op jit(solution)/shard_map/reshape;squeeze | solution.py:136
  13.2 1.4 %reshape.77 = bf16[32,32,27]{2,1,0:T(8,128)(2,1)S(1)} reshape(bf16[32,864]{1,0:T(8,128)(2,1)} %param.8) | data formatting | bytes 110592 | tf_op jit(solution)/shard_map/reshape | solution.py:137
  15.3 1.3 %convolution_bitcast_fusion.1 = f32[32,32]{1,0:T(8,128)S(1)} fusion(bf16[32,2,16,128]{3,2,1,0:T(8,128)(2,1)} %bitcast.68), kind=kOutput, calls=%fused_computation.19 | convolution fusion | flops 8388608 | bytes 266240 | tf_op jit(solution)/shard_map/dot_general | solution.py:140
  17.5 1.5 %pad_maximum_fusion.src_ref = bf16[3,4,18,32,128]{4,3,2,1,0:T(8,128)(2,1)} fusion(bf16[1,4,18,32,128]{4,3,2,1,0:T(8,128)(2,1)S(1)} %get-tuple-element.13, bf16[1,4,18,32,128]{4,3,2,1,0:T(8,128)(2,1)S(1)} %get-tuple-element.14, bf16[1,4,18,32,128]{4,3,2,1,0:T(8,128)(2,1)S(1)} %get-tuple-element.12), kind=kLoop, calls=%fused_computation.10 | loop fusion | flops 1769472 | bytes 3538944 | tf_op jit(solution)/shard_map/stack | solution.py:78
  19.0 5.2 %shard_map.93 = bf16[864,4096]{1,0:T(8,128)(2,1)} custom-call(bf16[3,4,18,32,128]{4,3,2,1,0:T(8,128)(2,1)} %pad_maximum_fusion.src_ref), custom_call_target="tpu_custom_call" | custom-call | tf_op jit(solution)/shard_map/pallas_call | solution.py:91
  24.2 5.1 %convolution_bitcast_fusion = f32[32,864]{1,0:T(8,128)S(1)} fusion(bf16[864,4096]{1,0:T(8,128)(2,1)} %shard_map.93, bf16[32,4096]{1,0:T(8,128)(2,1)S(1)} %reshape_squeeze.3), kind=kOutput, calls=%fused_computation.18 | convolution fusion | flops 226492416 | bytes 7450624 | tf_op jit(solution)/shard_map/dot_general | solution.py:139
  29.4 1.9 %collective-permute-start.8 = (f32[32,896]{1,0:T(8,128)S(1)}, f32[32,896]{1,0:T(8,128)S(1)}, u32[]{:S(2)}, u32[]{:S(2)}) collective-permute-start(f32[32,896]{1,0:T(8,128)S(1)} %pad_maximum_fusion.1), channel_id=1, source_target_pairs={{0,8},{4,12},{8,0},{12,4},{16,24},{20,28},{24,16},{28,20},{1,9},{5... | collective-permute-start | bytes 344072 | tf_op jit(solution)/shard_map/ppermute | solution.py:39
  31.6 15.5 %fusion.4 = bf16[864,864]{1,0:T(8,128)(2,1)} fusion(s32[864]{0:T(1024)S(1)} %fusion.21, bf16[864,4096]{1,0:T(8,128)(2,1)} %shard_map.93, f32[4096]{0:T(1024)S(1)} %convert_reduce_fusion), kind=kOutput, calls=%fused_computation.11 | convolution fusion | flops 7418843136 | bytes 8590720 | tf_op jit(solution)/shard_map/dot_general | solution.py:167
  47.1 5.2 %fusion.2 = f32[864,864]{1,0:T(8,128)} fusion(bf16[864,864]{1,0:T(8,128)(2,1)} %fusion.4, s32[864]{0:T(1024)S(1)} %fusion.21), kind=kOutput, calls=%fused_computation.8 | convolution fusion | flops 1290691584 | bytes 4482432 | tf_op jit(solution)/shard_map/dot_general | solution.py:168
  52.3 3.3 %reshape_reshape.6 = f32[4,2,108,864]{3,2,1,0:T(8,128)} reshape(f32[864,864]{1,0:T(8,128)} %fusion.2) | data formatting | bytes 5971968 | tf_op jit(solution)/shard_map/reshape;reshape | solution.py:54
  55.6 2.0 %collective-permute-start.10 = (f32[32,896]{1,0:T(8,128)S(1)}, f32[32,896]{1,0:T(8,128)S(1)}, u32[]{:S(2)}, u32[]{:S(2)}) collective-permute-start(f32[32,896]{1,0:T(8,128)S(1)} %add_add_fusion.1), channel_id=1, source_target_pairs={{0,16},{4,20},{8,24},{12,28},{16,0},{20,4},{24,8},{28,12},{1,17},{... | collective-permute-start | bytes 344072 | tf_op jit(solution)/shard_map/ppermute | solution.py:37
  57.6 1.5 %fusion.8 = bf16[4,108,864]{2,1,0:T(8,128)(2,1)S(1)} fusion(f32[4,2,108,864]{3,2,1,0:T(8,128)} %reshape_reshape.6, s32[]{:T(128)S(6)} %select_n.109), kind=kLoop, calls=%fused_computation.20 | loop fusion | bytes 1492996 | tf_op jit(solution)/shard_map/convert_element_type | solution.py:58
  59.5 1.5 %collective-permute-done.10 = f32[32,896]{1,0:T(8,128)S(1)} collective-permute-done((f32[32,896]{1,0:T(8,128)S(1)}, f32[32,896]{1,0:T(8,128)S(1)}, u32[]{:S(2)}, u32[]{:S(2)}) %collective-permute-start.10) | collective-permute-done | bytes 114720 | tf_op jit(solution)/shard_map/ppermute | solution.py:37
  61.9 1.8 %collective-permute-start.11 = (f32[32,2,216]{2,1,0:T(2,128)S(1)}, f32[32,2,216]{2,1,0:T(2,128)S(1)}, u32[]{:S(2)}, u32[]{:S(2)}) collective-permute-start(f32[32,2,216]{2,1,0:T(2,128)S(1)} %bitcast.71), channel_id=1, source_target_pairs={{0,1},{1,0},{2,3},{3,2},{4,5},{5,4},{6,7},{7,6},{8,9},{9,8},{10,11... | collective-permute-start | bytes 165896 | tf_op jit(solution)/shard_map/ppermute | solution.py:58
  63.7 4.3 %fusion.7 = bf16[4,8,32,128]{3,1,2,0:T(8,128)(2,1)S(1)} fusion(bf16[32,864]{1,0:T(8,128)(2,1)S(1)} %reshape.78, bf16[864,4096]{1,0:T(8,128)(2,1)} %shard_map.93), kind=kOutput, calls=%fused_computation.17 | convolution fusion | flops 226623488 | bytes 7395328 | tf_op jit(solution)/shard_map/dot_general | solution.py:172
  68.1 0.7 copy.56
  69.0 1.2 %collective-permute-start.12 = (f32[32,1,216]{2,1,0:T(1,128)S(1)}, f32[32,1,216]{2,1,0:T(1,128)S(1)}, u32[]{:S(2)}, u32[]{:S(2)}) collective-permute-start(f32[32,1,216]{2,1,0:T(1,128)S(1)} %constant_dynamic-slice_fusion), channel_id=1, source_target_pairs={{0,2},{1,3},{2,0},{3,1},{4,6},{5,7},{6,4},{7,5},{8,10},{9,11},{10,... | collective-permute-start | bytes 82952 | tf_op jit(solution)/shard_map/ppermute | solution.py:58
  70.4 1.6 %collective-permute-start.3 = (bf16[2,108,864]{2,1,0:T(8,128)(2,1)S(1)}, bf16[2,108,864]{2,1,0:T(8,128)(2,1)S(1)}, u32[]{:S(2)}, u32[]{:S(2)}) collective-permute-start(bf16[2,108,864]{2,1,0:T(8,128)(2,1)S(1)} %fusion.9), channel_id=1, source_target_pairs={{0,8},{4,12},{8,0},{12,4},{16,24},{20,28},{24,16},{28,20},{1,9},{5... | collective-permute-start | bytes 1119752 | tf_op jit(solution)/shard_map/ppermute | solution.py:58
  72.0 2.2 %collective-permute-done.12 = f32[32,1,216]{2,1,0:T(1,128)S(1)} collective-permute-done((f32[32,1,216]{2,1,0:T(1,128)S(1)}, f32[32,1,216]{2,1,0:T(1,128)S(1)}, u32[]{:S(2)}, u32[]{:S(2)}) %collective-permute-start.12) | collective-permute-done | bytes 27680 | tf_op jit(solution)/shard_map/ppermute | solution.py:58
  74.4 6.2 %collective-permute-done.3 = bf16[2,108,864]{2,1,0:T(8,128)(2,1)S(1)} collective-permute-done((bf16[2,108,864]{2,1,0:T(8,128)(2,1)S(1)}, bf16[2,108,864]{2,1,0:T(8,128)(2,1)S(1)}, u32[]{:S(2)}, u32[]{:S(2)}) %collective-permute-start.3) | collective-permute-done | bytes 373280 | tf_op jit(solution)/shard_map/ppermute | solution.py:58
  80.7 1.6 %collective-permute-start.4 = (bf16[1,108,864]{2,1,0:T(8,128)(2,1)S(1)}, bf16[1,108,864]{2,1,0:T(8,128)(2,1)S(1)}, u32[]{:S(2)}, u32[]{:S(2)}) collective-permute-start(bf16[1,108,864]{2,1,0:T(8,128)(2,1)S(1)} %dynamic-slice_convert_fusion.2), channel_id=1, source_target_pairs={{0,16},{4,20},{8,24},{12,28},{16,0},{20,4},{24,8},{28,12},{1,17},{... | collective-permute-start | bytes 559880 | tf_op jit(solution)/shard_map/ppermute | solution.py:58
  82.9 3.6 %collective-permute-done.4 = bf16[1,108,864]{2,1,0:T(8,128)(2,1)S(1)} collective-permute-done((bf16[1,108,864]{2,1,0:T(8,128)(2,1)S(1)}, bf16[1,108,864]{2,1,0:T(8,128)(2,1)S(1)}, u32[]{:S(2)}, u32[]{:S(2)}) %collective-permute-start.4) | collective-permute-done | bytes 186656 | tf_op jit(solution)/shard_map/ppermute | solution.py:58
  86.7 1.6 %collective-permute-start.5 = (bf16[108,2,216]{0,2,1:T(8,128)(2,1)S(1)}, bf16[108,2,216]{0,2,1:T(8,128)(2,1)S(1)}, u32[]{:S(2)}, u32[]{:S(2)}) collective-permute-start(bf16[108,2,216]{0,2,1:T(8,128)(2,1)S(1)} %fusion.11), channel_id=1, source_target_pairs={{0,1},{1,0},{2,3},{3,2},{4,5},{5,4},{6,7},{7,6},{8,9},{9,8},{10,11... | collective-permute-start | bytes 279944 | tf_op jit(solution)/shard_map/ppermute | solution.py:58
  88.5 0.8 collective-permute-start.14
  89.2 2.0 %collective-permute-start.15 = (f32[32,896]{1,0:T(8,128)S(1)}, f32[32,896]{1,0:T(8,128)S(1)}, u32[]{:S(2)}, u32[]{:S(2)}) collective-permute-start(f32[32,896]{1,0:T(8,128)S(1)} %pad_maximum_fusion.2), channel_id=1, source_target_pairs={{0,3},{1,2},{2,1},{3,0},{4,7},{5,6},{6,5},{7,4},{8,11},{9,10},{10,... | collective-permute-start | bytes 344072 | tf_op jit(solution)/shard_map/ppermute | solution.py:40
  92.0 2.9 %collective-permute-done.5 = bf16[108,2,216]{0,2,1:T(8,128)(2,1)S(1)} collective-permute-done((bf16[108,2,216]{0,2,1:T(8,128)(2,1)S(1)}, bf16[108,2,216]{0,2,1:T(8,128)(2,1)S(1)}, u32[]{:S(2)}, u32[]{:S(2)}) %collective-permute-start.5) | collective-permute-done | bytes 93344 | tf_op jit(solution)/shard_map/ppermute | solution.py:58
  95.0 3.2 %collective-permute-done.14 = f32[32,896]{1,0:T(8,128)S(1)} collective-permute-done((f32[32,896]{1,0:T(8,128)S(1)}, f32[32,896]{1,0:T(8,128)S(1)}, u32[]{:S(2)}, u32[]{:S(2)}) %collective-permute-start.14) | collective-permute-done | bytes 114720 | tf_op jit(solution)/shard_map/ppermute | solution.py:39
  99.4 1.1 %collective-permute-done.6 = bf16[108,1,216]{0,2,1:T(8,128)(2,1)S(1)} collective-permute-done((bf16[108,1,216]{0,2,1:T(8,128)(2,1)S(1)}, bf16[108,1,216]{0,2,1:T(8,128)(2,1)S(1)}, u32[]{:S(2)}, u32[]{:S(2)}) %collective-permute-start.6) | collective-permute-done | bytes 46688 | tf_op jit(solution)/shard_map/ppermute | solution.py:58
  (57 shorter events, 7.4 us)
Async XLA Ops:
  0.6 81.6 %copy-start = (f32[216,864]{1,0:T(8,128)S(1)}, f32[216,864]{1,0:T(8,128)}, u32[]{:S(2)}) copy-start(f32[216,864]{1,0:T(8,128)} %param.10) | copy-start | bytes 2239492
  1.8 14.8 %collective-permute-start.1 = (bf16[1,32,1,16,128]{4,1,3,2,0:T(8,128)(2,1)S(1)}, bf16[1,32,1,16,128]{4,1,3,2,0:T(8,128)(2,1)S(1)}, u32[]{:S(2)}, u32[]{:S(2)}) collective-permute-start(bf16[1,32,1,16,128]{4,1,3,2,0:T(8,128)(2,1)S(1)} %get-tuple-element.16), channel_id=1, source_target_pairs={{1,0},{2,1},{3,2},{5,4},{6,5},{7,6},{9,8},{10,9},{11,10},{13,12},{... | collective-permute-start | bytes 393224 | tf_op jit(solution)/shard_map/ppermute | solution.py:20
  3.1 13.5 %collective-permute-start = (bf16[1,32,1,16,128]{4,1,3,2,0:T(8,128)(2,1)S(1)}, bf16[1,32,1,16,128]{4,1,3,2,0:T(8,128)(2,1)S(1)}, u32[]{:S(2)}, u32[]{:S(2)}) collective-permute-start(bf16[1,32,1,16,128]{4,1,3,2,0:T(8,128)(2,1)S(1)} %get-tuple-element.15), channel_id=1, source_target_pairs={{0,1},{1,2},{2,3},{4,5},{5,6},{6,7},{8,9},{9,10},{10,11},{12,13},{... | collective-permute-start | bytes 393224 | tf_op jit(solution)/shard_map/ppermute | solution.py:18
  29.4 26.2 %collective-permute-start.8 = (f32[32,896]{1,0:T(8,128)S(1)}, f32[32,896]{1,0:T(8,128)S(1)}, u32[]{:S(2)}, u32[]{:S(2)}) collective-permute-start(f32[32,896]{1,0:T(8,128)S(1)} %pad_maximum_fusion.1), channel_id=1, source_target_pairs={{0,8},{4,12},{8,0},{12,4},{16,24},{20,28},{24,16},{28,20},{1,9},{5... | collective-permute-start | bytes 344072 | tf_op jit(solution)/shard_map/ppermute | solution.py:39
  31.3 24.2 %collective-permute-start.9 = (f32[32,896]{1,0:T(8,128)S(1)}, f32[32,896]{1,0:T(8,128)S(1)}, u32[]{:S(2)}, u32[]{:S(2)}) collective-permute-start(f32[32,896]{1,0:T(8,128)S(1)} %pad_maximum_fusion.1), channel_id=1, source_target_pairs={{0,12},{4,8},{8,4},{12,0},{16,28},{20,24},{24,20},{28,16},{1,13},{... | collective-permute-start | bytes 344072 | tf_op jit(solution)/shard_map/ppermute | solution.py:40
  31.3 24.2 %collective-permute-start.7 = (f32[32,896]{1,0:T(8,128)S(1)}, f32[32,896]{1,0:T(8,128)S(1)}, u32[]{:S(2)}, u32[]{:S(2)}) collective-permute-start(f32[32,896]{1,0:T(8,128)S(1)} %pad_maximum_fusion.1), channel_id=1, source_target_pairs={{0,4},{4,0},{8,12},{12,8},{16,20},{20,16},{24,28},{28,24},{1,5},{5... | collective-permute-start | bytes 344072 | tf_op jit(solution)/shard_map/ppermute | solution.py:37
  55.6 5.4 %collective-permute-start.10 = (f32[32,896]{1,0:T(8,128)S(1)}, f32[32,896]{1,0:T(8,128)S(1)}, u32[]{:S(2)}, u32[]{:S(2)}) collective-permute-start(f32[32,896]{1,0:T(8,128)S(1)} %add_add_fusion.1), channel_id=1, source_target_pairs={{0,16},{4,20},{8,24},{12,28},{16,0},{20,4},{24,8},{28,12},{1,17},{... | collective-permute-start | bytes 344072 | tf_op jit(solution)/shard_map/ppermute | solution.py:37
  59.4 10.8 %collective-permute-start.2 = (bf16[4,108,864]{2,0,1:T(4,128)(2,1)S(1)}, bf16[4,108,864]{2,0,1:T(4,128)(2,1)S(1)}, u32[]{:S(2)}, u32[]{:S(2)}) collective-permute-start(bf16[4,108,864]{2,0,1:T(4,128)(2,1)S(1)} %copy.48), channel_id=1, source_target_pairs={{0,4},{4,0},{8,12},{12,8},{16,20},{20,16},{24,28},{28,24},{1,5},{5... | collective-permute-start | bytes 2239496 | tf_op jit(solution)/shard_map/ppermute | solution.py:58
  61.9 8.3 %copy-start.1 = (f32[4,2,108,864]{3,2,1,0:T(8,128)S(1)}, f32[4,2,108,864]{3,2,1,0:T(8,128)}, u32[]{:S(2)}) copy-start(f32[4,2,108,864]{3,2,1,0:T(8,128)} %reshape_reshape.6) | copy-start | bytes 8957956
  61.9 6.9 %collective-permute-start.11 = (f32[32,2,216]{2,1,0:T(2,128)S(1)}, f32[32,2,216]{2,1,0:T(2,128)S(1)}, u32[]{:S(2)}, u32[]{:S(2)}) collective-permute-start(f32[32,2,216]{2,1,0:T(2,128)S(1)} %bitcast.71), channel_id=1, source_target_pairs={{0,1},{1,0},{2,3},{3,2},{4,5},{5,4},{6,7},{7,6},{8,9},{9,8},{10,11... | collective-permute-start | bytes 165896 | tf_op jit(solution)/shard_map/ppermute | solution.py:58
  68.0 6.2 %copy-start.3 = (f32[32,32]{1,0:T(8,128)S(1)}, f32[32,32]{1,0:T(8,128)}, u32[]{:S(2)}) copy-start(f32[32,32]{1,0:T(8,128)} %param.11) | copy-start | bytes 12292
  69.0 5.2 %collective-permute-start.12 = (f32[32,1,216]{2,1,0:T(1,128)S(1)}, f32[32,1,216]{2,1,0:T(1,128)S(1)}, u32[]{:S(2)}, u32[]{:S(2)}) collective-permute-start(f32[32,1,216]{2,1,0:T(1,128)S(1)} %constant_dynamic-slice_fusion), channel_id=1, source_target_pairs={{0,2},{1,3},{2,0},{3,1},{4,6},{5,7},{6,4},{7,5},{8,10},{9,11},{10,... | collective-permute-start | bytes 82952 | tf_op jit(solution)/shard_map/ppermute | solution.py:58
  70.4 10.1 %collective-permute-start.3 = (bf16[2,108,864]{2,1,0:T(8,128)(2,1)S(1)}, bf16[2,108,864]{2,1,0:T(8,128)(2,1)S(1)}, u32[]{:S(2)}, u32[]{:S(2)}) collective-permute-start(bf16[2,108,864]{2,1,0:T(8,128)(2,1)S(1)} %fusion.9), channel_id=1, source_target_pairs={{0,8},{4,12},{8,0},{12,4},{16,24},{20,28},{24,16},{28,20},{1,9},{5... | collective-permute-start | bytes 1119752 | tf_op jit(solution)/shard_map/ppermute | solution.py:58
  80.7 5.8 %collective-permute-start.4 = (bf16[1,108,864]{2,1,0:T(8,128)(2,1)S(1)}, bf16[1,108,864]{2,1,0:T(8,128)(2,1)S(1)}, u32[]{:S(2)}, u32[]{:S(2)}) collective-permute-start(bf16[1,108,864]{2,1,0:T(8,128)(2,1)S(1)} %dynamic-slice_convert_fusion.2), channel_id=1, source_target_pairs={{0,16},{4,20},{8,24},{12,28},{16,0},{20,4},{24,8},{28,12},{1,17},{... | collective-permute-start | bytes 559880 | tf_op jit(solution)/shard_map/ppermute | solution.py:58
  86.7 8.1 %collective-permute-start.5 = (bf16[108,2,216]{0,2,1:T(8,128)(2,1)S(1)}, bf16[108,2,216]{0,2,1:T(8,128)(2,1)S(1)}, u32[]{:S(2)}, u32[]{:S(2)}) collective-permute-start(bf16[108,2,216]{0,2,1:T(8,128)(2,1)S(1)} %fusion.11), channel_id=1, source_target_pairs={{0,1},{1,0},{2,3},{3,2},{4,5},{5,4},{6,7},{7,6},{8,9},{9,8},{10,11... | collective-permute-start | bytes 279944 | tf_op jit(solution)/shard_map/ppermute | solution.py:58
  88.5 9.7 %collective-permute-start.14 = (f32[32,896]{1,0:T(8,128)S(1)}, f32[32,896]{1,0:T(8,128)S(1)}, u32[]{:S(2)}, u32[]{:S(2)}) collective-permute-start(f32[32,896]{1,0:T(8,128)S(1)} %pad_maximum_fusion.2), channel_id=1, source_target_pairs={{0,2},{1,3},{2,0},{3,1},{4,6},{5,7},{6,4},{7,5},{8,10},{9,11},{10,... | collective-permute-start | bytes 344072 | tf_op jit(solution)/shard_map/ppermute | solution.py:39
  89.2 8.9 %collective-permute-start.15 = (f32[32,896]{1,0:T(8,128)S(1)}, f32[32,896]{1,0:T(8,128)S(1)}, u32[]{:S(2)}, u32[]{:S(2)}) collective-permute-start(f32[32,896]{1,0:T(8,128)S(1)} %pad_maximum_fusion.2), channel_id=1, source_target_pairs={{0,3},{1,2},{2,1},{3,0},{4,7},{5,6},{6,5},{7,4},{8,11},{9,10},{10,... | collective-permute-start | bytes 344072 | tf_op jit(solution)/shard_map/ppermute | solution.py:40
  91.3 7.3 %collective-permute-start.13 = (f32[32,896]{1,0:T(8,128)S(1)}, f32[32,896]{1,0:T(8,128)S(1)}, u32[]{:S(2)}, u32[]{:S(2)}) collective-permute-start(f32[32,896]{1,0:T(8,128)S(1)} %pad_maximum_fusion.2), channel_id=1, source_target_pairs={{0,1},{1,0},{2,3},{3,2},{4,5},{5,4},{6,7},{7,6},{8,9},{9,8},{10,11... | collective-permute-start | bytes 344072 | tf_op jit(solution)/shard_map/ppermute | solution.py:37
  94.9 5.6 %collective-permute-start.6 = (bf16[108,1,216]{0,2,1:T(8,128)(2,1)S(1)}, bf16[108,1,216]{0,2,1:T(8,128)(2,1)S(1)}, u32[]{:S(2)}, u32[]{:S(2)}) collective-permute-start(bf16[108,1,216]{0,2,1:T(8,128)(2,1)S(1)} %dynamic-slice_convert_fusion.4), channel_id=1, source_target_pairs={{0,2},{1,3},{2,0},{3,1},{4,6},{5,7},{6,4},{7,5},{8,10},{9,11},{10,... | collective-permute-start | bytes 139976 | tf_op jit(solution)/shard_map/ppermute | solution.py:58
  98.7 2.5 %copy-start.2 = (f32[32,896]{1,0:T(8,128)}, f32[32,896]{1,0:T(8,128)S(1)}, u32[]{:S(2)}) copy-start(f32[32,896]{1,0:T(8,128)S(1)} %add_add_fusion) | copy-start | bytes 344068

commit v13 on v12

--- a/solution.py
+++ b/solution.py
@@ -163,8 +163,8 @@
     a_perm = lax.dot_general(
         weighted, patches_t, contract_cells, preferred_element_type=f32
     ) / jnp.float32(total_samples)
-    order = tap_order(channels, n_taps)
-    a_rows = jnp.dot(order, a_perm.astype(jnp.bfloat16), preferred_element_type=f32)
+    order, a_bf = lax.optimization_barrier((tap_order(channels, n_taps), a_perm.astype(jnp.bfloat16)))
+    a_rows = jnp.dot(order, a_bf, preferred_element_type=f32)
     a_orig = lax.dot_general(
         a_rows.astype(jnp.bfloat16), order, contract_cells, preferred_element_type=f32
     )

time: 102 us -> 98.4 us (0.965)
  matrix products: 32.2 us -> 27.2 us
  other arithmetic: 6.26 us -> 7.54 us
    dot_general x1, matrix products: 15.5 us -> 8.67 us  [on_device(): lax.dot_general(weighted, patches_t, contract_cells, preferred_element_ty...]
    dot_general x1, matrix products: 5.18 us -> 6.85 us  [on_device(): lax.dot_general(a_rows.astype(jnp.bfloat16), order, contract_cells, prefe...]
  transfers between devices with their start and end apart: 16 -> 16, of which waited for: 8 -> 8; matrix products, arithmetic and copies ran while one was open for 41% -> 37% of each run, Pallas kernels for 0% -> 0%
where the time goes in v13:
time: 98.4 us; the launch traced here: 98 us
  matrix products  27.2 us (28%)
  starting transfers between devices  23.1 us (23%)
  waiting for transfers between devices  21.1 us (21%)
  local copies, waits for them, and re-layouts  12.8 us (13%)
  other arithmetic  7.54 us (8%)
  Pallas kernels  5.18 us (5%)
  between operations  1.09 us (1%)
    ppermute x7, waiting for transfers between devices, halving_scatter(): got = lax.ppermute(send.astype(wire), axis, partner(axis, step))  15.4 us
    dot_general x1, matrix products, on_device(): lax.dot_general(weighted, patches_t, contract_cells, preferred_element_ty...  8.67 us
    ppermute x7, starting transfers between devices, halving_scatter(): got = lax.ppermute(send.astype(wire), axis, partner(axis, step))  7.97 us
    dot_general x1, matrix products, on_device(): lax.dot_general(a_rows.astype(jnp.bfloat16), order, contract_cells, prefe...  6.85 us
    ppermute x1, starting transfers between devices, padded_2(): lax.ppermute(tail, axis, [(i, (i + 1) % count) for i in range(ends)])  6.21 us
    dot_general x1, matrix products, on_device(): lax.dot_general(grad_flat, patches_t, contract_cells, preferred_element_t...  5.26 us
    pallas_call x1, Pallas kernels, patch_matrix(): pl.pallas_call(body, grid=(3,), in_specs=[pl.BlockSpec(shifted.shape, lam...  5.18 us
    dot_general x1, matrix products, on_device(): forward = jnp.dot(kernel_perm, patches_t, preferred_element_type=f32)  4.32 us
  transfers between devices with their start and end apart: 16, of which 8 were waited for; matrix products, arithmetic and copies ran while one was open for 37% of the time, Pallas kernels for 0%

profile of v13, /device:TPU:0, one launch (start us, length us, event | category | flops | bytes accessed | tf_op | source)
XLA Modules:
  0.0 98.0 jit_solution(8182210235474457320)
XLA Ops:
  0.7 1.1 %copy.42 = bf16[1,32,2,16,128]{4,1,3,2,0:T(8,128)(2,1)S(1)} copy(bf16[1,32,2,16,128]{4,3,2,1,0:T(8,128)(2,1)} %param.6) | data formatting | bytes 524288 | tf_op args[0]
  1.8 0.7 fusion.21
  2.5 1.3 %collective-permute-start.1 = (bf16[1,32,1,16,128]{4,1,3,2,0:T(8,128)(2,1)}, bf16[1,32,1,16,128]{4,1,3,2,0:T(8,128)(2,1)}, u32[]{:S(2)}, u32[]{:S(2)}) collective-permute-start(bf16[1,32,1,16,128]{4,1,3,2,0:T(8,128)(2,1)} %get-tuple-element.20), channel_id=1, source_target_pairs={{1,0},{2,1},{3,2},{5,4},{6,5},{7,6},{9,8},{10,9},{11,10},{13,12},{... | collective-permute-start | bytes 393224 | tf_op jit(solution)/shard_map/ppermute | solution.py:20
  3.8 6.2 %collective-permute-start = (bf16[1,32,1,16,128]{4,1,3,2,0:T(8,128)(2,1)}, bf16[1,32,1,16,128]{4,1,3,2,0:T(8,128)(2,1)}, u32[]{:S(2)}, u32[]{:S(2)}) collective-permute-start(bf16[1,32,1,16,128]{4,1,3,2,0:T(8,128)(2,1)} %get-tuple-element.19), channel_id=1, source_target_pairs={{0,1},{1,2},{2,3},{4,5},{5,6},{6,7},{8,9},{9,10},{10,11},{12,13},{... | collective-permute-start | bytes 393224 | tf_op jit(solution)/shard_map/ppermute | solution.py:18
  10.5 3.4 %convert_reduce_fusion = f32[4096]{0:T(1024)S(1)} fusion(s32[1024]{0:T(1024)} %bitcast.74), kind=kLoop, calls=%fused_computation | loop fusion | flops 12578816 | bytes 20480 | tf_op jit(solution)/shard_map/reduce_sum | solution.py:158
  13.8 1.1 %reshape_squeeze.3 = bf16[32,4096]{1,0:T(8,128)(2,1)S(1)} reshape(bf16[1,32,2,16,128]{4,3,2,1,0:T(8,128)(2,1)} %param.7) | data formatting | bytes 524288 | tf_op jit(solution)/shard_map/reshape;squeeze | solution.py:136
  16.2 1.3 %convolution_bitcast_fusion.1 = f32[32,32]{1,0:T(8,128)S(1)} fusion(bf16[32,2,16,128]{3,2,1,0:T(8,128)(2,1)} %bitcast.70), kind=kOutput, calls=%fused_computation.16 | convolution fusion | flops 8388608 | bytes 266240 | tf_op jit(solution)/shard_map/dot_general | solution.py:140
  17.5 1.0 %maximum_bitcast_fusion = bf16[32,4,16,128]{3,0,2,1:T(8,128)(2,1)S(1)} fusion(bf16[1,32,1,16,128]{4,1,3,2,0:T(8,128)(2,1)} %collective-permute-done.1, bf16[1,32,2,16,128]{4,1,3,2,0:T(8,128)(2,1)S(1)} %copy.42, bf16[1,32,1,16,128]{4,1,3,2,0:T(8,128)(2,1)} %collective-permute-done), kind=kLoop, calls=%fused_computation.24 | loop fusion | flops 524288 | bytes 1048576 | tf_op jit(solution)/shard_map/squeeze | solution.py:133
  19.4 1.5 %pad_maximum_fusion.src_ref = bf16[3,4,18,32,128]{4,3,2,1,0:T(8,128)(2,1)} fusion(bf16[1,4,18,32,128]{4,3,2,1,0:T(8,128)(2,1)S(1)} %get-tuple-element.17, bf16[1,4,18,32,128]{4,3,2,1,0:T(8,128)(2,1)S(1)} %get-tuple-element.18, bf16[1,4,18,32,128]{4,3,2,1,0:T(8,128)(2,1)S(1)} %get-tuple-element.16), kind=kLoop, calls=%fused_computation.9 | loop fusion | flops 1769472 | bytes 3538944 | tf_op jit(solution)/shard_map/stack | solution.py:78
  20.8 5.2 %shard_map.93 = bf16[864,4096]{1,0:T(8,128)(2,1)} custom-call(bf16[3,4,18,32,128]{4,3,2,1,0:T(8,128)(2,1)} %pad_maximum_fusion.src_ref), custom_call_target="tpu_custom_call" | custom-call | tf_op jit(solution)/shard_map/pallas_call | solution.py:91
  26.0 5.3 %convolution_bitcast_fusion = f32[32,864]{1,0:T(8,128)S(1)} fusion(bf16[864,4096]{1,0:T(8,128)(2,1)} %shard_map.93, bf16[32,4096]{1,0:T(8,128)(2,1)S(1)} %reshape_squeeze.3), kind=kOutput, calls=%fused_computation.15 | convolution fusion | flops 226492416 | bytes 7450624 | tf_op jit(solution)/shard_map/dot_general | solution.py:139
  31.4 1.9 %collective-permute-start.8 = (f32[32,896]{1,0:T(8,128)S(1)}, f32[32,896]{1,0:T(8,128)S(1)}, u32[]{:S(2)}, u32[]{:S(2)}) collective-permute-start(f32[32,896]{1,0:T(8,128)S(1)} %pad_maximum_fusion.1), channel_id=1, source_target_pairs={{0,8},{4,12},{8,0},{12,4},{16,24},{20,28},{24,16},{28,20},{1,9},{5... | collective-permute-start | bytes 344072 | tf_op jit(solution)/shard_map/ppermute | solution.py:39
  33.5 8.7 %multiply_convert_fusion.2 = bf16[864,864]{1,0:T(8,128)(2,1)} fusion(bf16[864,4096]{1,0:T(8,128)(2,1)S(1)} %copy-done.1, f32[4096]{0:T(1024)S(1)} %convert_reduce_fusion), kind=kOutput, calls=%fused_computation.6 | convolution fusion | flops 6127405056 | bytes 8587264 | tf_op jit(solution)/shard_map/dot_general | solution.py:163
  42.2 6.9 %fusion.5 = f32[864,864]{1,0:T(8,128)} fusion(bf16[864,864]{1,0:T(8,128)(2,1)S(1)} %fusion.2, bf16[864,864]{1,0:T(8,128)(2,1)} %multiply_convert_fusion.2), kind=kOutput, calls=%fused_computation.20 | convolution fusion | flops 2580636672 | bytes 5971968 | tf_op jit(solution)/shard_map/dot_general | solution.py:168
  49.1 3.3 %reshape_reshape.6 = f32[4,2,108,864]{3,2,1,0:T(8,128)} reshape(f32[864,864]{1,0:T(8,128)} %fusion.5) | data formatting | bytes 5971968 | tf_op jit(solution)/shard_map/reshape;reshape | solution.py:54
  52.4 2.0 %collective-permute-start.10 = (f32[32,896]{1,0:T(8,128)S(1)}, f32[32,896]{1,0:T(8,128)S(1)}, u32[]{:S(2)}, u32[]{:S(2)}) collective-permute-start(f32[32,896]{1,0:T(8,128)S(1)} %add_add_fusion.1), channel_id=1, source_target_pairs={{0,16},{4,20},{8,24},{12,28},{16,0},{20,4},{24,8},{28,12},{1,17},{... | collective-permute-start | bytes 344072 | tf_op jit(solution)/shard_map/ppermute | solution.py:37
  54.4 1.5 %fusion.4 = bf16[4,108,864]{2,1,0:T(8,128)(2,1)S(1)} fusion(f32[4,2,108,864]{3,2,1,0:T(8,128)} %reshape_reshape.6, s32[]{:T(128)S(6)} %select_n.105), kind=kLoop, calls=%fused_computation.17 | loop fusion | bytes 1492996 | tf_op jit(solution)/shard_map/convert_element_type | solution.py:58
  56.3 1.5 %collective-permute-done.10 = f32[32,896]{1,0:T(8,128)S(1)} collective-permute-done((f32[32,896]{1,0:T(8,128)S(1)}, f32[32,896]{1,0:T(8,128)S(1)}, u32[]{:S(2)}, u32[]{:S(2)}) %collective-permute-start.10) | collective-permute-done | bytes 114720 | tf_op jit(solution)/shard_map/ppermute | solution.py:37
  58.7 1.2 %collective-permute-start.11 = (f32[32,2,216]{2,1,0:T(2,128)S(1)}, f32[32,2,216]{2,1,0:T(2,128)S(1)}, u32[]{:S(2)}, u32[]{:S(2)}) collective-permute-start(f32[32,2,216]{2,1,0:T(2,128)S(1)} %bitcast.73), channel_id=1, source_target_pairs={{0,1},{1,0},{2,3},{3,2},{4,5},{5,4},{6,7},{7,6},{8,9},{9,8},{10,11... | collective-permute-start | bytes 165896 | tf_op jit(solution)/shard_map/ppermute | solution.py:58
  59.9 4.3 %fusion.3 = bf16[4,8,32,128]{3,1,2,0:T(8,128)(2,1)S(1)} fusion(bf16[32,864]{1,0:T(8,128)(2,1)S(1)} %reshape.78, bf16[864,4096]{1,0:T(8,128)(2,1)} %shard_map.93), kind=kOutput, calls=%fused_computation.14 | convolution fusion | flops 226623488 | bytes 7395328 | tf_op jit(solution)/shard_map/dot_general | solution.py:172
  64.2 0.7 copy.56
  65.1 1.9 %collective-permute-start.12 = (f32[32,1,216]{2,1,0:T(1,128)S(1)}, f32[32,1,216]{2,1,0:T(1,128)S(1)}, u32[]{:S(2)}, u32[]{:S(2)}) collective-permute-start(f32[32,1,216]{2,1,0:T(1,128)S(1)} %constant_dynamic-slice_fusion), channel_id=1, source_target_pairs={{0,2},{1,3},{2,0},{3,1},{4,6},{5,7},{6,4},{7,5},{8,10},{9,11},{10,... | collective-permute-start | bytes 82952 | tf_op jit(solution)/shard_map/ppermute | solution.py:58
  67.2 1.6 %collective-permute-start.3 = (bf16[2,108,864]{2,1,0:T(8,128)(2,1)S(1)}, bf16[2,108,864]{2,1,0:T(8,128)(2,1)S(1)}, u32[]{:S(2)}, u32[]{:S(2)}) collective-permute-start(bf16[2,108,864]{2,1,0:T(8,128)(2,1)S(1)} %fusion.6), channel_id=1, source_target_pairs={{0,8},{4,12},{8,0},{12,4},{16,24},{20,28},{24,16},{28,20},{1,9},{5... | collective-permute-start | bytes 1119752 | tf_op jit(solution)/shard_map/ppermute | solution.py:58
  68.8 1.2 %collective-permute-done.12 = f32[32,1,216]{2,1,0:T(1,128)S(1)} collective-permute-done((f32[32,1,216]{2,1,0:T(1,128)S(1)}, f32[32,1,216]{2,1,0:T(1,128)S(1)}, u32[]{:S(2)}, u32[]{:S(2)}) %collective-permute-start.12) | collective-permute-done | bytes 27680 | tf_op jit(solution)/shard_map/ppermute | solution.py:58
  70.2 7.1 %collective-permute-done.3 = bf16[2,108,864]{2,1,0:T(8,128)(2,1)S(1)} collective-permute-done((bf16[2,108,864]{2,1,0:T(8,128)(2,1)S(1)}, bf16[2,108,864]{2,1,0:T(8,128)(2,1)S(1)}, u32[]{:S(2)}, u32[]{:S(2)}) %collective-permute-start.3) | collective-permute-done | bytes 373280 | tf_op jit(solution)/shard_map/ppermute | solution.py:58
  77.5 1.6 %collective-permute-start.4 = (bf16[1,108,864]{2,1,0:T(8,128)(2,1)S(1)}, bf16[1,108,864]{2,1,0:T(8,128)(2,1)S(1)}, u32[]{:S(2)}, u32[]{:S(2)}) collective-permute-start(bf16[1,108,864]{2,1,0:T(8,128)(2,1)S(1)} %dynamic-slice_convert_fusion.2), channel_id=1, source_target_pairs={{0,16},{4,20},{8,24},{12,28},{16,0},{20,4},{24,8},{28,12},{1,17},{... | collective-permute-start | bytes 559880 | tf_op jit(solution)/shard_map/ppermute | solution.py:58
  79.7 3.6 %collective-permute-done.4 = bf16[1,108,864]{2,1,0:T(8,128)(2,1)S(1)} collective-permute-done((bf16[1,108,864]{2,1,0:T(8,128)(2,1)S(1)}, bf16[1,108,864]{2,1,0:T(8,128)(2,1)S(1)}, u32[]{:S(2)}, u32[]{:S(2)}) %collective-permute-start.4) | collective-permute-done | bytes 186656 | tf_op jit(solution)/shard_map/ppermute | solution.py:58
  83.5 1.7 %collective-permute-start.5 = (bf16[108,2,216]{0,2,1:T(8,128)(2,1)S(1)}, bf16[108,2,216]{0,2,1:T(8,128)(2,1)S(1)}, u32[]{:S(2)}, u32[]{:S(2)}) collective-permute-start(bf16[108,2,216]{0,2,1:T(8,128)(2,1)S(1)} %fusion.8), channel_id=1, source_target_pairs={{0,1},{1,0},{2,3},{3,2},{4,5},{5,4},{6,7},{7,6},{8,9},{9,8},{10,11... | collective-permute-start | bytes 279944 | tf_op jit(solution)/shard_map/ppermute | solution.py:58
  85.8 2.3 %collective-permute-start.15 = (f32[32,896]{1,0:T(8,128)S(1)}, f32[32,896]{1,0:T(8,128)S(1)}, u32[]{:S(2)}, u32[]{:S(2)}) collective-permute-start(f32[32,896]{1,0:T(8,128)S(1)} %pad_maximum_fusion.2), channel_id=1, source_target_pairs={{0,3},{1,2},{2,1},{3,0},{4,7},{5,6},{6,5},{7,4},{8,11},{9,10},{10,... | collective-permute-start | bytes 344072 | tf_op jit(solution)/shard_map/ppermute | solution.py:40
  88.8 2.6 %collective-permute-done.5 = bf16[108,2,216]{0,2,1:T(8,128)(2,1)S(1)} collective-permute-done((bf16[108,2,216]{0,2,1:T(8,128)(2,1)S(1)}, bf16[108,2,216]{0,2,1:T(8,128)(2,1)S(1)}, u32[]{:S(2)}, u32[]{:S(2)}) %collective-permute-start.5) | collective-permute-done | bytes 93344 | tf_op jit(solution)/shard_map/ppermute | solution.py:58
  91.5 3.4 %collective-permute-done.14 = f32[32,896]{1,0:T(8,128)S(1)} collective-permute-done((f32[32,896]{1,0:T(8,128)S(1)}, f32[32,896]{1,0:T(8,128)S(1)}, u32[]{:S(2)}, u32[]{:S(2)}) %collective-permute-start.14) | collective-permute-done | bytes 114720 | tf_op jit(solution)/shard_map/ppermute | solution.py:39
  96.4 0.9 collective-permute-done.6
  (62 shorter events, 9.1 us)
Async XLA Ops:
  0.6 78.4 %copy-start = (f32[216,864]{1,0:T(8,128)S(1)}, f32[216,864]{1,0:T(8,128)}, u32[]{:S(2)}) copy-start(f32[216,864]{1,0:T(8,128)} %param.10) | copy-start | bytes 2239492
  0.6 14.2 %copy-start.4 = (bf16[32,864]{1,0:T(8,128)(2,1)S(1)}, bf16[32,864]{1,0:T(8,128)(2,1)}, u32[]{:S(2)}) copy-start(bf16[32,864]{1,0:T(8,128)(2,1)} %param.8) | copy-start | bytes 165892
  2.5 14.9 %collective-permute-start.1 = (bf16[1,32,1,16,128]{4,1,3,2,0:T(8,128)(2,1)}, bf16[1,32,1,16,128]{4,1,3,2,0:T(8,128)(2,1)}, u32[]{:S(2)}, u32[]{:S(2)}) collective-permute-start(bf16[1,32,1,16,128]{4,1,3,2,0:T(8,128)(2,1)} %get-tuple-element.20), channel_id=1, source_target_pairs={{1,0},{2,1},{3,2},{5,4},{6,5},{7,6},{9,8},{10,9},{11,10},{13,12},{... | collective-permute-start | bytes 393224 | tf_op jit(solution)/shard_map/ppermute | solution.py:20
  3.8 13.7 %collective-permute-start = (bf16[1,32,1,16,128]{4,1,3,2,0:T(8,128)(2,1)}, bf16[1,32,1,16,128]{4,1,3,2,0:T(8,128)(2,1)}, u32[]{:S(2)}, u32[]{:S(2)}) collective-permute-start(bf16[1,32,1,16,128]{4,1,3,2,0:T(8,128)(2,1)} %get-tuple-element.19), channel_id=1, source_target_pairs={{0,1},{1,2},{2,3},{4,5},{5,6},{6,7},{8,9},{9,10},{10,11},{12,13},{... | collective-permute-start | bytes 393224 | tf_op jit(solution)/shard_map/ppermute | solution.py:18
  26.0 7.5 %copy-start.1 = (bf16[864,4096]{1,0:T(8,128)(2,1)S(1)}, bf16[864,4096]{1,0:T(8,128)(2,1)}, u32[]{:S(2)}) copy-start(bf16[864,4096]{1,0:T(8,128)(2,1)} %shard_map.93) | copy-start | bytes 21233668
  31.4 21.0 %collective-permute-start.8 = (f32[32,896]{1,0:T(8,128)S(1)}, f32[32,896]{1,0:T(8,128)S(1)}, u32[]{:S(2)}, u32[]{:S(2)}) collective-permute-start(f32[32,896]{1,0:T(8,128)S(1)} %pad_maximum_fusion.1), channel_id=1, source_target_pairs={{0,8},{4,12},{8,0},{12,4},{16,24},{20,28},{24,16},{28,20},{1,9},{5... | collective-permute-start | bytes 344072 | tf_op jit(solution)/shard_map/ppermute | solution.py:39
  33.3 19.0 %collective-permute-start.9 = (f32[32,896]{1,0:T(8,128)S(1)}, f32[32,896]{1,0:T(8,128)S(1)}, u32[]{:S(2)}, u32[]{:S(2)}) collective-permute-start(f32[32,896]{1,0:T(8,128)S(1)} %pad_maximum_fusion.1), channel_id=1, source_target_pairs={{0,12},{4,8},{8,4},{12,0},{16,28},{20,24},{24,20},{28,16},{1,13},{... | collective-permute-start | bytes 344072 | tf_op jit(solution)/shard_map/ppermute | solution.py:40
  33.3 19.0 %collective-permute-start.7 = (f32[32,896]{1,0:T(8,128)S(1)}, f32[32,896]{1,0:T(8,128)S(1)}, u32[]{:S(2)}, u32[]{:S(2)}) collective-permute-start(f32[32,896]{1,0:T(8,128)S(1)} %pad_maximum_fusion.1), channel_id=1, source_target_pairs={{0,4},{4,0},{8,12},{12,8},{16,20},{20,16},{24,28},{28,24},{1,5},{5... | collective-permute-start | bytes 344072 | tf_op jit(solution)/shard_map/ppermute | solution.py:37
  52.4 5.4 %collective-permute-start.10 = (f32[32,896]{1,0:T(8,128)S(1)}, f32[32,896]{1,0:T(8,128)S(1)}, u32[]{:S(2)}, u32[]{:S(2)}) collective-permute-start(f32[32,896]{1,0:T(8,128)S(1)} %add_add_fusion.1), channel_id=1, source_target_pairs={{0,16},{4,20},{8,24},{12,28},{16,0},{20,4},{24,8},{28,12},{1,17},{... | collective-permute-start | bytes 344072 | tf_op jit(solution)/shard_map/ppermute | solution.py:37
  56.2 10.8 %collective-permute-start.2 = (bf16[4,108,864]{2,0,1:T(4,128)(2,1)S(1)}, bf16[4,108,864]{2,0,1:T(4,128)(2,1)S(1)}, u32[]{:S(2)}, u32[]{:S(2)}) collective-permute-start(bf16[4,108,864]{2,0,1:T(4,128)(2,1)S(1)} %copy.48), channel_id=1, source_target_pairs={{0,4},{4,0},{8,12},{12,8},{16,20},{20,16},{24,28},{28,24},{1,5},{5... | collective-permute-start | bytes 2239496 | tf_op jit(solution)/shard_map/ppermute | solution.py:58
  58.7 8.3 %copy-start.2 = (f32[4,2,108,864]{3,2,1,0:T(8,128)S(1)}, f32[4,2,108,864]{3,2,1,0:T(8,128)}, u32[]{:S(2)}) copy-start(f32[4,2,108,864]{3,2,1,0:T(8,128)} %reshape_reshape.6) | copy-start | bytes 8957956
  58.7 6.3 %collective-permute-start.11 = (f32[32,2,216]{2,1,0:T(2,128)S(1)}, f32[32,2,216]{2,1,0:T(2,128)S(1)}, u32[]{:S(2)}, u32[]{:S(2)}) collective-permute-start(f32[32,2,216]{2,1,0:T(2,128)S(1)} %bitcast.73), channel_id=1, source_target_pairs={{0,1},{1,0},{2,3},{3,2},{4,5},{5,4},{6,7},{7,6},{8,9},{9,8},{10,11... | collective-permute-start | bytes 165896 | tf_op jit(solution)/shard_map/ppermute | solution.py:58
  64.2 5.9 %copy-start.5 = (f32[32,32]{1,0:T(8,128)S(1)}, f32[32,32]{1,0:T(8,128)}, u32[]{:S(2)}) copy-start(f32[32,32]{1,0:T(8,128)} %param.11) | copy-start | bytes 12292
  65.1 4.9 %collective-permute-start.12 = (f32[32,1,216]{2,1,0:T(1,128)S(1)}, f32[32,1,216]{2,1,0:T(1,128)S(1)}, u32[]{:S(2)}, u32[]{:S(2)}) collective-permute-start(f32[32,1,216]{2,1,0:T(1,128)S(1)} %constant_dynamic-slice_fusion), channel_id=1, source_target_pairs={{0,2},{1,3},{2,0},{3,1},{4,6},{5,7},{6,4},{7,5},{8,10},{9,11},{10,... | collective-permute-start | bytes 82952 | tf_op jit(solution)/shard_map/ppermute | solution.py:58
  67.2 10.1 %collective-permute-start.3 = (bf16[2,108,864]{2,1,0:T(8,128)(2,1)S(1)}, bf16[2,108,864]{2,1,0:T(8,128)(2,1)S(1)}, u32[]{:S(2)}, u32[]{:S(2)}) collective-permute-start(bf16[2,108,864]{2,1,0:T(8,128)(2,1)S(1)} %fusion.6), channel_id=1, source_target_pairs={{0,8},{4,12},{8,0},{12,4},{16,24},{20,28},{24,16},{28,20},{1,9},{5... | collective-permute-start | bytes 1119752 | tf_op jit(solution)/shard_map/ppermute | solution.py:58
  77.5 5.8 %collective-permute-start.4 = (bf16[1,108,864]{2,1,0:T(8,128)(2,1)S(1)}, bf16[1,108,864]{2,1,0:T(8,128)(2,1)S(1)}, u32[]{:S(2)}, u32[]{:S(2)}) collective-permute-start(bf16[1,108,864]{2,1,0:T(8,128)(2,1)S(1)} %dynamic-slice_convert_fusion.2), channel_id=1, source_target_pairs={{0,16},{4,20},{8,24},{12,28},{16,0},{20,4},{24,8},{28,12},{1,17},{... | collective-permute-start | bytes 559880 | tf_op jit(solution)/shard_map/ppermute | solution.py:58
  83.5 7.8 %collective-permute-start.5 = (bf16[108,2,216]{0,2,1:T(8,128)(2,1)S(1)}, bf16[108,2,216]{0,2,1:T(8,128)(2,1)S(1)}, u32[]{:S(2)}, u32[]{:S(2)}) collective-permute-start(bf16[108,2,216]{0,2,1:T(8,128)(2,1)S(1)} %fusion.8), channel_id=1, source_target_pairs={{0,1},{1,0},{2,3},{3,2},{4,5},{5,4},{6,7},{7,6},{8,9},{9,8},{10,11... | collective-permute-start | bytes 279944 | tf_op jit(solution)/shard_map/ppermute | solution.py:58
  85.3 9.7 %collective-permute-start.14 = (f32[32,896]{1,0:T(8,128)S(1)}, f32[32,896]{1,0:T(8,128)S(1)}, u32[]{:S(2)}, u32[]{:S(2)}) collective-permute-start(f32[32,896]{1,0:T(8,128)S(1)} %pad_maximum_fusion.2), channel_id=1, source_target_pairs={{0,2},{1,3},{2,0},{3,1},{4,6},{5,7},{6,4},{7,5},{8,10},{9,11},{10,... | collective-permute-start | bytes 344072 | tf_op jit(solution)/shard_map/ppermute | solution.py:39
  85.8 9.1 %collective-permute-start.15 = (f32[32,896]{1,0:T(8,128)S(1)}, f32[32,896]{1,0:T(8,128)S(1)}, u32[]{:S(2)}, u32[]{:S(2)}) collective-permute-start(f32[32,896]{1,0:T(8,128)S(1)} %pad_maximum_fusion.2), channel_id=1, source_target_pairs={{0,3},{1,2},{2,1},{3,0},{4,7},{5,6},{6,5},{7,4},{8,11},{9,10},{10,... | collective-permute-start | bytes 344072 | tf_op jit(solution)/shard_map/ppermute | solution.py:40
  88.1 7.6 %collective-permute-start.13 = (f32[32,896]{1,0:T(8,128)S(1)}, f32[32,896]{1,0:T(8,128)S(1)}, u32[]{:S(2)}, u32[]{:S(2)}) collective-permute-start(f32[32,896]{1,0:T(8,128)S(1)} %pad_maximum_fusion.2), channel_id=1, source_target_pairs={{0,1},{1,0},{2,3},{3,2},{4,5},{5,4},{6,7},{7,6},{8,9},{9,8},{10,11... | collective-permute-start | bytes 344072 | tf_op jit(solution)/shard_map/ppermute | solution.py:37
  91.4 5.9 %collective-permute-start.6 = (bf16[108,1,216]{0,2,1:T(8,128)(2,1)S(1)}, bf16[108,1,216]{0,2,1:T(8,128)(2,1)S(1)}, u32[]{:S(2)}, u32[]{:S(2)}) collective-permute-start(bf16[108,1,216]{0,2,1:T(8,128)(2,1)S(1)} %dynamic-slice_convert_fusion.4), channel_id=1, source_target_pairs={{0,2},{1,3},{2,0},{3,1},{4,6},{5,7},{6,4},{7,5},{8,10},{9,11},{10,... | collective-permute-start | bytes 139976 | tf_op jit(solution)/shard_map/ppermute | solution.py:58
  95.7 2.2 %copy-start.3 = (f32[32,896]{1,0:T(8,128)}, f32[32,896]{1,0:T(8,128)S(1)}, u32[]{:S(2)}) copy-start(f32[32,896]{1,0:T(8,128)S(1)} %add_add_fusion) | copy-start | bytes 344068

commit v14 on v13

--- a/solution.py
+++ b/solution.py
@@ -102,6 +102,18 @@
     new = jnp.arange(size, dtype=jnp.int32)
     old = (new % n_taps) * channels + new // n_taps
     return (old[:, None] == jnp.arange(size, dtype=jnp.int32)[None, :]).astype(jnp.bfloat16)
+
+
+def halving_order(channels, n_taps, rows, axis):
+    size = channels * n_taps
+    bits = lax.axis_size(axis).bit_length() - 1
+    spot = jnp.arange(size, dtype=jnp.int32)
+    rank = spot // rows
+    flipped = sum(((rank >> b) & 1) << (bits - 1 - b) for b in range(bits))
+    block = jnp.bitwise_xor(flipped, lax.axis_index(axis))
+    original = block * rows + spot % rows
+    source = (original % n_taps) * channels + original // n_taps
+    return (source[:, None] == jnp.arange(size, dtype=jnp.int32)[None, :]).astype(jnp.bfloat16)
 
 
 def block_order(n_grains, n_taps, grain):
@@ -163,18 +175,25 @@
     a_perm = lax.dot_general(
         weighted, patches_t, contract_cells, preferred_element_type=f32
     ) / jnp.float32(total_samples)
-    order, a_bf = lax.optimization_barrier((tap_order(channels, n_taps), a_perm.astype(jnp.bfloat16)))
-    a_rows = jnp.dot(order, a_bf, preferred_element_type=f32)
-    a_orig = lax.dot_general(
-        a_rows.astype(jnp.bfloat16), order, contract_cells, preferred_element_type=f32
-    )
-    a_orig, kernel_perm = lax.optimization_barrier((a_orig, kernel_perm))
+    rows = patch // n_dp
+    cols = patch // n_sp
+    order, placed, a_bf = lax.optimization_barrier(
+        (tap_order(channels, n_taps), halving_order(channels, n_taps, rows, "dp"), a_perm.astype(jnp.bfloat16))
+    )
+    a_rows = jnp.dot(placed, a_bf, preferred_element_type=f32)
+    a_orig, kernel_perm = lax.optimization_barrier((a_rows, kernel_perm))
     forward = jnp.dot(kernel_perm, patches_t, preferred_element_type=f32)
     conv_out = forward.astype(jnp.bfloat16).reshape(1, channels, planes, y_cells, x_cells)
-    rows = patch // n_dp
-    cols = patch // n_sp
-    a_rows = halving_scatter(a_orig.reshape(n_dp, rows, patch), "dp", 0)
-    a_factor = halving_scatter(a_rows.reshape(rows, n_sp, cols), "space", 1).reshape(rows, cols)
+    step = 1
+    while step < n_dp:
+        half = a_orig.shape[0] // 2
+        got = lax.ppermute(a_orig[half:].astype(jnp.bfloat16), "dp", partner("dp", step))
+        a_orig = a_orig[:half] + got.astype(f32)
+        step *= 2
+    a_block = lax.dot_general(
+        a_orig, order.astype(f32), contract_cells, precision=lax.Precision.HIGH
+    )
+    a_factor = halving_scatter(a_block.reshape(rows, n_sp, cols), "space", 1).reshape(rows, cols)
     return (conv_out, a_factor, g_factor, pre_grad)
 
 

time: 98.4 us -> 89 us (0.904)
  matrix products: 27.2 us -> 22.1 us
  local copies, waits for them, and re-layouts: 12.8 us -> 9.43 us
  waiting for transfers between devices: 21.1 us -> 17.8 us
  other arithmetic: 7.54 us -> 10.3 us
    ppermute x0 -> x3, waiting for transfers between devices: none -> 8.72 us  [on_device(): lax.ppermute(a_orig[half:].astype(jnp.bfloat16), 'dp', partner('dp', step))]
    ppermute x7 -> x4, waiting for transfers between devices: 15.4 us -> 8.62 us  [halving_scatter(): got = lax.ppermute(send.astype(wire), axis, partner(axis, step))]
    dot_general x1 -> x2, matrix products: 6.85 us -> 2.97 us  [the longest x1 1.92 us: on_device(): a_rows = jnp.dot(placed, a_bf, preferred_element_type=f32)]
    ppermute x2, waiting for transfers between devices: 3.44 us -> 0.01 us  [butterfly_sum(): pair = lax.ppermute(x, axis, partner(axis, high))]
    ppermute x7 -> x4, starting transfers between devices: 7.97 us -> 4.98 us  [halving_scatter(): got = lax.ppermute(send.astype(wire), axis, partner(axis, step))]
    another operation x2, local copies, waits for them, and re-layouts: 3.54 us -> 0.95 us  [halving_scatter(): split = blocks.reshape(shape[:dim] + (shape[dim] // 2, 2) + shape[dim + 1:])]
    ppermute x0 -> x3, starting transfers between devices: none -> 2.28 us  [on_device(): lax.ppermute(a_orig[half:].astype(jnp.bfloat16), 'dp', partner('dp', step))]
    convert_element_type x6 -> x1, local copies, waits for them, and re-layouts: 1.93 us -> 0.02 us  [halving_scatter(): got = lax.ppermute(send.astype(wire), axis, partner(axis, step))]
  transfers between devices with their start and end apart: 16 -> 16, of which waited for: 8 -> 6; matrix products, arithmetic and copies ran while one was open for 37% -> 34% of each run, Pallas kernels for 0% -> 0%
where the time goes in v14:
time: 89 us; the launch traced here: 88.7 us
  starting transfers between devices  22.9 us (26%)
  matrix products  22.1 us (25%)
  waiting for transfers between devices  17.8 us (20%)
  other arithmetic  10.3 us (12%)
  local copies, waits for them, and re-layouts  9.43 us (11%)
  Pallas kernels  5.15 us (6%)
  between operations  1.02 us (1%)
    ppermute x3, waiting for transfers between devices, on_device(): lax.ppermute(a_orig[half:].astype(jnp.bfloat16), 'dp', partner('dp', step))  8.72 us
    ppermute x4, waiting for transfers between devices, halving_scatter(): got = lax.ppermute(send.astype(wire), axis, partner(axis, step))  8.62 us
    dot_general x1, matrix products, on_device(): lax.dot_general(weighted, patches_t, contract_cells, preferred_element_ty...  7.49 us
    ppermute x1, starting transfers between devices, padded_2(): lax.ppermute(tail, axis, [(i, (i + 1) % count) for i in range(ends)])  6.21 us
    dot_general x1, matrix products, on_device(): lax.dot_general(grad_flat, patches_t, contract_cells, preferred_element_t...  5.26 us
    pallas_call x1, Pallas kernels, patch_matrix(): pl.pallas_call(body, grid=(3,), in_specs=[pl.BlockSpec(shifted.shape, lam...  5.15 us
    ppermute x4, starting transfers between devices, halving_scatter(): got = lax.ppermute(send.astype(wire), axis, partner(axis, step))  4.98 us
    dot_general x1, matrix products, on_device(): forward = jnp.dot(kernel_perm, patches_t, preferred_element_type=f32)  4.33 us
  transfers between devices with their start and end apart: 16, of which 6 were waited for; matrix products, arithmetic and copies ran while one was open for 34% of the time, Pallas kernels for 0%

profile of v14, /device:TPU:0, one launch (start us, length us, event | category | flops | bytes accessed | tf_op | source)
XLA Modules:
  0.0 88.7 jit_solution(16878371662995320976)
XLA Ops:
  0.7 1.1 %copy.26 = bf16[1,32,2,16,128]{4,1,3,2,0:T(8,128)(2,1)S(1)} copy(bf16[1,32,2,16,128]{4,3,2,1,0:T(8,128)(2,1)} %param.6) | data formatting | bytes 524288 | tf_op args[0]
  1.8 0.7 fusion.28
  2.5 1.3 %collective-permute-start.1 = (bf16[1,32,1,16,128]{4,1,3,2,0:T(8,128)(2,1)}, bf16[1,32,1,16,128]{4,1,3,2,0:T(8,128)(2,1)}, u32[]{:S(2)}, u32[]{:S(2)}) collective-permute-start(bf16[1,32,1,16,128]{4,1,3,2,0:T(8,128)(2,1)} %get-tuple-element.22), channel_id=1, source_target_pairs={{1,0},{2,1},{3,2},{5,4},{6,5},{7,6},{9,8},{10,9},{11,10},{13,12},{... | collective-permute-start | bytes 393224 | tf_op jit(solution)/shard_map/ppermute | solution.py:20
  3.8 6.2 %collective-permute-start = (bf16[1,32,1,16,128]{4,1,3,2,0:T(8,128)(2,1)}, bf16[1,32,1,16,128]{4,1,3,2,0:T(8,128)(2,1)}, u32[]{:S(2)}, u32[]{:S(2)}) collective-permute-start(bf16[1,32,1,16,128]{4,1,3,2,0:T(8,128)(2,1)} %get-tuple-element.21), channel_id=1, source_target_pairs={{0,1},{1,2},{2,3},{4,5},{5,6},{6,7},{8,9},{9,10},{10,11},{12,13},{... | collective-permute-start | bytes 393224 | tf_op jit(solution)/shard_map/ppermute | solution.py:18
  10.1 3.4 %convert_reduce_fusion = f32[4096]{0:T(1024)S(1)} fusion(s32[1024]{0:T(1024)} %bitcast.62), kind=kLoop, calls=%fused_computation | loop fusion | flops 12578816 | bytes 20480 | tf_op jit(solution)/shard_map/reduce_sum | solution.py:170
  13.5 1.7 %fusion.2 = (bf16[864,864]{1,0:T(8,128)(2,1)S(1)}, bf16[864,864]{1,0:T(8,128)(2,1)}) fusion(s32[864]{0:T(1024)S(1)} %fusion.21, s32[864]{0:T(1024)S(1)} %fusion.24), kind=kLoop, calls=%fused_computation.9 | loop fusion | flops 2985984 | bytes 2992896 | tf_op jit(solution)/shard_map/convert_element_type | solution.py:104
  16.5 1.3 %convolution_bitcast_fusion.1 = f32[32,32]{1,0:T(8,128)S(1)} fusion(bf16[32,2,16,128]{3,2,1,0:T(8,128)(2,1)} %bitcast.57), kind=kOutput, calls=%fused_computation.17 | convolution fusion | flops 8388608 | bytes 266240 | tf_op jit(solution)/shard_map/dot_general | solution.py:152
  17.8 1.0 %maximum_bitcast_fusion = bf16[32,4,16,128]{3,0,2,1:T(8,128)(2,1)S(1)} fusion(bf16[1,32,1,16,128]{4,1,3,2,0:T(8,128)(2,1)} %collective-permute-done.1, bf16[1,32,2,16,128]{4,1,3,2,0:T(8,128)(2,1)S(1)} %copy.26, bf16[1,32,1,16,128]{4,1,3,2,0:T(8,128)(2,1)} %collective-permute-done), kind=kLoop, calls=%fused_computation.23 | loop fusion | flops 524288 | bytes 1048576 | tf_op jit(solution)/shard_map/squeeze | solution.py:145
  19.7 1.5 %pad_maximum_fusion.src_ref = bf16[3,4,18,32,128]{4,3,2,1,0:T(8,128)(2,1)} fusion(bf16[1,4,18,32,128]{4,3,2,1,0:T(8,128)(2,1)S(1)} %get-tuple-element.19, bf16[1,4,18,32,128]{4,3,2,1,0:T(8,128)(2,1)S(1)} %get-tuple-element.20, bf16[1,4,18,32,128]{4,3,2,1,0:T(8,128)(2,1)S(1)} %get-tuple-element.18), kind=kLoop, calls=%fused_computation.11 | loop fusion | flops 1769472 | bytes 3538944 | tf_op jit(solution)/shard_map/stack | solution.py:78
  21.2 5.2 %shard_map.93 = bf16[864,4096]{1,0:T(8,128)(2,1)} custom-call(bf16[3,4,18,32,128]{4,3,2,1,0:T(8,128)(2,1)} %pad_maximum_fusion.src_ref), custom_call_target="tpu_custom_call" | custom-call | tf_op jit(solution)/shard_map/pallas_call | solution.py:91
  26.4 5.3 %convolution_bitcast_fusion = f32[32,864]{1,0:T(8,128)S(1)} fusion(bf16[864,4096]{1,0:T(8,128)(2,1)} %shard_map.93, bf16[32,4096]{1,0:T(8,128)(2,1)S(1)} %reshape_squeeze.3), kind=kOutput, calls=%fused_computation.16 | convolution fusion | flops 226492416 | bytes 7450624 | tf_op jit(solution)/shard_map/dot_general | solution.py:151
  31.7 2.0 %collective-permute-start.8 = (f32[32,896]{1,0:T(8,128)S(1)}, f32[32,896]{1,0:T(8,128)S(1)}, u32[]{:S(2)}, u32[]{:S(2)}) collective-permute-start(f32[32,896]{1,0:T(8,128)S(1)} %pad_maximum_fusion.1), channel_id=1, source_target_pairs={{0,8},{4,12},{8,0},{12,4},{16,24},{20,28},{24,16},{28,20},{1,9},{5... | collective-permute-start | bytes 344072 | tf_op jit(solution)/shard_map/ppermute | solution.py:39
  33.9 7.5 %multiply_convert_fusion.2 = bf16[864,864]{1,0:T(8,128)(2,1)S(1)} fusion(bf16[864,4096]{1,0:T(8,128)(2,1)S(1)} %copy-done.1, f32[4096]{0:T(1024)S(1)} %convert_reduce_fusion), kind=kOutput, calls=%fused_computation.6 | convolution fusion | flops 6127405056 | bytes 8587264 | tf_op jit(solution)/shard_map/dot_general | solution.py:175
  41.5 2.0 %collective-permute-start.10 = (f32[32,896]{1,0:T(8,128)S(1)}, f32[32,896]{1,0:T(8,128)S(1)}, u32[]{:S(2)}, u32[]{:S(2)}) collective-permute-start(f32[32,896]{1,0:T(8,128)S(1)} %add_add_fusion.1), channel_id=1, source_target_pairs={{0,16},{4,20},{8,24},{12,28},{16,0},{20,4},{24,8},{28,12},{1,17},{... | collective-permute-start | bytes 344072 | tf_op jit(solution)/shard_map/ppermute | solution.py:37
  43.5 1.9 %fusion.29 = f32[864,864]{1,0:T(8,128)S(1)} fusion(bf16[864,864]{1,0:T(8,128)(2,1)S(1)} %copy-done.4, bf16[864,864]{1,0:T(8,128)(2,1)S(1)} %multiply_convert_fusion.2), kind=kOutput, calls=%fused_computation.78 | convolution fusion | flops 1289945088 | bytes 5971968 | tf_op jit(solution)/shard_map/dot_general | solution.py:183
  45.4 1.0 %slice.87 = bf16[432,864]{1,0:T(8,128)(2,1)} slice(f32[864,864]{1,0:T(8,128)S(1)} %fusion.29), slice={[432:864], [0:864]} | slice | bytes 1492992 | tf_op jit(solution)/shard_map/slice | solution.py:190
  48.2 1.0 %collective-permute-start.11 = (f32[32,2,216]{2,1,0:T(2,128)S(1)}, f32[32,2,216]{2,1,0:T(2,128)S(1)}, u32[]{:S(2)}, u32[]{:S(2)}) collective-permute-start(f32[32,2,216]{2,1,0:T(2,128)S(1)} %bitcast.61), channel_id=1, source_target_pairs={{0,1},{1,0},{2,3},{3,2},{4,5},{5,4},{6,7},{7,6},{8,9},{9,8},{10,11... | collective-permute-start | bytes 165896 | tf_op jit(solution)/shard_map/ppermute | solution.py:58
  49.2 4.3 %fusion.4 = bf16[4,8,32,128]{3,1,2,0:T(8,128)(2,1)S(1)} fusion(bf16[32,864]{1,0:T(8,128)(2,1)S(1)} %reshape.110, bf16[864,4096]{1,0:T(8,128)(2,1)} %shard_map.93), kind=kOutput, calls=%fused_computation.15 | convolution fusion | flops 226623488 | bytes 7395328 | tf_op jit(solution)/shard_map/dot_general | solution.py:185
  53.6 0.7 copy.40
  54.5 1.9 %collective-permute-start.12 = (f32[32,1,216]{2,1,0:T(1,128)S(1)}, f32[32,1,216]{2,1,0:T(1,128)S(1)}, u32[]{:S(2)}, u32[]{:S(2)}) collective-permute-start(f32[32,1,216]{2,1,0:T(1,128)S(1)} %constant_dynamic-slice_fusion), channel_id=1, source_target_pairs={{0,2},{1,3},{2,0},{3,1},{4,6},{5,7},{6,4},{7,5},{8,10},{9,11},{10,... | collective-permute-start | bytes 82952 | tf_op jit(solution)/shard_map/ppermute | solution.py:58
  56.4 1.3 %convert_add_fusion = f32[432,864]{1,0:T(8,128)S(1)} fusion(bf16[432,864]{1,0:T(8,128)(2,1)} %collective-permute-done.2, f32[864,864]{1,0:T(8,128)S(1)} %copy-done.3), kind=kLoop, calls=%fused_computation.13 | loop fusion | flops 746496 | bytes 3732480 | tf_op jit(solution)/shard_map/add | solution.py:191
  57.7 1.6 %collective-permute-start.3 = (bf16[216,864]{1,0:T(8,128)(2,1)S(1)}, bf16[216,864]{1,0:T(8,128)(2,1)S(1)}, u32[]{:S(2)}, u32[]{:S(2)}) collective-permute-start(bf16[216,864]{1,0:T(8,128)(2,1)S(1)} %slice.88), channel_id=1, source_target_pairs={{0,8},{4,12},{8,0},{12,4},{16,24},{20,28},{24,16},{28,20},{1,9},{5... | collective-permute-start | bytes 1119752 | tf_op jit(solution)/shard_map/ppermute | solution.py:190
  59.6 8.5 %collective-permute-done.3 = bf16[216,864]{1,0:T(8,128)(2,1)S(1)} collective-permute-done((bf16[216,864]{1,0:T(8,128)(2,1)S(1)}, bf16[216,864]{1,0:T(8,128)(2,1)S(1)}, u32[]{:S(2)}, u32[]{:S(2)}) %collective-permute-start.3) | collective-permute-done | bytes 373280 | tf_op jit(solution)/shard_map/ppermute | solution.py:190
  68.3 0.7 collective-permute-start.4
  69.9 1.0 %collective-permute-start.14 = (f32[32,896]{1,0:T(8,128)S(1)}, f32[32,896]{1,0:T(8,128)S(1)}, u32[]{:S(2)}, u32[]{:S(2)}) collective-permute-start(f32[32,896]{1,0:T(8,128)S(1)} %pad_maximum_fusion.2), channel_id=1, source_target_pairs={{0,2},{1,3},{2,0},{3,1},{4,6},{5,7},{6,4},{7,5},{8,10},{9,11},{10,... | collective-permute-start | bytes 344072 | tf_op jit(solution)/shard_map/ppermute | solution.py:39
  70.9 2.9 %collective-permute-start.15 = (f32[32,896]{1,0:T(8,128)S(1)}, f32[32,896]{1,0:T(8,128)S(1)}, u32[]{:S(2)}, u32[]{:S(2)}) collective-permute-start(f32[32,896]{1,0:T(8,128)S(1)} %pad_maximum_fusion.2), channel_id=1, source_target_pairs={{0,3},{1,2},{2,1},{3,0},{4,7},{5,6},{6,5},{7,4},{8,11},{9,10},{10,... | collective-permute-start | bytes 344072 | tf_op jit(solution)/shard_map/ppermute | solution.py:40
  74.0 1.0 %fusion.5 = f32[108,864]{1,0:T(8,128)S(1)} fusion(bf16[864,864]{1,0:T(8,128)(2,1)S(1)} %get-tuple-element.16, f32[216,864]{1,0:T(8,128)S(1)} %slice_add_fusion, bf16[108,864]{1,0:T(8,128)(2,1)S(1)} %collective-permute-done.4), kind=kOutput, calls=%fused_computation.26 | convolution fusion | flops 483916032 | bytes 2523648 | tf_op jit(solution)/shard_map/dot_general | solution.py:193
  75.1 0.7 reshape_reshape.3
  76.2 1.9 %collective-permute-start.5 = (bf16[108,2,216]{0,2,1:T(8,128)(2,1)S(1)}, bf16[108,2,216]{0,2,1:T(8,128)(2,1)S(1)}, u32[]{:S(2)}, u32[]{:S(2)}) collective-permute-start(bf16[108,2,216]{0,2,1:T(8,128)(2,1)S(1)} %bitcast.60), channel_id=1, source_target_pairs={{0,1},{1,0},{2,3},{3,2},{4,5},{5,4},{6,7},{7,6},{8,9},{9,8},{10,11... | collective-permute-start | bytes 279944 | tf_op jit(solution)/shard_map/ppermute | solution.py:58
  78.5 3.8 %collective-permute-done.5 = bf16[108,2,216]{0,2,1:T(8,128)(2,1)S(1)} collective-permute-done((bf16[108,2,216]{0,2,1:T(8,128)(2,1)S(1)}, bf16[108,2,216]{0,2,1:T(8,128)(2,1)S(1)}, u32[]{:S(2)}, u32[]{:S(2)}) %collective-permute-start.5) | collective-permute-done | bytes 93344 | tf_op jit(solution)/shard_map/ppermute | solution.py:58
  82.6 0.7 slice.75
  83.3 4.8 %collective-permute-done.6 = bf16[108,1,216]{0,2,1:T(8,128)(2,1)S(1)} collective-permute-done((bf16[108,1,216]{0,2,1:T(8,128)(2,1)S(1)}, bf16[108,1,216]{0,2,1:T(8,128)(2,1)S(1)}, u32[]{:S(2)}, u32[]{:S(2)}) %collective-permute-start.6) | collective-permute-done | bytes 46688 | tf_op jit(solution)/shard_map/ppermute | solution.py:58
  (70 shorter events, 7.7 us)
Async XLA Ops:
  0.6 68.4 %copy-start = (f32[216,864]{1,0:T(8,128)S(1)}, f32[216,864]{1,0:T(8,128)}, u32[]{:S(2)}) copy-start(f32[216,864]{1,0:T(8,128)} %param.10) | copy-start | bytes 2239492
  0.6 14.5 %copy-start.5 = (bf16[1,32,2,16,128]{4,3,2,1,0:T(8,128)(2,1)S(1)}, bf16[1,32,2,16,128]{4,3,2,1,0:T(8,128)(2,1)}, u32[]{:S(2)}) copy-start(bf16[1,32,2,16,128]{4,3,2,1,0:T(8,128)(2,1)} %param.7) | copy-start | bytes 786436
  0.7 14.7 %copy-start.7 = (bf16[32,864]{1,0:T(8,128)(2,1)S(1)}, bf16[32,864]{1,0:T(8,128)(2,1)}, u32[]{:S(2)}) copy-start(bf16[32,864]{1,0:T(8,128)(2,1)} %param.8) | copy-start | bytes 165892
  2.5 15.3 %collective-permute-start.1 = (bf16[1,32,1,16,128]{4,1,3,2,0:T(8,128)(2,1)}, bf16[1,32,1,16,128]{4,1,3,2,0:T(8,128)(2,1)}, u32[]{:S(2)}, u32[]{:S(2)}) collective-permute-start(bf16[1,32,1,16,128]{4,1,3,2,0:T(8,128)(2,1)} %get-tuple-element.22), channel_id=1, source_target_pairs={{1,0},{2,1},{3,2},{5,4},{6,5},{7,6},{9,8},{10,9},{11,10},{13,12},{... | collective-permute-start | bytes 393224 | tf_op jit(solution)/shard_map/ppermute | solution.py:20
  3.8 14.0 %collective-permute-start = (bf16[1,32,1,16,128]{4,1,3,2,0:T(8,128)(2,1)}, bf16[1,32,1,16,128]{4,1,3,2,0:T(8,128)(2,1)}, u32[]{:S(2)}, u32[]{:S(2)}) collective-permute-start(bf16[1,32,1,16,128]{4,1,3,2,0:T(8,128)(2,1)} %get-tuple-element.21), channel_id=1, source_target_pairs={{0,1},{1,2},{2,3},{4,5},{5,6},{6,7},{8,9},{9,10},{10,11},{12,13},{... | collective-permute-start | bytes 393224 | tf_op jit(solution)/shard_map/ppermute | solution.py:18
  26.4 7.5 %copy-start.1 = (bf16[864,4096]{1,0:T(8,128)(2,1)S(1)}, bf16[864,4096]{1,0:T(8,128)(2,1)}, u32[]{:S(2)}) copy-start(bf16[864,4096]{1,0:T(8,128)(2,1)} %shard_map.93) | copy-start | bytes 21233668
  31.7 11.8 %copy-start.4 = (bf16[864,864]{1,0:T(8,128)(2,1)S(1)}, bf16[864,864]{1,0:T(8,128)(2,1)}, u32[]{:S(2)}) copy-start(bf16[864,864]{1,0:T(8,128)(2,1)} %get-tuple-element.12) | copy-start | bytes 4478980
  31.7 9.7 %collective-permute-start.8 = (f32[32,896]{1,0:T(8,128)S(1)}, f32[32,896]{1,0:T(8,128)S(1)}, u32[]{:S(2)}, u32[]{:S(2)}) collective-permute-start(f32[32,896]{1,0:T(8,128)S(1)} %pad_maximum_fusion.1), channel_id=1, source_target_pairs={{0,8},{4,12},{8,0},{12,4},{16,24},{20,28},{24,16},{28,20},{1,9},{5... | collective-permute-start | bytes 344072 | tf_op jit(solution)/shard_map/ppermute | solution.py:39
  33.7 7.7 %collective-permute-start.9 = (f32[32,896]{1,0:T(8,128)S(1)}, f32[32,896]{1,0:T(8,128)S(1)}, u32[]{:S(2)}, u32[]{:S(2)}) collective-permute-start(f32[32,896]{1,0:T(8,128)S(1)} %pad_maximum_fusion.1), channel_id=1, source_target_pairs={{0,12},{4,8},{8,4},{12,0},{16,28},{20,24},{24,20},{28,16},{1,13},{... | collective-permute-start | bytes 344072 | tf_op jit(solution)/shard_map/ppermute | solution.py:40
  33.7 7.7 %collective-permute-start.7 = (f32[32,896]{1,0:T(8,128)S(1)}, f32[32,896]{1,0:T(8,128)S(1)}, u32[]{:S(2)}, u32[]{:S(2)}) collective-permute-start(f32[32,896]{1,0:T(8,128)S(1)} %pad_maximum_fusion.1), channel_id=1, source_target_pairs={{0,4},{4,0},{8,12},{12,8},{16,20},{20,16},{24,28},{28,24},{1,5},{5... | collective-permute-start | bytes 344072 | tf_op jit(solution)/shard_map/ppermute | solution.py:37
  41.5 5.4 %collective-permute-start.10 = (f32[32,896]{1,0:T(8,128)S(1)}, f32[32,896]{1,0:T(8,128)S(1)}, u32[]{:S(2)}, u32[]{:S(2)}) collective-permute-start(f32[32,896]{1,0:T(8,128)S(1)} %add_add_fusion.1), channel_id=1, source_target_pairs={{0,16},{4,20},{8,24},{12,28},{16,0},{20,4},{24,8},{28,12},{1,17},{... | collective-permute-start | bytes 344072 | tf_op jit(solution)/shard_map/ppermute | solution.py:37
  45.4 1.9 %copy-start.2 = (f32[864,864]{1,0:T(8,128)}, f32[864,864]{1,0:T(8,128)S(1)}, u32[]{:S(2)}) copy-start(f32[864,864]{1,0:T(8,128)S(1)} %fusion.29) | copy-start | bytes 8957956
  46.5 9.9 %collective-permute-start.2 = (bf16[432,864]{1,0:T(8,128)(2,1)}, bf16[432,864]{1,0:T(8,128)(2,1)}, u32[]{:S(2)}, u32[]{:S(2)}) collective-permute-start(bf16[432,864]{1,0:T(8,128)(2,1)} %slice.87), channel_id=1, source_target_pairs={{0,4},{4,0},{8,12},{12,8},{16,20},{20,16},{24,28},{28,24},{1,5},{5... | collective-permute-start | bytes 2239496 | tf_op jit(solution)/shard_map/ppermute | solution.py:190
  48.2 8.2 %copy-start.3 = (f32[864,864]{1,0:T(8,128)S(1)}, f32[864,864]{1,0:T(8,128)}, u32[]{:S(2)}) copy-start(f32[864,864]{1,0:T(8,128)} %copy-done.2) | copy-start | bytes 8957956
  48.2 6.2 %collective-permute-start.11 = (f32[32,2,216]{2,1,0:T(2,128)S(1)}, f32[32,2,216]{2,1,0:T(2,128)S(1)}, u32[]{:S(2)}, u32[]{:S(2)}) collective-permute-start(f32[32,2,216]{2,1,0:T(2,128)S(1)} %bitcast.61), channel_id=1, source_target_pairs={{0,1},{1,0},{2,3},{3,2},{4,5},{5,4},{6,7},{7,6},{8,9},{9,8},{10,11... | collective-permute-start | bytes 165896 | tf_op jit(solution)/shard_map/ppermute | solution.py:58
  53.6 5.9 %copy-start.8 = (f32[32,32]{1,0:T(8,128)S(1)}, f32[32,32]{1,0:T(8,128)}, u32[]{:S(2)}) copy-start(f32[32,32]{1,0:T(8,128)} %param.11) | copy-start | bytes 12292
  54.5 4.9 %collective-permute-start.12 = (f32[32,1,216]{2,1,0:T(1,128)S(1)}, f32[32,1,216]{2,1,0:T(1,128)S(1)}, u32[]{:S(2)}, u32[]{:S(2)}) collective-permute-start(f32[32,1,216]{2,1,0:T(1,128)S(1)} %constant_dynamic-slice_fusion), channel_id=1, source_target_pairs={{0,2},{1,3},{2,0},{3,1},{4,6},{5,7},{6,4},{7,5},{8,10},{9,11},{10,... | collective-permute-start | bytes 82952 | tf_op jit(solution)/shard_map/ppermute | solution.py:58
  57.7 10.4 %collective-permute-start.3 = (bf16[216,864]{1,0:T(8,128)(2,1)S(1)}, bf16[216,864]{1,0:T(8,128)(2,1)S(1)}, u32[]{:S(2)}, u32[]{:S(2)}) collective-permute-start(bf16[216,864]{1,0:T(8,128)(2,1)S(1)} %slice.88), channel_id=1, source_target_pairs={{0,8},{4,12},{8,0},{12,4},{16,24},{20,28},{24,16},{28,20},{1,9},{5... | collective-permute-start | bytes 1119752 | tf_op jit(solution)/shard_map/ppermute | solution.py:190
  68.3 5.8 %collective-permute-start.4 = (bf16[108,864]{1,0:T(8,128)(2,1)S(1)}, bf16[108,864]{1,0:T(8,128)(2,1)S(1)}, u32[]{:S(2)}, u32[]{:S(2)}) collective-permute-start(bf16[108,864]{1,0:T(8,128)(2,1)S(1)} %slice.89), channel_id=1, source_target_pairs={{0,16},{4,20},{8,24},{12,28},{16,0},{20,4},{24,8},{28,12},{1,17},{... | collective-permute-start | bytes 559880 | tf_op jit(solution)/shard_map/ppermute | solution.py:190
  69.9 12.6 %collective-permute-start.14 = (f32[32,896]{1,0:T(8,128)S(1)}, f32[32,896]{1,0:T(8,128)S(1)}, u32[]{:S(2)}, u32[]{:S(2)}) collective-permute-start(f32[32,896]{1,0:T(8,128)S(1)} %pad_maximum_fusion.2), channel_id=1, source_target_pairs={{0,2},{1,3},{2,0},{3,1},{4,6},{5,7},{6,4},{7,5},{8,10},{9,11},{10,... | collective-permute-start | bytes 344072 | tf_op jit(solution)/shard_map/ppermute | solution.py:39
  70.9 11.6 %collective-permute-start.15 = (f32[32,896]{1,0:T(8,128)S(1)}, f32[32,896]{1,0:T(8,128)S(1)}, u32[]{:S(2)}, u32[]{:S(2)}) collective-permute-start(f32[32,896]{1,0:T(8,128)S(1)} %pad_maximum_fusion.2), channel_id=1, source_target_pairs={{0,3},{1,2},{2,1},{3,0},{4,7},{5,6},{6,5},{7,4},{8,11},{9,10},{10,... | collective-permute-start | bytes 344072 | tf_op jit(solution)/shard_map/ppermute | solution.py:40
  73.9 8.6 %collective-permute-start.13 = (f32[32,896]{1,0:T(8,128)S(1)}, f32[32,896]{1,0:T(8,128)S(1)}, u32[]{:S(2)}, u32[]{:S(2)}) collective-permute-start(f32[32,896]{1,0:T(8,128)S(1)} %pad_maximum_fusion.2), channel_id=1, source_target_pairs={{0,1},{1,0},{2,3},{3,2},{4,5},{5,4},{6,7},{7,6},{8,9},{9,8},{10,11... | collective-permute-start | bytes 344072 | tf_op jit(solution)/shard_map/ppermute | solution.py:37
  76.2 6.1 %collective-permute-start.5 = (bf16[108,2,216]{0,2,1:T(8,128)(2,1)S(1)}, bf16[108,2,216]{0,2,1:T(8,128)(2,1)S(1)}, u32[]{:S(2)}, u32[]{:S(2)}) collective-permute-start(bf16[108,2,216]{0,2,1:T(8,128)(2,1)S(1)} %bitcast.60), channel_id=1, source_target_pairs={{0,1},{1,0},{2,3},{3,2},{4,5},{5,4},{6,7},{7,6},{8,9},{9,8},{10,11... | collective-permute-start | bytes 279944 | tf_op jit(solution)/shard_map/ppermute | solution.py:58
  82.3 5.7 %collective-permute-start.6 = (bf16[108,1,216]{0,2,1:T(8,128)(2,1)S(1)}, bf16[108,1,216]{0,2,1:T(8,128)(2,1)S(1)}, u32[]{:S(2)}, u32[]{:S(2)}) collective-permute-start(bf16[108,1,216]{0,2,1:T(8,128)(2,1)S(1)} %dynamic-slice_convert_fusion), channel_id=1, source_target_pairs={{0,2},{1,3},{2,0},{3,1},{4,6},{5,7},{6,4},{7,5},{8,10},{9,11},{10,... | collective-permute-start | bytes 139976 | tf_op jit(solution)/shard_map/ppermute | solution.py:58
  82.6 6.1 %copy-start.6 = (f32[32,896]{1,0:T(8,128)}, f32[32,896]{1,0:T(8,128)S(1)}, u32[]{:S(2)}) copy-start(f32[32,896]{1,0:T(8,128)S(1)} %add_add_fusion) | copy-start | bytes 344068

commit v15 on v14

--- a/solution.py
+++ b/solution.py
@@ -58,6 +58,37 @@
         got = lax.ppermute(send.astype(wire), axis, partner(axis, step))
         blocks = keep + got.astype(jnp.float32)
         step *= 2
+    return blocks
+
+
+def quad_scatter(blocks, axis, dim):
+    me = lax.axis_index(axis)
+    low = 1
+    while low < lax.axis_size(axis):
+        shape = blocks.shape
+        if low * 2 < lax.axis_size(axis):
+            split = blocks.reshape(shape[:dim] + (shape[dim] // 4, 4) + shape[dim + 1 :])
+            digit = (me // low) % 4
+
+            def pick(d):
+                return lax.dynamic_index_in_dim(split, d, axis=dim + 1, keepdims=False)
+
+            got = [
+                lax.ppermute(pick(digit ^ k).astype(jnp.bfloat16), axis, partner(axis, k * low)).astype(
+                    jnp.float32
+                )
+                for k in (1, 2, 3)
+            ]
+            blocks = (pick(digit) + got[0]) + (got[1] + got[2])
+            low *= 4
+        else:
+            split = blocks.reshape(shape[:dim] + (shape[dim] // 2, 2) + shape[dim + 1 :])
+            bit = (me // low) % 2
+            keep = lax.dynamic_index_in_dim(split, bit, axis=dim + 1, keepdims=False)
+            send = lax.dynamic_index_in_dim(split, 1 - bit, axis=dim + 1, keepdims=False)
+            got = lax.ppermute(send.astype(jnp.bfloat16), axis, partner(axis, low))
+            blocks = keep + got.astype(jnp.float32)
+            low *= 2
     return blocks
 
 
@@ -193,7 +224,7 @@
     a_block = lax.dot_general(
         a_orig, order.astype(f32), contract_cells, precision=lax.Precision.HIGH
     )
-    a_factor = halving_scatter(a_block.reshape(rows, n_sp, cols), "space", 1).reshape(rows, cols)
+    a_factor = quad_scatter(a_block.reshape(rows, n_sp, cols), "space", 1).reshape(rows, cols)
     return (conv_out, a_factor, g_factor, pre_grad)
 
 

time: 89 us -> 91.7 us (1.030)
  matrix products: 22.1 us -> 29.7 us
  waiting for transfers between devices: 17.8 us -> 15.2 us
  other arithmetic: 10.3 us -> 7.97 us
  local copies, waits for them, and re-layouts: 9.43 us -> 8.09 us
  starting transfers between devices: 22.9 us -> 24.1 us
    ppermute x4 -> x2, waiting for transfers between devices: 8.62 us -> 0.01 us  [halving_scatter(): got = lax.ppermute(send.astype(wire), axis, partner(axis, step))]
    dot_general x1, matrix products: 7.49 us -> 13.4 us  [on_device(): lax.dot_general(weighted, patches_t, contract_cells, preferred_element_ty...]
    ppermute x0 -> x3, starting transfers between devices: none -> 4.57 us  [quad_scatter(): lax.ppermute(pick(digit ^ k).astype(jnp.bfloat16), axis, partner(axis, k...]
    ppermute x0 -> x3, waiting for transfers between devices: none -> 3.55 us  [quad_scatter(): lax.ppermute(pick(digit ^ k).astype(jnp.bfloat16), axis, partner(axis, k...]
    ppermute x2, waiting for transfers between devices: 0.01 us -> 2.12 us  [butterfly_sum(): other = lax.ppermute(x, axis, partner(axis, low + high))]
    ppermute x4 -> x2, starting transfers between devices: 4.98 us -> 3.01 us  [halving_scatter(): got = lax.ppermute(send.astype(wire), axis, partner(axis, step))]
    ppermute x2, waiting for transfers between devices: 0.01 us -> 1.95 us  [butterfly_sum(): pair = lax.ppermute(x, axis, partner(axis, high))]
    dot_general x1, matrix products: 1.92 us -> 3.78 us  [on_device(): a_rows = jnp.dot(placed, a_bf, preferred_element_type=f32)]
  transfers between devices with their start and end apart: 16 -> 17, of which waited for: 6 -> 7; matrix products, arithmetic and copies ran while one was open for 34% -> 37% of each run, Pallas kernels for 0% -> 0%
where the time goes in v15:
time: 91.7 us; the launch traced here: 91.3 us
  matrix products  29.7 us (32%)
  starting transfers between devices  24.1 us (26%)
  waiting for transfers between devices  15.2 us (17%)
  local copies, waits for them, and re-layouts  8.09 us (9%)
  other arithmetic  7.97 us (9%)
  Pallas kernels  5.16 us (6%)
  between operations  1 us (1%)
    dot_general x1, matrix products, on_device(): lax.dot_general(weighted, patches_t, contract_cells, preferred_element_ty...  13.4 us
    ppermute x3, waiting for transfers between devices, on_device(): lax.ppermute(a_orig[half:].astype(jnp.bfloat16), 'dp', partner('dp', step))  7.53 us
    ppermute x1, starting transfers between devices, padded_2(): lax.ppermute(tail, axis, [(i, (i + 1) % count) for i in range(ends)])  5.56 us
    pallas_call x1, Pallas kernels, patch_matrix(): pl.pallas_call(body, grid=(3,), in_specs=[pl.BlockSpec(shifted.shape, lam...  5.16 us
    dot_general x1, matrix products, on_device(): lax.dot_general(grad_flat, patches_t, contract_cells, preferred_element_t...  5.12 us
    ppermute x3, starting transfers between devices, quad_scatter(): lax.ppermute(pick(digit ^ k).astype(jnp.bfloat16), axis, partner(axis, k...  4.57 us
    dot_general x1, matrix products, on_device(): forward = jnp.dot(kernel_perm, patches_t, preferred_element_type=f32)  4.33 us
    dot_general x1, matrix products, on_device(): a_rows = jnp.dot(placed, a_bf, preferred_element_type=f32)  3.78 us
  transfers between devices with their start and end apart: 17, of which 7 were waited for; matrix products, arithmetic and copies ran while one was open for 37% of the time, Pallas kernels for 0%

profile of v15, /device:TPU:0, one launch (start us, length us, event | category | flops | bytes accessed | tf_op | source)
XLA Modules:
  0.0 91.3 jit_solution(8834366854655883723)
XLA Ops:
  0.6 1.1 %copy.30 = bf16[1,32,2,16,128]{4,1,3,2,0:T(8,128)(2,1)S(1)} copy(bf16[1,32,2,16,128]{4,3,2,1,0:T(8,128)(2,1)} %param.6) | data formatting | bytes 524288 | tf_op args[0]
  1.8 1.3 %collective-permute-start.1 = (bf16[1,32,1,16,128]{4,1,3,2,0:T(8,128)(2,1)S(1)}, bf16[1,32,1,16,128]{4,1,3,2,0:T(8,128)(2,1)S(1)}, u32[]{:S(2)}, u32[]{:S(2)}) collective-permute-start(bf16[1,32,1,16,128]{4,1,3,2,0:T(8,128)(2,1)S(1)} %get-tuple-element.25), channel_id=1, source_target_pairs={{1,0},{2,1},{3,2},{5,4},{6,5},{7,6},{9,8},{10,9},{11,10},{13,12},{... | collective-permute-start | bytes 393224 | tf_op jit(solution)/shard_map/ppermute | solution.py:20
  3.1 5.6 %collective-permute-start = (bf16[1,32,1,16,128]{4,1,3,2,0:T(8,128)(2,1)S(1)}, bf16[1,32,1,16,128]{4,1,3,2,0:T(8,128)(2,1)S(1)}, u32[]{:S(2)}, u32[]{:S(2)}) collective-permute-start(bf16[1,32,1,16,128]{4,1,3,2,0:T(8,128)(2,1)S(1)} %get-tuple-element.24), channel_id=1, source_target_pairs={{0,1},{1,2},{2,3},{4,5},{5,6},{6,7},{8,9},{9,10},{10,11},{12,13},{... | collective-permute-start | bytes 393224 | tf_op jit(solution)/shard_map/ppermute | solution.py:18
  8.7 3.4 %convert_reduce_fusion = f32[4096]{0:T(1024)S(1)} fusion(s32[1024]{0:T(1024)} %bitcast.74), kind=kLoop, calls=%fused_computation | loop fusion | flops 12578816 | bytes 20480 | tf_op jit(solution)/shard_map/reduce_sum | solution.py:201
  12.1 1.1 %reshape_squeeze.3 = bf16[32,4096]{1,0:T(8,128)(2,1)S(1)} reshape(bf16[1,32,2,16,128]{4,3,2,1,0:T(8,128)(2,1)} %param.7) | data formatting | bytes 524288 | tf_op jit(solution)/shard_map/reshape;squeeze | solution.py:179
  13.2 1.3 %convolution_bitcast_fusion.1 = f32[32,32]{1,0:T(8,128)S(1)} fusion(bf16[32,2,16,128]{3,2,1,0:T(8,128)(2,1)} %bitcast.67), kind=kOutput, calls=%fused_computation.17 | convolution fusion | flops 8388608 | bytes 266240 | tf_op jit(solution)/shard_map/dot_general | solution.py:183
  15.4 1.5 %pad_maximum_fusion.src_ref = bf16[3,4,18,32,128]{4,3,2,1,0:T(8,128)(2,1)} fusion(bf16[1,4,18,32,128]{4,3,2,1,0:T(8,128)(2,1)S(1)} %get-tuple-element.19, bf16[1,4,18,32,128]{4,3,2,1,0:T(8,128)(2,1)S(1)} %get-tuple-element.20, bf16[1,4,18,32,128]{4,3,2,1,0:T(8,128)(2,1)S(1)} %get-tuple-element.18), kind=kLoop, calls=%fused_computation.11 | loop fusion | flops 1769472 | bytes 3538944 | tf_op jit(solution)/shard_map/stack | solution.py:109
  16.9 5.2 %shard_map.93 = bf16[864,4096]{1,0:T(8,128)(2,1)} custom-call(bf16[3,4,18,32,128]{4,3,2,1,0:T(8,128)(2,1)} %pad_maximum_fusion.src_ref), custom_call_target="tpu_custom_call" | custom-call | tf_op jit(solution)/shard_map/pallas_call | solution.py:122
  22.0 5.1 %convolution_bitcast_fusion = f32[32,864]{1,0:T(8,128)S(1)} fusion(bf16[864,4096]{1,0:T(8,128)(2,1)} %shard_map.93, bf16[32,4096]{1,0:T(8,128)(2,1)S(1)} %reshape_squeeze.3), kind=kOutput, calls=%fused_computation.16 | convolution fusion | flops 226492416 | bytes 7450624 | tf_op jit(solution)/shard_map/dot_general | solution.py:182
  27.3 1.9 %collective-permute-start.9 = (f32[32,896]{1,0:T(8,128)S(1)}, f32[32,896]{1,0:T(8,128)S(1)}, u32[]{:S(2)}, u32[]{:S(2)}) collective-permute-start(f32[32,896]{1,0:T(8,128)S(1)} %pad_maximum_fusion.1), channel_id=1, source_target_pairs={{0,8},{4,12},{8,0},{12,4},{16,24},{20,28},{24,16},{28,20},{1,9},{5... | collective-permute-start | bytes 344072 | tf_op jit(solution)/shard_map/ppermute | solution.py:39
  29.4 1.7 %fusion.2 = (bf16[864,864]{1,0:T(8,128)(2,1)S(1)}, bf16[864,864]{1,0:T(8,128)(2,1)}) fusion(s32[864]{0:T(1024)S(1)} %fusion.23, s32[864]{0:T(1024)S(1)} %fusion.26), kind=kLoop, calls=%fused_computation.9 | loop fusion | flops 2985984 | bytes 2992896 | tf_op jit(solution)/shard_map/convert_element_type | solution.py:135
  32.4 2.1 %collective-permute-done.10 = f32[32,896]{1,0:T(8,128)S(1)} collective-permute-done((f32[32,896]{1,0:T(8,128)S(1)}, f32[32,896]{1,0:T(8,128)S(1)}, u32[]{:S(2)}, u32[]{:S(2)}) %collective-permute-start.10) | collective-permute-done | bytes 114720 | tf_op jit(solution)/shard_map/ppermute | solution.py:40
  34.5 1.7 %collective-permute-start.11 = (f32[32,896]{1,0:T(8,128)S(1)}, f32[32,896]{1,0:T(8,128)S(1)}, u32[]{:S(2)}, u32[]{:S(2)}) collective-permute-start(f32[32,896]{1,0:T(8,128)S(1)} %add_add_fusion.1), channel_id=1, source_target_pairs={{0,16},{4,20},{8,24},{12,28},{16,0},{20,4},{24,8},{28,12},{1,17},{... | collective-permute-start | bytes 344072 | tf_op jit(solution)/shard_map/ppermute | solution.py:37
  36.2 13.4 %multiply_convert_fusion.2 = bf16[864,864]{1,0:T(8,128)(2,1)} fusion(bf16[864,4096]{1,0:T(8,128)(2,1)} %shard_map.93, f32[4096]{0:T(1024)S(1)} %convert_reduce_fusion), kind=kOutput, calls=%fused_computation.6 | convolution fusion | flops 6127405056 | bytes 8587264 | tf_op jit(solution)/shard_map/dot_general | solution.py:206
  50.6 1.7 %collective-permute-start.12 = (f32[32,2,216]{2,1,0:T(2,128)S(1)}, f32[32,2,216]{2,1,0:T(2,128)S(1)}, u32[]{:S(2)}, u32[]{:S(2)}) collective-permute-start(f32[32,2,216]{2,1,0:T(2,128)S(1)} %bitcast.70), channel_id=1, source_target_pairs={{0,1},{1,0},{2,3},{3,2},{4,5},{5,4},{6,7},{7,6},{8,9},{9,8},{10,11... | collective-permute-start | bytes 165896 | tf_op jit(solution)/shard_map/ppermute | solution.py:58
  52.2 3.8 %fusion.31 = f32[864,864]{1,0:T(8,128)S(1)} fusion(bf16[864,864]{1,0:T(8,128)(2,1)} %get-tuple-element.12, bf16[864,864]{1,0:T(8,128)(2,1)} %multiply_convert_fusion.2), kind=kOutput, calls=%fused_computation.82 | convolution fusion | flops 1289945088 | bytes 5971968 | tf_op jit(solution)/shard_map/dot_general | solution.py:214
  56.3 1.4 %collective-permute-start.13 = (f32[32,1,216]{2,1,0:T(1,128)S(1)}, f32[32,1,216]{2,1,0:T(1,128)S(1)}, u32[]{:S(2)}, u32[]{:S(2)}) collective-permute-start(f32[32,1,216]{2,1,0:T(1,128)S(1)} %constant_dynamic-slice_fusion), channel_id=1, source_target_pairs={{0,2},{1,3},{2,0},{3,1},{4,6},{5,7},{6,4},{7,5},{8,10},{9,11},{10,... | collective-permute-start | bytes 82952 | tf_op jit(solution)/shard_map/ppermute | solution.py:58
  57.6 4.3 %fusion.4 = bf16[4,8,32,128]{3,1,2,0:T(8,128)(2,1)S(1)} fusion(bf16[32,864]{1,0:T(8,128)(2,1)S(1)} %reshape.141, bf16[864,4096]{1,0:T(8,128)(2,1)} %shard_map.93), kind=kOutput, calls=%fused_computation.15 | convolution fusion | flops 226623488 | bytes 7395328 | tf_op jit(solution)/shard_map/dot_general | solution.py:216
  62.0 0.7 copy.48
  63.1 1.1 %collective-permute-start.3 = (bf16[216,864]{1,0:T(8,128)(2,1)S(1)}, bf16[216,864]{1,0:T(8,128)(2,1)S(1)}, u32[]{:S(2)}, u32[]{:S(2)}) collective-permute-start(bf16[216,864]{1,0:T(8,128)(2,1)S(1)} %slice.88), channel_id=1, source_target_pairs={{0,8},{4,12},{8,0},{12,4},{16,24},{20,28},{24,16},{28,20},{1,9},{5... | collective-permute-start | bytes 1119752 | tf_op jit(solution)/shard_map/ppermute | solution.py:221
  65.0 1.6 %collective-permute-start.15 = (f32[32,896]{1,0:T(8,128)S(1)}, f32[32,896]{1,0:T(8,128)S(1)}, u32[]{:S(2)}, u32[]{:S(2)}) collective-permute-start(f32[32,896]{1,0:T(8,128)S(1)} %pad_maximum_fusion.2), channel_id=1, source_target_pairs={{0,2},{1,3},{2,0},{3,1},{4,6},{5,7},{6,4},{7,5},{8,10},{9,11},{10,... | collective-permute-start | bytes 344072 | tf_op jit(solution)/shard_map/ppermute | solution.py:39
  66.6 2.5 %collective-permute-start.16 = (f32[32,896]{1,0:T(8,128)S(1)}, f32[32,896]{1,0:T(8,128)S(1)}, u32[]{:S(2)}, u32[]{:S(2)}) collective-permute-start(f32[32,896]{1,0:T(8,128)S(1)} %pad_maximum_fusion.2), channel_id=1, source_target_pairs={{0,3},{1,2},{2,1},{3,0},{4,7},{5,6},{6,5},{7,4},{8,11},{9,10},{10,... | collective-permute-start | bytes 344072 | tf_op jit(solution)/shard_map/ppermute | solution.py:40
  69.1 4.8 %collective-permute-done.3 = bf16[216,864]{1,0:T(8,128)(2,1)S(1)} collective-permute-done((bf16[216,864]{1,0:T(8,128)(2,1)S(1)}, bf16[216,864]{1,0:T(8,128)(2,1)S(1)}, u32[]{:S(2)}, u32[]{:S(2)}) %collective-permute-start.3) | collective-permute-done | bytes 373280 | tf_op jit(solution)/shard_map/ppermute | solution.py:221
  74.6 2.0 %collective-permute-done.15 = f32[32,896]{1,0:T(8,128)S(1)} collective-permute-done((f32[32,896]{1,0:T(8,128)S(1)}, f32[32,896]{1,0:T(8,128)S(1)}, u32[]{:S(2)}, u32[]{:S(2)}) %collective-permute-start.15) | collective-permute-done | bytes 114720 | tf_op jit(solution)/shard_map/ppermute | solution.py:39
  76.7 0.7 slice.75
  77.4 2.7 %collective-permute-done.4 = bf16[108,864]{1,0:T(8,128)(2,1)S(1)} collective-permute-done((bf16[108,864]{1,0:T(8,128)(2,1)S(1)}, bf16[108,864]{1,0:T(8,128)(2,1)S(1)}, u32[]{:S(2)}, u32[]{:S(2)}) %collective-permute-start.4) | collective-permute-done | bytes 186656 | tf_op jit(solution)/shard_map/ppermute | solution.py:221
  80.1 1.0 %fusion.5 = f32[108,864]{1,0:T(8,128)S(1)} fusion(bf16[864,864]{1,0:T(8,128)(2,1)S(1)} %get-tuple-element.16, f32[216,864]{1,0:T(8,128)S(1)} %slice_add_fusion, bf16[108,864]{1,0:T(8,128)(2,1)S(1)} %collective-permute-done.4), kind=kOutput, calls=%fused_computation.26 | convolution fusion | flops 483916032 | bytes 2523648 | tf_op jit(solution)/shard_map/dot_general | solution.py:224
  82.0 2.2 %collective-permute-start.7 = (bf16[108,1,216]{0,2,1:T(8,128)(2,1)S(1)}, bf16[108,1,216]{0,2,1:T(8,128)(2,1)S(1)}, u32[]{:S(2)}, u32[]{:S(2)}) collective-permute-start(bf16[108,1,216]{0,2,1:T(8,128)(2,1)S(1)} %bitcast.71), channel_id=1, source_target_pairs={{0,3},{1,2},{2,1},{3,0},{4,7},{5,6},{6,5},{7,4},{8,11},{9,10},{10,... | collective-permute-start | bytes 139976 | tf_op jit(solution)/shard_map/ppermute | solution.py:77
  84.3 1.8 %collective-permute-start.6 = (bf16[108,1,216]{0,2,1:T(8,128)(2,1)S(1)}, bf16[108,1,216]{0,2,1:T(8,128)(2,1)S(1)}, u32[]{:S(2)}, u32[]{:S(2)}) collective-permute-start(bf16[108,1,216]{0,2,1:T(8,128)(2,1)S(1)} %bitcast.72), channel_id=1, source_target_pairs={{0,2},{1,3},{2,0},{3,1},{4,6},{5,7},{6,4},{7,5},{8,10},{9,11},{10,... | collective-permute-start | bytes 139976 | tf_op jit(solution)/shard_map/ppermute | solution.py:77
  87.0 1.5 %collective-permute-done.7 = bf16[108,1,216]{0,2,1:T(8,128)(2,1)S(1)} collective-permute-done((bf16[108,1,216]{0,2,1:T(8,128)(2,1)S(1)}, bf16[108,1,216]{0,2,1:T(8,128)(2,1)S(1)}, u32[]{:S(2)}, u32[]{:S(2)}) %collective-permute-start.7) | collective-permute-done | bytes 46688 | tf_op jit(solution)/shard_map/ppermute | solution.py:77
  88.6 1.4 %collective-permute-done.6 = bf16[108,1,216]{0,2,1:T(8,128)(2,1)S(1)} collective-permute-done((bf16[108,1,216]{0,2,1:T(8,128)(2,1)S(1)}, bf16[108,1,216]{0,2,1:T(8,128)(2,1)S(1)}, u32[]{:S(2)}, u32[]{:S(2)}) %collective-permute-start.6) | collective-permute-done | bytes 46688 | tf_op jit(solution)/shard_map/ppermute | solution.py:77
  90.6 0.7 fusion.9
  (62 shorter events, 8.1 us)
Async XLA Ops:
  0.6 63.7 %copy-start = (f32[216,864]{1,0:T(8,128)S(1)}, f32[216,864]{1,0:T(8,128)}, u32[]{:S(2)}) copy-start(f32[216,864]{1,0:T(8,128)} %param.10) | copy-start | bytes 2239492
  1.8 12.7 %collective-permute-start.1 = (bf16[1,32,1,16,128]{4,1,3,2,0:T(8,128)(2,1)S(1)}, bf16[1,32,1,16,128]{4,1,3,2,0:T(8,128)(2,1)S(1)}, u32[]{:S(2)}, u32[]{:S(2)}) collective-permute-start(bf16[1,32,1,16,128]{4,1,3,2,0:T(8,128)(2,1)S(1)} %get-tuple-element.25), channel_id=1, source_target_pairs={{1,0},{2,1},{3,2},{5,4},{6,5},{7,6},{9,8},{10,9},{11,10},{13,12},{... | collective-permute-start | bytes 393224 | tf_op jit(solution)/shard_map/ppermute | solution.py:20
  3.1 11.4 %collective-permute-start = (bf16[1,32,1,16,128]{4,1,3,2,0:T(8,128)(2,1)S(1)}, bf16[1,32,1,16,128]{4,1,3,2,0:T(8,128)(2,1)S(1)}, u32[]{:S(2)}, u32[]{:S(2)}) collective-permute-start(bf16[1,32,1,16,128]{4,1,3,2,0:T(8,128)(2,1)S(1)} %get-tuple-element.24), channel_id=1, source_target_pairs={{0,1},{1,2},{2,3},{4,5},{5,6},{6,7},{8,9},{9,10},{10,11},{12,13},{... | collective-permute-start | bytes 393224 | tf_op jit(solution)/shard_map/ppermute | solution.py:18
  27.2 4.0 %copy-start.2 = (bf16[32,864]{1,0:T(8,128)(2,1)S(1)}, bf16[32,864]{1,0:T(8,128)(2,1)}, u32[]{:S(2)}) copy-start(bf16[32,864]{1,0:T(8,128)(2,1)} %param.8) | copy-start | bytes 165892
  27.3 5.1 %collective-permute-start.9 = (f32[32,896]{1,0:T(8,128)S(1)}, f32[32,896]{1,0:T(8,128)S(1)}, u32[]{:S(2)}, u32[]{:S(2)}) collective-permute-start(f32[32,896]{1,0:T(8,128)S(1)} %pad_maximum_fusion.1), channel_id=1, source_target_pairs={{0,8},{4,12},{8,0},{12,4},{16,24},{20,28},{24,16},{28,20},{1,9},{5... | collective-permute-start | bytes 344072 | tf_op jit(solution)/shard_map/ppermute | solution.py:39
  29.2 5.3 %collective-permute-start.10 = (f32[32,896]{1,0:T(8,128)S(1)}, f32[32,896]{1,0:T(8,128)S(1)}, u32[]{:S(2)}, u32[]{:S(2)}) collective-permute-start(f32[32,896]{1,0:T(8,128)S(1)} %pad_maximum_fusion.1), channel_id=1, source_target_pairs={{0,12},{4,8},{8,4},{12,0},{16,28},{20,24},{24,20},{28,16},{1,13},{... | collective-permute-start | bytes 344072 | tf_op jit(solution)/shard_map/ppermute | solution.py:40
  29.2 5.3 %collective-permute-start.8 = (f32[32,896]{1,0:T(8,128)S(1)}, f32[32,896]{1,0:T(8,128)S(1)}, u32[]{:S(2)}, u32[]{:S(2)}) collective-permute-start(f32[32,896]{1,0:T(8,128)S(1)} %pad_maximum_fusion.1), channel_id=1, source_target_pairs={{0,4},{4,0},{8,12},{12,8},{16,20},{20,16},{24,28},{28,24},{1,5},{5... | collective-permute-start | bytes 344072 | tf_op jit(solution)/shard_map/ppermute | solution.py:37
  34.5 15.1 %collective-permute-start.11 = (f32[32,896]{1,0:T(8,128)S(1)}, f32[32,896]{1,0:T(8,128)S(1)}, u32[]{:S(2)}, u32[]{:S(2)}) collective-permute-start(f32[32,896]{1,0:T(8,128)S(1)} %add_add_fusion.1), channel_id=1, source_target_pairs={{0,16},{4,20},{8,24},{12,28},{16,0},{20,4},{24,8},{28,12},{1,17},{... | collective-permute-start | bytes 344072 | tf_op jit(solution)/shard_map/ppermute | solution.py:37
  50.6 5.6 %collective-permute-start.12 = (f32[32,2,216]{2,1,0:T(2,128)S(1)}, f32[32,2,216]{2,1,0:T(2,128)S(1)}, u32[]{:S(2)}, u32[]{:S(2)}) collective-permute-start(f32[32,2,216]{2,1,0:T(2,128)S(1)} %bitcast.70), channel_id=1, source_target_pairs={{0,1},{1,0},{2,3},{3,2},{4,5},{5,4},{6,7},{7,6},{8,9},{9,8},{10,11... | collective-permute-start | bytes 165896 | tf_op jit(solution)/shard_map/ppermute | solution.py:58
  56.1 6.8 %collective-permute-start.2 = (bf16[432,864]{1,0:T(8,128)(2,1)S(1)}, bf16[432,864]{1,0:T(8,128)(2,1)S(1)}, u32[]{:S(2)}, u32[]{:S(2)}) collective-permute-start(bf16[432,864]{1,0:T(8,128)(2,1)S(1)} %slice.87), channel_id=1, source_target_pairs={{0,4},{4,0},{8,12},{12,8},{16,20},{20,16},{24,28},{28,24},{1,5},{5... | collective-permute-start | bytes 2239496 | tf_op jit(solution)/shard_map/ppermute | solution.py:221
  56.3 6.5 %collective-permute-start.13 = (f32[32,1,216]{2,1,0:T(1,128)S(1)}, f32[32,1,216]{2,1,0:T(1,128)S(1)}, u32[]{:S(2)}, u32[]{:S(2)}) collective-permute-start(f32[32,1,216]{2,1,0:T(1,128)S(1)} %constant_dynamic-slice_fusion), channel_id=1, source_target_pairs={{0,2},{1,3},{2,0},{3,1},{4,6},{5,7},{6,4},{7,5},{8,10},{9,11},{10,... | collective-permute-start | bytes 82952 | tf_op jit(solution)/shard_map/ppermute | solution.py:58
  62.0 2.2 %copy-start.3 = (f32[32,32]{1,0:T(8,128)S(1)}, f32[32,32]{1,0:T(8,128)}, u32[]{:S(2)}) copy-start(f32[32,32]{1,0:T(8,128)} %param.11) | copy-start | bytes 12292
  63.1 10.9 %collective-permute-start.3 = (bf16[216,864]{1,0:T(8,128)(2,1)S(1)}, bf16[216,864]{1,0:T(8,128)(2,1)S(1)}, u32[]{:S(2)}, u32[]{:S(2)}) collective-permute-start(bf16[216,864]{1,0:T(8,128)(2,1)S(1)} %slice.88), channel_id=1, source_target_pairs={{0,8},{4,12},{8,0},{12,4},{16,24},{20,28},{24,16},{28,20},{1,9},{5... | collective-permute-start | bytes 1119752 | tf_op jit(solution)/shard_map/ppermute | solution.py:221
  65.0 11.5 %collective-permute-start.15 = (f32[32,896]{1,0:T(8,128)S(1)}, f32[32,896]{1,0:T(8,128)S(1)}, u32[]{:S(2)}, u32[]{:S(2)}) collective-permute-start(f32[32,896]{1,0:T(8,128)S(1)} %pad_maximum_fusion.2), channel_id=1, source_target_pairs={{0,2},{1,3},{2,0},{3,1},{4,6},{5,7},{6,4},{7,5},{8,10},{9,11},{10,... | collective-permute-start | bytes 344072 | tf_op jit(solution)/shard_map/ppermute | solution.py:39
  66.6 10.0 %collective-permute-start.16 = (f32[32,896]{1,0:T(8,128)S(1)}, f32[32,896]{1,0:T(8,128)S(1)}, u32[]{:S(2)}, u32[]{:S(2)}) collective-permute-start(f32[32,896]{1,0:T(8,128)S(1)} %pad_maximum_fusion.2), channel_id=1, source_target_pairs={{0,3},{1,2},{2,1},{3,0},{4,7},{5,6},{6,5},{7,4},{8,11},{9,10},{10,... | collective-permute-start | bytes 344072 | tf_op jit(solution)/shard_map/ppermute | solution.py:40
  69.1 7.5 %collective-permute-start.14 = (f32[32,896]{1,0:T(8,128)S(1)}, f32[32,896]{1,0:T(8,128)S(1)}, u32[]{:S(2)}, u32[]{:S(2)}) collective-permute-start(f32[32,896]{1,0:T(8,128)S(1)} %pad_maximum_fusion.2), channel_id=1, source_target_pairs={{0,1},{1,0},{2,3},{3,2},{4,5},{5,4},{6,7},{7,6},{8,9},{9,8},{10,11... | collective-permute-start | bytes 344072 | tf_op jit(solution)/shard_map/ppermute | solution.py:37
  74.1 6.0 %collective-permute-start.4 = (bf16[108,864]{1,0:T(8,128)(2,1)S(1)}, bf16[108,864]{1,0:T(8,128)(2,1)S(1)}, u32[]{:S(2)}, u32[]{:S(2)}) collective-permute-start(bf16[108,864]{1,0:T(8,128)(2,1)S(1)} %slice.89), channel_id=1, source_target_pairs={{0,16},{4,20},{8,24},{12,28},{16,0},{20,4},{24,8},{28,12},{1,17},{... | collective-permute-start | bytes 559880 | tf_op jit(solution)/shard_map/ppermute | solution.py:221
  76.7 14.6 %copy-start.1 = (f32[32,896]{1,0:T(8,128)}, f32[32,896]{1,0:T(8,128)S(1)}, u32[]{:S(2)}) copy-start(f32[32,896]{1,0:T(8,128)S(1)} %add_add_fusion) | copy-start | bytes 344068
  82.0 6.6 %collective-permute-start.7 = (bf16[108,1,216]{0,2,1:T(8,128)(2,1)S(1)}, bf16[108,1,216]{0,2,1:T(8,128)(2,1)S(1)}, u32[]{:S(2)}, u32[]{:S(2)}) collective-permute-start(bf16[108,1,216]{0,2,1:T(8,128)(2,1)S(1)} %bitcast.71), channel_id=1, source_target_pairs={{0,3},{1,2},{2,1},{3,0},{4,7},{5,6},{6,5},{7,4},{8,11},{9,10},{10,... | collective-permute-start | bytes 139976 | tf_op jit(solution)/shard_map/ppermute | solution.py:77
  84.3 5.7 %collective-permute-start.6 = (bf16[108,1,216]{0,2,1:T(8,128)(2,1)S(1)}, bf16[108,1,216]{0,2,1:T(8,128)(2,1)S(1)}, u32[]{:S(2)}, u32[]{:S(2)}) collective-permute-start(bf16[108,1,216]{0,2,1:T(8,128)(2,1)S(1)} %bitcast.72), channel_id=1, source_target_pairs={{0,2},{1,3},{2,0},{3,1},{4,6},{5,7},{6,4},{7,5},{8,10},{9,11},{10,... | collective-permute-start | bytes 139976 | tf_op jit(solution)/shard_map/ppermute | solution.py:77
  86.2 4.4 %collective-permute-start.5 = (bf16[108,1,216]{0,2,1:T(8,128)(2,1)S(1)}, bf16[108,1,216]{0,2,1:T(8,128)(2,1)S(1)}, u32[]{:S(2)}, u32[]{:S(2)}) collective-permute-start(bf16[108,1,216]{0,2,1:T(8,128)(2,1)S(1)} %bitcast.73), channel_id=1, source_target_pairs={{0,1},{1,0},{2,3},{3,2},{4,5},{5,4},{6,7},{7,6},{8,9},{9,8},{10,11... | collective-permute-start | bytes 139976 | tf_op jit(solution)/shard_map/ppermute | solution.py:77

commit v16 on v15

--- a/solution.py
+++ b/solution.py
@@ -61,7 +61,7 @@
     return blocks
 
 
-def quad_scatter(blocks, axis, dim):
+def quad_scatter(blocks, axis, dim, wire=jnp.bfloat16):
     me = lax.axis_index(axis)
     low = 1
     while low < lax.axis_size(axis):
@@ -74,7 +74,7 @@
                 return lax.dynamic_index_in_dim(split, d, axis=dim + 1, keepdims=False)
 
             got = [
-                lax.ppermute(pick(digit ^ k).astype(jnp.bfloat16), axis, partner(axis, k * low)).astype(
+                lax.ppermute(pick(digit ^ k).astype(wire), axis, partner(axis, k * low)).astype(
                     jnp.float32
                 )
                 for k in (1, 2, 3)
@@ -86,7 +86,7 @@
             bit = (me // low) % 2
             keep = lax.dynamic_index_in_dim(split, bit, axis=dim + 1, keepdims=False)
             send = lax.dynamic_index_in_dim(split, 1 - bit, axis=dim + 1, keepdims=False)
-            got = lax.ppermute(send.astype(jnp.bfloat16), axis, partner(axis, low))
+            got = lax.ppermute(send.astype(wire), axis, partner(axis, low))
             blocks = keep + got.astype(jnp.float32)
             low *= 2
     return blocks
@@ -187,7 +187,7 @@
     grad_plane = (
         plane[:, :patch].reshape(channels, n_taps, channels).transpose(0, 2, 1).reshape(channels, patch)
     )
-    own_cols = halving_scatter(
+    own_cols = quad_scatter(
         grad_plane.reshape(channels, n_sp, patch // n_sp), "space", 1, wire=f32
     ).reshape(channels, patch // n_sp)
     left = jnp.dot(g_inverse, own_cols, precision=highest)

time: 91.7 us -> 85.5 us (0.932)
  matrix products: 29.7 us -> 22.1 us
  waiting for transfers between devices: 15.2 us -> 11.2 us
  starting transfers between devices: 24.1 us -> 26.5 us
  other arithmetic: 7.97 us -> 10.1 us
  local copies, waits for them, and re-layouts: 8.09 us -> 9.13 us
    dot_general x1, matrix products: 13.4 us -> 7.49 us  [on_device(): lax.dot_general(weighted, patches_t, contract_cells, preferred_element_ty...]
    ppermute x2, waiting for transfers between devices: 2.12 us -> 0.01 us  [butterfly_sum(): other = lax.ppermute(x, axis, partner(axis, low + high))]
    dot_general x1, matrix products: 3.78 us -> 1.92 us  [on_device(): a_rows = jnp.dot(placed, a_bf, preferred_element_type=f32)]
    ppermute x3, waiting for transfers between devices: 7.53 us -> 5.76 us  [on_device(): lax.ppermute(a_orig[half:].astype(jnp.bfloat16), 'dp', partner('dp', step))]
    ppermute x2, starting transfers between devices: 2.49 us -> 1.06 us  [butterfly_sum(): other = lax.ppermute(x, axis, partner(axis, low + high))]
    ppermute x5 -> x6, starting transfers between devices: 7.59 us -> 9.02 us  [quad_scatter(): lax.ppermute(pick(digit ^ k).astype(wire), axis, partner(axis, k * low))]
    add x2, other arithmetic: 0.21 us -> 1.38 us  [on_device(): a_orig = a_orig[:half] + got.astype(f32)]
    ppermute x3, starting transfers between devices: 1.9 us -> 2.99 us  [butterfly_sum(): got = lax.ppermute(x, axis, partner(axis, low))]
  transfers between devices with their start and end apart: 17 -> 18, of which waited for: 7 -> 7; matrix products, arithmetic and copies ran while one was open for 37% -> 31% of each run, Pallas kernels for 0% -> 0%
where the time goes in v16:
time: 85.5 us; the launch traced here: 85.2 us
  starting transfers between devices  26.5 us (31%)
  matrix products  22.1 us (26%)
  waiting for transfers between devices  11.2 us (13%)
  other arithmetic  10.1 us (12%)
  local copies, waits for them, and re-layouts  9.13 us (11%)
  Pallas kernels  5.16 us (6%)
  between operations  0.98 us (1%)
    ppermute x6, starting transfers between devices, quad_scatter(): lax.ppermute(pick(digit ^ k).astype(wire), axis, partner(axis, k * low))  9.02 us
    dot_general x1, matrix products, on_device(): lax.dot_general(weighted, patches_t, contract_cells, preferred_element_ty...  7.49 us
    ppermute x1, starting transfers between devices, padded_2(): lax.ppermute(tail, axis, [(i, (i + 1) % count) for i in range(ends)])  6.21 us
    ppermute x3, waiting for transfers between devices, on_device(): lax.ppermute(a_orig[half:].astype(jnp.bfloat16), 'dp', partner('dp', step))  5.76 us
    dot_general x1, matrix products, on_device(): lax.dot_general(grad_flat, patches_t, contract_cells, preferred_element_t...  5.27 us
    pallas_call x1, Pallas kernels, patch_matrix(): pl.pallas_call(body, grid=(3,), in_specs=[pl.BlockSpec(shifted.shape, lam...  5.16 us
    dot_general x1, matrix products, on_device(): forward = jnp.dot(kernel_perm, patches_t, preferred_element_type=f32)  4.33 us
    ppermute x2, starting transfers between devices, butterfly_sum(): pair = lax.ppermute(x, axis, partner(axis, high))  3.64 us
  transfers between devices with their start and end apart: 18, of which 7 were waited for; matrix products, arithmetic and copies ran while one was open for 31% of the time, Pallas kernels for 0%

profile of v16, /device:TPU:0, one launch (start us, length us, event | category | flops | bytes accessed | tf_op | source)
XLA Modules:
  0.0 85.2 jit_solution(3957617307674847957)
XLA Ops:
  0.7 1.1 %copy.30 = bf16[1,32,2,16,128]{4,1,3,2,0:T(8,128)(2,1)S(1)} copy(bf16[1,32,2,16,128]{4,3,2,1,0:T(8,128)(2,1)} %param.6) | data formatting | bytes 524288 | tf_op args[0]
  2.5 1.3 %collective-permute-start.1 = (bf16[1,32,1,16,128]{4,1,3,2,0:T(8,128)(2,1)}, bf16[1,32,1,16,128]{4,1,3,2,0:T(8,128)(2,1)}, u32[]{:S(2)}, u32[]{:S(2)}) collective-permute-start(bf16[1,32,1,16,128]{4,1,3,2,0:T(8,128)(2,1)} %get-tuple-element.25), channel_id=1, source_target_pairs={{1,0},{2,1},{3,2},{5,4},{6,5},{7,6},{9,8},{10,9},{11,10},{13,12},{... | collective-permute-start | bytes 393224 | tf_op jit(solution)/shard_map/ppermute | solution.py:20
  3.8 6.2 %collective-permute-start = (bf16[1,32,1,16,128]{4,1,3,2,0:T(8,128)(2,1)}, bf16[1,32,1,16,128]{4,1,3,2,0:T(8,128)(2,1)}, u32[]{:S(2)}, u32[]{:S(2)}) collective-permute-start(bf16[1,32,1,16,128]{4,1,3,2,0:T(8,128)(2,1)} %get-tuple-element.24), channel_id=1, source_target_pairs={{0,1},{1,2},{2,3},{4,5},{5,6},{6,7},{8,9},{9,10},{10,11},{12,13},{... | collective-permute-start | bytes 393224 | tf_op jit(solution)/shard_map/ppermute | solution.py:18
  10.1 3.4 %convert_reduce_fusion = f32[4096]{0:T(1024)S(1)} fusion(s32[1024]{0:T(1024)} %bitcast.78), kind=kLoop, calls=%fused_computation | loop fusion | flops 12578816 | bytes 20480 | tf_op jit(solution)/shard_map/reduce_sum | solution.py:201
  13.4 1.7 %fusion.2 = (bf16[864,864]{1,0:T(8,128)(2,1)S(1)}, bf16[864,864]{1,0:T(8,128)(2,1)}) fusion(s32[864]{0:T(1024)S(1)} %fusion.24, s32[864]{0:T(1024)S(1)} %fusion.27), kind=kLoop, calls=%fused_computation.9 | loop fusion | flops 2985984 | bytes 2992896 | tf_op jit(solution)/shard_map/convert_element_type | solution.py:135
  16.5 1.3 %convolution_bitcast_fusion.1 = f32[32,32]{1,0:T(8,128)S(1)} fusion(bf16[32,2,16,128]{3,2,1,0:T(8,128)(2,1)} %bitcast.72), kind=kOutput, calls=%fused_computation.17 | convolution fusion | flops 8388608 | bytes 266240 | tf_op jit(solution)/shard_map/dot_general | solution.py:183
  17.8 1.0 %maximum_bitcast_fusion = bf16[32,4,16,128]{3,0,2,1:T(8,128)(2,1)S(1)} fusion(bf16[1,32,1,16,128]{4,1,3,2,0:T(8,128)(2,1)} %collective-permute-done.1, bf16[1,32,2,16,128]{4,1,3,2,0:T(8,128)(2,1)S(1)} %copy.30, bf16[1,32,1,16,128]{4,1,3,2,0:T(8,128)(2,1)} %collective-permute-done), kind=kLoop, calls=%fused_computation.23 | loop fusion | flops 524288 | bytes 1048576 | tf_op jit(solution)/shard_map/squeeze | solution.py:176
  19.7 1.5 %pad_maximum_fusion.src_ref = bf16[3,4,18,32,128]{4,3,2,1,0:T(8,128)(2,1)} fusion(bf16[1,4,18,32,128]{4,3,2,1,0:T(8,128)(2,1)S(1)} %get-tuple-element.19, bf16[1,4,18,32,128]{4,3,2,1,0:T(8,128)(2,1)S(1)} %get-tuple-element.20, bf16[1,4,18,32,128]{4,3,2,1,0:T(8,128)(2,1)S(1)} %get-tuple-element.18), kind=kLoop, calls=%fused_computation.11 | loop fusion | flops 1769472 | bytes 3538944 | tf_op jit(solution)/shard_map/stack | solution.py:109
  21.2 5.2 %shard_map.93 = bf16[864,4096]{1,0:T(8,128)(2,1)} custom-call(bf16[3,4,18,32,128]{4,3,2,1,0:T(8,128)(2,1)} %pad_maximum_fusion.src_ref), custom_call_target="tpu_custom_call" | custom-call | tf_op jit(solution)/shard_map/pallas_call | solution.py:122
  26.3 5.3 %convolution_bitcast_fusion = f32[32,864]{1,0:T(8,128)S(1)} fusion(bf16[864,4096]{1,0:T(8,128)(2,1)} %shard_map.93, bf16[32,4096]{1,0:T(8,128)(2,1)S(1)} %reshape_squeeze.3), kind=kOutput, calls=%fused_computation.16 | convolution fusion | flops 226492416 | bytes 7450624 | tf_op jit(solution)/shard_map/dot_general | solution.py:182
  31.7 1.9 %collective-permute-start.9 = (f32[32,896]{1,0:T(8,128)S(1)}, f32[32,896]{1,0:T(8,128)S(1)}, u32[]{:S(2)}, u32[]{:S(2)}) collective-permute-start(f32[32,896]{1,0:T(8,128)S(1)} %pad_maximum_fusion.1), channel_id=1, source_target_pairs={{0,8},{4,12},{8,0},{12,4},{16,24},{20,28},{24,16},{28,20},{1,9},{5... | collective-permute-start | bytes 344072 | tf_op jit(solution)/shard_map/ppermute | solution.py:39
  33.9 7.5 %multiply_convert_fusion.2 = bf16[864,864]{1,0:T(8,128)(2,1)S(1)} fusion(bf16[864,4096]{1,0:T(8,128)(2,1)S(1)} %copy-done.1, f32[4096]{0:T(1024)S(1)} %convert_reduce_fusion), kind=kOutput, calls=%fused_computation.6 | convolution fusion | flops 6127405056 | bytes 8587264 | tf_op jit(solution)/shard_map/dot_general | solution.py:206
  41.4 2.0 %collective-permute-start.11 = (f32[32,896]{1,0:T(8,128)S(1)}, f32[32,896]{1,0:T(8,128)S(1)}, u32[]{:S(2)}, u32[]{:S(2)}) collective-permute-start(f32[32,896]{1,0:T(8,128)S(1)} %add_add_fusion.1), channel_id=1, source_target_pairs={{0,16},{4,20},{8,24},{12,28},{16,0},{20,4},{24,8},{28,12},{1,17},{... | collective-permute-start | bytes 344072 | tf_op jit(solution)/shard_map/ppermute | solution.py:37
  43.4 1.9 %fusion.32 = f32[864,864]{1,0:T(8,128)S(1)} fusion(bf16[864,864]{1,0:T(8,128)(2,1)S(1)} %copy-done.4, bf16[864,864]{1,0:T(8,128)(2,1)S(1)} %multiply_convert_fusion.2), kind=kOutput, calls=%fused_computation.81 | convolution fusion | flops 1289945088 | bytes 5971968 | tf_op jit(solution)/shard_map/dot_general | solution.py:214
  45.4 1.1 %slice.87 = bf16[432,864]{1,0:T(8,128)(2,1)} slice(f32[864,864]{1,0:T(8,128)S(1)} %fusion.32), slice={[432:864], [0:864]} | slice | bytes 1492992 | tf_op jit(solution)/shard_map/slice | solution.py:221
  48.1 1.0 %collective-permute-start.12 = (f32[32,1,216]{2,1,0:T(1,128)S(1)}, f32[32,1,216]{2,1,0:T(1,128)S(1)}, u32[]{:S(2)}, u32[]{:S(2)}) collective-permute-start(f32[32,1,216]{2,1,0:T(1,128)S(1)} %get-tuple-element.28), channel_id=1, source_target_pairs={{0,1},{1,0},{2,3},{3,2},{4,5},{5,4},{6,7},{7,6},{8,9},{9,8},{10,11... | collective-permute-start | bytes 82952 | tf_op jit(solution)/shard_map/ppermute | solution.py:77
  49.1 1.7 %collective-permute-start.13 = (f32[32,1,216]{2,1,0:T(1,128)S(1)}, f32[32,1,216]{2,1,0:T(1,128)S(1)}, u32[]{:S(2)}, u32[]{:S(2)}) collective-permute-start(f32[32,1,216]{2,1,0:T(1,128)S(1)} %get-tuple-element.27), channel_id=1, source_target_pairs={{0,2},{1,3},{2,0},{3,1},{4,6},{5,7},{6,4},{7,5},{8,10},{9,11},{10,... | collective-permute-start | bytes 82952 | tf_op jit(solution)/shard_map/ppermute | solution.py:77
  50.8 1.7 %collective-permute-start.14 = (f32[32,1,216]{2,1,0:T(1,128)S(1)}, f32[32,1,216]{2,1,0:T(1,128)S(1)}, u32[]{:S(2)}, u32[]{:S(2)}) collective-permute-start(f32[32,1,216]{2,1,0:T(1,128)S(1)} %get-tuple-element.26), channel_id=1, source_target_pairs={{0,3},{1,2},{2,1},{3,0},{4,7},{5,6},{6,5},{7,4},{8,11},{9,10},{10,... | collective-permute-start | bytes 82952 | tf_op jit(solution)/shard_map/ppermute | solution.py:77
  52.5 4.3 %fusion.4 = bf16[4,8,32,128]{3,1,2,0:T(8,128)(2,1)S(1)} fusion(bf16[32,864]{1,0:T(8,128)(2,1)S(1)} %reshape.136, bf16[864,4096]{1,0:T(8,128)(2,1)} %shard_map.93), kind=kOutput, calls=%fused_computation.15 | convolution fusion | flops 226623488 | bytes 7395328 | tf_op jit(solution)/shard_map/dot_general | solution.py:216
  57.8 1.3 %convert_add_fusion = f32[432,864]{1,0:T(8,128)S(1)} fusion(bf16[432,864]{1,0:T(8,128)(2,1)} %collective-permute-done.2, f32[864,864]{1,0:T(8,128)S(1)} %copy-done.3), kind=kLoop, calls=%fused_computation.13 | loop fusion | flops 746496 | bytes 3732480 | tf_op jit(solution)/shard_map/add | solution.py:222
  59.1 1.6 %collective-permute-start.3 = (bf16[216,864]{1,0:T(8,128)(2,1)S(1)}, bf16[216,864]{1,0:T(8,128)(2,1)S(1)}, u32[]{:S(2)}, u32[]{:S(2)}) collective-permute-start(bf16[216,864]{1,0:T(8,128)(2,1)S(1)} %slice.88), channel_id=1, source_target_pairs={{0,8},{4,12},{8,0},{12,4},{16,24},{20,28},{24,16},{28,20},{1,9},{5... | collective-permute-start | bytes 1119752 | tf_op jit(solution)/shard_map/ppermute | solution.py:221
  61.6 1.7 %collective-permute-start.16 = (f32[32,896]{1,0:T(8,128)S(1)}, f32[32,896]{1,0:T(8,128)S(1)}, u32[]{:S(2)}, u32[]{:S(2)}) collective-permute-start(f32[32,896]{1,0:T(8,128)S(1)} %pad_maximum_fusion.2), channel_id=1, source_target_pairs={{0,2},{1,3},{2,0},{3,1},{4,6},{5,7},{6,4},{7,5},{8,10},{9,11},{10,... | collective-permute-start | bytes 344072 | tf_op jit(solution)/shard_map/ppermute | solution.py:39
  63.3 1.1 %collective-permute-start.17 = (f32[32,896]{1,0:T(8,128)S(1)}, f32[32,896]{1,0:T(8,128)S(1)}, u32[]{:S(2)}, u32[]{:S(2)}) collective-permute-start(f32[32,896]{1,0:T(8,128)S(1)} %pad_maximum_fusion.2), channel_id=1, source_target_pairs={{0,3},{1,2},{2,1},{3,0},{4,7},{5,6},{6,5},{7,4},{8,11},{9,10},{10,... | collective-permute-start | bytes 344072 | tf_op jit(solution)/shard_map/ppermute | solution.py:40
  64.3 0.8 collective-permute-start.15
  65.1 3.9 %collective-permute-done.3 = bf16[216,864]{1,0:T(8,128)(2,1)S(1)} collective-permute-done((bf16[216,864]{1,0:T(8,128)(2,1)S(1)}, bf16[216,864]{1,0:T(8,128)(2,1)S(1)}, u32[]{:S(2)}, u32[]{:S(2)}) %collective-permute-start.3) | collective-permute-done | bytes 373280 | tf_op jit(solution)/shard_map/ppermute | solution.py:221
  69.9 2.3 %collective-permute-done.16 = f32[32,896]{1,0:T(8,128)S(1)} collective-permute-done((f32[32,896]{1,0:T(8,128)S(1)}, f32[32,896]{1,0:T(8,128)S(1)}, u32[]{:S(2)}, u32[]{:S(2)}) %collective-permute-start.16) | collective-permute-done | bytes 114720 | tf_op jit(solution)/shard_map/ppermute | solution.py:39
  73.0 1.9 %collective-permute-done.4 = bf16[108,864]{1,0:T(8,128)(2,1)S(1)} collective-permute-done((bf16[108,864]{1,0:T(8,128)(2,1)S(1)}, bf16[108,864]{1,0:T(8,128)(2,1)S(1)}, u32[]{:S(2)}, u32[]{:S(2)}) %collective-permute-start.4) | collective-permute-done | bytes 186656 | tf_op jit(solution)/shard_map/ppermute | solution.py:221
  74.9 1.1 %fusion.5 = f32[108,864]{1,0:T(8,128)S(1)} fusion(bf16[864,864]{1,0:T(8,128)(2,1)S(1)} %get-tuple-element.16, f32[216,864]{1,0:T(8,128)S(1)} %slice_add_fusion, bf16[108,864]{1,0:T(8,128)(2,1)S(1)} %collective-permute-done.4), kind=kOutput, calls=%fused_computation.26 | convolution fusion | flops 483916032 | bytes 2523648 | tf_op jit(solution)/shard_map/dot_general | solution.py:224
  76.8 2.4 %collective-permute-start.7 = (bf16[108,1,216]{0,2,1:T(8,128)(2,1)S(1)}, bf16[108,1,216]{0,2,1:T(8,128)(2,1)S(1)}, u32[]{:S(2)}, u32[]{:S(2)}) collective-permute-start(bf16[108,1,216]{0,2,1:T(8,128)(2,1)S(1)} %bitcast.75), channel_id=1, source_target_pairs={{0,3},{1,2},{2,1},{3,0},{4,7},{5,6},{6,5},{7,4},{8,11},{9,10},{10,... | collective-permute-start | bytes 139976 | tf_op jit(solution)/shard_map/ppermute | solution.py:77
  79.6 2.0 %collective-permute-start.5 = (bf16[108,1,216]{0,2,1:T(8,128)(2,1)S(1)}, bf16[108,1,216]{0,2,1:T(8,128)(2,1)S(1)}, u32[]{:S(2)}, u32[]{:S(2)}) collective-permute-start(bf16[108,1,216]{0,2,1:T(8,128)(2,1)S(1)} %bitcast.77), channel_id=1, source_target_pairs={{0,1},{1,0},{2,3},{3,2},{4,5},{5,4},{6,7},{7,6},{8,9},{9,8},{10,11... | collective-permute-start | bytes 139976 | tf_op jit(solution)/shard_map/ppermute | solution.py:77
  81.9 1.0 %collective-permute-done.7 = bf16[108,1,216]{0,2,1:T(8,128)(2,1)S(1)} collective-permute-done((bf16[108,1,216]{0,2,1:T(8,128)(2,1)S(1)}, bf16[108,1,216]{0,2,1:T(8,128)(2,1)S(1)}, u32[]{:S(2)}, u32[]{:S(2)}) %collective-permute-start.7) | collective-permute-done | bytes 46688 | tf_op jit(solution)/shard_map/ppermute | solution.py:77
  82.8 1.7 %collective-permute-done.6 = bf16[108,1,216]{0,2,1:T(8,128)(2,1)S(1)} collective-permute-done((bf16[108,1,216]{0,2,1:T(8,128)(2,1)S(1)}, bf16[108,1,216]{0,2,1:T(8,128)(2,1)S(1)}, u32[]{:S(2)}, u32[]{:S(2)}) %collective-permute-start.6) | collective-permute-done | bytes 46688 | tf_op jit(solution)/shard_map/ppermute | solution.py:77
  (71 shorter events, 10.4 us)
Async XLA Ops:
  0.6 60.2 %copy-start = (f32[216,864]{1,0:T(8,128)S(1)}, f32[216,864]{1,0:T(8,128)}, u32[]{:S(2)}) copy-start(f32[216,864]{1,0:T(8,128)} %param.10) | copy-start | bytes 2239492
  0.6 14.5 %copy-start.5 = (bf16[1,32,2,16,128]{4,3,2,1,0:T(8,128)(2,1)S(1)}, bf16[1,32,2,16,128]{4,3,2,1,0:T(8,128)(2,1)}, u32[]{:S(2)}) copy-start(bf16[1,32,2,16,128]{4,3,2,1,0:T(8,128)(2,1)} %param.7) | copy-start | bytes 786436
  0.7 14.6 %copy-start.7 = (bf16[32,864]{1,0:T(8,128)(2,1)S(1)}, bf16[32,864]{1,0:T(8,128)(2,1)}, u32[]{:S(2)}) copy-start(bf16[32,864]{1,0:T(8,128)(2,1)} %param.8) | copy-start | bytes 165892
  2.5 15.3 %collective-permute-start.1 = (bf16[1,32,1,16,128]{4,1,3,2,0:T(8,128)(2,1)}, bf16[1,32,1,16,128]{4,1,3,2,0:T(8,128)(2,1)}, u32[]{:S(2)}, u32[]{:S(2)}) collective-permute-start(bf16[1,32,1,16,128]{4,1,3,2,0:T(8,128)(2,1)} %get-tuple-element.25), channel_id=1, source_target_pairs={{1,0},{2,1},{3,2},{5,4},{6,5},{7,6},{9,8},{10,9},{11,10},{13,12},{... | collective-permute-start | bytes 393224 | tf_op jit(solution)/shard_map/ppermute | solution.py:20
  3.8 14.0 %collective-permute-start = (bf16[1,32,1,16,128]{4,1,3,2,0:T(8,128)(2,1)}, bf16[1,32,1,16,128]{4,1,3,2,0:T(8,128)(2,1)}, u32[]{:S(2)}, u32[]{:S(2)}) collective-permute-start(bf16[1,32,1,16,128]{4,1,3,2,0:T(8,128)(2,1)} %get-tuple-element.24), channel_id=1, source_target_pairs={{0,1},{1,2},{2,3},{4,5},{5,6},{6,7},{8,9},{9,10},{10,11},{12,13},{... | collective-permute-start | bytes 393224 | tf_op jit(solution)/shard_map/ppermute | solution.py:18
  26.3 7.5 %copy-start.1 = (bf16[864,4096]{1,0:T(8,128)(2,1)S(1)}, bf16[864,4096]{1,0:T(8,128)(2,1)}, u32[]{:S(2)}) copy-start(bf16[864,4096]{1,0:T(8,128)(2,1)} %shard_map.93) | copy-start | bytes 21233668
  31.7 11.8 %copy-start.4 = (bf16[864,864]{1,0:T(8,128)(2,1)S(1)}, bf16[864,864]{1,0:T(8,128)(2,1)}, u32[]{:S(2)}) copy-start(bf16[864,864]{1,0:T(8,128)(2,1)} %get-tuple-element.12) | copy-start | bytes 4478980
  31.7 9.7 %collective-permute-start.9 = (f32[32,896]{1,0:T(8,128)S(1)}, f32[32,896]{1,0:T(8,128)S(1)}, u32[]{:S(2)}, u32[]{:S(2)}) collective-permute-start(f32[32,896]{1,0:T(8,128)S(1)} %pad_maximum_fusion.1), channel_id=1, source_target_pairs={{0,8},{4,12},{8,0},{12,4},{16,24},{20,28},{24,16},{28,20},{1,9},{5... | collective-permute-start | bytes 344072 | tf_op jit(solution)/shard_map/ppermute | solution.py:39
  33.6 7.7 %collective-permute-start.10 = (f32[32,896]{1,0:T(8,128)S(1)}, f32[32,896]{1,0:T(8,128)S(1)}, u32[]{:S(2)}, u32[]{:S(2)}) collective-permute-start(f32[32,896]{1,0:T(8,128)S(1)} %pad_maximum_fusion.1), channel_id=1, source_target_pairs={{0,12},{4,8},{8,4},{12,0},{16,28},{20,24},{24,20},{28,16},{1,13},{... | collective-permute-start | bytes 344072 | tf_op jit(solution)/shard_map/ppermute | solution.py:40
  33.6 7.7 %collective-permute-start.8 = (f32[32,896]{1,0:T(8,128)S(1)}, f32[32,896]{1,0:T(8,128)S(1)}, u32[]{:S(2)}, u32[]{:S(2)}) collective-permute-start(f32[32,896]{1,0:T(8,128)S(1)} %pad_maximum_fusion.1), channel_id=1, source_target_pairs={{0,4},{4,0},{8,12},{12,8},{16,20},{20,16},{24,28},{28,24},{1,5},{5... | collective-permute-start | bytes 344072 | tf_op jit(solution)/shard_map/ppermute | solution.py:37
  41.4 5.4 %collective-permute-start.11 = (f32[32,896]{1,0:T(8,128)S(1)}, f32[32,896]{1,0:T(8,128)S(1)}, u32[]{:S(2)}, u32[]{:S(2)}) collective-permute-start(f32[32,896]{1,0:T(8,128)S(1)} %add_add_fusion.1), channel_id=1, source_target_pairs={{0,16},{4,20},{8,24},{12,28},{16,0},{20,4},{24,8},{28,12},{1,17},{... | collective-permute-start | bytes 344072 | tf_op jit(solution)/shard_map/ppermute | solution.py:37
  45.4 1.9 %copy-start.2 = (f32[864,864]{1,0:T(8,128)}, f32[864,864]{1,0:T(8,128)S(1)}, u32[]{:S(2)}) copy-start(f32[864,864]{1,0:T(8,128)S(1)} %fusion.32) | copy-start | bytes 8957956
  46.4 11.3 %collective-permute-start.2 = (bf16[432,864]{1,0:T(8,128)(2,1)}, bf16[432,864]{1,0:T(8,128)(2,1)}, u32[]{:S(2)}, u32[]{:S(2)}) collective-permute-start(bf16[432,864]{1,0:T(8,128)(2,1)} %slice.87), channel_id=1, source_target_pairs={{0,4},{4,0},{8,12},{12,8},{16,20},{20,16},{24,28},{28,24},{1,5},{5... | collective-permute-start | bytes 2239496 | tf_op jit(solution)/shard_map/ppermute | solution.py:221
  48.1 9.6 %collective-permute-start.12 = (f32[32,1,216]{2,1,0:T(1,128)S(1)}, f32[32,1,216]{2,1,0:T(1,128)S(1)}, u32[]{:S(2)}, u32[]{:S(2)}) collective-permute-start(f32[32,1,216]{2,1,0:T(1,128)S(1)} %get-tuple-element.28), channel_id=1, source_target_pairs={{0,1},{1,0},{2,3},{3,2},{4,5},{5,4},{6,7},{7,6},{8,9},{9,8},{10,11... | collective-permute-start | bytes 82952 | tf_op jit(solution)/shard_map/ppermute | solution.py:77
  49.1 8.6 %collective-permute-start.13 = (f32[32,1,216]{2,1,0:T(1,128)S(1)}, f32[32,1,216]{2,1,0:T(1,128)S(1)}, u32[]{:S(2)}, u32[]{:S(2)}) collective-permute-start(f32[32,1,216]{2,1,0:T(1,128)S(1)} %get-tuple-element.27), channel_id=1, source_target_pairs={{0,2},{1,3},{2,0},{3,1},{4,6},{5,7},{6,4},{7,5},{8,10},{9,11},{10,... | collective-permute-start | bytes 82952 | tf_op jit(solution)/shard_map/ppermute | solution.py:77
  50.8 7.0 %copy-start.3 = (f32[864,864]{1,0:T(8,128)S(1)}, f32[864,864]{1,0:T(8,128)}, u32[]{:S(2)}) copy-start(f32[864,864]{1,0:T(8,128)} %copy-done.2) | copy-start | bytes 8957956
  50.8 6.9 %collective-permute-start.14 = (f32[32,1,216]{2,1,0:T(1,128)S(1)}, f32[32,1,216]{2,1,0:T(1,128)S(1)}, u32[]{:S(2)}, u32[]{:S(2)}) collective-permute-start(f32[32,1,216]{2,1,0:T(1,128)S(1)} %get-tuple-element.26), channel_id=1, source_target_pairs={{0,3},{1,2},{2,1},{3,0},{4,7},{5,6},{6,5},{7,4},{8,11},{9,10},{10,... | collective-permute-start | bytes 82952 | tf_op jit(solution)/shard_map/ppermute | solution.py:77
  56.8 3.9 %copy-start.8 = (f32[32,32]{1,0:T(8,128)S(1)}, f32[32,32]{1,0:T(8,128)}, u32[]{:S(2)}) copy-start(f32[32,32]{1,0:T(8,128)} %param.11) | copy-start | bytes 12292
  59.1 9.8 %collective-permute-start.3 = (bf16[216,864]{1,0:T(8,128)(2,1)S(1)}, bf16[216,864]{1,0:T(8,128)(2,1)S(1)}, u32[]{:S(2)}, u32[]{:S(2)}) collective-permute-start(bf16[216,864]{1,0:T(8,128)(2,1)S(1)} %slice.88), channel_id=1, source_target_pairs={{0,8},{4,12},{8,0},{12,4},{16,24},{20,28},{24,16},{28,20},{1,9},{5... | collective-permute-start | bytes 1119752 | tf_op jit(solution)/shard_map/ppermute | solution.py:221
  61.6 10.6 %collective-permute-start.16 = (f32[32,896]{1,0:T(8,128)S(1)}, f32[32,896]{1,0:T(8,128)S(1)}, u32[]{:S(2)}, u32[]{:S(2)}) collective-permute-start(f32[32,896]{1,0:T(8,128)S(1)} %pad_maximum_fusion.2), channel_id=1, source_target_pairs={{0,2},{1,3},{2,0},{3,1},{4,6},{5,7},{6,4},{7,5},{8,10},{9,11},{10,... | collective-permute-start | bytes 344072 | tf_op jit(solution)/shard_map/ppermute | solution.py:39
  63.3 8.9 %collective-permute-start.17 = (f32[32,896]{1,0:T(8,128)S(1)}, f32[32,896]{1,0:T(8,128)S(1)}, u32[]{:S(2)}, u32[]{:S(2)}) collective-permute-start(f32[32,896]{1,0:T(8,128)S(1)} %pad_maximum_fusion.2), channel_id=1, source_target_pairs={{0,3},{1,2},{2,1},{3,0},{4,7},{5,6},{6,5},{7,4},{8,11},{9,10},{10,... | collective-permute-start | bytes 344072 | tf_op jit(solution)/shard_map/ppermute | solution.py:40
  64.3 8.0 %collective-permute-start.15 = (f32[32,896]{1,0:T(8,128)S(1)}, f32[32,896]{1,0:T(8,128)S(1)}, u32[]{:S(2)}, u32[]{:S(2)}) collective-permute-start(f32[32,896]{1,0:T(8,128)S(1)} %pad_maximum_fusion.2), channel_id=1, source_target_pairs={{0,1},{1,0},{2,3},{3,2},{4,5},{5,4},{6,7},{7,6},{8,9},{9,8},{10,11... | collective-permute-start | bytes 344072 | tf_op jit(solution)/shard_map/ppermute | solution.py:37
  69.1 5.8 %collective-permute-start.4 = (bf16[108,864]{1,0:T(8,128)(2,1)S(1)}, bf16[108,864]{1,0:T(8,128)(2,1)S(1)}, u32[]{:S(2)}, u32[]{:S(2)}) collective-permute-start(bf16[108,864]{1,0:T(8,128)(2,1)S(1)} %slice.89), channel_id=1, source_target_pairs={{0,16},{4,20},{8,24},{12,28},{16,0},{20,4},{24,8},{28,12},{1,17},{... | collective-permute-start | bytes 559880 | tf_op jit(solution)/shard_map/ppermute | solution.py:221
  72.4 12.8 %copy-start.6 = (f32[32,896]{1,0:T(8,128)}, f32[32,896]{1,0:T(8,128)S(1)}, u32[]{:S(2)}) copy-start(f32[32,896]{1,0:T(8,128)S(1)} %add_add_fusion) | copy-start | bytes 344068
  76.8 6.0 %collective-permute-start.7 = (bf16[108,1,216]{0,2,1:T(8,128)(2,1)S(1)}, bf16[108,1,216]{0,2,1:T(8,128)(2,1)S(1)}, u32[]{:S(2)}, u32[]{:S(2)}) collective-permute-start(bf16[108,1,216]{0,2,1:T(8,128)(2,1)S(1)} %bitcast.75), channel_id=1, source_target_pairs={{0,3},{1,2},{2,1},{3,0},{4,7},{5,6},{6,5},{7,4},{8,11},{9,10},{10,... | collective-permute-start | bytes 139976 | tf_op jit(solution)/shard_map/ppermute | solution.py:77
  79.4 5.1 %collective-permute-start.6 = (bf16[108,1,216]{0,2,1:T(8,128)(2,1)S(1)}, bf16[108,1,216]{0,2,1:T(8,128)(2,1)S(1)}, u32[]{:S(2)}, u32[]{:S(2)}) collective-permute-start(bf16[108,1,216]{0,2,1:T(8,128)(2,1)S(1)} %bitcast.76), channel_id=1, source_target_pairs={{0,2},{1,3},{2,0},{3,1},{4,6},{5,7},{6,4},{7,5},{8,10},{9,11},{10,... | collective-permute-start | bytes 139976 | tf_op jit(solution)/shard_map/ppermute | solution.py:77
  79.6 4.9 %collective-permute-start.5 = (bf16[108,1,216]{0,2,1:T(8,128)(2,1)S(1)}, bf16[108,1,216]{0,2,1:T(8,128)(2,1)S(1)}, u32[]{:S(2)}, u32[]{:S(2)}) collective-permute-start(bf16[108,1,216]{0,2,1:T(8,128)(2,1)S(1)} %bitcast.77), channel_id=1, source_target_pairs={{0,1},{1,0},{2,3},{3,2},{4,5},{5,4},{6,7},{7,6},{8,9},{9,8},{10,11... | collective-permute-start | bytes 139976 | tf_op jit(solution)/shard_map/ppermute | solution.py:77

commit v17 on v16

--- a/solution.py
+++ b/solution.py
@@ -216,6 +216,18 @@
     forward = jnp.dot(kernel_perm, patches_t, preferred_element_type=f32)
     conv_out = forward.astype(jnp.bfloat16).reshape(1, channels, planes, y_cells, x_cells)
     step = 1
+    if n_dp >= 4:
+        quarter = a_orig.shape[0] // 4
+        got = [
+            lax.ppermute(
+                a_orig[((s & 1) * 2 + (s >> 1)) * quarter :][:quarter].astype(jnp.bfloat16),
+                "dp",
+                partner("dp", s),
+            ).astype(f32)
+            for s in (1, 2, 3)
+        ]
+        a_orig = (a_orig[:quarter] + got[0]) + (got[1] + got[2])
+        step = 4
     while step < n_dp:
         half = a_orig.shape[0] // 2
         got = lax.ppermute(a_orig[half:].astype(jnp.bfloat16), "dp", partner("dp", step))

time: 85.5 us -> 95.8 us (1.12)
  waiting for transfers between devices: 11.2 us -> 21 us
  matrix products: 22.1 us -> 19.8 us
  other arithmetic: 10.1 us -> 11.3 us
    ppermute x0 -> x3, waiting for transfers between devices: none -> 13.4 us  [on_device(): lax.ppermute(a_orig[((s & 1) * 2 + (s >> 1)) * quarter:][:quarter].astype...]
    ppermute x2, waiting for transfers between devices: 2.32 us -> 0.01 us  [butterfly_sum(): pair = lax.ppermute(x, axis, partner(axis, high))]
    dot_general x1, matrix products: 4.33 us -> 2.04 us  [on_device(): forward = jnp.dot(kernel_perm, patches_t, preferred_element_type=f32)]
    ppermute x0 -> x3, starting transfers between devices: none -> 1.86 us  [on_device(): lax.ppermute(a_orig[((s & 1) * 2 + (s >> 1)) * quarter:][:quarter].astype...]
    another operation x0 -> x1, other arithmetic: none -> 1.34 us
    slice x0 -> x1, local copies, waits for them, and re-layouts: none -> 1.32 us  [on_device(): a_orig[((s & 1) * 2 + (s >> 1)) * quarter:][:quarter].astype(jnp.bfloat16)]
    ppermute x3 -> x1, waiting for transfers between devices: 5.76 us -> 4.45 us  [on_device(): lax.ppermute(a_orig[half:].astype(jnp.bfloat16), 'dp', partner('dp', step))]
    slice x3 -> x1, local copies, waits for them, and re-layouts: 1.14 us -> 0.04 us  [on_device(): a_orig[half:].astype(jnp.bfloat16)]
  transfers between devices with their start and end apart: 18 -> 19, of which waited for: 7 -> 6; matrix products, arithmetic and copies ran while one was open for 31% -> 28% of each run, Pallas kernels for 0% -> 0%
where the time goes in v17:
time: 95.8 us; the launch traced here: 95.4 us
  starting transfers between devices  27.4 us (29%)
  waiting for transfers between devices  21 us (22%)
  matrix products  19.8 us (21%)
  other arithmetic  11.3 us (12%)
  local copies, waits for them, and re-layouts  9.68 us (10%)
  Pallas kernels  5.17 us (5%)
    ppermute x3, waiting for transfers between devices, on_device(): lax.ppermute(a_orig[((s & 1) * 2 + (s >> 1)) * quarter:][:quarter].astype...  13.4 us
    ppermute x6, starting transfers between devices, quad_scatter(): lax.ppermute(pick(digit ^ k).astype(wire), axis, partner(axis, k * low))  9.02 us
    dot_general x1, matrix products, on_device(): lax.dot_general(weighted, patches_t, contract_cells, preferred_element_ty...  7.5 us
    ppermute x1, starting transfers between devices, padded_2(): lax.ppermute(tail, axis, [(i, (i + 1) % count) for i in range(ends)])  6.21 us
    dot_general x1, matrix products, on_device(): lax.dot_general(grad_flat, patches_t, contract_cells, preferred_element_t...  5.27 us
    pallas_call x1, Pallas kernels, patch_matrix(): pl.pallas_call(body, grid=(3,), in_specs=[pl.BlockSpec(shifted.shape, lam...  5.17 us
    ppermute x1, waiting for transfers between devices, on_device(): lax.ppermute(a_orig[half:].astype(jnp.bfloat16), 'dp', partner('dp', step))  4.45 us
    ppermute x2, starting transfers between devices, butterfly_sum(): pair = lax.ppermute(x, axis, partner(axis, high))  3.68 us
  transfers between devices with their start and end apart: 19, of which 6 were waited for; matrix products, arithmetic and copies ran while one was open for 28% of the time, Pallas kernels for 0%

profile of v17, /device:TPU:0, one launch (start us, length us, event | category | flops | bytes accessed | tf_op | source)
XLA Modules:
  0.0 95.4 jit_solution(10644725082114593229)
XLA Ops:
  0.7 1.1 %copy.30 = bf16[1,32,2,16,128]{4,1,3,2,0:T(8,128)(2,1)S(1)} copy(bf16[1,32,2,16,128]{4,3,2,1,0:T(8,128)(2,1)} %param.6) | data formatting | bytes 524288 | tf_op args[0]
  2.5 1.3 %collective-permute-start.1 = (bf16[1,32,1,16,128]{4,1,3,2,0:T(8,128)(2,1)}, bf16[1,32,1,16,128]{4,1,3,2,0:T(8,128)(2,1)}, u32[]{:S(2)}, u32[]{:S(2)}) collective-permute-start(bf16[1,32,1,16,128]{4,1,3,2,0:T(8,128)(2,1)} %get-tuple-element.28), channel_id=1, source_target_pairs={{1,0},{2,1},{3,2},{5,4},{6,5},{7,6},{9,8},{10,9},{11,10},{13,12},{... | collective-permute-start | bytes 393224 | tf_op jit(solution)/shard_map/ppermute | solution.py:20
  3.8 6.2 %collective-permute-start = (bf16[1,32,1,16,128]{4,1,3,2,0:T(8,128)(2,1)S(1)}, bf16[1,32,1,16,128]{4,1,3,2,0:T(8,128)(2,1)}, u32[]{:S(2)}, u32[]{:S(2)}) collective-permute-start(bf16[1,32,1,16,128]{4,1,3,2,0:T(8,128)(2,1)S(1)} %get-tuple-element.27), channel_id=1, source_target_pairs={{0,1},{1,2},{2,3},{4,5},{5,6},{6,7},{8,9},{9,10},{10,11},{12,13},{... | collective-permute-start | bytes 393224 | tf_op jit(solution)/shard_map/ppermute | solution.py:18
  10.0 3.4 %convert_reduce_fusion = f32[4096]{0:T(1024)S(1)} fusion(s32[1024]{0:T(1024)} %bitcast.78), kind=kLoop, calls=%fused_computation | loop fusion | flops 12578816 | bytes 20480 | tf_op jit(solution)/shard_map/reduce_sum | solution.py:201
  13.4 1.7 %fusion.2 = (bf16[864,864]{1,0:T(8,128)(2,1)S(1)}, bf16[864,864]{1,0:T(8,128)(2,1)}) fusion(s32[864]{0:T(1024)S(1)} %fusion.24, s32[864]{0:T(1024)S(1)} %fusion.27), kind=kLoop, calls=%fused_computation.9 | loop fusion | flops 2985984 | bytes 2992896 | tf_op jit(solution)/shard_map/convert_element_type | solution.py:135
  15.2 1.4 %reshape.135 = bf16[32,32,27]{2,1,0:T(8,128)(2,1)S(1)} reshape(bf16[32,864]{1,0:T(8,128)(2,1)} %param.8) | data formatting | bytes 110592 | tf_op jit(solution)/shard_map/reshape | solution.py:180
  17.3 1.3 %convolution_bitcast_fusion.1 = f32[32,32]{1,0:T(8,128)S(1)} fusion(bf16[32,2,16,128]{3,2,1,0:T(8,128)(2,1)} %bitcast.72), kind=kOutput, calls=%fused_computation.15 | convolution fusion | flops 8388608 | bytes 266240 | tf_op jit(solution)/shard_map/dot_general | solution.py:183
  18.6 1.0 %maximum_bitcast_fusion = bf16[32,4,16,128]{3,0,2,1:T(8,128)(2,1)S(1)} fusion(bf16[1,32,1,16,128]{4,1,3,2,0:T(8,128)(2,1)} %collective-permute-done.1, bf16[1,32,2,16,128]{4,1,3,2,0:T(8,128)(2,1)S(1)} %copy.30, bf16[1,32,1,16,128]{4,1,3,2,0:T(8,128)(2,1)} %collective-permute-done), kind=kLoop, calls=%fused_computation.20 | loop fusion | flops 524288 | bytes 1048576 | tf_op jit(solution)/shard_map/squeeze | solution.py:176
  20.5 1.5 %pad_maximum_fusion.src_ref = bf16[3,4,18,32,128]{4,3,2,1,0:T(8,128)(2,1)} fusion(bf16[1,4,18,32,128]{4,3,2,1,0:T(8,128)(2,1)S(1)} %get-tuple-element.22, bf16[1,4,18,32,128]{4,3,2,1,0:T(8,128)(2,1)S(1)} %get-tuple-element.23, bf16[1,4,18,32,128]{4,3,2,1,0:T(8,128)(2,1)S(1)} %get-tuple-element.21), kind=kLoop, calls=%fused_computation.11 | loop fusion | flops 1769472 | bytes 3538944 | tf_op jit(solution)/shard_map/stack | solution.py:109
  21.9 5.2 %shard_map.93 = bf16[864,4096]{1,0:T(8,128)(2,1)} custom-call(bf16[3,4,18,32,128]{4,3,2,1,0:T(8,128)(2,1)} %pad_maximum_fusion.src_ref), custom_call_target="tpu_custom_call" | custom-call | tf_op jit(solution)/shard_map/pallas_call | solution.py:122
  27.1 5.3 %convolution_bitcast_fusion = f32[32,864]{1,0:T(8,128)S(1)} fusion(bf16[864,4096]{1,0:T(8,128)(2,1)} %shard_map.93, bf16[32,4096]{1,0:T(8,128)(2,1)S(1)} %reshape_squeeze.3), kind=kOutput, calls=%fused_computation.14 | convolution fusion | flops 226492416 | bytes 7450624 | tf_op jit(solution)/shard_map/dot_general | solution.py:182
  32.5 1.9 %collective-permute-start.10 = (f32[32,896]{1,0:T(8,128)S(1)}, f32[32,896]{1,0:T(8,128)S(1)}, u32[]{:S(2)}, u32[]{:S(2)}) collective-permute-start(f32[32,896]{1,0:T(8,128)S(1)} %pad_maximum_fusion.1), channel_id=1, source_target_pairs={{0,8},{4,12},{8,0},{12,4},{16,24},{20,28},{24,16},{28,20},{1,9},{5... | collective-permute-start | bytes 344072 | tf_op jit(solution)/shard_map/ppermute | solution.py:39
  34.6 7.5 %multiply_convert_fusion.2 = bf16[864,864]{1,0:T(8,128)(2,1)S(1)} fusion(bf16[864,4096]{1,0:T(8,128)(2,1)S(1)} %copy-done.1, f32[4096]{0:T(1024)S(1)} %convert_reduce_fusion), kind=kOutput, calls=%fused_computation.6 | convolution fusion | flops 6127405056 | bytes 8587264 | tf_op jit(solution)/shard_map/dot_general | solution.py:206
  42.1 1.9 %fusion.33 = f32[864,864]{1,0:T(8,128)S(1)} fusion(bf16[864,864]{1,0:T(8,128)(2,1)S(1)} %copy-done.3, bf16[864,864]{1,0:T(8,128)(2,1)S(1)} %multiply_convert_fusion.2), kind=kOutput, calls=%fused_computation.79 | convolution fusion | flops 1289945088 | bytes 5971968 | tf_op jit(solution)/shard_map/dot_general | solution.py:214
  44.1 2.0 %collective-permute-start.12 = (f32[32,896]{1,0:T(8,128)S(1)}, f32[32,896]{1,0:T(8,128)S(1)}, u32[]{:S(2)}, u32[]{:S(2)}) collective-permute-start(f32[32,896]{1,0:T(8,128)S(1)} %add_add_fusion.2), channel_id=1, source_target_pairs={{0,16},{4,20},{8,24},{12,28},{16,0},{20,4},{24,8},{28,12},{1,17},{... | collective-permute-start | bytes 344072 | tf_op jit(solution)/shard_map/ppermute | solution.py:37
  46.2 2.0 %fusion.4 = bf16[4,8,32,128]{3,1,2,0:T(8,128)(2,1)} fusion(bf16[32,864]{1,0:T(8,128)(2,1)S(1)} %reshape.136, bf16[864,4096]{1,0:T(8,128)(2,1)S(1)} %copy-done.1), kind=kOutput, calls=%fused_computation.13 | convolution fusion | flops 226623488 | bytes 7395328 | tf_op jit(solution)/shard_map/dot_general | solution.py:216
  48.2 1.3 %convert.8 = bf16[864,864]{1,0:T(8,128)(2,1)} convert(f32[864,864]{1,0:T(8,128)S(1)} %fusion.33) | non-fusion elementwise | flops 746496 | bytes 4478976 | tf_op jit(solution)/shard_map/convert.3
  50.3 1.1 %collective-permute-start.13 = (f32[32,1,216]{2,1,0:T(1,128)S(1)}, f32[32,1,216]{2,1,0:T(1,128)S(1)}, u32[]{:S(2)}, u32[]{:S(2)}) collective-permute-start(f32[32,1,216]{2,1,0:T(1,128)S(1)} %get-tuple-element.31), channel_id=1, source_target_pairs={{0,1},{1,0},{2,3},{3,2},{4,5},{5,4},{6,7},{7,6},{8,9},{9,8},{10,11... | collective-permute-start | bytes 82952 | tf_op jit(solution)/shard_map/ppermute | solution.py:77
  51.5 1.7 %collective-permute-start.14 = (f32[32,1,216]{2,1,0:T(1,128)S(1)}, f32[32,1,216]{2,1,0:T(1,128)S(1)}, u32[]{:S(2)}, u32[]{:S(2)}) collective-permute-start(f32[32,1,216]{2,1,0:T(1,128)S(1)} %get-tuple-element.30), channel_id=1, source_target_pairs={{0,2},{1,3},{2,0},{3,1},{4,6},{5,7},{6,4},{7,5},{8,10},{9,11},{10,... | collective-permute-start | bytes 82952 | tf_op jit(solution)/shard_map/ppermute | solution.py:77
  53.2 1.6 %collective-permute-start.15 = (f32[32,1,216]{2,1,0:T(1,128)S(1)}, f32[32,1,216]{2,1,0:T(1,128)S(1)}, u32[]{:S(2)}, u32[]{:S(2)}) collective-permute-start(f32[32,1,216]{2,1,0:T(1,128)S(1)} %get-tuple-element.29), channel_id=1, source_target_pairs={{0,3},{1,2},{2,1},{3,0},{4,7},{5,6},{6,5},{7,4},{8,11},{9,10},{10,... | collective-permute-start | bytes 82952 | tf_op jit(solution)/shard_map/ppermute | solution.py:77
  54.8 1.3 %fusion.31 = (bf16[216,864]{1,0:T(8,128)(2,1)S(1)}, bf16[216,864]{1,0:T(8,128)(2,1)S(1)}, bf16[216,864]{1,0:T(8,128)(2,1)S(1)}) fusion(bf16[864,864]{1,0:T(8,128)(2,1)} %convert.8), kind=kLoop, calls=%fused_computation.77 | loop fusion | bytes 2239488 | tf_op jit(solution)/shard_map/slice | solution.py:223
  56.9 1.7 %collective-permute-start.3 = (bf16[216,864]{1,0:T(8,128)(2,1)S(1)}, bf16[216,864]{1,0:T(8,128)(2,1)S(1)}, u32[]{:S(2)}, u32[]{:S(2)}) collective-permute-start(bf16[216,864]{1,0:T(8,128)(2,1)S(1)} %get-tuple-element.20), channel_id=1, source_target_pairs={{0,8},{4,12},{8,0},{12,4},{16,24},{20,28},{24,16},{28,20},{1,9},{5... | collective-permute-start | bytes 1119752 | tf_op jit(solution)/shard_map/ppermute | solution.py:222
  59.9 1.7 %collective-permute-start.17 = (f32[32,896]{1,0:T(8,128)S(1)}, f32[32,896]{1,0:T(8,128)S(1)}, u32[]{:S(2)}, u32[]{:S(2)}) collective-permute-start(f32[32,896]{1,0:T(8,128)S(1)} %pad_maximum_fusion.2), channel_id=1, source_target_pairs={{0,2},{1,3},{2,0},{3,1},{4,6},{5,7},{6,4},{7,5},{8,10},{9,11},{10,... | collective-permute-start | bytes 344072 | tf_op jit(solution)/shard_map/ppermute | solution.py:39
  62.5 5.5 %collective-permute-done.4 = bf16[216,864]{1,0:T(8,128)(2,1)S(1)} collective-permute-done((bf16[216,864]{1,0:T(8,128)(2,1)S(1)}, bf16[216,864]{1,0:T(8,128)(2,1)S(1)}, u32[]{:S(2)}, u32[]{:S(2)}) %collective-permute-start.4) | collective-permute-done | bytes 373280 | tf_op jit(solution)/shard_map/ppermute | solution.py:222
  68.5 8.0 %collective-permute-done.3 = bf16[216,864]{1,0:T(8,128)(2,1)S(1)} collective-permute-done((bf16[216,864]{1,0:T(8,128)(2,1)S(1)}, bf16[216,864]{1,0:T(8,128)(2,1)S(1)}, u32[]{:S(2)}, u32[]{:S(2)}) %collective-permute-start.3) | collective-permute-done | bytes 373280 | tf_op jit(solution)/shard_map/ppermute | solution.py:222
  76.5 1.3 %add_add_fusion = f32[216,864]{1,0:T(8,128)S(1)} fusion(bf16[216,864]{1,0:T(8,128)(2,1)S(1)} %collective-permute-done.4, bf16[216,864]{1,0:T(8,128)(2,1)S(1)} %collective-permute-done.3, bf16[216,864]{1,0:T(8,128)(2,1)S(1)} %collective-permute-done.2, f32[864,864]{1,0:T(8,128)} %copy-done.2), kind=kLoop, calls=%fused_computation.16 | loop fusion | flops 1119744 | bytes 2612736 | tf_op jit(solution)/shard_map/add | solution.py:229
  77.8 1.7 %collective-permute-start.5 = (bf16[108,864]{1,0:T(8,128)(2,1)S(1)}, bf16[108,864]{1,0:T(8,128)(2,1)S(1)}, u32[]{:S(2)}, u32[]{:S(2)}) collective-permute-start(bf16[108,864]{1,0:T(8,128)(2,1)S(1)} %slice.89), channel_id=1, source_target_pairs={{0,16},{4,20},{8,24},{12,28},{16,0},{20,4},{24,8},{28,12},{1,17},{... | collective-permute-start | bytes 559880 | tf_op jit(solution)/shard_map/ppermute | solution.py:233
  80.3 4.4 %collective-permute-done.5 = bf16[108,864]{1,0:T(8,128)(2,1)S(1)} collective-permute-done((bf16[108,864]{1,0:T(8,128)(2,1)S(1)}, bf16[108,864]{1,0:T(8,128)(2,1)S(1)}, u32[]{:S(2)}, u32[]{:S(2)}) %collective-permute-start.5) | collective-permute-done | bytes 186656 | tf_op jit(solution)/shard_map/ppermute | solution.py:233
  84.8 1.0 %fusion.5 = f32[108,864]{1,0:T(8,128)S(1)} fusion(bf16[864,864]{1,0:T(8,128)(2,1)S(1)} %get-tuple-element.16, f32[216,864]{1,0:T(8,128)S(1)} %add_add_fusion, bf16[108,864]{1,0:T(8,128)(2,1)S(1)} %collective-permute-done.5), kind=kOutput, calls=%fused_computation.23 | convolution fusion | flops 483916032 | bytes 2523648 | tf_op jit(solution)/shard_map/dot_general | solution.py:236
  86.7 2.4 %collective-permute-start.8 = (bf16[108,1,216]{0,2,1:T(8,128)(2,1)S(1)}, bf16[108,1,216]{0,2,1:T(8,128)(2,1)S(1)}, u32[]{:S(2)}, u32[]{:S(2)}) collective-permute-start(bf16[108,1,216]{0,2,1:T(8,128)(2,1)S(1)} %bitcast.75), channel_id=1, source_target_pairs={{0,3},{1,2},{2,1},{3,0},{4,7},{5,6},{6,5},{7,4},{8,11},{9,10},{10,... | collective-permute-start | bytes 139976 | tf_op jit(solution)/shard_map/ppermute | solution.py:77
  89.4 2.1 %collective-permute-start.6 = (bf16[108,1,216]{0,2,1:T(8,128)(2,1)S(1)}, bf16[108,1,216]{0,2,1:T(8,128)(2,1)S(1)}, u32[]{:S(2)}, u32[]{:S(2)}) collective-permute-start(bf16[108,1,216]{0,2,1:T(8,128)(2,1)S(1)} %bitcast.77), channel_id=1, source_target_pairs={{0,1},{1,0},{2,3},{3,2},{4,5},{5,4},{6,7},{7,6},{8,9},{9,8},{10,11... | collective-permute-start | bytes 139976 | tf_op jit(solution)/shard_map/ppermute | solution.py:77
  92.7 2.0 %collective-permute-done.7 = bf16[108,1,216]{0,2,1:T(8,128)(2,1)S(1)} collective-permute-done((bf16[108,1,216]{0,2,1:T(8,128)(2,1)S(1)}, bf16[108,1,216]{0,2,1:T(8,128)(2,1)S(1)}, u32[]{:S(2)}, u32[]{:S(2)}) %collective-permute-start.7) | collective-permute-done | bytes 46688 | tf_op jit(solution)/shard_map/ppermute | solution.py:77
  (70 shorter events, 10.7 us)
Async XLA Ops:
  0.6 58.5 %copy-start = (f32[216,864]{1,0:T(8,128)S(1)}, f32[216,864]{1,0:T(8,128)}, u32[]{:S(2)}) copy-start(f32[216,864]{1,0:T(8,128)} %param.10) | copy-start | bytes 2239492
  0.6 14.5 %copy-start.5 = (bf16[1,32,2,16,128]{4,3,2,1,0:T(8,128)(2,1)S(1)}, bf16[1,32,2,16,128]{4,3,2,1,0:T(8,128)(2,1)}, u32[]{:S(2)}) copy-start(bf16[1,32,2,16,128]{4,3,2,1,0:T(8,128)(2,1)} %param.7) | copy-start | bytes 786436
  2.5 16.1 %collective-permute-start.1 = (bf16[1,32,1,16,128]{4,1,3,2,0:T(8,128)(2,1)}, bf16[1,32,1,16,128]{4,1,3,2,0:T(8,128)(2,1)}, u32[]{:S(2)}, u32[]{:S(2)}) collective-permute-start(bf16[1,32,1,16,128]{4,1,3,2,0:T(8,128)(2,1)} %get-tuple-element.28), channel_id=1, source_target_pairs={{1,0},{2,1},{3,2},{5,4},{6,5},{7,6},{9,8},{10,9},{11,10},{13,12},{... | collective-permute-start | bytes 393224 | tf_op jit(solution)/shard_map/ppermute | solution.py:20
  3.8 14.8 %collective-permute-start = (bf16[1,32,1,16,128]{4,1,3,2,0:T(8,128)(2,1)S(1)}, bf16[1,32,1,16,128]{4,1,3,2,0:T(8,128)(2,1)}, u32[]{:S(2)}, u32[]{:S(2)}) collective-permute-start(bf16[1,32,1,16,128]{4,1,3,2,0:T(8,128)(2,1)S(1)} %get-tuple-element.27), channel_id=1, source_target_pairs={{0,1},{1,2},{2,3},{4,5},{5,6},{6,7},{8,9},{9,10},{10,11},{12,13},{... | collective-permute-start | bytes 393224 | tf_op jit(solution)/shard_map/ppermute | solution.py:18
  27.1 7.5 %copy-start.1 = (bf16[864,4096]{1,0:T(8,128)(2,1)S(1)}, bf16[864,4096]{1,0:T(8,128)(2,1)}, u32[]{:S(2)}) copy-start(bf16[864,4096]{1,0:T(8,128)(2,1)} %shard_map.93) | copy-start | bytes 21233668
  32.5 9.7 %copy-start.3 = (bf16[864,864]{1,0:T(8,128)(2,1)S(1)}, bf16[864,864]{1,0:T(8,128)(2,1)}, u32[]{:S(2)}) copy-start(bf16[864,864]{1,0:T(8,128)(2,1)} %get-tuple-element.12) | copy-start | bytes 4478980
  32.5 11.6 %collective-permute-start.10 = (f32[32,896]{1,0:T(8,128)S(1)}, f32[32,896]{1,0:T(8,128)S(1)}, u32[]{:S(2)}, u32[]{:S(2)}) collective-permute-start(f32[32,896]{1,0:T(8,128)S(1)} %pad_maximum_fusion.1), channel_id=1, source_target_pairs={{0,8},{4,12},{8,0},{12,4},{16,24},{20,28},{24,16},{28,20},{1,9},{5... | collective-permute-start | bytes 344072 | tf_op jit(solution)/shard_map/ppermute | solution.py:39
  34.4 9.7 %collective-permute-start.11 = (f32[32,896]{1,0:T(8,128)S(1)}, f32[32,896]{1,0:T(8,128)S(1)}, u32[]{:S(2)}, u32[]{:S(2)}) collective-permute-start(f32[32,896]{1,0:T(8,128)S(1)} %pad_maximum_fusion.1), channel_id=1, source_target_pairs={{0,12},{4,8},{8,4},{12,0},{16,28},{20,24},{24,20},{28,16},{1,13},{... | collective-permute-start | bytes 344072 | tf_op jit(solution)/shard_map/ppermute | solution.py:40
  34.4 9.7 %collective-permute-start.9 = (f32[32,896]{1,0:T(8,128)S(1)}, f32[32,896]{1,0:T(8,128)S(1)}, u32[]{:S(2)}, u32[]{:S(2)}) collective-permute-start(f32[32,896]{1,0:T(8,128)S(1)} %pad_maximum_fusion.1), channel_id=1, source_target_pairs={{0,4},{4,0},{8,12},{12,8},{16,20},{20,16},{24,28},{28,24},{1,5},{5... | collective-permute-start | bytes 344072 | tf_op jit(solution)/shard_map/ppermute | solution.py:37
  44.1 4.1 %copy-start.2 = (f32[864,864]{1,0:T(8,128)}, f32[864,864]{1,0:T(8,128)S(1)}, u32[]{:S(2)}) copy-start(f32[864,864]{1,0:T(8,128)S(1)} %fusion.33) | copy-start | bytes 8957956
  44.1 5.4 %collective-permute-start.12 = (f32[32,896]{1,0:T(8,128)S(1)}, f32[32,896]{1,0:T(8,128)S(1)}, u32[]{:S(2)}, u32[]{:S(2)}) collective-permute-start(f32[32,896]{1,0:T(8,128)S(1)} %add_add_fusion.2), channel_id=1, source_target_pairs={{0,16},{4,20},{8,24},{12,28},{16,0},{20,4},{24,8},{28,12},{1,17},{... | collective-permute-start | bytes 344072 | tf_op jit(solution)/shard_map/ppermute | solution.py:37
  49.5 9.5 %copy-start.7 = (f32[32,32]{1,0:T(8,128)S(1)}, f32[32,32]{1,0:T(8,128)}, u32[]{:S(2)}) copy-start(f32[32,32]{1,0:T(8,128)} %param.11) | copy-start | bytes 12292
  50.0 6.1 %copy-start.4 = (bf16[4,8,32,128]{3,1,2,0:T(8,128)(2,1)S(1)}, bf16[4,8,32,128]{3,1,2,0:T(8,128)(2,1)}, u32[]{:S(2)}) copy-start(bf16[4,8,32,128]{3,1,2,0:T(8,128)(2,1)} %fusion.4) | copy-start | bytes 786436
  50.3 8.3 %collective-permute-start.13 = (f32[32,1,216]{2,1,0:T(1,128)S(1)}, f32[32,1,216]{2,1,0:T(1,128)S(1)}, u32[]{:S(2)}, u32[]{:S(2)}) collective-permute-start(f32[32,1,216]{2,1,0:T(1,128)S(1)} %get-tuple-element.31), channel_id=1, source_target_pairs={{0,1},{1,0},{2,3},{3,2},{4,5},{5,4},{6,7},{7,6},{8,9},{9,8},{10,11... | collective-permute-start | bytes 82952 | tf_op jit(solution)/shard_map/ppermute | solution.py:77
  51.5 7.3 %collective-permute-start.14 = (f32[32,1,216]{2,1,0:T(1,128)S(1)}, f32[32,1,216]{2,1,0:T(1,128)S(1)}, u32[]{:S(2)}, u32[]{:S(2)}) collective-permute-start(f32[32,1,216]{2,1,0:T(1,128)S(1)} %get-tuple-element.30), channel_id=1, source_target_pairs={{0,2},{1,3},{2,0},{3,1},{4,6},{5,7},{6,4},{7,5},{8,10},{9,11},{10,... | collective-permute-start | bytes 82952 | tf_op jit(solution)/shard_map/ppermute | solution.py:77
  53.2 5.7 %collective-permute-start.15 = (f32[32,1,216]{2,1,0:T(1,128)S(1)}, f32[32,1,216]{2,1,0:T(1,128)S(1)}, u32[]{:S(2)}, u32[]{:S(2)}) collective-permute-start(f32[32,1,216]{2,1,0:T(1,128)S(1)} %get-tuple-element.29), channel_id=1, source_target_pairs={{0,3},{1,2},{2,1},{3,0},{4,7},{5,6},{6,5},{7,4},{8,11},{9,10},{10,... | collective-permute-start | bytes 82952 | tf_op jit(solution)/shard_map/ppermute | solution.py:77
  56.9 11.1 %collective-permute-start.4 = (bf16[216,864]{1,0:T(8,128)(2,1)S(1)}, bf16[216,864]{1,0:T(8,128)(2,1)S(1)}, u32[]{:S(2)}, u32[]{:S(2)}) collective-permute-start(bf16[216,864]{1,0:T(8,128)(2,1)S(1)} %get-tuple-element.19), channel_id=1, source_target_pairs={{0,12},{4,8},{8,4},{12,0},{16,28},{20,24},{24,20},{28,16},{1,13},{... | collective-permute-start | bytes 1119752 | tf_op jit(solution)/shard_map/ppermute | solution.py:222
  56.9 19.6 %collective-permute-start.3 = (bf16[216,864]{1,0:T(8,128)(2,1)S(1)}, bf16[216,864]{1,0:T(8,128)(2,1)S(1)}, u32[]{:S(2)}, u32[]{:S(2)}) collective-permute-start(bf16[216,864]{1,0:T(8,128)(2,1)S(1)} %get-tuple-element.20), channel_id=1, source_target_pairs={{0,8},{4,12},{8,0},{12,4},{16,24},{20,28},{24,16},{28,20},{1,9},{5... | collective-permute-start | bytes 1119752 | tf_op jit(solution)/shard_map/ppermute | solution.py:222
  58.6 17.8 %collective-permute-start.2 = (bf16[216,864]{1,0:T(8,128)(2,1)S(1)}, bf16[216,864]{1,0:T(8,128)(2,1)S(1)}, u32[]{:S(2)}, u32[]{:S(2)}) collective-permute-start(bf16[216,864]{1,0:T(8,128)(2,1)S(1)} %get-tuple-element.18), channel_id=1, source_target_pairs={{0,4},{4,0},{8,12},{12,8},{16,20},{20,16},{24,28},{28,24},{1,5},{5... | collective-permute-start | bytes 1119752 | tf_op jit(solution)/shard_map/ppermute | solution.py:222
  59.9 19.7 %collective-permute-start.17 = (f32[32,896]{1,0:T(8,128)S(1)}, f32[32,896]{1,0:T(8,128)S(1)}, u32[]{:S(2)}, u32[]{:S(2)}) collective-permute-start(f32[32,896]{1,0:T(8,128)S(1)} %pad_maximum_fusion.2), channel_id=1, source_target_pairs={{0,2},{1,3},{2,0},{3,1},{4,6},{5,7},{6,4},{7,5},{8,10},{9,11},{10,... | collective-permute-start | bytes 344072 | tf_op jit(solution)/shard_map/ppermute | solution.py:39
  61.6 17.9 %collective-permute-start.18 = (f32[32,896]{1,0:T(8,128)S(1)}, f32[32,896]{1,0:T(8,128)S(1)}, u32[]{:S(2)}, u32[]{:S(2)}) collective-permute-start(f32[32,896]{1,0:T(8,128)S(1)} %pad_maximum_fusion.2), channel_id=1, source_target_pairs={{0,3},{1,2},{2,1},{3,0},{4,7},{5,6},{6,5},{7,4},{8,11},{9,10},{10,... | collective-permute-start | bytes 344072 | tf_op jit(solution)/shard_map/ppermute | solution.py:40
  68.0 11.6 %collective-permute-start.16 = (f32[32,896]{1,0:T(8,128)S(1)}, f32[32,896]{1,0:T(8,128)S(1)}, u32[]{:S(2)}, u32[]{:S(2)}) collective-permute-start(f32[32,896]{1,0:T(8,128)S(1)} %pad_maximum_fusion.2), channel_id=1, source_target_pairs={{0,1},{1,0},{2,3},{3,2},{4,5},{5,4},{6,7},{7,6},{8,9},{9,8},{10,11... | collective-permute-start | bytes 344072 | tf_op jit(solution)/shard_map/ppermute | solution.py:37
  77.8 7.0 %collective-permute-start.5 = (bf16[108,864]{1,0:T(8,128)(2,1)S(1)}, bf16[108,864]{1,0:T(8,128)(2,1)S(1)}, u32[]{:S(2)}, u32[]{:S(2)}) collective-permute-start(bf16[108,864]{1,0:T(8,128)(2,1)S(1)} %slice.89), channel_id=1, source_target_pairs={{0,16},{4,20},{8,24},{12,28},{16,0},{20,4},{24,8},{28,12},{1,17},{... | collective-permute-start | bytes 559880 | tf_op jit(solution)/shard_map/ppermute | solution.py:233
  79.6 15.7 %copy-start.6 = (f32[32,896]{1,0:T(8,128)}, f32[32,896]{1,0:T(8,128)S(1)}, u32[]{:S(2)}) copy-start(f32[32,896]{1,0:T(8,128)S(1)} %add_add_fusion.1) | copy-start | bytes 344068
  86.7 6.0 %collective-permute-start.8 = (bf16[108,1,216]{0,2,1:T(8,128)(2,1)S(1)}, bf16[108,1,216]{0,2,1:T(8,128)(2,1)S(1)}, u32[]{:S(2)}, u32[]{:S(2)}) collective-permute-start(bf16[108,1,216]{0,2,1:T(8,128)(2,1)S(1)} %bitcast.75), channel_id=1, source_target_pairs={{0,3},{1,2},{2,1},{3,0},{4,7},{5,6},{6,5},{7,4},{8,11},{9,10},{10,... | collective-permute-start | bytes 139976 | tf_op jit(solution)/shard_map/ppermute | solution.py:77
  89.2 5.5 %collective-permute-start.7 = (bf16[108,1,216]{0,2,1:T(8,128)(2,1)S(1)}, bf16[108,1,216]{0,2,1:T(8,128)(2,1)S(1)}, u32[]{:S(2)}, u32[]{:S(2)}) collective-permute-start(bf16[108,1,216]{0,2,1:T(8,128)(2,1)S(1)} %bitcast.76), channel_id=1, source_target_pairs={{0,2},{1,3},{2,0},{3,1},{4,6},{5,7},{6,4},{7,5},{8,10},{9,11},{10,... | collective-permute-start | bytes 139976 | tf_op jit(solution)/shard_map/ppermute | solution.py:77
  89.4 5.3 %collective-permute-start.6 = (bf16[108,1,216]{0,2,1:T(8,128)(2,1)S(1)}, bf16[108,1,216]{0,2,1:T(8,128)(2,1)S(1)}, u32[]{:S(2)}, u32[]{:S(2)}) collective-permute-start(bf16[108,1,216]{0,2,1:T(8,128)(2,1)S(1)} %bitcast.77), channel_id=1, source_target_pairs={{0,1},{1,0},{2,3},{3,2},{4,5},{5,4},{6,7},{7,6},{8,9},{9,8},{10,11... | collective-permute-start | bytes 139976 | tf_op jit(solution)/shard_map/ppermute | solution.py:77

commit v18 on v16

--- a/solution.py
+++ b/solution.py
@@ -216,6 +216,16 @@
     forward = jnp.dot(kernel_perm, patches_t, preferred_element_type=f32)
     conv_out = forward.astype(jnp.bfloat16).reshape(1, channels, planes, y_cells, x_cells)
     step = 1
+    if n_dp >= 2:
+        quarter = a_orig.shape[0] // 4
+        got = [
+            lax.ppermute(a_orig[(2 + q) * quarter :][:quarter].astype(jnp.bfloat16), "dp", partner("dp", 1))
+            for q in (0, 1)
+        ]
+        a_orig = jnp.concatenate(
+            [a_orig[q * quarter :][:quarter] + got[q].astype(f32) for q in (0, 1)], axis=0
+        )
+        step = 2
     while step < n_dp:
         half = a_orig.shape[0] // 2
         got = lax.ppermute(a_orig[half:].astype(jnp.bfloat16), "dp", partner("dp", step))

time: 85.5 us -> 89.7 us (1.049)
  waiting for transfers between devices: 11.2 us -> 14.8 us
  starting transfers between devices: 26.5 us -> 27.6 us
    ppermute x3, waiting for transfers between devices: 0.5 us -> 3.7 us  [butterfly_sum(): got = lax.ppermute(x, axis, partner(axis, low))]
    ppermute x3 -> x2, waiting for transfers between devices: 5.76 us -> 8.13 us  [on_device(): lax.ppermute(a_orig[half:].astype(jnp.bfloat16), 'dp', partner('dp', step))]
    ppermute x2, waiting for transfers between devices: 2.32 us -> 0.2 us  [butterfly_sum(): pair = lax.ppermute(x, axis, partner(axis, high))]
    add x2 -> x1, other arithmetic: 1.38 us -> 0.15 us  [on_device(): a_orig = a_orig[:half] + got.astype(f32)]
    ppermute x3 -> x2, starting transfers between devices: 2.3 us -> 3.43 us  [on_device(): lax.ppermute(a_orig[half:].astype(jnp.bfloat16), 'dp', partner('dp', step))]
    slice x3 -> x1, local copies, waits for them, and re-layouts: 1.14 us -> 0.04 us  [on_device(): a_orig[half:].astype(jnp.bfloat16)]
    convert_element_type x0 -> x1, other arithmetic: none -> 1.08 us  [on_device(): a_orig[half:].astype(jnp.bfloat16)]
    slice x0 -> x1, local copies, waits for them, and re-layouts: none -> 0.94 us  [on_device(): a_orig[(2 + q) * quarter:][:quarter].astype(jnp.bfloat16)]
  transfers between devices with their start and end apart: 18 -> 19, of which waited for: 7 -> 7; matrix products, arithmetic and copies ran while one was open for 31% -> 31% of each run, Pallas kernels for 0% -> 0%
where the time goes in v18:
time: 89.7 us; the launch traced here: 89.3 us
  starting transfers between devices  27.6 us (31%)
  matrix products  22.2 us (25%)
  waiting for transfers between devices  14.8 us (16%)
  other arithmetic  10.1 us (11%)
  local copies, waits for them, and re-layouts  8.55 us (10%)
  Pallas kernels  5.15 us (6%)
  between operations  0.98 us (1%)
    ppermute x6, starting transfers between devices, quad_scatter(): lax.ppermute(pick(digit ^ k).astype(wire), axis, partner(axis, k * low))  9.02 us
    ppermute x2, waiting for transfers between devices, on_device(): lax.ppermute(a_orig[half:].astype(jnp.bfloat16), 'dp', partner('dp', step))  8.13 us
    dot_general x1, matrix products, on_device(): lax.dot_general(weighted, patches_t, contract_cells, preferred_element_ty...  7.49 us
    ppermute x1, starting transfers between devices, padded_2(): lax.ppermute(tail, axis, [(i, (i + 1) % count) for i in range(ends)])  6.23 us
    dot_general x1, matrix products, on_device(): lax.dot_general(grad_flat, patches_t, contract_cells, preferred_element_t...  5.27 us
    pallas_call x1, Pallas kernels, patch_matrix(): pl.pallas_call(body, grid=(3,), in_specs=[pl.BlockSpec(shifted.shape, lam...  5.15 us
    dot_general x1, matrix products, on_device(): forward = jnp.dot(kernel_perm, patches_t, preferred_element_type=f32)  4.33 us
    ppermute x3, waiting for transfers between devices, butterfly_sum(): got = lax.ppermute(x, axis, partner(axis, low))  3.7 us
  transfers between devices with their start and end apart: 19, of which 7 were waited for; matrix products, arithmetic and copies ran while one was open for 31% of the time, Pallas kernels for 0%

profile of v18, /device:TPU:0, one launch (start us, length us, event | category | flops | bytes accessed | tf_op | source)
XLA Modules:
  0.0 89.3 jit_solution(12292500670175633982)
XLA Ops:
  0.7 1.1 %copy.30 = bf16[1,32,2,16,128]{4,1,3,2,0:T(8,128)(2,1)S(1)} copy(bf16[1,32,2,16,128]{4,3,2,1,0:T(8,128)(2,1)} %param.6) | data formatting | bytes 524288 | tf_op args[0]
  2.5 1.3 %collective-permute-start.1 = (bf16[1,32,1,16,128]{4,1,3,2,0:T(8,128)(2,1)}, bf16[1,32,1,16,128]{4,1,3,2,0:T(8,128)(2,1)}, u32[]{:S(2)}, u32[]{:S(2)}) collective-permute-start(bf16[1,32,1,16,128]{4,1,3,2,0:T(8,128)(2,1)} %get-tuple-element.27), channel_id=1, source_target_pairs={{1,0},{2,1},{3,2},{5,4},{6,5},{7,6},{9,8},{10,9},{11,10},{13,12},{... | collective-permute-start | bytes 393224 | tf_op jit(solution)/shard_map/ppermute | solution.py:20
  3.8 6.2 %collective-permute-start = (bf16[1,32,1,16,128]{4,1,3,2,0:T(8,128)(2,1)}, bf16[1,32,1,16,128]{4,1,3,2,0:T(8,128)(2,1)}, u32[]{:S(2)}, u32[]{:S(2)}) collective-permute-start(bf16[1,32,1,16,128]{4,1,3,2,0:T(8,128)(2,1)} %get-tuple-element.26), channel_id=1, source_target_pairs={{0,1},{1,2},{2,3},{4,5},{5,6},{6,7},{8,9},{9,10},{10,11},{12,13},{... | collective-permute-start | bytes 393224 | tf_op jit(solution)/shard_map/ppermute | solution.py:18
  10.1 3.4 %convert_reduce_fusion = f32[4096]{0:T(1024)S(1)} fusion(s32[1024]{0:T(1024)} %bitcast.78), kind=kLoop, calls=%fused_computation | loop fusion | flops 12578816 | bytes 20480 | tf_op jit(solution)/shard_map/reduce_sum | solution.py:201
  13.5 1.7 %fusion.2 = (bf16[864,864]{1,0:T(8,128)(2,1)S(1)}, bf16[864,864]{1,0:T(8,128)(2,1)}) fusion(s32[864]{0:T(1024)S(1)} %fusion.24, s32[864]{0:T(1024)S(1)} %fusion.27), kind=kLoop, calls=%fused_computation.9 | loop fusion | flops 2985984 | bytes 2992896 | tf_op jit(solution)/shard_map/convert_element_type | solution.py:135
  16.5 1.3 %convolution_bitcast_fusion.1 = f32[32,32]{1,0:T(8,128)S(1)} fusion(bf16[32,2,16,128]{3,2,1,0:T(8,128)(2,1)} %bitcast.72), kind=kOutput, calls=%fused_computation.15 | convolution fusion | flops 8388608 | bytes 266240 | tf_op jit(solution)/shard_map/dot_general | solution.py:183
  17.9 1.0 %maximum_bitcast_fusion = bf16[32,4,16,128]{3,0,2,1:T(8,128)(2,1)S(1)} fusion(bf16[1,32,1,16,128]{4,1,3,2,0:T(8,128)(2,1)} %collective-permute-done.1, bf16[1,32,2,16,128]{4,1,3,2,0:T(8,128)(2,1)S(1)} %copy.30, bf16[1,32,1,16,128]{4,1,3,2,0:T(8,128)(2,1)} %collective-permute-done), kind=kLoop, calls=%fused_computation.21 | loop fusion | flops 524288 | bytes 1048576 | tf_op jit(solution)/shard_map/squeeze | solution.py:176
  19.8 1.5 %pad_maximum_fusion.src_ref = bf16[3,4,18,32,128]{4,3,2,1,0:T(8,128)(2,1)} fusion(bf16[1,4,18,32,128]{4,3,2,1,0:T(8,128)(2,1)S(1)} %get-tuple-element.21, bf16[1,4,18,32,128]{4,3,2,1,0:T(8,128)(2,1)S(1)} %get-tuple-element.22, bf16[1,4,18,32,128]{4,3,2,1,0:T(8,128)(2,1)S(1)} %get-tuple-element.20), kind=kLoop, calls=%fused_computation.11 | loop fusion | flops 1769472 | bytes 3538944 | tf_op jit(solution)/shard_map/stack | solution.py:109
  21.2 5.1 %shard_map.93 = bf16[864,4096]{1,0:T(8,128)(2,1)} custom-call(bf16[3,4,18,32,128]{4,3,2,1,0:T(8,128)(2,1)} %pad_maximum_fusion.src_ref), custom_call_target="tpu_custom_call" | custom-call | tf_op jit(solution)/shard_map/pallas_call | solution.py:122
  26.4 5.3 %convolution_bitcast_fusion = f32[32,864]{1,0:T(8,128)S(1)} fusion(bf16[864,4096]{1,0:T(8,128)(2,1)} %shard_map.93, bf16[32,4096]{1,0:T(8,128)(2,1)S(1)} %reshape_squeeze.3), kind=kOutput, calls=%fused_computation.14 | convolution fusion | flops 226492416 | bytes 7450624 | tf_op jit(solution)/shard_map/dot_general | solution.py:182
  31.7 1.9 %collective-permute-start.10 = (f32[32,896]{1,0:T(8,128)S(1)}, f32[32,896]{1,0:T(8,128)S(1)}, u32[]{:S(2)}, u32[]{:S(2)}) collective-permute-start(f32[32,896]{1,0:T(8,128)S(1)} %pad_maximum_fusion.1), channel_id=1, source_target_pairs={{0,8},{4,12},{8,0},{12,4},{16,24},{20,28},{24,16},{28,20},{1,9},{5... | collective-permute-start | bytes 344072 | tf_op jit(solution)/shard_map/ppermute | solution.py:39
  33.9 7.5 %multiply_convert_fusion.2 = bf16[864,864]{1,0:T(8,128)(2,1)S(1)} fusion(bf16[864,4096]{1,0:T(8,128)(2,1)S(1)} %copy-done.1, f32[4096]{0:T(1024)S(1)} %convert_reduce_fusion), kind=kOutput, calls=%fused_computation.6 | convolution fusion | flops 6127405056 | bytes 8587264 | tf_op jit(solution)/shard_map/dot_general | solution.py:206
  41.4 1.9 %fusion.33 = f32[864,864]{1,0:T(8,128)S(1)} fusion(bf16[864,864]{1,0:T(8,128)(2,1)S(1)} %copy-done.4, bf16[864,864]{1,0:T(8,128)(2,1)S(1)} %multiply_convert_fusion.2), kind=kOutput, calls=%fused_computation.80 | convolution fusion | flops 1289945088 | bytes 5971968 | tf_op jit(solution)/shard_map/dot_general | solution.py:214
  43.6 2.0 %collective-permute-start.12 = (f32[32,896]{1,0:T(8,128)S(1)}, f32[32,896]{1,0:T(8,128)S(1)}, u32[]{:S(2)}, u32[]{:S(2)}) collective-permute-start(f32[32,896]{1,0:T(8,128)S(1)} %add_add_fusion.1), channel_id=1, source_target_pairs={{0,16},{4,20},{8,24},{12,28},{16,0},{20,4},{24,8},{28,12},{1,17},{... | collective-permute-start | bytes 344072 | tf_op jit(solution)/shard_map/ppermute | solution.py:37
  46.6 2.4 %collective-permute-done.12 = f32[32,896]{1,0:T(8,128)S(1)} collective-permute-done((f32[32,896]{1,0:T(8,128)S(1)}, f32[32,896]{1,0:T(8,128)S(1)}, u32[]{:S(2)}, u32[]{:S(2)}) %collective-permute-start.12) | collective-permute-done | bytes 114720 | tf_op jit(solution)/shard_map/ppermute | solution.py:37
  49.8 1.1 %collective-permute-start.13 = (f32[32,1,216]{2,1,0:T(1,128)S(1)}, f32[32,1,216]{2,1,0:T(1,128)S(1)}, u32[]{:S(2)}, u32[]{:S(2)}) collective-permute-start(f32[32,1,216]{2,1,0:T(1,128)S(1)} %get-tuple-element.30), channel_id=1, source_target_pairs={{0,1},{1,0},{2,3},{3,2},{4,5},{5,4},{6,7},{7,6},{8,9},{9,8},{10,11... | collective-permute-start | bytes 82952 | tf_op jit(solution)/shard_map/ppermute | solution.py:77
  50.9 1.7 %collective-permute-start.14 = (f32[32,1,216]{2,1,0:T(1,128)S(1)}, f32[32,1,216]{2,1,0:T(1,128)S(1)}, u32[]{:S(2)}, u32[]{:S(2)}) collective-permute-start(f32[32,1,216]{2,1,0:T(1,128)S(1)} %get-tuple-element.29), channel_id=1, source_target_pairs={{0,2},{1,3},{2,0},{3,1},{4,6},{5,7},{6,4},{7,5},{8,10},{9,11},{10,... | collective-permute-start | bytes 82952 | tf_op jit(solution)/shard_map/ppermute | solution.py:77
  52.7 1.6 %collective-permute-start.15 = (f32[32,1,216]{2,1,0:T(1,128)S(1)}, f32[32,1,216]{2,1,0:T(1,128)S(1)}, u32[]{:S(2)}, u32[]{:S(2)}) collective-permute-start(f32[32,1,216]{2,1,0:T(1,128)S(1)} %get-tuple-element.28), channel_id=1, source_target_pairs={{0,3},{1,2},{2,1},{3,0},{4,7},{5,6},{6,5},{7,4},{8,11},{9,10},{10,... | collective-permute-start | bytes 82952 | tf_op jit(solution)/shard_map/ppermute | solution.py:77
  54.3 4.3 %fusion.4 = bf16[4,8,32,128]{3,1,2,0:T(8,128)(2,1)S(1)} fusion(bf16[32,864]{1,0:T(8,128)(2,1)S(1)} %reshape.136, bf16[864,4096]{1,0:T(8,128)(2,1)} %shard_map.93), kind=kOutput, calls=%fused_computation.13 | convolution fusion | flops 226623488 | bytes 7395328 | tf_op jit(solution)/shard_map/dot_general | solution.py:216
  59.5 1.1 %add_convert_fusion = bf16[216,864]{1,0:T(8,128)(2,1)S(1)} fusion(bf16[216,864]{1,0:T(8,128)(2,1)} %collective-permute-done.3, f32[864,864]{1,0:T(8,128)S(1)} %copy-done.3), kind=kLoop, calls=%fused_computation.17 | loop fusion | flops 559872 | bytes 1492992 | tf_op jit(solution)/shard_map/convert_element_type | solution.py:231
  60.6 1.7 %collective-permute-start.4 = (bf16[216,864]{1,0:T(8,128)(2,1)S(1)}, bf16[216,864]{1,0:T(8,128)(2,1)S(1)}, u32[]{:S(2)}, u32[]{:S(2)}) collective-permute-start(bf16[216,864]{1,0:T(8,128)(2,1)S(1)} %add_convert_fusion), channel_id=1, source_target_pairs={{0,8},{4,12},{8,0},{12,4},{16,24},{20,28},{24,16},{28,20},{1,9},{5... | collective-permute-start | bytes 1119752 | tf_op jit(solution)/shard_map/ppermute | solution.py:231
  63.2 1.7 %collective-permute-start.17 = (f32[32,896]{1,0:T(8,128)S(1)}, f32[32,896]{1,0:T(8,128)S(1)}, u32[]{:S(2)}, u32[]{:S(2)}) collective-permute-start(f32[32,896]{1,0:T(8,128)S(1)} %pad_maximum_fusion.2), channel_id=1, source_target_pairs={{0,2},{1,3},{2,0},{3,1},{4,6},{5,7},{6,4},{7,5},{8,10},{9,11},{10,... | collective-permute-start | bytes 344072 | tf_op jit(solution)/shard_map/ppermute | solution.py:39
  64.9 1.1 %collective-permute-start.18 = (f32[32,896]{1,0:T(8,128)S(1)}, f32[32,896]{1,0:T(8,128)S(1)}, u32[]{:S(2)}, u32[]{:S(2)}) collective-permute-start(f32[32,896]{1,0:T(8,128)S(1)} %pad_maximum_fusion.2), channel_id=1, source_target_pairs={{0,3},{1,2},{2,1},{3,0},{4,7},{5,6},{6,5},{7,4},{8,11},{9,10},{10,... | collective-permute-start | bytes 344072 | tf_op jit(solution)/shard_map/ppermute | solution.py:40
  66.7 5.4 %collective-permute-done.4 = bf16[216,864]{1,0:T(8,128)(2,1)S(1)} collective-permute-done((bf16[216,864]{1,0:T(8,128)(2,1)S(1)}, bf16[216,864]{1,0:T(8,128)(2,1)S(1)}, u32[]{:S(2)}, u32[]{:S(2)}) %collective-permute-start.4) | collective-permute-done | bytes 373280 | tf_op jit(solution)/shard_map/ppermute | solution.py:231
  72.3 1.7 %collective-permute-start.5 = (bf16[108,864]{1,0:T(8,128)(2,1)S(1)}, bf16[108,864]{1,0:T(8,128)(2,1)S(1)}, u32[]{:S(2)}, u32[]{:S(2)}) collective-permute-start(bf16[108,864]{1,0:T(8,128)(2,1)S(1)} %slice.88), channel_id=1, source_target_pairs={{0,16},{4,20},{8,24},{12,28},{16,0},{20,4},{24,8},{28,12},{1,17},{... | collective-permute-start | bytes 559880 | tf_op jit(solution)/shard_map/ppermute | solution.py:231
  74.2 1.3 %collective-permute-done.16 = f32[32,896]{1,0:T(8,128)S(1)} collective-permute-done((f32[32,896]{1,0:T(8,128)S(1)}, f32[32,896]{1,0:T(8,128)S(1)}, u32[]{:S(2)}, u32[]{:S(2)}) %collective-permute-start.16) | collective-permute-done | bytes 114720 | tf_op jit(solution)/shard_map/ppermute | solution.py:37
  76.2 2.7 %collective-permute-done.5 = bf16[108,864]{1,0:T(8,128)(2,1)S(1)} collective-permute-done((bf16[108,864]{1,0:T(8,128)(2,1)S(1)}, bf16[108,864]{1,0:T(8,128)(2,1)S(1)}, u32[]{:S(2)}, u32[]{:S(2)}) %collective-permute-start.5) | collective-permute-done | bytes 186656 | tf_op jit(solution)/shard_map/ppermute | solution.py:231
  79.0 1.0 %fusion.5 = f32[108,864]{1,0:T(8,128)S(1)} fusion(bf16[864,864]{1,0:T(8,128)(2,1)S(1)} %get-tuple-element.16, f32[216,864]{1,0:T(8,128)S(1)} %convert_add_fusion, bf16[108,864]{1,0:T(8,128)(2,1)S(1)} %collective-permute-done.5), kind=kOutput, calls=%fused_computation.24 | convolution fusion | flops 483916032 | bytes 2523648 | tf_op jit(solution)/shard_map/dot_general | solution.py:234
  80.9 2.3 %collective-permute-start.8 = (bf16[108,1,216]{0,2,1:T(8,128)(2,1)S(1)}, bf16[108,1,216]{0,2,1:T(8,128)(2,1)S(1)}, u32[]{:S(2)}, u32[]{:S(2)}) collective-permute-start(bf16[108,1,216]{0,2,1:T(8,128)(2,1)S(1)} %bitcast.75), channel_id=1, source_target_pairs={{0,3},{1,2},{2,1},{3,0},{4,7},{5,6},{6,5},{7,4},{8,11},{9,10},{10,... | collective-permute-start | bytes 139976 | tf_op jit(solution)/shard_map/ppermute | solution.py:77
  83.5 2.2 %collective-permute-start.6 = (bf16[108,1,216]{0,2,1:T(8,128)(2,1)S(1)}, bf16[108,1,216]{0,2,1:T(8,128)(2,1)S(1)}, u32[]{:S(2)}, u32[]{:S(2)}) collective-permute-start(bf16[108,1,216]{0,2,1:T(8,128)(2,1)S(1)} %bitcast.77), channel_id=1, source_target_pairs={{0,1},{1,0},{2,3},{3,2},{4,5},{5,4},{6,7},{7,6},{8,9},{9,8},{10,11... | collective-permute-start | bytes 139976 | tf_op jit(solution)/shard_map/ppermute | solution.py:77
  85.9 1.1 %collective-permute-done.8 = bf16[108,1,216]{0,2,1:T(8,128)(2,1)S(1)} collective-permute-done((bf16[108,1,216]{0,2,1:T(8,128)(2,1)S(1)}, bf16[108,1,216]{0,2,1:T(8,128)(2,1)S(1)}, u32[]{:S(2)}, u32[]{:S(2)}) %collective-permute-start.8) | collective-permute-done | bytes 46688 | tf_op jit(solution)/shard_map/ppermute | solution.py:77
  87.0 1.6 %collective-permute-done.7 = bf16[108,1,216]{0,2,1:T(8,128)(2,1)S(1)} collective-permute-done((bf16[108,1,216]{0,2,1:T(8,128)(2,1)S(1)}, bf16[108,1,216]{0,2,1:T(8,128)(2,1)S(1)}, u32[]{:S(2)}, u32[]{:S(2)}) %collective-permute-start.7) | collective-permute-done | bytes 46688 | tf_op jit(solution)/shard_map/ppermute | solution.py:77
  (75 shorter events, 10.9 us)
Async XLA Ops:
  0.6 61.9 %copy-start = (f32[216,864]{1,0:T(8,128)S(1)}, f32[216,864]{1,0:T(8,128)}, u32[]{:S(2)}) copy-start(f32[216,864]{1,0:T(8,128)} %param.10) | copy-start | bytes 2239492
  0.6 14.6 %copy-start.6 = (bf16[1,32,2,16,128]{4,3,2,1,0:T(8,128)(2,1)S(1)}, bf16[1,32,2,16,128]{4,3,2,1,0:T(8,128)(2,1)}, u32[]{:S(2)}) copy-start(bf16[1,32,2,16,128]{4,3,2,1,0:T(8,128)(2,1)} %param.7) | copy-start | bytes 786436
  0.7 14.7 %copy-start.8 = (bf16[32,864]{1,0:T(8,128)(2,1)S(1)}, bf16[32,864]{1,0:T(8,128)(2,1)}, u32[]{:S(2)}) copy-start(bf16[32,864]{1,0:T(8,128)(2,1)} %param.8) | copy-start | bytes 165892
  2.5 15.3 %collective-permute-start.1 = (bf16[1,32,1,16,128]{4,1,3,2,0:T(8,128)(2,1)}, bf16[1,32,1,16,128]{4,1,3,2,0:T(8,128)(2,1)}, u32[]{:S(2)}, u32[]{:S(2)}) collective-permute-start(bf16[1,32,1,16,128]{4,1,3,2,0:T(8,128)(2,1)} %get-tuple-element.27), channel_id=1, source_target_pairs={{1,0},{2,1},{3,2},{5,4},{6,5},{7,6},{9,8},{10,9},{11,10},{13,12},{... | collective-permute-start | bytes 393224 | tf_op jit(solution)/shard_map/ppermute | solution.py:20
  3.8 14.1 %collective-permute-start = (bf16[1,32,1,16,128]{4,1,3,2,0:T(8,128)(2,1)}, bf16[1,32,1,16,128]{4,1,3,2,0:T(8,128)(2,1)}, u32[]{:S(2)}, u32[]{:S(2)}) collective-permute-start(bf16[1,32,1,16,128]{4,1,3,2,0:T(8,128)(2,1)} %get-tuple-element.26), channel_id=1, source_target_pairs={{0,1},{1,2},{2,3},{4,5},{5,6},{6,7},{8,9},{9,10},{10,11},{12,13},{... | collective-permute-start | bytes 393224 | tf_op jit(solution)/shard_map/ppermute | solution.py:18
  26.4 7.5 %copy-start.1 = (bf16[864,4096]{1,0:T(8,128)(2,1)S(1)}, bf16[864,4096]{1,0:T(8,128)(2,1)}, u32[]{:S(2)}) copy-start(bf16[864,4096]{1,0:T(8,128)(2,1)} %shard_map.93) | copy-start | bytes 21233668
  31.7 9.7 %copy-start.4 = (bf16[864,864]{1,0:T(8,128)(2,1)S(1)}, bf16[864,864]{1,0:T(8,128)(2,1)}, u32[]{:S(2)}) copy-start(bf16[864,864]{1,0:T(8,128)(2,1)} %get-tuple-element.12) | copy-start | bytes 4478980
  31.7 11.8 %collective-permute-start.10 = (f32[32,896]{1,0:T(8,128)S(1)}, f32[32,896]{1,0:T(8,128)S(1)}, u32[]{:S(2)}, u32[]{:S(2)}) collective-permute-start(f32[32,896]{1,0:T(8,128)S(1)} %pad_maximum_fusion.1), channel_id=1, source_target_pairs={{0,8},{4,12},{8,0},{12,4},{16,24},{20,28},{24,16},{28,20},{1,9},{5... | collective-permute-start | bytes 344072 | tf_op jit(solution)/shard_map/ppermute | solution.py:39
  33.7 9.8 %collective-permute-start.11 = (f32[32,896]{1,0:T(8,128)S(1)}, f32[32,896]{1,0:T(8,128)S(1)}, u32[]{:S(2)}, u32[]{:S(2)}) collective-permute-start(f32[32,896]{1,0:T(8,128)S(1)} %pad_maximum_fusion.1), channel_id=1, source_target_pairs={{0,12},{4,8},{8,4},{12,0},{16,28},{20,24},{24,20},{28,16},{1,13},{... | collective-permute-start | bytes 344072 | tf_op jit(solution)/shard_map/ppermute | solution.py:40
  33.7 9.9 %collective-permute-start.9 = (f32[32,896]{1,0:T(8,128)S(1)}, f32[32,896]{1,0:T(8,128)S(1)}, u32[]{:S(2)}, u32[]{:S(2)}) collective-permute-start(f32[32,896]{1,0:T(8,128)S(1)} %pad_maximum_fusion.1), channel_id=1, source_target_pairs={{0,4},{4,0},{8,12},{12,8},{16,20},{20,16},{24,28},{28,24},{1,5},{5... | collective-permute-start | bytes 344072 | tf_op jit(solution)/shard_map/ppermute | solution.py:37
  43.4 3.2 %copy-start.2 = (f32[864,864]{1,0:T(8,128)}, f32[864,864]{1,0:T(8,128)S(1)}, u32[]{:S(2)}) copy-start(f32[864,864]{1,0:T(8,128)S(1)} %fusion.33) | copy-start | bytes 8957956
  43.6 5.4 %collective-permute-start.12 = (f32[32,896]{1,0:T(8,128)S(1)}, f32[32,896]{1,0:T(8,128)S(1)}, u32[]{:S(2)}, u32[]{:S(2)}) collective-permute-start(f32[32,896]{1,0:T(8,128)S(1)} %add_add_fusion.1), channel_id=1, source_target_pairs={{0,16},{4,20},{8,24},{12,28},{16,0},{20,4},{24,8},{28,12},{1,17},{... | collective-permute-start | bytes 344072 | tf_op jit(solution)/shard_map/ppermute | solution.py:37
  46.6 12.9 %collective-permute-start.3 = (bf16[216,864]{1,0:T(8,128)(2,1)}, bf16[216,864]{1,0:T(8,128)(2,1)}, u32[]{:S(2)}, u32[]{:S(2)}) collective-permute-start(bf16[216,864]{1,0:T(8,128)(2,1)} %get-tuple-element.19), channel_id=1, source_target_pairs={{0,4},{4,0},{8,12},{12,8},{16,20},{20,16},{24,28},{28,24},{1,5},{5... | collective-permute-start | bytes 1119752 | tf_op jit(solution)/shard_map/ppermute | solution.py:222
  49.8 9.6 %collective-permute-start.13 = (f32[32,1,216]{2,1,0:T(1,128)S(1)}, f32[32,1,216]{2,1,0:T(1,128)S(1)}, u32[]{:S(2)}, u32[]{:S(2)}) collective-permute-start(f32[32,1,216]{2,1,0:T(1,128)S(1)} %get-tuple-element.30), channel_id=1, source_target_pairs={{0,1},{1,0},{2,3},{3,2},{4,5},{5,4},{6,7},{7,6},{8,9},{9,8},{10,11... | collective-permute-start | bytes 82952 | tf_op jit(solution)/shard_map/ppermute | solution.py:77
  50.9 8.5 %collective-permute-start.14 = (f32[32,1,216]{2,1,0:T(1,128)S(1)}, f32[32,1,216]{2,1,0:T(1,128)S(1)}, u32[]{:S(2)}, u32[]{:S(2)}) collective-permute-start(f32[32,1,216]{2,1,0:T(1,128)S(1)} %get-tuple-element.29), channel_id=1, source_target_pairs={{0,2},{1,3},{2,0},{3,1},{4,6},{5,7},{6,4},{7,5},{8,10},{9,11},{10,... | collective-permute-start | bytes 82952 | tf_op jit(solution)/shard_map/ppermute | solution.py:77
  52.6 6.7 %copy-start.5 = (bf16[216,864]{1,0:T(8,128)(2,1)S(1)}, bf16[216,864]{1,0:T(8,128)(2,1)}, u32[]{:S(2)}) copy-start(bf16[216,864]{1,0:T(8,128)(2,1)} %get-tuple-element.18) | copy-start | bytes 1119748
  52.7 6.9 %copy-start.3 = (f32[864,864]{1,0:T(8,128)S(1)}, f32[864,864]{1,0:T(8,128)}, u32[]{:S(2)}) copy-start(f32[864,864]{1,0:T(8,128)} %copy-done.2) | copy-start | bytes 8957956
  52.7 9.7 %copy-start.9 = (f32[32,32]{1,0:T(8,128)S(1)}, f32[32,32]{1,0:T(8,128)}, u32[]{:S(2)}) copy-start(f32[32,32]{1,0:T(8,128)} %param.11) | copy-start | bytes 12292
  52.7 6.8 %collective-permute-start.15 = (f32[32,1,216]{2,1,0:T(1,128)S(1)}, f32[32,1,216]{2,1,0:T(1,128)S(1)}, u32[]{:S(2)}, u32[]{:S(2)}) collective-permute-start(f32[32,1,216]{2,1,0:T(1,128)S(1)} %get-tuple-element.28), channel_id=1, source_target_pairs={{0,3},{1,2},{2,1},{3,0},{4,7},{5,6},{6,5},{7,4},{8,11},{9,10},{10,... | collective-permute-start | bytes 82952 | tf_op jit(solution)/shard_map/ppermute | solution.py:77
  59.3 7.3 %collective-permute-start.2 = (bf16[216,864]{1,0:T(8,128)(2,1)S(1)}, bf16[216,864]{1,0:T(8,128)(2,1)S(1)}, u32[]{:S(2)}, u32[]{:S(2)}) collective-permute-start(bf16[216,864]{1,0:T(8,128)(2,1)S(1)} %copy-done.5), channel_id=1, source_target_pairs={{0,4},{4,0},{8,12},{12,8},{16,20},{20,16},{24,28},{28,24},{1,5},{5... | collective-permute-start | bytes 1119752 | tf_op jit(solution)/shard_map/ppermute | solution.py:222
  60.6 11.5 %collective-permute-start.4 = (bf16[216,864]{1,0:T(8,128)(2,1)S(1)}, bf16[216,864]{1,0:T(8,128)(2,1)S(1)}, u32[]{:S(2)}, u32[]{:S(2)}) collective-permute-start(bf16[216,864]{1,0:T(8,128)(2,1)S(1)} %add_convert_fusion), channel_id=1, source_target_pairs={{0,8},{4,12},{8,0},{12,4},{16,24},{20,28},{24,16},{28,20},{1,9},{5... | collective-permute-start | bytes 1119752 | tf_op jit(solution)/shard_map/ppermute | solution.py:231
  63.2 11.0 %collective-permute-start.17 = (f32[32,896]{1,0:T(8,128)S(1)}, f32[32,896]{1,0:T(8,128)S(1)}, u32[]{:S(2)}, u32[]{:S(2)}) collective-permute-start(f32[32,896]{1,0:T(8,128)S(1)} %pad_maximum_fusion.2), channel_id=1, source_target_pairs={{0,2},{1,3},{2,0},{3,1},{4,6},{5,7},{6,4},{7,5},{8,10},{9,11},{10,... | collective-permute-start | bytes 344072 | tf_op jit(solution)/shard_map/ppermute | solution.py:39
  64.9 9.3 %collective-permute-start.18 = (f32[32,896]{1,0:T(8,128)S(1)}, f32[32,896]{1,0:T(8,128)S(1)}, u32[]{:S(2)}, u32[]{:S(2)}) collective-permute-start(f32[32,896]{1,0:T(8,128)S(1)} %pad_maximum_fusion.2), channel_id=1, source_target_pairs={{0,3},{1,2},{2,1},{3,0},{4,7},{5,6},{6,5},{7,4},{8,11},{9,10},{10,... | collective-permute-start | bytes 344072 | tf_op jit(solution)/shard_map/ppermute | solution.py:40
  65.9 9.5 %collective-permute-start.16 = (f32[32,896]{1,0:T(8,128)S(1)}, f32[32,896]{1,0:T(8,128)S(1)}, u32[]{:S(2)}, u32[]{:S(2)}) collective-permute-start(f32[32,896]{1,0:T(8,128)S(1)} %pad_maximum_fusion.2), channel_id=1, source_target_pairs={{0,1},{1,0},{2,3},{3,2},{4,5},{5,4},{6,7},{7,6},{8,9},{9,8},{10,11... | collective-permute-start | bytes 344072 | tf_op jit(solution)/shard_map/ppermute | solution.py:37
  72.3 6.7 %collective-permute-start.5 = (bf16[108,864]{1,0:T(8,128)(2,1)S(1)}, bf16[108,864]{1,0:T(8,128)(2,1)S(1)}, u32[]{:S(2)}, u32[]{:S(2)}) collective-permute-start(bf16[108,864]{1,0:T(8,128)(2,1)S(1)} %slice.88), channel_id=1, source_target_pairs={{0,16},{4,20},{8,24},{12,28},{16,0},{20,4},{24,8},{28,12},{1,17},{... | collective-permute-start | bytes 559880 | tf_op jit(solution)/shard_map/ppermute | solution.py:231
  75.5 13.8 %copy-start.7 = (f32[32,896]{1,0:T(8,128)}, f32[32,896]{1,0:T(8,128)S(1)}, u32[]{:S(2)}) copy-start(f32[32,896]{1,0:T(8,128)S(1)} %add_add_fusion) | copy-start | bytes 344068
  80.9 6.2 %collective-permute-start.8 = (bf16[108,1,216]{0,2,1:T(8,128)(2,1)S(1)}, bf16[108,1,216]{0,2,1:T(8,128)(2,1)S(1)}, u32[]{:S(2)}, u32[]{:S(2)}) collective-permute-start(bf16[108,1,216]{0,2,1:T(8,128)(2,1)S(1)} %bitcast.75), channel_id=1, source_target_pairs={{0,3},{1,2},{2,1},{3,0},{4,7},{5,6},{6,5},{7,4},{8,11},{9,10},{10,... | collective-permute-start | bytes 139976 | tf_op jit(solution)/shard_map/ppermute | solution.py:77
  83.3 5.4 %collective-permute-start.7 = (bf16[108,1,216]{0,2,1:T(8,128)(2,1)S(1)}, bf16[108,1,216]{0,2,1:T(8,128)(2,1)S(1)}, u32[]{:S(2)}, u32[]{:S(2)}) collective-permute-start(bf16[108,1,216]{0,2,1:T(8,128)(2,1)S(1)} %bitcast.76), channel_id=1, source_target_pairs={{0,2},{1,3},{2,0},{3,1},{4,6},{5,7},{6,4},{7,5},{8,10},{9,11},{10,... | collective-permute-start | bytes 139976 | tf_op jit(solution)/shard_map/ppermute | solution.py:77
  83.5 5.2 %collective-permute-start.6 = (bf16[108,1,216]{0,2,1:T(8,128)(2,1)S(1)}, bf16[108,1,216]{0,2,1:T(8,128)(2,1)S(1)}, u32[]{:S(2)}, u32[]{:S(2)}) collective-permute-start(bf16[108,1,216]{0,2,1:T(8,128)(2,1)S(1)} %bitcast.77), channel_id=1, source_target_pairs={{0,1},{1,0},{2,3},{3,2},{4,5},{5,4},{6,7},{7,6},{8,9},{9,8},{10,11... | collective-permute-start | bytes 139976 | tf_op jit(solution)/shard_map/ppermute | solution.py:77

commit v19 on v16

--- a/solution.py
+++ b/solution.py
@@ -172,6 +172,13 @@
     n_grains = channels // grain
     contract_cells = (((1,), (1,)), ((), ()))
 
+    cell_ids = sample_idx[0]
+    counts = jnp.sum(
+        (cell_ids[:, None] == jnp.arange(cells, dtype=jnp.int32)[None, :]).astype(f32), axis=0
+    )
+    grad_flat = out_grad[0].reshape(channels, cells)
+    g_part = lax.dot_general(grad_flat, grad_flat, contract_cells, preferred_element_type=f32)
+    volume, counts, g_part = lax.optimization_barrier((volume, counts, g_part))
     block = padded_2(volume, (("space", 2),), 1)
     padded = jnp.pad(block[0], ((0, 0), (0, 0), (1, 1), (1, 1)))
     slab = jnp.transpose(padded, (1, 2, 0, 3))
@@ -180,7 +187,6 @@
     kernel_perm = kernel.reshape(channels, channels, n_taps).transpose(0, 2, 1).reshape(channels, patch)
 
     grad_perm = lax.dot_general(grad_flat, patches_t, contract_cells, preferred_element_type=f32)
-    g_part = lax.dot_general(grad_flat, grad_flat, contract_cells, preferred_element_type=f32)
     terms = jnp.concatenate([grad_perm, g_part], axis=1)
     terms, patches_t = lax.optimization_barrier((terms, patches_t))
     plane = butterfly_sum(terms, ("dp",))
@@ -197,10 +203,6 @@
     g_factor = both[:, patch:]
 
 
-    cell_ids = sample_idx[0]
-    counts = jnp.sum(
-        (cell_ids[:, None] == jnp.arange(cells, dtype=jnp.int32)[None, :]).astype(f32), axis=0
-    )
     weighted = (patches_t.astype(f32) * counts[None, :]).astype(jnp.bfloat16)
     total_samples = sample_idx.shape[1] * n_sp * n_dp
     a_perm = lax.dot_general(

time: 85.5 us -> 87.3 us (1.021)
  waiting for transfers between devices: 11.2 us -> 12.2 us
    ppermute x6, waiting for transfers between devices: 2.65 us -> 4.05 us  [quad_scatter(): lax.ppermute(pick(digit ^ k).astype(wire), axis, partner(axis, k * low))]
    ppermute x2, starting transfers between devices: 1.06 us -> 2.37 us  [butterfly_sum(): other = lax.ppermute(x, axis, partner(axis, low + high))]
    unnamed x23 -> x22, local copies, waits for them, and re-layouts: 2.79 us -> 1.65 us
    optimization_barrier x0 -> x1, local copies, waits for them, and re-layouts: none -> 1.06 us  [on_device(): volume, counts, g_part = lax.optimization_barrier((volume, counts, g_part))]
  transfers between devices with their start and end apart: 18 -> 18, of which waited for: 7 -> 8; matrix products, arithmetic and copies ran while one was open for 31% -> 25% of each run, Pallas kernels for 0% -> 0%
where the time goes in v19:
time: 87.3 us; the launch traced here: 86.9 us
  starting transfers between devices  27.1 us (31%)
  matrix products  22.3 us (26%)
  waiting for transfers between devices  12.2 us (14%)
  other arithmetic  10.2 us (12%)
  local copies, waits for them, and re-layouts  9.07 us (10%)
  Pallas kernels  5.16 us (6%)
  between operations  0.98 us (1%)
    ppermute x6, starting transfers between devices, quad_scatter(): lax.ppermute(pick(digit ^ k).astype(wire), axis, partner(axis, k * low))  9.29 us
    dot_general x1, matrix products, on_device(): lax.dot_general(weighted, patches_t, contract_cells, preferred_element_ty...  7.5 us
    ppermute x1, starting transfers between devices, padded_2(): lax.ppermute(tail, axis, [(i, (i + 1) % count) for i in range(ends)])  6.21 us
    ppermute x3, waiting for transfers between devices, on_device(): lax.ppermute(a_orig[half:].astype(jnp.bfloat16), 'dp', partner('dp', step))  5.3 us
    dot_general x1, matrix products, on_device(): lax.dot_general(grad_flat, patches_t, contract_cells, preferred_element_t...  5.26 us
    pallas_call x1, Pallas kernels, patch_matrix(): pl.pallas_call(body, grid=(3,), in_specs=[pl.BlockSpec(shifted.shape, lam...  5.16 us
    dot_general x1, matrix products, on_device(): forward = jnp.dot(kernel_perm, patches_t, preferred_element_type=f32)  4.48 us
    ppermute x6, waiting for transfers between devices, quad_scatter(): lax.ppermute(pick(digit ^ k).astype(wire), axis, partner(axis, k * low))  4.05 us
  transfers between devices with their start and end apart: 18, of which 8 were waited for; matrix products, arithmetic and copies ran while one was open for 25% of the time, Pallas kernels for 0%

profile of v19, /device:TPU:0, one launch (start us, length us, event | category | flops | bytes accessed | tf_op | source)
XLA Modules:
  0.0 86.9 jit_solution(9617900591637433222)
XLA Ops:
  0.7 3.4 %convert_reduce_fusion = f32[4096]{0:T(1024)S(1)} fusion(s32[1024]{0:T(1024)} %bitcast.78), kind=kLoop, calls=%fused_computation | loop fusion | flops 12578816 | bytes 20480 | tf_op jit(solution)/shard_map/reduce_sum | solution.py:176
  4.1 1.3 %convolution_bitcast_fusion.1 = f32[32,32]{1,0:T(8,128)S(1)} fusion(bf16[32,2,16,128]{3,2,1,0:T(8,128)(2,1)} %bitcast.72), kind=kOutput, calls=%fused_computation.17 | convolution fusion | flops 8388608 | bytes 266240 | tf_op jit(solution)/shard_map/dot_general | solution.py:180
  5.4 1.1 %copy.32 = bf16[1,32,2,16,128]{4,1,3,2,0:T(8,128)(2,1)S(1)} copy(bf16[1,32,2,16,128]{4,3,2,1,0:T(8,128)(2,1)} %param.6) | data formatting | bytes 524288 | tf_op jit(solution)/shard_map/optimization_barrier | solution.py:181
  7.2 1.3 %collective-permute-start.1 = (bf16[1,32,1,16,128]{4,1,3,2,0:T(8,128)(2,1)}, bf16[1,32,1,16,128]{4,1,3,2,0:T(8,128)(2,1)}, u32[]{:S(2)}, u32[]{:S(2)}) collective-permute-start(bf16[1,32,1,16,128]{4,1,3,2,0:T(8,128)(2,1)} %get-tuple-element.31), channel_id=1, source_target_pairs={{1,0},{2,1},{3,2},{5,4},{6,5},{7,6},{9,8},{10,9},{11,10},{13,12},{... | collective-permute-start | bytes 393224 | tf_op jit(solution)/shard_map/ppermute | solution.py:20
  8.5 6.2 %collective-permute-start = (bf16[1,32,1,16,128]{4,1,3,2,0:T(8,128)(2,1)}, bf16[1,32,1,16,128]{4,1,3,2,0:T(8,128)(2,1)}, u32[]{:S(2)}, u32[]{:S(2)}) collective-permute-start(bf16[1,32,1,16,128]{4,1,3,2,0:T(8,128)(2,1)} %get-tuple-element.30), channel_id=1, source_target_pairs={{0,1},{1,2},{2,3},{4,5},{5,6},{6,7},{8,9},{9,10},{10,11},{12,13},{... | collective-permute-start | bytes 393224 | tf_op jit(solution)/shard_map/ppermute | solution.py:18
  14.7 1.7 %fusion.2 = (bf16[864,864]{1,0:T(8,128)(2,1)S(1)}, bf16[864,864]{1,0:T(8,128)(2,1)}) fusion(s32[864]{0:T(1024)S(1)} %fusion.24, s32[864]{0:T(1024)S(1)} %fusion.27), kind=kLoop, calls=%fused_computation.9 | loop fusion | flops 2985984 | bytes 2992896 | tf_op jit(solution)/shard_map/convert_element_type | solution.py:135
  17.9 1.0 %maximum_bitcast_fusion = bf16[32,4,16,128]{3,0,2,1:T(8,128)(2,1)S(1)} fusion(bf16[1,32,1,16,128]{4,1,3,2,0:T(8,128)(2,1)} %collective-permute-done.1, bf16[1,32,2,16,128]{4,1,3,2,0:T(8,128)(2,1)S(1)} %copy.32, bf16[1,32,1,16,128]{4,1,3,2,0:T(8,128)(2,1)} %collective-permute-done), kind=kLoop, calls=%fused_computation.23 | loop fusion | flops 524288 | bytes 1048576 | tf_op jit(solution)/shard_map/squeeze | solution.py:183
  19.7 1.5 %pad_maximum_fusion.src_ref = bf16[3,4,18,32,128]{4,3,2,1,0:T(8,128)(2,1)} fusion(bf16[1,4,18,32,128]{4,3,2,1,0:T(8,128)(2,1)S(1)} %get-tuple-element.25, bf16[1,4,18,32,128]{4,3,2,1,0:T(8,128)(2,1)S(1)} %get-tuple-element.26, bf16[1,4,18,32,128]{4,3,2,1,0:T(8,128)(2,1)S(1)} %get-tuple-element.24), kind=kLoop, calls=%fused_computation.11 | loop fusion | flops 1769472 | bytes 3538944 | tf_op jit(solution)/shard_map/stack | solution.py:109
  21.2 5.2 %shard_map.93 = bf16[864,4096]{1,0:T(8,128)(2,1)} custom-call(bf16[3,4,18,32,128]{4,3,2,1,0:T(8,128)(2,1)} %pad_maximum_fusion.src_ref), custom_call_target="tpu_custom_call" | custom-call | tf_op jit(solution)/shard_map/pallas_call | solution.py:122
  26.4 5.3 %convolution_bitcast_fusion = f32[32,864]{1,0:T(8,128)S(1)} fusion(bf16[864,4096]{1,0:T(8,128)(2,1)} %shard_map.93, bf16[32,4096]{1,0:T(8,128)(2,1)S(1)} %reshape_squeeze.4), kind=kOutput, calls=%fused_computation.16 | convolution fusion | flops 226492416 | bytes 7450624 | tf_op jit(solution)/shard_map/dot_general | solution.py:189
  31.7 1.9 %collective-permute-start.9 = (f32[32,896]{1,0:T(8,128)S(1)}, f32[32,896]{1,0:T(8,128)S(1)}, u32[]{:S(2)}, u32[]{:S(2)}) collective-permute-start(f32[32,896]{1,0:T(8,128)S(1)} %pad_maximum_fusion.1), channel_id=1, source_target_pairs={{0,8},{4,12},{8,0},{12,4},{16,24},{20,28},{24,16},{28,20},{1,9},{5... | collective-permute-start | bytes 344072 | tf_op jit(solution)/shard_map/ppermute | solution.py:39
  33.9 7.5 %multiply_convert_fusion.2 = bf16[864,864]{1,0:T(8,128)(2,1)S(1)} fusion(bf16[864,4096]{1,0:T(8,128)(2,1)S(1)} %copy-done.1, f32[4096]{0:T(1024)S(1)} %convert_reduce_fusion), kind=kOutput, calls=%fused_computation.6 | convolution fusion | flops 6127405056 | bytes 8587264 | tf_op jit(solution)/shard_map/dot_general | solution.py:208
  41.5 2.0 %collective-permute-start.11 = (f32[32,896]{1,0:T(8,128)S(1)}, f32[32,896]{1,0:T(8,128)S(1)}, u32[]{:S(2)}, u32[]{:S(2)}) collective-permute-start(f32[32,896]{1,0:T(8,128)S(1)} %add_add_fusion.1), channel_id=1, source_target_pairs={{0,16},{4,20},{8,24},{12,28},{16,0},{20,4},{24,8},{28,12},{1,17},{... | collective-permute-start | bytes 344072 | tf_op jit(solution)/shard_map/ppermute | solution.py:37
  43.5 1.9 %fusion.32 = f32[864,864]{1,0:T(8,128)S(1)} fusion(bf16[864,864]{1,0:T(8,128)(2,1)S(1)} %copy-done.4, bf16[864,864]{1,0:T(8,128)(2,1)S(1)} %multiply_convert_fusion.2), kind=kOutput, calls=%fused_computation.81 | convolution fusion | flops 1289945088 | bytes 5971968 | tf_op jit(solution)/shard_map/dot_general | solution.py:216
  45.4 1.1 %slice.87 = bf16[432,864]{1,0:T(8,128)(2,1)} slice(f32[864,864]{1,0:T(8,128)S(1)} %fusion.32), slice={[432:864], [0:864]} | slice | bytes 1492992 | tf_op jit(solution)/shard_map/slice | solution.py:223
  48.1 1.5 %collective-permute-start.12 = (f32[32,1,216]{2,1,0:T(1,128)S(1)}, f32[32,1,216]{2,1,0:T(1,128)S(1)}, u32[]{:S(2)}, u32[]{:S(2)}) collective-permute-start(f32[32,1,216]{2,1,0:T(1,128)S(1)} %get-tuple-element.34), channel_id=1, source_target_pairs={{0,1},{1,0},{2,3},{3,2},{4,5},{5,4},{6,7},{7,6},{8,9},{9,8},{10,11... | collective-permute-start | bytes 82952 | tf_op jit(solution)/shard_map/ppermute | solution.py:77
  49.6 3.2 %collective-permute-start.13 = (f32[32,1,216]{2,1,0:T(1,128)S(1)}, f32[32,1,216]{2,1,0:T(1,128)S(1)}, u32[]{:S(2)}, u32[]{:S(2)}) collective-permute-start(f32[32,1,216]{2,1,0:T(1,128)S(1)} %get-tuple-element.33), channel_id=1, source_target_pairs={{0,2},{1,3},{2,0},{3,1},{4,6},{5,7},{6,4},{7,5},{8,10},{9,11},{10,... | collective-permute-start | bytes 82952 | tf_op jit(solution)/shard_map/ppermute | solution.py:77
  52.8 4.5 %fusion.4 = bf16[4,8,32,128]{3,1,2,0:T(8,128)(2,1)S(1)} fusion(bf16[32,864]{1,0:T(8,128)(2,1)S(1)} %reshape.136, bf16[864,4096]{1,0:T(8,128)(2,1)} %shard_map.93), kind=kOutput, calls=%fused_computation.15 | convolution fusion | flops 226623488 | bytes 7395328 | tf_op jit(solution)/shard_map/dot_general | solution.py:218
  57.3 0.7 copy.46
  58.6 1.3 %convert_add_fusion = f32[432,864]{1,0:T(8,128)S(1)} fusion(bf16[432,864]{1,0:T(8,128)(2,1)} %collective-permute-done.2, f32[864,864]{1,0:T(8,128)S(1)} %copy-done.3), kind=kLoop, calls=%fused_computation.13 | loop fusion | flops 746496 | bytes 3732480 | tf_op jit(solution)/shard_map/add | solution.py:224
  60.0 1.6 %collective-permute-start.3 = (bf16[216,864]{1,0:T(8,128)(2,1)S(1)}, bf16[216,864]{1,0:T(8,128)(2,1)S(1)}, u32[]{:S(2)}, u32[]{:S(2)}) collective-permute-start(bf16[216,864]{1,0:T(8,128)(2,1)S(1)} %slice.88), channel_id=1, source_target_pairs={{0,8},{4,12},{8,0},{12,4},{16,24},{20,28},{24,16},{28,20},{1,9},{5... | collective-permute-start | bytes 1119752 | tf_op jit(solution)/shard_map/ppermute | solution.py:223
  62.4 1.0 %collective-permute-start.16 = (f32[32,896]{1,0:T(8,128)S(1)}, f32[32,896]{1,0:T(8,128)S(1)}, u32[]{:S(2)}, u32[]{:S(2)}) collective-permute-start(f32[32,896]{1,0:T(8,128)S(1)} %pad_maximum_fusion.2), channel_id=1, source_target_pairs={{0,2},{1,3},{2,0},{3,1},{4,6},{5,7},{6,4},{7,5},{8,10},{9,11},{10,... | collective-permute-start | bytes 344072 | tf_op jit(solution)/shard_map/ppermute | solution.py:39
  63.4 2.4 %collective-permute-start.17 = (f32[32,896]{1,0:T(8,128)S(1)}, f32[32,896]{1,0:T(8,128)S(1)}, u32[]{:S(2)}, u32[]{:S(2)}) collective-permute-start(f32[32,896]{1,0:T(8,128)S(1)} %pad_maximum_fusion.2), channel_id=1, source_target_pairs={{0,3},{1,2},{2,1},{3,0},{4,7},{5,6},{6,5},{7,4},{8,11},{9,10},{10,... | collective-permute-start | bytes 344072 | tf_op jit(solution)/shard_map/ppermute | solution.py:40
  66.3 3.4 %collective-permute-done.3 = bf16[216,864]{1,0:T(8,128)(2,1)S(1)} collective-permute-done((bf16[216,864]{1,0:T(8,128)(2,1)S(1)}, bf16[216,864]{1,0:T(8,128)(2,1)S(1)}, u32[]{:S(2)}, u32[]{:S(2)}) %collective-permute-start.3) | collective-permute-done | bytes 373280 | tf_op jit(solution)/shard_map/ppermute | solution.py:223
  69.9 0.7 collective-permute-start.4
  70.6 2.1 %collective-permute-done.16 = f32[32,896]{1,0:T(8,128)S(1)} collective-permute-done((f32[32,896]{1,0:T(8,128)S(1)}, f32[32,896]{1,0:T(8,128)S(1)}, u32[]{:S(2)}, u32[]{:S(2)}) %collective-permute-start.16) | collective-permute-done | bytes 114720 | tf_op jit(solution)/shard_map/ppermute | solution.py:39
  73.8 1.9 %collective-permute-done.4 = bf16[108,864]{1,0:T(8,128)(2,1)S(1)} collective-permute-done((bf16[108,864]{1,0:T(8,128)(2,1)S(1)}, bf16[108,864]{1,0:T(8,128)(2,1)S(1)}, u32[]{:S(2)}, u32[]{:S(2)}) %collective-permute-start.4) | collective-permute-done | bytes 186656 | tf_op jit(solution)/shard_map/ppermute | solution.py:223
  75.7 1.0 %fusion.5 = f32[108,864]{1,0:T(8,128)S(1)} fusion(bf16[864,864]{1,0:T(8,128)(2,1)S(1)} %get-tuple-element.22, f32[216,864]{1,0:T(8,128)S(1)} %slice_add_fusion, bf16[108,864]{1,0:T(8,128)(2,1)S(1)} %collective-permute-done.4), kind=kOutput, calls=%fused_computation.26 | convolution fusion | flops 483916032 | bytes 2523648 | tf_op jit(solution)/shard_map/dot_general | solution.py:226
  77.5 3.5 %collective-permute-start.7 = (bf16[108,1,216]{0,2,1:T(8,128)(2,1)S(1)}, bf16[108,1,216]{0,2,1:T(8,128)(2,1)S(1)}, u32[]{:S(2)}, u32[]{:S(2)}) collective-permute-start(bf16[108,1,216]{0,2,1:T(8,128)(2,1)S(1)} %bitcast.75), channel_id=1, source_target_pairs={{0,3},{1,2},{2,1},{3,0},{4,7},{5,6},{6,5},{7,4},{8,11},{9,10},{10,... | collective-permute-start | bytes 139976 | tf_op jit(solution)/shard_map/ppermute | solution.py:77
  81.4 1.0 %collective-permute-start.5 = (bf16[108,1,216]{0,2,1:T(8,128)(2,1)S(1)}, bf16[108,1,216]{0,2,1:T(8,128)(2,1)S(1)}, u32[]{:S(2)}, u32[]{:S(2)}) collective-permute-start(bf16[108,1,216]{0,2,1:T(8,128)(2,1)S(1)} %bitcast.77), channel_id=1, source_target_pairs={{0,1},{1,0},{2,3},{3,2},{4,5},{5,4},{6,7},{7,6},{8,9},{9,8},{10,11... | collective-permute-start | bytes 139976 | tf_op jit(solution)/shard_map/ppermute | solution.py:77
  82.6 1.2 %collective-permute-done.7 = bf16[108,1,216]{0,2,1:T(8,128)(2,1)S(1)} collective-permute-done((bf16[108,1,216]{0,2,1:T(8,128)(2,1)S(1)}, bf16[108,1,216]{0,2,1:T(8,128)(2,1)S(1)}, u32[]{:S(2)}, u32[]{:S(2)}) %collective-permute-start.7) | collective-permute-done | bytes 46688 | tf_op jit(solution)/shard_map/ppermute | solution.py:77
  83.8 2.5 %collective-permute-done.6 = bf16[108,1,216]{0,2,1:T(8,128)(2,1)S(1)} collective-permute-done((bf16[108,1,216]{0,2,1:T(8,128)(2,1)S(1)}, bf16[108,1,216]{0,2,1:T(8,128)(2,1)S(1)}, u32[]{:S(2)}, u32[]{:S(2)}) %collective-permute-start.6) | collective-permute-done | bytes 46688 | tf_op jit(solution)/shard_map/ppermute | solution.py:77
  (71 shorter events, 10.0 us)
Async XLA Ops:
  0.6 61.1 %copy-start = (f32[216,864]{1,0:T(8,128)S(1)}, f32[216,864]{1,0:T(8,128)}, u32[]{:S(2)}) copy-start(f32[216,864]{1,0:T(8,128)} %param.10) | copy-start | bytes 2239492
  0.6 15.8 %copy-start.5 = (bf16[1,32,2,16,128]{4,3,2,1,0:T(8,128)(2,1)S(1)}, bf16[1,32,2,16,128]{4,3,2,1,0:T(8,128)(2,1)}, u32[]{:S(2)}) copy-start(bf16[1,32,2,16,128]{4,3,2,1,0:T(8,128)(2,1)} %param.7) | copy-start | bytes 786436
  0.7 15.9 %copy-start.7 = (bf16[32,864]{1,0:T(8,128)(2,1)S(1)}, bf16[32,864]{1,0:T(8,128)(2,1)}, u32[]{:S(2)}) copy-start(bf16[32,864]{1,0:T(8,128)(2,1)} %param.8) | copy-start | bytes 165892
  7.2 10.7 %collective-permute-start.1 = (bf16[1,32,1,16,128]{4,1,3,2,0:T(8,128)(2,1)}, bf16[1,32,1,16,128]{4,1,3,2,0:T(8,128)(2,1)}, u32[]{:S(2)}, u32[]{:S(2)}) collective-permute-start(bf16[1,32,1,16,128]{4,1,3,2,0:T(8,128)(2,1)} %get-tuple-element.31), channel_id=1, source_target_pairs={{1,0},{2,1},{3,2},{5,4},{6,5},{7,6},{9,8},{10,9},{11,10},{13,12},{... | collective-permute-start | bytes 393224 | tf_op jit(solution)/shard_map/ppermute | solution.py:20
  8.5 9.4 %collective-permute-start = (bf16[1,32,1,16,128]{4,1,3,2,0:T(8,128)(2,1)}, bf16[1,32,1,16,128]{4,1,3,2,0:T(8,128)(2,1)}, u32[]{:S(2)}, u32[]{:S(2)}) collective-permute-start(bf16[1,32,1,16,128]{4,1,3,2,0:T(8,128)(2,1)} %get-tuple-element.30), channel_id=1, source_target_pairs={{0,1},{1,2},{2,3},{4,5},{5,6},{6,7},{8,9},{9,10},{10,11},{12,13},{... | collective-permute-start | bytes 393224 | tf_op jit(solution)/shard_map/ppermute | solution.py:18
  26.4 7.5 %copy-start.1 = (bf16[864,4096]{1,0:T(8,128)(2,1)S(1)}, bf16[864,4096]{1,0:T(8,128)(2,1)}, u32[]{:S(2)}) copy-start(bf16[864,4096]{1,0:T(8,128)(2,1)} %shard_map.93) | copy-start | bytes 21233668
  31.7 11.8 %copy-start.4 = (bf16[864,864]{1,0:T(8,128)(2,1)S(1)}, bf16[864,864]{1,0:T(8,128)(2,1)}, u32[]{:S(2)}) copy-start(bf16[864,864]{1,0:T(8,128)(2,1)} %get-tuple-element.18) | copy-start | bytes 4478980
  31.7 9.7 %collective-permute-start.9 = (f32[32,896]{1,0:T(8,128)S(1)}, f32[32,896]{1,0:T(8,128)S(1)}, u32[]{:S(2)}, u32[]{:S(2)}) collective-permute-start(f32[32,896]{1,0:T(8,128)S(1)} %pad_maximum_fusion.1), channel_id=1, source_target_pairs={{0,8},{4,12},{8,0},{12,4},{16,24},{20,28},{24,16},{28,20},{1,9},{5... | collective-permute-start | bytes 344072 | tf_op jit(solution)/shard_map/ppermute | solution.py:39
  33.7 7.7 %collective-permute-start.10 = (f32[32,896]{1,0:T(8,128)S(1)}, f32[32,896]{1,0:T(8,128)S(1)}, u32[]{:S(2)}, u32[]{:S(2)}) collective-permute-start(f32[32,896]{1,0:T(8,128)S(1)} %pad_maximum_fusion.1), channel_id=1, source_target_pairs={{0,12},{4,8},{8,4},{12,0},{16,28},{20,24},{24,20},{28,16},{1,13},{... | collective-permute-start | bytes 344072 | tf_op jit(solution)/shard_map/ppermute | solution.py:40
  33.7 7.7 %collective-permute-start.8 = (f32[32,896]{1,0:T(8,128)S(1)}, f32[32,896]{1,0:T(8,128)S(1)}, u32[]{:S(2)}, u32[]{:S(2)}) collective-permute-start(f32[32,896]{1,0:T(8,128)S(1)} %pad_maximum_fusion.1), channel_id=1, source_target_pairs={{0,4},{4,0},{8,12},{12,8},{16,20},{20,16},{24,28},{28,24},{1,5},{5... | collective-permute-start | bytes 344072 | tf_op jit(solution)/shard_map/ppermute | solution.py:37
  41.5 5.4 %collective-permute-start.11 = (f32[32,896]{1,0:T(8,128)S(1)}, f32[32,896]{1,0:T(8,128)S(1)}, u32[]{:S(2)}, u32[]{:S(2)}) collective-permute-start(f32[32,896]{1,0:T(8,128)S(1)} %add_add_fusion.1), channel_id=1, source_target_pairs={{0,16},{4,20},{8,24},{12,28},{16,0},{20,4},{24,8},{28,12},{1,17},{... | collective-permute-start | bytes 344072 | tf_op jit(solution)/shard_map/ppermute | solution.py:37
  45.4 1.9 %copy-start.2 = (f32[864,864]{1,0:T(8,128)}, f32[864,864]{1,0:T(8,128)S(1)}, u32[]{:S(2)}) copy-start(f32[864,864]{1,0:T(8,128)S(1)} %fusion.32) | copy-start | bytes 8957956
  46.5 12.1 %collective-permute-start.2 = (bf16[432,864]{1,0:T(8,128)(2,1)}, bf16[432,864]{1,0:T(8,128)(2,1)}, u32[]{:S(2)}, u32[]{:S(2)}) collective-permute-start(bf16[432,864]{1,0:T(8,128)(2,1)} %slice.87), channel_id=1, source_target_pairs={{0,4},{4,0},{8,12},{12,8},{16,20},{20,16},{24,28},{28,24},{1,5},{5... | collective-permute-start | bytes 2239496 | tf_op jit(solution)/shard_map/ppermute | solution.py:223
  48.1 10.0 %collective-permute-start.12 = (f32[32,1,216]{2,1,0:T(1,128)S(1)}, f32[32,1,216]{2,1,0:T(1,128)S(1)}, u32[]{:S(2)}, u32[]{:S(2)}) collective-permute-start(f32[32,1,216]{2,1,0:T(1,128)S(1)} %get-tuple-element.34), channel_id=1, source_target_pairs={{0,1},{1,0},{2,3},{3,2},{4,5},{5,4},{6,7},{7,6},{8,9},{9,8},{10,11... | collective-permute-start | bytes 82952 | tf_op jit(solution)/shard_map/ppermute | solution.py:77
  49.6 8.5 %collective-permute-start.13 = (f32[32,1,216]{2,1,0:T(1,128)S(1)}, f32[32,1,216]{2,1,0:T(1,128)S(1)}, u32[]{:S(2)}, u32[]{:S(2)}) collective-permute-start(f32[32,1,216]{2,1,0:T(1,128)S(1)} %get-tuple-element.33), channel_id=1, source_target_pairs={{0,2},{1,3},{2,0},{3,1},{4,6},{5,7},{6,4},{7,5},{8,10},{9,11},{10,... | collective-permute-start | bytes 82952 | tf_op jit(solution)/shard_map/ppermute | solution.py:77
  52.8 5.8 %copy-start.3 = (f32[864,864]{1,0:T(8,128)S(1)}, f32[864,864]{1,0:T(8,128)}, u32[]{:S(2)}) copy-start(f32[864,864]{1,0:T(8,128)} %copy-done.2) | copy-start | bytes 8957956
  52.8 5.7 %collective-permute-start.14 = (f32[32,1,216]{2,1,0:T(1,128)S(1)}, f32[32,1,216]{2,1,0:T(1,128)S(1)}, u32[]{:S(2)}, u32[]{:S(2)}) collective-permute-start(f32[32,1,216]{2,1,0:T(1,128)S(1)} %get-tuple-element.32), channel_id=1, source_target_pairs={{0,3},{1,2},{2,1},{3,0},{4,7},{5,6},{6,5},{7,4},{8,11},{9,10},{10,... | collective-permute-start | bytes 82952 | tf_op jit(solution)/shard_map/ppermute | solution.py:77
  57.3 4.2 %copy-start.8 = (f32[32,32]{1,0:T(8,128)S(1)}, f32[32,32]{1,0:T(8,128)}, u32[]{:S(2)}) copy-start(f32[32,32]{1,0:T(8,128)} %param.11) | copy-start | bytes 12292
  60.0 9.7 %collective-permute-start.3 = (bf16[216,864]{1,0:T(8,128)(2,1)S(1)}, bf16[216,864]{1,0:T(8,128)(2,1)S(1)}, u32[]{:S(2)}, u32[]{:S(2)}) collective-permute-start(bf16[216,864]{1,0:T(8,128)(2,1)S(1)} %slice.88), channel_id=1, source_target_pairs={{0,8},{4,12},{8,0},{12,4},{16,24},{20,28},{24,16},{28,20},{1,9},{5... | collective-permute-start | bytes 1119752 | tf_op jit(solution)/shard_map/ppermute | solution.py:223
  62.4 10.3 %collective-permute-start.16 = (f32[32,896]{1,0:T(8,128)S(1)}, f32[32,896]{1,0:T(8,128)S(1)}, u32[]{:S(2)}, u32[]{:S(2)}) collective-permute-start(f32[32,896]{1,0:T(8,128)S(1)} %pad_maximum_fusion.2), channel_id=1, source_target_pairs={{0,2},{1,3},{2,0},{3,1},{4,6},{5,7},{6,4},{7,5},{8,10},{9,11},{10,... | collective-permute-start | bytes 344072 | tf_op jit(solution)/shard_map/ppermute | solution.py:39
  63.4 9.3 %collective-permute-start.17 = (f32[32,896]{1,0:T(8,128)S(1)}, f32[32,896]{1,0:T(8,128)S(1)}, u32[]{:S(2)}, u32[]{:S(2)}) collective-permute-start(f32[32,896]{1,0:T(8,128)S(1)} %pad_maximum_fusion.2), channel_id=1, source_target_pairs={{0,3},{1,2},{2,1},{3,0},{4,7},{5,6},{6,5},{7,4},{8,11},{9,10},{10,... | collective-permute-start | bytes 344072 | tf_op jit(solution)/shard_map/ppermute | solution.py:40
  65.8 7.2 %collective-permute-start.15 = (f32[32,896]{1,0:T(8,128)S(1)}, f32[32,896]{1,0:T(8,128)S(1)}, u32[]{:S(2)}, u32[]{:S(2)}) collective-permute-start(f32[32,896]{1,0:T(8,128)S(1)} %pad_maximum_fusion.2), channel_id=1, source_target_pairs={{0,1},{1,0},{2,3},{3,2},{4,5},{5,4},{6,7},{7,6},{8,9},{9,8},{10,11... | collective-permute-start | bytes 344072 | tf_op jit(solution)/shard_map/ppermute | solution.py:37
  69.9 5.8 %collective-permute-start.4 = (bf16[108,864]{1,0:T(8,128)(2,1)S(1)}, bf16[108,864]{1,0:T(8,128)(2,1)S(1)}, u32[]{:S(2)}, u32[]{:S(2)}) collective-permute-start(bf16[108,864]{1,0:T(8,128)(2,1)S(1)} %slice.89), channel_id=1, source_target_pairs={{0,16},{4,20},{8,24},{12,28},{16,0},{20,4},{24,8},{28,12},{1,17},{... | collective-permute-start | bytes 559880 | tf_op jit(solution)/shard_map/ppermute | solution.py:223
  73.1 13.8 %copy-start.6 = (f32[32,896]{1,0:T(8,128)}, f32[32,896]{1,0:T(8,128)S(1)}, u32[]{:S(2)}) copy-start(f32[32,896]{1,0:T(8,128)S(1)} %add_add_fusion) | copy-start | bytes 344068
  77.5 6.2 %collective-permute-start.7 = (bf16[108,1,216]{0,2,1:T(8,128)(2,1)S(1)}, bf16[108,1,216]{0,2,1:T(8,128)(2,1)S(1)}, u32[]{:S(2)}, u32[]{:S(2)}) collective-permute-start(bf16[108,1,216]{0,2,1:T(8,128)(2,1)S(1)} %bitcast.75), channel_id=1, source_target_pairs={{0,3},{1,2},{2,1},{3,0},{4,7},{5,6},{6,5},{7,4},{8,11},{9,10},{10,... | collective-permute-start | bytes 139976 | tf_op jit(solution)/shard_map/ppermute | solution.py:77
  81.1 5.1 %collective-permute-start.6 = (bf16[108,1,216]{0,2,1:T(8,128)(2,1)S(1)}, bf16[108,1,216]{0,2,1:T(8,128)(2,1)S(1)}, u32[]{:S(2)}, u32[]{:S(2)}) collective-permute-start(bf16[108,1,216]{0,2,1:T(8,128)(2,1)S(1)} %bitcast.76), channel_id=1, source_target_pairs={{0,2},{1,3},{2,0},{3,1},{4,6},{5,7},{6,4},{7,5},{8,10},{9,11},{10,... | collective-permute-start | bytes 139976 | tf_op jit(solution)/shard_map/ppermute | solution.py:77
  81.4 4.9 %collective-permute-start.5 = (bf16[108,1,216]{0,2,1:T(8,128)(2,1)S(1)}, bf16[108,1,216]{0,2,1:T(8,128)(2,1)S(1)}, u32[]{:S(2)}, u32[]{:S(2)}) collective-permute-start(bf16[108,1,216]{0,2,1:T(8,128)(2,1)S(1)} %bitcast.77), channel_id=1, source_target_pairs={{0,1},{1,0},{2,3},{3,2},{4,5},{5,4},{6,7},{7,6},{8,9},{9,8},{10,11... | collective-permute-start | bytes 139976 | tf_op jit(solution)/shard_map/ppermute | solution.py:77

commit v20 on v16

--- a/solution.py
+++ b/solution.py
@@ -179,23 +179,6 @@
     grad_flat = out_grad[0].reshape(channels, cells)
     kernel_perm = kernel.reshape(channels, channels, n_taps).transpose(0, 2, 1).reshape(channels, patch)
 
-    grad_perm = lax.dot_general(grad_flat, patches_t, contract_cells, preferred_element_type=f32)
-    g_part = lax.dot_general(grad_flat, grad_flat, contract_cells, preferred_element_type=f32)
-    terms = jnp.concatenate([grad_perm, g_part], axis=1)
-    terms, patches_t = lax.optimization_barrier((terms, patches_t))
-    plane = butterfly_sum(terms, ("dp",))
-    grad_plane = (
-        plane[:, :patch].reshape(channels, n_taps, channels).transpose(0, 2, 1).reshape(channels, patch)
-    )
-    own_cols = quad_scatter(
-        grad_plane.reshape(channels, n_sp, patch // n_sp), "space", 1, wire=f32
-    ).reshape(channels, patch // n_sp)
-    left = jnp.dot(g_inverse, own_cols, precision=highest)
-    partial = jnp.dot(left, a_inverse, precision=highest)
-    both = butterfly_sum(jnp.concatenate([partial, plane[:, patch:]], axis=1), ("space",))
-    pre_grad = both[:, :patch]
-    g_factor = both[:, patch:]
-
 
     cell_ids = sample_idx[0]
     counts = jnp.sum(
@@ -212,7 +195,22 @@
         (tap_order(channels, n_taps), halving_order(channels, n_taps, rows, "dp"), a_perm.astype(jnp.bfloat16))
     )
     a_rows = jnp.dot(placed, a_bf, preferred_element_type=f32)
-    a_orig, kernel_perm = lax.optimization_barrier((a_rows, kernel_perm))
+    a_orig, kernel_perm, grad_late = lax.optimization_barrier((a_rows, kernel_perm, grad_flat))
+    grad_perm = lax.dot_general(grad_late, patches_t, contract_cells, preferred_element_type=f32)
+    g_part = lax.dot_general(grad_late, grad_late, contract_cells, preferred_element_type=f32)
+    terms = jnp.concatenate([grad_perm, g_part], axis=1)
+    plane = butterfly_sum(terms, ("dp",))
+    grad_plane = (
+        plane[:, :patch].reshape(channels, n_taps, channels).transpose(0, 2, 1).reshape(channels, patch)
+    )
+    own_cols = quad_scatter(
+        grad_plane.reshape(channels, n_sp, patch // n_sp), "space", 1, wire=f32
+    ).reshape(channels, patch // n_sp)
+    left = jnp.dot(g_inverse, own_cols, precision=highest)
+    partial = jnp.dot(left, a_inverse, precision=highest)
+    both = butterfly_sum(jnp.concatenate([partial, plane[:, patch:]], axis=1), ("space",))
+    pre_grad = both[:, :patch]
+    g_factor = both[:, patch:]
     forward = jnp.dot(kernel_perm, patches_t, preferred_element_type=f32)
     conv_out = forward.astype(jnp.bfloat16).reshape(1, channels, planes, y_cells, x_cells)
     step = 1

time: 85.5 us -> 98.1 us (1.15)
  waiting for transfers between devices: 11.2 us -> 19.4 us
  matrix products: 22.1 us -> 25 us
    dot_general x1, matrix products: 7.49 us -> 12.8 us  [on_device(): lax.dot_general(weighted, patches_t, contract_cells, preferred_element_ty...]
    dot_general x2, matrix products: 6.56 us -> 2.34 us  [the longest x1 2.13 us: on_device(): lax.dot_general(grad_late, patches_t, contract_cells, preferred_element_t...]
    ppermute x2, waiting for transfers between devices: 0.01 us -> 3.26 us  [butterfly_sum(): other = lax.ppermute(x, axis, partner(axis, low + high))]
    ppermute x6, waiting for transfers between devices: 2.65 us -> 5.7 us  [quad_scatter(): lax.ppermute(pick(digit ^ k).astype(wire), axis, partner(axis, k * low))]
    ppermute x2, waiting for transfers between devices: 2.32 us -> 4.57 us  [butterfly_sum(): pair = lax.ppermute(x, axis, partner(axis, high))]
    dot_general x1, matrix products: 1.92 us -> 3.62 us  [on_device(): a_rows = jnp.dot(placed, a_bf, preferred_element_type=f32)]
    slice x3, local copies, waits for them, and re-layouts: 1.14 us -> 2.43 us  [on_device(): a_orig[half:].astype(jnp.bfloat16)]
    ppermute x3, waiting for transfers between devices: 5.76 us -> 4.64 us  [on_device(): lax.ppermute(a_orig[half:].astype(jnp.bfloat16), 'dp', partner('dp', step))]
  transfers between devices with their start and end apart: 18 -> 18, of which waited for: 7 -> 9; matrix products, arithmetic and copies ran while one was open for 31% -> 17% of each run, Pallas kernels for 0% -> 0%
where the time goes in v20:
time: 98.1 us; the launch traced here: 97.8 us
  starting transfers between devices  27.1 us (28%)
  matrix products  25 us (25%)
  waiting for transfers between devices  19.4 us (20%)
  other arithmetic  10.1 us (10%)
  local copies, waits for them, and re-layouts  10 us (10%)
  Pallas kernels  5.17 us (5%)
    dot_general x1, matrix products, on_device(): lax.dot_general(weighted, patches_t, contract_cells, preferred_element_ty...  12.8 us
    ppermute x6, starting transfers between devices, quad_scatter(): lax.ppermute(pick(digit ^ k).astype(wire), axis, partner(axis, k * low))  9.87 us
    ppermute x6, waiting for transfers between devices, quad_scatter(): lax.ppermute(pick(digit ^ k).astype(wire), axis, partner(axis, k * low))  5.7 us
    ppermute x1, starting transfers between devices, padded_2(): lax.ppermute(tail, axis, [(i, (i + 1) % count) for i in range(ends)])  5.58 us
    pallas_call x1, Pallas kernels, patch_matrix(): pl.pallas_call(body, grid=(3,), in_specs=[pl.BlockSpec(shifted.shape, lam...  5.17 us
    ppermute x3, waiting for transfers between devices, on_device(): lax.ppermute(a_orig[half:].astype(jnp.bfloat16), 'dp', partner('dp', step))  4.64 us
    ppermute x2, waiting for transfers between devices, butterfly_sum(): pair = lax.ppermute(x, axis, partner(axis, high))  4.57 us
    dot_general x1, matrix products, on_device(): forward = jnp.dot(kernel_perm, patches_t, preferred_element_type=f32)  4.47 us
  transfers between devices with their start and end apart: 18, of which 9 were waited for; matrix products, arithmetic and copies ran while one was open for 17% of the time, Pallas kernels for 0%

profile of v20, /device:TPU:0, one launch (start us, length us, event | category | flops | bytes accessed | tf_op | source)
XLA Modules:
  0.0 97.8 jit_solution(18209746903498573887)
XLA Ops:
  0.7 1.1 %copy.26 = bf16[1,32,2,16,128]{4,1,3,2,0:T(8,128)(2,1)S(1)} copy(bf16[1,32,2,16,128]{4,3,2,1,0:T(8,128)(2,1)} %param.6) | data formatting | bytes 524288 | tf_op args[0]
  2.5 5.6 %collective-permute-start = (bf16[1,32,1,16,128]{4,1,3,2,0:T(8,128)(2,1)}, bf16[1,32,1,16,128]{4,1,3,2,0:T(8,128)(2,1)}, u32[]{:S(2)}, u32[]{:S(2)}) collective-permute-start(bf16[1,32,1,16,128]{4,1,3,2,0:T(8,128)(2,1)} %get-tuple-element.22), channel_id=1, source_target_pairs={{0,1},{1,2},{2,3},{4,5},{5,6},{6,7},{8,9},{9,10},{10,11},{12,13},{... | collective-permute-start | bytes 393224 | tf_op jit(solution)/shard_map/ppermute | solution.py:18
  8.1 1.3 %collective-permute-start.1 = (bf16[1,32,1,16,128]{4,1,3,2,0:T(8,128)(2,1)}, bf16[1,32,1,16,128]{4,1,3,2,0:T(8,128)(2,1)}, u32[]{:S(2)}, u32[]{:S(2)}) collective-permute-start(bf16[1,32,1,16,128]{4,1,3,2,0:T(8,128)(2,1)} %get-tuple-element.23), channel_id=1, source_target_pairs={{1,0},{2,1},{3,2},{5,4},{6,5},{7,6},{9,8},{10,9},{11,10},{13,12},{... | collective-permute-start | bytes 393224 | tf_op jit(solution)/shard_map/ppermute | solution.py:20
  9.4 3.4 %convert_reduce_fusion = f32[4096]{0:T(1024)S(1)} fusion(s32[1024]{0:T(1024)} %bitcast.72), kind=kLoop, calls=%fused_computation | loop fusion | flops 12578816 | bytes 20480 | tf_op jit(solution)/shard_map/reduce_sum | solution.py:184
  12.8 1.7 %fusion.2 = (bf16[864,864]{1,0:T(8,128)(2,1)S(1)}, bf16[864,864]{1,0:T(8,128)(2,1)}) fusion(s32[864]{0:T(1024)S(1)} %fusion.23, s32[864]{0:T(1024)S(1)} %fusion.26), kind=kLoop, calls=%fused_computation.9 | loop fusion | flops 2985984 | bytes 2992896 | tf_op jit(solution)/shard_map/convert_element_type | solution.py:135
  15.9 1.0 %maximum_bitcast_fusion = bf16[32,4,16,128]{3,0,2,1:T(8,128)(2,1)S(1)} fusion(bf16[1,32,1,16,128]{4,1,3,2,0:T(8,128)(2,1)} %collective-permute-done.1, bf16[1,32,2,16,128]{4,1,3,2,0:T(8,128)(2,1)S(1)} %copy.26, bf16[1,32,1,16,128]{4,1,3,2,0:T(8,128)(2,1)} %collective-permute-done), kind=kLoop, calls=%fused_computation.21 | loop fusion | flops 524288 | bytes 1048576 | tf_op jit(solution)/shard_map/squeeze | solution.py:176
  17.8 1.5 %pad_maximum_fusion.src_ref = bf16[3,4,18,32,128]{4,3,2,1,0:T(8,128)(2,1)} fusion(bf16[1,4,18,32,128]{4,3,2,1,0:T(8,128)(2,1)S(1)} %get-tuple-element.17, bf16[1,4,18,32,128]{4,3,2,1,0:T(8,128)(2,1)S(1)} %get-tuple-element.18, bf16[1,4,18,32,128]{4,3,2,1,0:T(8,128)(2,1)S(1)} %get-tuple-element.16), kind=kLoop, calls=%fused_computation.11 | loop fusion | flops 1769472 | bytes 3538944 | tf_op jit(solution)/shard_map/stack | solution.py:109
  19.3 5.2 %shard_map.93 = bf16[864,4096]{1,0:T(8,128)(2,1)} custom-call(bf16[3,4,18,32,128]{4,3,2,1,0:T(8,128)(2,1)} %pad_maximum_fusion.src_ref), custom_call_target="tpu_custom_call" | custom-call | tf_op jit(solution)/shard_map/pallas_call | solution.py:122
  24.4 12.8 %multiply_convert_fusion.2 = bf16[864,864]{1,0:T(8,128)(2,1)S(1)} fusion(bf16[864,4096]{1,0:T(8,128)(2,1)} %shard_map.93, f32[4096]{0:T(1024)S(1)} %convert_reduce_fusion), kind=kOutput, calls=%fused_computation.6 | convolution fusion | flops 6127405056 | bytes 8587264 | tf_op jit(solution)/shard_map/dot_general | solution.py:189
  37.2 3.6 %fusion.31 = f32[864,864]{1,0:T(8,128)} fusion(bf16[864,864]{1,0:T(8,128)(2,1)S(1)} %copy-done.3, bf16[864,864]{1,0:T(8,128)(2,1)S(1)} %multiply_convert_fusion.2), kind=kOutput, calls=%fused_computation.78 | convolution fusion | flops 1289945088 | bytes 5971968 | tf_op jit(solution)/shard_map/dot_general | solution.py:197
  40.9 2.1 %fusion.32 = f32[32,864]{1,0:T(8,128)S(1)} fusion(bf16[32,4096]{1,0:T(8,128)(2,1)S(1)} %reshape_squeeze.3, bf16[864,4096]{1,0:T(8,128)(2,1)S(1)} %copy-done.1), kind=kOutput, calls=%fused_computation.79 | convolution fusion | flops 226492416 | bytes 7450624 | tf_op jit(solution)/shard_map/dot_general | solution.py:199
  43.9 1.0 collective-permute-start.8
  45.4 3.3 %collective-permute-done.10 = f32[32,896]{1,0:T(8,128)S(1)} collective-permute-done((f32[32,896]{1,0:T(8,128)S(1)}, f32[32,896]{1,0:T(8,128)S(1)}, u32[]{:S(2)}, u32[]{:S(2)}) %collective-permute-start.10) | collective-permute-done | bytes 114720 | tf_op jit(solution)/shard_map/ppermute | solution.py:40
  48.7 2.5 %collective-permute-done.9 = f32[32,896]{1,0:T(8,128)S(1)} collective-permute-done((f32[32,896]{1,0:T(8,128)S(1)}, f32[32,896]{1,0:T(8,128)S(1)}, u32[]{:S(2)}, u32[]{:S(2)}) %collective-permute-start.9) | collective-permute-done | bytes 114720 | tf_op jit(solution)/shard_map/ppermute | solution.py:39
  51.3 1.5 %collective-permute-start.11 = (f32[32,896]{1,0:T(8,128)S(1)}, f32[32,896]{1,0:T(8,128)S(1)}, u32[]{:S(2)}, u32[]{:S(2)}) collective-permute-start(f32[32,896]{1,0:T(8,128)S(1)} %add_add_fusion.1), channel_id=1, source_target_pairs={{0,16},{4,20},{8,24},{12,28},{16,0},{20,4},{24,8},{28,12},{1,17},{... | collective-permute-start | bytes 344072 | tf_op jit(solution)/shard_map/ppermute | solution.py:37
  52.8 2.4 %slice.87 = bf16[432,864]{1,0:T(8,128)(2,1)} slice(f32[864,864]{1,0:T(8,128)} %fusion.31), slice={[432:864], [0:864]} | slice | bytes 1492992 | tf_op jit(solution)/shard_map/slice | solution.py:219
  55.2 1.2 %collective-permute-done.11 = f32[32,896]{1,0:T(8,128)S(1)} collective-permute-done((f32[32,896]{1,0:T(8,128)S(1)}, f32[32,896]{1,0:T(8,128)S(1)}, u32[]{:S(2)}, u32[]{:S(2)}) %collective-permute-start.11) | collective-permute-done | bytes 114720 | tf_op jit(solution)/shard_map/ppermute | solution.py:37
  57.2 2.7 %collective-permute-start.12 = (f32[32,1,216]{2,1,0:T(1,128)S(1)}, f32[32,1,216]{2,1,0:T(1,128)S(1)}, u32[]{:S(2)}, u32[]{:S(2)}) collective-permute-start(f32[32,1,216]{2,1,0:T(1,128)S(1)} %get-tuple-element.26), channel_id=1, source_target_pairs={{0,1},{1,0},{2,3},{3,2},{4,5},{5,4},{6,7},{7,6},{8,9},{9,8},{10,11... | collective-permute-start | bytes 82952 | tf_op jit(solution)/shard_map/ppermute | solution.py:77
  59.9 2.6 %collective-permute-start.13 = (f32[32,1,216]{2,1,0:T(1,128)S(1)}, f32[32,1,216]{2,1,0:T(1,128)S(1)}, u32[]{:S(2)}, u32[]{:S(2)}) collective-permute-start(f32[32,1,216]{2,1,0:T(1,128)S(1)} %get-tuple-element.25), channel_id=1, source_target_pairs={{0,2},{1,3},{2,0},{3,1},{4,6},{5,7},{6,4},{7,5},{8,10},{9,11},{10,... | collective-permute-start | bytes 82952 | tf_op jit(solution)/shard_map/ppermute | solution.py:77
  62.5 4.5 %fusion.4 = bf16[4,8,32,128]{3,1,2,0:T(8,128)(2,1)S(1)} fusion(bf16[32,864]{1,0:T(8,128)(2,1)S(1)} %reshape.131, bf16[864,4096]{1,0:T(8,128)(2,1)} %shard_map.93), kind=kOutput, calls=%fused_computation.15 | convolution fusion | flops 226623488 | bytes 7395328 | tf_op jit(solution)/shard_map/dot_general | solution.py:214
  67.0 0.7 copy.39
  68.3 1.3 %convert_add_fusion = f32[432,864]{1,0:T(8,128)S(1)} fusion(bf16[432,864]{1,0:T(8,128)(2,1)} %collective-permute-done.2, f32[864,864]{1,0:T(8,128)S(1)} %copy-done.2), kind=kLoop, calls=%fused_computation.13 | loop fusion | flops 746496 | bytes 3732480 | tf_op jit(solution)/shard_map/add | solution.py:220
  69.7 0.8 collective-permute-start.3
  71.8 3.4 %collective-permute-start.16 = (f32[32,896]{1,0:T(8,128)S(1)}, f32[32,896]{1,0:T(8,128)S(1)}, u32[]{:S(2)}, u32[]{:S(2)}) collective-permute-start(f32[32,896]{1,0:T(8,128)S(1)} %pad_maximum_fusion.2), channel_id=1, source_target_pairs={{0,2},{1,3},{2,0},{3,1},{4,6},{5,7},{6,4},{7,5},{8,10},{9,11},{10,... | collective-permute-start | bytes 344072 | tf_op jit(solution)/shard_map/ppermute | solution.py:39
  75.7 3.3 %collective-permute-done.3 = bf16[216,864]{1,0:T(8,128)(2,1)S(1)} collective-permute-done((bf16[216,864]{1,0:T(8,128)(2,1)S(1)}, bf16[216,864]{1,0:T(8,128)(2,1)S(1)}, u32[]{:S(2)}, u32[]{:S(2)}) %collective-permute-start.3) | collective-permute-done | bytes 373280 | tf_op jit(solution)/shard_map/ppermute | solution.py:219
  79.1 1.6 %collective-permute-start.4 = (bf16[108,864]{1,0:T(8,128)(2,1)S(1)}, bf16[108,864]{1,0:T(8,128)(2,1)S(1)}, u32[]{:S(2)}, u32[]{:S(2)}) collective-permute-start(bf16[108,864]{1,0:T(8,128)(2,1)S(1)} %slice.89), channel_id=1, source_target_pairs={{0,16},{4,20},{8,24},{12,28},{16,0},{20,4},{24,8},{28,12},{1,17},{... | collective-permute-start | bytes 559880 | tf_op jit(solution)/shard_map/ppermute | solution.py:219
  80.6 2.1 %collective-permute-done.16 = f32[32,896]{1,0:T(8,128)S(1)} collective-permute-done((f32[32,896]{1,0:T(8,128)S(1)}, f32[32,896]{1,0:T(8,128)S(1)}, u32[]{:S(2)}, u32[]{:S(2)}) %collective-permute-start.16) | collective-permute-done | bytes 114720 | tf_op jit(solution)/shard_map/ppermute | solution.py:39
  83.5 1.4 %collective-permute-done.4 = bf16[108,864]{1,0:T(8,128)(2,1)S(1)} collective-permute-done((bf16[108,864]{1,0:T(8,128)(2,1)S(1)}, bf16[108,864]{1,0:T(8,128)(2,1)S(1)}, u32[]{:S(2)}, u32[]{:S(2)}) %collective-permute-start.4) | collective-permute-done | bytes 186656 | tf_op jit(solution)/shard_map/ppermute | solution.py:219
  84.9 1.1 %fusion.5 = f32[108,864]{1,0:T(8,128)S(1)} fusion(bf16[864,864]{1,0:T(8,128)(2,1)S(1)} %get-tuple-element.14, f32[216,864]{1,0:T(8,128)S(1)} %slice_add_fusion, bf16[108,864]{1,0:T(8,128)(2,1)S(1)} %collective-permute-done.4), kind=kOutput, calls=%fused_computation.24 | convolution fusion | flops 483916032 | bytes 2523648 | tf_op jit(solution)/shard_map/dot_general | solution.py:222
  87.6 3.4 %collective-permute-start.6 = (bf16[108,1,216]{0,2,1:T(8,128)(2,1)S(1)}, bf16[108,1,216]{0,2,1:T(8,128)(2,1)S(1)}, u32[]{:S(2)}, u32[]{:S(2)}) collective-permute-start(bf16[108,1,216]{0,2,1:T(8,128)(2,1)S(1)} %bitcast.70), channel_id=1, source_target_pairs={{0,2},{1,3},{2,0},{3,1},{4,6},{5,7},{6,4},{7,5},{8,10},{9,11},{10,... | collective-permute-start | bytes 139976 | tf_op jit(solution)/shard_map/ppermute | solution.py:77
  91.8 2.0 %collective-permute-done.6 = bf16[108,1,216]{0,2,1:T(8,128)(2,1)S(1)} collective-permute-done((bf16[108,1,216]{0,2,1:T(8,128)(2,1)S(1)}, bf16[108,1,216]{0,2,1:T(8,128)(2,1)S(1)}, u32[]{:S(2)}, u32[]{:S(2)}) %collective-permute-start.6) | collective-permute-done | bytes 46688 | tf_op jit(solution)/shard_map/ppermute | solution.py:77
  93.8 3.3 %collective-permute-done.7 = bf16[108,1,216]{0,2,1:T(8,128)(2,1)S(1)} collective-permute-done((bf16[108,1,216]{0,2,1:T(8,128)(2,1)S(1)}, bf16[108,1,216]{0,2,1:T(8,128)(2,1)S(1)}, u32[]{:S(2)}, u32[]{:S(2)}) %collective-permute-start.7) | collective-permute-done | bytes 46688 | tf_op jit(solution)/shard_map/ppermute | solution.py:77
  (69 shorter events, 11.8 us)
Async XLA Ops:
  0.6 70.0 %copy-start = (f32[216,864]{1,0:T(8,128)S(1)}, f32[216,864]{1,0:T(8,128)}, u32[]{:S(2)}) copy-start(f32[216,864]{1,0:T(8,128)} %param.10) | copy-start | bytes 2239492
  0.6 13.9 %copy-start.6 = (bf16[32,864]{1,0:T(8,128)(2,1)S(1)}, bf16[32,864]{1,0:T(8,128)(2,1)}, u32[]{:S(2)}) copy-start(bf16[32,864]{1,0:T(8,128)(2,1)} %param.8) | copy-start | bytes 165892
  0.7 15.1 %copy-start.4 = (bf16[1,32,2,16,128]{4,3,2,1,0:T(8,128)(2,1)S(1)}, bf16[1,32,2,16,128]{4,3,2,1,0:T(8,128)(2,1)}, u32[]{:S(2)}) copy-start(bf16[1,32,2,16,128]{4,3,2,1,0:T(8,128)(2,1)} %param.7) | copy-start | bytes 786436
  2.5 13.3 %collective-permute-start = (bf16[1,32,1,16,128]{4,1,3,2,0:T(8,128)(2,1)}, bf16[1,32,1,16,128]{4,1,3,2,0:T(8,128)(2,1)}, u32[]{:S(2)}, u32[]{:S(2)}) collective-permute-start(bf16[1,32,1,16,128]{4,1,3,2,0:T(8,128)(2,1)} %get-tuple-element.22), channel_id=1, source_target_pairs={{0,1},{1,2},{2,3},{4,5},{5,6},{6,7},{8,9},{9,10},{10,11},{12,13},{... | collective-permute-start | bytes 393224 | tf_op jit(solution)/shard_map/ppermute | solution.py:18
  8.1 7.8 %collective-permute-start.1 = (bf16[1,32,1,16,128]{4,1,3,2,0:T(8,128)(2,1)}, bf16[1,32,1,16,128]{4,1,3,2,0:T(8,128)(2,1)}, u32[]{:S(2)}, u32[]{:S(2)}) collective-permute-start(bf16[1,32,1,16,128]{4,1,3,2,0:T(8,128)(2,1)} %get-tuple-element.23), channel_id=1, source_target_pairs={{1,0},{2,1},{3,2},{5,4},{6,5},{7,6},{9,8},{10,9},{11,10},{13,12},{... | collective-permute-start | bytes 393224 | tf_op jit(solution)/shard_map/ppermute | solution.py:20
  24.4 12.8 %copy-start.3 = (bf16[864,864]{1,0:T(8,128)(2,1)S(1)}, bf16[864,864]{1,0:T(8,128)(2,1)}, u32[]{:S(2)}) copy-start(bf16[864,864]{1,0:T(8,128)(2,1)} %get-tuple-element.10) | copy-start | bytes 4478980
  37.2 3.6 %copy-start.1 = (bf16[864,4096]{1,0:T(8,128)(2,1)S(1)}, bf16[864,4096]{1,0:T(8,128)(2,1)}, u32[]{:S(2)}) copy-start(bf16[864,4096]{1,0:T(8,128)(2,1)} %shard_map.93) | copy-start | bytes 21233668
  43.3 5.4 %collective-permute-start.10 = (f32[32,896]{1,0:T(8,128)S(1)}, f32[32,896]{1,0:T(8,128)S(1)}, u32[]{:S(2)}, u32[]{:S(2)}) collective-permute-start(f32[32,896]{1,0:T(8,128)S(1)} %pad_maximum_fusion.1), channel_id=1, source_target_pairs={{0,12},{4,8},{8,4},{12,0},{16,28},{20,24},{24,20},{28,16},{1,13},{... | collective-permute-start | bytes 344072 | tf_op jit(solution)/shard_map/ppermute | solution.py:40
  43.9 4.8 %collective-permute-start.8 = (f32[32,896]{1,0:T(8,128)S(1)}, f32[32,896]{1,0:T(8,128)S(1)}, u32[]{:S(2)}, u32[]{:S(2)}) collective-permute-start(f32[32,896]{1,0:T(8,128)S(1)} %pad_maximum_fusion.1), channel_id=1, source_target_pairs={{0,4},{4,0},{8,12},{12,8},{16,20},{20,16},{24,28},{28,24},{1,5},{5... | collective-permute-start | bytes 344072 | tf_op jit(solution)/shard_map/ppermute | solution.py:37
  44.9 6.3 %collective-permute-start.9 = (f32[32,896]{1,0:T(8,128)S(1)}, f32[32,896]{1,0:T(8,128)S(1)}, u32[]{:S(2)}, u32[]{:S(2)}) collective-permute-start(f32[32,896]{1,0:T(8,128)S(1)} %pad_maximum_fusion.1), channel_id=1, source_target_pairs={{0,8},{4,12},{8,0},{12,4},{16,24},{20,28},{24,16},{28,20},{1,9},{5... | collective-permute-start | bytes 344072 | tf_op jit(solution)/shard_map/ppermute | solution.py:39
  51.3 5.1 %collective-permute-start.11 = (f32[32,896]{1,0:T(8,128)S(1)}, f32[32,896]{1,0:T(8,128)S(1)}, u32[]{:S(2)}, u32[]{:S(2)}) collective-permute-start(f32[32,896]{1,0:T(8,128)S(1)} %add_add_fusion.1), channel_id=1, source_target_pairs={{0,16},{4,20},{8,24},{12,28},{16,0},{20,4},{24,8},{28,12},{1,17},{... | collective-permute-start | bytes 344072 | tf_op jit(solution)/shard_map/ppermute | solution.py:37
  55.2 13.1 %collective-permute-start.2 = (bf16[432,864]{1,0:T(8,128)(2,1)}, bf16[432,864]{1,0:T(8,128)(2,1)}, u32[]{:S(2)}, u32[]{:S(2)}) collective-permute-start(bf16[432,864]{1,0:T(8,128)(2,1)} %slice.87), channel_id=1, source_target_pairs={{0,4},{4,0},{8,12},{12,8},{16,20},{20,16},{24,28},{28,24},{1,5},{5... | collective-permute-start | bytes 2239496 | tf_op jit(solution)/shard_map/ppermute | solution.py:219
  57.2 10.6 %collective-permute-start.12 = (f32[32,1,216]{2,1,0:T(1,128)S(1)}, f32[32,1,216]{2,1,0:T(1,128)S(1)}, u32[]{:S(2)}, u32[]{:S(2)}) collective-permute-start(f32[32,1,216]{2,1,0:T(1,128)S(1)} %get-tuple-element.26), channel_id=1, source_target_pairs={{0,1},{1,0},{2,3},{3,2},{4,5},{5,4},{6,7},{7,6},{8,9},{9,8},{10,11... | collective-permute-start | bytes 82952 | tf_op jit(solution)/shard_map/ppermute | solution.py:77
  59.9 7.9 %collective-permute-start.13 = (f32[32,1,216]{2,1,0:T(1,128)S(1)}, f32[32,1,216]{2,1,0:T(1,128)S(1)}, u32[]{:S(2)}, u32[]{:S(2)}) collective-permute-start(f32[32,1,216]{2,1,0:T(1,128)S(1)} %get-tuple-element.25), channel_id=1, source_target_pairs={{0,2},{1,3},{2,0},{3,1},{4,6},{5,7},{6,4},{7,5},{8,10},{9,11},{10,... | collective-permute-start | bytes 82952 | tf_op jit(solution)/shard_map/ppermute | solution.py:77
  62.5 5.8 %copy-start.2 = (f32[864,864]{1,0:T(8,128)S(1)}, f32[864,864]{1,0:T(8,128)}, u32[]{:S(2)}) copy-start(f32[864,864]{1,0:T(8,128)} %fusion.31) | copy-start | bytes 8957956
  62.5 5.7 %collective-permute-start.14 = (f32[32,1,216]{2,1,0:T(1,128)S(1)}, f32[32,1,216]{2,1,0:T(1,128)S(1)}, u32[]{:S(2)}, u32[]{:S(2)}) collective-permute-start(f32[32,1,216]{2,1,0:T(1,128)S(1)} %get-tuple-element.24), channel_id=1, source_target_pairs={{0,3},{1,2},{2,1},{3,0},{4,7},{5,6},{6,5},{7,4},{8,11},{9,10},{10,... | collective-permute-start | bytes 82952 | tf_op jit(solution)/shard_map/ppermute | solution.py:77
  67.0 3.4 %copy-start.7 = (f32[32,32]{1,0:T(8,128)S(1)}, f32[32,32]{1,0:T(8,128)}, u32[]{:S(2)}) copy-start(f32[32,32]{1,0:T(8,128)} %param.11) | copy-start | bytes 12292
  69.7 9.3 %collective-permute-start.3 = (bf16[216,864]{1,0:T(8,128)(2,1)S(1)}, bf16[216,864]{1,0:T(8,128)(2,1)S(1)}, u32[]{:S(2)}, u32[]{:S(2)}) collective-permute-start(bf16[216,864]{1,0:T(8,128)(2,1)S(1)} %slice.88), channel_id=1, source_target_pairs={{0,8},{4,12},{8,0},{12,4},{16,24},{20,28},{24,16},{28,20},{1,9},{5... | collective-permute-start | bytes 1119752 | tf_op jit(solution)/shard_map/ppermute | solution.py:219
  71.3 9.3 %collective-permute-start.15 = (f32[32,896]{1,0:T(8,128)S(1)}, f32[32,896]{1,0:T(8,128)S(1)}, u32[]{:S(2)}, u32[]{:S(2)}) collective-permute-start(f32[32,896]{1,0:T(8,128)S(1)} %pad_maximum_fusion.2), channel_id=1, source_target_pairs={{0,1},{1,0},{2,3},{3,2},{4,5},{5,4},{6,7},{7,6},{8,9},{9,8},{10,11... | collective-permute-start | bytes 344072 | tf_op jit(solution)/shard_map/ppermute | solution.py:37
  71.8 10.9 %collective-permute-start.16 = (f32[32,896]{1,0:T(8,128)S(1)}, f32[32,896]{1,0:T(8,128)S(1)}, u32[]{:S(2)}, u32[]{:S(2)}) collective-permute-start(f32[32,896]{1,0:T(8,128)S(1)} %pad_maximum_fusion.2), channel_id=1, source_target_pairs={{0,2},{1,3},{2,0},{3,1},{4,6},{5,7},{6,4},{7,5},{8,10},{9,11},{10,... | collective-permute-start | bytes 344072 | tf_op jit(solution)/shard_map/ppermute | solution.py:39
  75.2 7.5 %collective-permute-start.17 = (f32[32,896]{1,0:T(8,128)S(1)}, f32[32,896]{1,0:T(8,128)S(1)}, u32[]{:S(2)}, u32[]{:S(2)}) collective-permute-start(f32[32,896]{1,0:T(8,128)S(1)} %pad_maximum_fusion.2), channel_id=1, source_target_pairs={{0,3},{1,2},{2,1},{3,0},{4,7},{5,6},{6,5},{7,4},{8,11},{9,10},{10,... | collective-permute-start | bytes 344072 | tf_op jit(solution)/shard_map/ppermute | solution.py:40
  79.1 5.8 %collective-permute-start.4 = (bf16[108,864]{1,0:T(8,128)(2,1)S(1)}, bf16[108,864]{1,0:T(8,128)(2,1)S(1)}, u32[]{:S(2)}, u32[]{:S(2)}) collective-permute-start(bf16[108,864]{1,0:T(8,128)(2,1)S(1)} %slice.89), channel_id=1, source_target_pairs={{0,16},{4,20},{8,24},{12,28},{16,0},{20,4},{24,8},{28,12},{1,17},{... | collective-permute-start | bytes 559880 | tf_op jit(solution)/shard_map/ppermute | solution.py:219
  82.8 15.0 %copy-start.5 = (f32[32,896]{1,0:T(8,128)}, f32[32,896]{1,0:T(8,128)S(1)}, u32[]{:S(2)}) copy-start(f32[32,896]{1,0:T(8,128)S(1)} %add_add_fusion) | copy-start | bytes 344068
  86.8 5.1 %collective-permute-start.5 = (bf16[108,1,216]{0,2,1:T(8,128)(2,1)S(1)}, bf16[108,1,216]{0,2,1:T(8,128)(2,1)S(1)}, u32[]{:S(2)}, u32[]{:S(2)}) collective-permute-start(bf16[108,1,216]{0,2,1:T(8,128)(2,1)S(1)} %bitcast.69), channel_id=1, source_target_pairs={{0,1},{1,0},{2,3},{3,2},{4,5},{5,4},{6,7},{7,6},{8,9},{9,8},{10,11... | collective-permute-start | bytes 139976 | tf_op jit(solution)/shard_map/ppermute | solution.py:77
  87.6 6.2 %collective-permute-start.6 = (bf16[108,1,216]{0,2,1:T(8,128)(2,1)S(1)}, bf16[108,1,216]{0,2,1:T(8,128)(2,1)S(1)}, u32[]{:S(2)}, u32[]{:S(2)}) collective-permute-start(bf16[108,1,216]{0,2,1:T(8,128)(2,1)S(1)} %bitcast.70), channel_id=1, source_target_pairs={{0,2},{1,3},{2,0},{3,1},{4,6},{5,7},{6,4},{7,5},{8,10},{9,11},{10,... | collective-permute-start | bytes 139976 | tf_op jit(solution)/shard_map/ppermute | solution.py:77
  91.1 6.0 %collective-permute-start.7 = (bf16[108,1,216]{0,2,1:T(8,128)(2,1)S(1)}, bf16[108,1,216]{0,2,1:T(8,128)(2,1)S(1)}, u32[]{:S(2)}, u32[]{:S(2)}) collective-permute-start(bf16[108,1,216]{0,2,1:T(8,128)(2,1)S(1)} %bitcast.71), channel_id=1, source_target_pairs={{0,3},{1,2},{2,1},{3,0},{4,7},{5,6},{6,5},{7,4},{8,11},{9,10},{10,... | collective-permute-start | bytes 139976 | tf_op jit(solution)/shard_map/ppermute | solution.py:77

commit v21 on v16

--- a/solution.py
+++ b/solution.py
@@ -203,19 +203,29 @@
     )
     weighted = (patches_t.astype(f32) * counts[None, :]).astype(jnp.bfloat16)
     total_samples = sample_idx.shape[1] * n_sp * n_dp
-    a_perm = lax.dot_general(
-        weighted, patches_t, contract_cells, preferred_element_type=f32
-    ) / jnp.float32(total_samples)
+    split = patch // 2
+    halves = [
+        lax.dot_general(weighted, part, contract_cells, preferred_element_type=f32) / jnp.float32(total_samples)
+        for part in (patches_t[:split], patches_t[split:])
+    ]
     rows = patch // n_dp
     cols = patch // n_sp
-    order, placed, a_bf = lax.optimization_barrier(
-        (tap_order(channels, n_taps), halving_order(channels, n_taps, rows, "dp"), a_perm.astype(jnp.bfloat16))
-    )
-    a_rows = jnp.dot(placed, a_bf, preferred_element_type=f32)
-    a_orig, kernel_perm = lax.optimization_barrier((a_rows, kernel_perm))
+    order, placed, left_bf = lax.optimization_barrier(
+        (tap_order(channels, n_taps), halving_order(channels, n_taps, rows, "dp"), halves[0].astype(jnp.bfloat16))
+    )
+    left_rows = jnp.dot(placed, left_bf, preferred_element_type=f32)
+    (right_bf,) = lax.optimization_barrier((halves[1].astype(jnp.bfloat16),))
+    right_rows = jnp.dot(placed, right_bf, preferred_element_type=f32)
+    left_rows, kernel_perm = lax.optimization_barrier((left_rows, kernel_perm))
     forward = jnp.dot(kernel_perm, patches_t, preferred_element_type=f32)
     conv_out = forward.astype(jnp.bfloat16).reshape(1, channels, planes, y_cells, x_cells)
-    step = 1
+    half = patch // 2
+    summed = [
+        part[:half] + lax.ppermute(part[half:].astype(jnp.bfloat16), "dp", partner("dp", 1)).astype(f32)
+        for part in (left_rows, right_rows)
+    ]
+    a_orig = jnp.concatenate(summed, axis=1)
+    step = 2
     while step < n_dp:
         half = a_orig.shape[0] // 2
         got = lax.ppermute(a_orig[half:].astype(jnp.bfloat16), "dp", partner("dp", step))

time: 85.5 us -> 94.2 us (1.10)
  waiting for transfers between devices: 11.2 us -> 18.4 us
    ppermute x3 -> x2, waiting for transfers between devices: 5.76 us -> 10.7 us  [on_device(): lax.ppermute(a_orig[half:].astype(jnp.bfloat16), 'dp', partner('dp', step))]
    dot_general x2 -> x4, matrix products: 9.41 us -> 12.4 us  [the longest x2 8.63 us: on_device(): lax.dot_general(weighted, part, contract_cells, preferred_element_type=f32)]
    dot_general x1, matrix products: 4.33 us -> 2.04 us  [on_device(): forward = jnp.dot(kernel_perm, patches_t, preferred_element_type=f32)]
    ppermute x2, waiting for transfers between devices: 0.01 us -> 2.25 us  [butterfly_sum(): other = lax.ppermute(x, axis, partner(axis, low + high))]
    add x0 -> x2, other arithmetic: none -> 1.26 us  [on_device(): part[:half]]
    add x2 -> x1, other arithmetic: 1.38 us -> 0.13 us  [on_device(): a_orig = a_orig[:half] + got.astype(f32)]
    slice x0 -> x2, local copies, waits for them, and re-layouts: none -> 1.13 us  [on_device(): part[half:].astype(jnp.bfloat16)]
    slice x3 -> x1, local copies, waits for them, and re-layouts: 1.14 us -> 0.12 us  [on_device(): a_orig[half:].astype(jnp.bfloat16)]
  transfers between devices with their start and end apart: 18 -> 19, of which waited for: 7 -> 8; matrix products, arithmetic and copies ran while one was open for 31% -> 21% of each run, Pallas kernels for 0% -> 0%
where the time goes in v21:
time: 94.2 us; the launch traced here: 93.9 us
  starting transfers between devices  27.1 us (29%)
  matrix products  23 us (24%)
  waiting for transfers between devices  18.4 us (20%)
  other arithmetic  10.5 us (11%)
  local copies, waits for them, and re-layouts  8.76 us (9%)
  Pallas kernels  5.16 us (5%)
  between operations  1.01 us (1%)
    ppermute x2, waiting for transfers between devices, on_device(): lax.ppermute(a_orig[half:].astype(jnp.bfloat16), 'dp', partner('dp', step))  10.7 us
    ppermute x6, starting transfers between devices, quad_scatter(): lax.ppermute(pick(digit ^ k).astype(wire), axis, partner(axis, k * low))  9.02 us
    dot_general x2, matrix products, on_device(): lax.dot_general(weighted, part, contract_cells, preferred_element_type=f32)  8.63 us
    ppermute x1, starting transfers between devices, padded_2(): lax.ppermute(tail, axis, [(i, (i + 1) % count) for i in range(ends)])  6.2 us
    dot_general x1, matrix products, on_device(): lax.dot_general(grad_flat, patches_t, contract_cells, preferred_element_t...  5.26 us
    pallas_call x1, Pallas kernels, patch_matrix(): pl.pallas_call(body, grid=(3,), in_specs=[pl.BlockSpec(shifted.shape, lam...  5.16 us
    ppermute x2, starting transfers between devices, butterfly_sum(): pair = lax.ppermute(x, axis, partner(axis, high))  3.88 us
    reduce_sum x1, other arithmetic, on_device(): jnp.sum((cell_ids[:, None] == jnp.arange(cells, dtype=jnp.int32)[None, :]...  3.35 us
  transfers between devices with their start and end apart: 19, of which 8 were waited for; matrix products, arithmetic and copies ran while one was open for 21% of the time, Pallas kernels for 0%

profile of v21, /device:TPU:0, one launch (start us, length us, event | category | flops | bytes accessed | tf_op | source)
XLA Modules:
  0.0 93.9 jit_solution(7210826024437895298)
XLA Ops:
  0.6 1.1 %copy.30 = bf16[1,32,2,16,128]{4,1,3,2,0:T(8,128)(2,1)S(1)} copy(bf16[1,32,2,16,128]{4,3,2,1,0:T(8,128)(2,1)} %param.6) | data formatting | bytes 524288 | tf_op args[0]
  2.5 1.3 %collective-permute-start.1 = (bf16[1,32,1,16,128]{4,1,3,2,0:T(8,128)(2,1)}, bf16[1,32,1,16,128]{4,1,3,2,0:T(8,128)(2,1)}, u32[]{:S(2)}, u32[]{:S(2)}) collective-permute-start(bf16[1,32,1,16,128]{4,1,3,2,0:T(8,128)(2,1)} %get-tuple-element.25), channel_id=1, source_target_pairs={{1,0},{2,1},{3,2},{5,4},{6,5},{7,6},{9,8},{10,9},{11,10},{13,12},{... | collective-permute-start | bytes 393224 | tf_op jit(solution)/shard_map/ppermute | solution.py:20
  3.7 6.2 %collective-permute-start = (bf16[1,32,1,16,128]{4,1,3,2,0:T(8,128)(2,1)S(1)}, bf16[1,32,1,16,128]{4,1,3,2,0:T(8,128)(2,1)}, u32[]{:S(2)}, u32[]{:S(2)}) collective-permute-start(bf16[1,32,1,16,128]{4,1,3,2,0:T(8,128)(2,1)S(1)} %get-tuple-element.24), channel_id=1, source_target_pairs={{0,1},{1,2},{2,3},{4,5},{5,6},{6,7},{8,9},{9,10},{10,11},{12,13},{... | collective-permute-start | bytes 393224 | tf_op jit(solution)/shard_map/ppermute | solution.py:18
  10.0 3.4 %convert_reduce_fusion = f32[4096]{0:T(1024)S(1)} fusion(s32[1024]{0:T(1024)} %bitcast.79), kind=kLoop, calls=%fused_computation | loop fusion | flops 12578816 | bytes 20480 | tf_op jit(solution)/shard_map/reduce_sum | solution.py:201
  13.4 1.7 %fusion.4 = (bf16[864,864]{1,0:T(8,128)(2,1)S(1)}, bf16[864,864]{1,0:T(8,128)(2,1)}) fusion(s32[864]{0:T(1024)S(1)} %fusion.33, s32[864]{0:T(1024)S(1)} %fusion.36), kind=kLoop, calls=%fused_computation.10 | loop fusion | flops 2985984 | bytes 2992896 | tf_op jit(solution)/shard_map/convert_element_type | solution.py:135
  16.5 1.3 %convolution_bitcast_fusion.1 = f32[32,32]{1,0:T(8,128)S(1)} fusion(bf16[32,2,16,128]{3,2,1,0:T(8,128)(2,1)} %bitcast.73), kind=kOutput, calls=%fused_computation.20 | convolution fusion | flops 8388608 | bytes 266240 | tf_op jit(solution)/shard_map/dot_general | solution.py:183
  19.7 1.5 %pad_maximum_fusion.src_ref = bf16[3,4,18,32,128]{4,3,2,1,0:T(8,128)(2,1)} fusion(bf16[1,4,18,32,128]{4,3,2,1,0:T(8,128)(2,1)S(1)} %get-tuple-element.19, bf16[1,4,18,32,128]{4,3,2,1,0:T(8,128)(2,1)S(1)} %get-tuple-element.20, bf16[1,4,18,32,128]{4,3,2,1,0:T(8,128)(2,1)S(1)} %get-tuple-element.18), kind=kLoop, calls=%fused_computation.12 | loop fusion | flops 1769472 | bytes 3538944 | tf_op jit(solution)/shard_map/stack | solution.py:109
  21.1 5.2 %shard_map.93 = bf16[864,4096]{1,0:T(8,128)(2,1)} custom-call(bf16[3,4,18,32,128]{4,3,2,1,0:T(8,128)(2,1)} %pad_maximum_fusion.src_ref), custom_call_target="tpu_custom_call" | custom-call | tf_op jit(solution)/shard_map/pallas_call | solution.py:122
  26.3 5.3 %convolution_bitcast_fusion = f32[32,864]{1,0:T(8,128)S(1)} fusion(bf16[864,4096]{1,0:T(8,128)(2,1)} %shard_map.93, bf16[32,4096]{1,0:T(8,128)(2,1)S(1)} %reshape_squeeze.3), kind=kOutput, calls=%fused_computation.19 | convolution fusion | flops 226492416 | bytes 7450624 | tf_op jit(solution)/shard_map/dot_general | solution.py:182
  31.6 3.9 %multiply_convert_fusion.4 = bf16[864,432]{0,1:T(8,128)(2,1)S(1)} fusion(bf16[864,4096]{1,0:T(8,128)(2,1)S(1)} %copy-done.1, f32[4096]{0:T(1024)S(1)} %convert_reduce_fusion), kind=kOutput, calls=%fused_computation.16 | convolution fusion | flops 3069010944 | bytes 11379712 | tf_op jit(solution)/shard_map/dot_general | solution.py:208
  35.5 4.8 %multiply_convert_fusion.3 = bf16[864,432]{0,1:T(8,128)(2,1)} fusion(bf16[864,4096]{1,0:T(8,128)(2,1)S(1)} %copy-done.1, f32[4096]{0:T(1024)S(1)} %convert_reduce_fusion), kind=kOutput, calls=%fused_computation.15 | convolution fusion | flops 3069010944 | bytes 11379712 | tf_op jit(solution)/shard_map/dot_general | solution.py:208
  40.3 1.9 %collective-permute-start.10 = (f32[32,896]{1,0:T(8,128)S(1)}, f32[32,896]{1,0:T(8,128)S(1)}, u32[]{:S(2)}, u32[]{:S(2)}) collective-permute-start(f32[32,896]{1,0:T(8,128)S(1)} %pad_maximum_fusion.2), channel_id=1, source_target_pairs={{0,8},{4,12},{8,0},{12,4},{16,24},{20,28},{24,16},{28,20},{1,9},{5... | collective-permute-start | bytes 344072 | tf_op jit(solution)/shard_map/ppermute | solution.py:39
  42.4 1.1 %fusion.41 = f32[864,432]{0,1:T(8,128)S(1)} fusion(bf16[864,864]{1,0:T(8,128)(2,1)S(1)} %copy-done.2, bf16[864,432]{0,1:T(8,128)(2,1)S(1)} %multiply_convert_fusion.4), kind=kOutput, calls=%fused_computation.90 | convolution fusion | flops 644972544 | bytes 3732480 | tf_op jit(solution)/shard_map/dot_general | solution.py:216
  43.6 1.7 %collective-permute-done.10 = f32[32,896]{1,0:T(8,128)S(1)} collective-permute-done((f32[32,896]{1,0:T(8,128)S(1)}, f32[32,896]{1,0:T(8,128)S(1)}, u32[]{:S(2)}, u32[]{:S(2)}) %collective-permute-start.10) | collective-permute-done | bytes 114720 | tf_op jit(solution)/shard_map/ppermute | solution.py:39
  45.3 2.2 %collective-permute-done.11 = f32[32,896]{1,0:T(8,128)S(1)} collective-permute-done((f32[32,896]{1,0:T(8,128)S(1)}, f32[32,896]{1,0:T(8,128)S(1)}, u32[]{:S(2)}, u32[]{:S(2)}) %collective-permute-start.11) | collective-permute-done | bytes 114720 | tf_op jit(solution)/shard_map/ppermute | solution.py:40
  47.6 1.7 %collective-permute-start.12 = (f32[32,896]{1,0:T(8,128)S(1)}, f32[32,896]{1,0:T(8,128)S(1)}, u32[]{:S(2)}, u32[]{:S(2)}) collective-permute-start(f32[32,896]{1,0:T(8,128)S(1)} %add_add_fusion.1), channel_id=1, source_target_pairs={{0,16},{4,20},{8,24},{12,28},{16,0},{20,4},{24,8},{28,12},{1,17},{... | collective-permute-start | bytes 344072 | tf_op jit(solution)/shard_map/ppermute | solution.py:37
  49.3 2.0 %fusion.10 = bf16[4,8,32,128]{3,1,2,0:T(8,128)(2,1)} fusion(bf16[32,864]{1,0:T(8,128)(2,1)S(1)} %reshape.136, bf16[864,4096]{1,0:T(8,128)(2,1)S(1)} %copy-done.1), kind=kOutput, calls=%fused_computation.18 | convolution fusion | flops 226623488 | bytes 7395328 | tf_op jit(solution)/shard_map/dot_general | solution.py:220
  53.5 1.2 %collective-permute-start.13 = (f32[32,1,216]{2,1,0:T(1,128)S(1)}, f32[32,1,216]{2,1,0:T(1,128)S(1)}, u32[]{:S(2)}, u32[]{:S(2)}) collective-permute-start(f32[32,1,216]{2,1,0:T(1,128)S(1)} %get-tuple-element.28), channel_id=1, source_target_pairs={{0,1},{1,0},{2,3},{3,2},{4,5},{5,4},{6,7},{7,6},{8,9},{9,8},{10,11... | collective-permute-start | bytes 82952 | tf_op jit(solution)/shard_map/ppermute | solution.py:77
  54.8 1.7 %collective-permute-start.14 = (f32[32,1,216]{2,1,0:T(1,128)S(1)}, f32[32,1,216]{2,1,0:T(1,128)S(1)}, u32[]{:S(2)}, u32[]{:S(2)}) collective-permute-start(f32[32,1,216]{2,1,0:T(1,128)S(1)} %get-tuple-element.27), channel_id=1, source_target_pairs={{0,2},{1,3},{2,0},{3,1},{4,6},{5,7},{6,4},{7,5},{8,10},{9,11},{10,... | collective-permute-start | bytes 82952 | tf_op jit(solution)/shard_map/ppermute | solution.py:77
  56.5 1.5 %collective-permute-start.15 = (f32[32,1,216]{2,1,0:T(1,128)S(1)}, f32[32,1,216]{2,1,0:T(1,128)S(1)}, u32[]{:S(2)}, u32[]{:S(2)}) collective-permute-start(f32[32,1,216]{2,1,0:T(1,128)S(1)} %get-tuple-element.26), channel_id=1, source_target_pairs={{0,3},{1,2},{2,1},{3,0},{4,7},{5,6},{6,5},{7,4},{8,11},{9,10},{10,... | collective-permute-start | bytes 82952 | tf_op jit(solution)/shard_map/ppermute | solution.py:77
  58.0 2.7 %fusion.42 = f32[864,432]{0,1:T(8,128)S(1)} fusion(bf16[864,864]{1,0:T(8,128)(2,1)} %get-tuple-element.12, bf16[864,432]{0,1:T(8,128)(2,1)} %multiply_convert_fusion.3), kind=kOutput, calls=%fused_computation.91 | convolution fusion | flops 644972544 | bytes 3732480 | tf_op jit(solution)/shard_map/dot_general | solution.py:218
  62.3 1.1 %convert_add_fusion = f32[432,432]{0,1:T(8,128)S(1)} fusion(bf16[432,432]{0,1:T(8,128)(2,1)} %collective-permute-done.2, f32[864,432]{0,1:T(8,128)S(1)} %copy-done.4), kind=kLoop, calls=%fused_computation.28 | loop fusion | flops 373248 | bytes 1866240 | tf_op jit(solution)/shard_map/add | solution.py:224
  64.0 1.4 %collective-permute-start.4 = (bf16[216,864]{0,1:T(8,128)(2,1)S(1)}, bf16[216,864]{0,1:T(8,128)(2,1)S(1)}, u32[]{:S(2)}, u32[]{:S(2)}) collective-permute-start(bf16[216,864]{0,1:T(8,128)(2,1)S(1)} %fusion.13), channel_id=1, source_target_pairs={{0,8},{4,12},{8,0},{12,4},{16,24},{20,28},{24,16},{28,20},{1,9},{5... | collective-permute-start | bytes 1119752 | tf_op jit(solution)/shard_map/ppermute | solution.py:231
  66.2 1.9 %collective-permute-start.17 = (f32[32,896]{1,0:T(8,128)S(1)}, f32[32,896]{1,0:T(8,128)S(1)}, u32[]{:S(2)}, u32[]{:S(2)}) collective-permute-start(f32[32,896]{1,0:T(8,128)S(1)} %pad_maximum_fusion.3), channel_id=1, source_target_pairs={{0,2},{1,3},{2,0},{3,1},{4,6},{5,7},{6,4},{7,5},{8,10},{9,11},{10,... | collective-permute-start | bytes 344072 | tf_op jit(solution)/shard_map/ppermute | solution.py:39
  69.7 6.6 %collective-permute-done.4 = bf16[216,864]{0,1:T(8,128)(2,1)S(1)} collective-permute-done((bf16[216,864]{0,1:T(8,128)(2,1)S(1)}, bf16[216,864]{0,1:T(8,128)(2,1)S(1)}, u32[]{:S(2)}, u32[]{:S(2)}) %collective-permute-start.4) | collective-permute-done | bytes 373280 | tf_op jit(solution)/shard_map/ppermute | solution.py:231
  76.6 1.8 %collective-permute-start.5 = (bf16[108,864]{0,1:T(8,128)(2,1)S(1)}, bf16[108,864]{0,1:T(8,128)(2,1)S(1)}, u32[]{:S(2)}, u32[]{:S(2)}) collective-permute-start(bf16[108,864]{0,1:T(8,128)(2,1)S(1)} %slice.124), channel_id=1, source_target_pairs={{0,16},{4,20},{8,24},{12,28},{16,0},{20,4},{24,8},{28,12},{1,17},{... | collective-permute-start | bytes 559880 | tf_op jit(solution)/shard_map/ppermute | solution.py:231
  79.1 4.1 %collective-permute-done.5 = bf16[108,864]{0,1:T(8,128)(2,1)S(1)} collective-permute-done((bf16[108,864]{0,1:T(8,128)(2,1)S(1)}, bf16[108,864]{0,1:T(8,128)(2,1)S(1)}, u32[]{:S(2)}, u32[]{:S(2)}) %collective-permute-start.5) | collective-permute-done | bytes 186656 | tf_op jit(solution)/shard_map/ppermute | solution.py:231
  83.3 1.2 %fusion.14 = f32[108,864]{1,0:T(8,128)S(1)} fusion(bf16[864,864]{1,0:T(8,128)(2,1)S(1)} %get-tuple-element.16, f32[216,864]{0,1:T(8,128)S(1)} %fusion.12, bf16[108,864]{0,1:T(8,128)(2,1)S(1)} %collective-permute-done.5), kind=kOutput, calls=%fused_computation.35 | convolution fusion | flops 483916032 | bytes 2585088 | tf_op jit(solution)/shard_map/dot_general | solution.py:234
  85.3 2.4 %collective-permute-start.8 = (bf16[108,1,216]{0,2,1:T(8,128)(2,1)S(1)}, bf16[108,1,216]{0,2,1:T(8,128)(2,1)S(1)}, u32[]{:S(2)}, u32[]{:S(2)}) collective-permute-start(bf16[108,1,216]{0,2,1:T(8,128)(2,1)S(1)} %bitcast.76), channel_id=1, source_target_pairs={{0,3},{1,2},{2,1},{3,0},{4,7},{5,6},{6,5},{7,4},{8,11},{9,10},{10,... | collective-permute-start | bytes 139976 | tf_op jit(solution)/shard_map/ppermute | solution.py:77
  88.1 2.1 %collective-permute-start.6 = (bf16[108,1,216]{0,2,1:T(8,128)(2,1)S(1)}, bf16[108,1,216]{0,2,1:T(8,128)(2,1)S(1)}, u32[]{:S(2)}, u32[]{:S(2)}) collective-permute-start(bf16[108,1,216]{0,2,1:T(8,128)(2,1)S(1)} %bitcast.78), channel_id=1, source_target_pairs={{0,1},{1,0},{2,3},{3,2},{4,5},{5,4},{6,7},{7,6},{8,9},{9,8},{10,11... | collective-permute-start | bytes 139976 | tf_op jit(solution)/shard_map/ppermute | solution.py:77
  90.4 1.4 %collective-permute-done.8 = bf16[108,1,216]{0,2,1:T(8,128)(2,1)S(1)} collective-permute-done((bf16[108,1,216]{0,2,1:T(8,128)(2,1)S(1)}, bf16[108,1,216]{0,2,1:T(8,128)(2,1)S(1)}, u32[]{:S(2)}, u32[]{:S(2)}) %collective-permute-start.8) | collective-permute-done | bytes 46688 | tf_op jit(solution)/shard_map/ppermute | solution.py:77
  91.8 1.4 %collective-permute-done.7 = bf16[108,1,216]{0,2,1:T(8,128)(2,1)S(1)} collective-permute-done((bf16[108,1,216]{0,2,1:T(8,128)(2,1)S(1)}, bf16[108,1,216]{0,2,1:T(8,128)(2,1)S(1)}, u32[]{:S(2)}, u32[]{:S(2)}) %collective-permute-start.7) | collective-permute-done | bytes 46688 | tf_op jit(solution)/shard_map/ppermute | solution.py:77
  (79 shorter events, 14.0 us)
Async XLA Ops:
  0.6 64.9 %copy-start = (f32[216,864]{1,0:T(8,128)S(1)}, f32[216,864]{1,0:T(8,128)}, u32[]{:S(2)}) copy-start(f32[216,864]{1,0:T(8,128)} %param.10) | copy-start | bytes 2239492
  1.8 13.3 %copy-start.6 = (bf16[1,32,2,16,128]{4,3,2,1,0:T(8,128)(2,1)S(1)}, bf16[1,32,2,16,128]{4,3,2,1,0:T(8,128)(2,1)}, u32[]{:S(2)}) copy-start(bf16[1,32,2,16,128]{4,3,2,1,0:T(8,128)(2,1)} %param.7) | copy-start | bytes 786436
  2.5 15.3 %collective-permute-start.1 = (bf16[1,32,1,16,128]{4,1,3,2,0:T(8,128)(2,1)}, bf16[1,32,1,16,128]{4,1,3,2,0:T(8,128)(2,1)}, u32[]{:S(2)}, u32[]{:S(2)}) collective-permute-start(bf16[1,32,1,16,128]{4,1,3,2,0:T(8,128)(2,1)} %get-tuple-element.25), channel_id=1, source_target_pairs={{1,0},{2,1},{3,2},{5,4},{6,5},{7,6},{9,8},{10,9},{11,10},{13,12},{... | collective-permute-start | bytes 393224 | tf_op jit(solution)/shard_map/ppermute | solution.py:20
  3.7 14.0 %collective-permute-start = (bf16[1,32,1,16,128]{4,1,3,2,0:T(8,128)(2,1)S(1)}, bf16[1,32,1,16,128]{4,1,3,2,0:T(8,128)(2,1)}, u32[]{:S(2)}, u32[]{:S(2)}) collective-permute-start(bf16[1,32,1,16,128]{4,1,3,2,0:T(8,128)(2,1)S(1)} %get-tuple-element.24), channel_id=1, source_target_pairs={{0,1},{1,2},{2,3},{4,5},{5,6},{6,7},{8,9},{9,10},{10,11},{12,13},{... | collective-permute-start | bytes 393224 | tf_op jit(solution)/shard_map/ppermute | solution.py:18
  13.4 1.9 %copy-start.8 = (bf16[32,864]{1,0:T(8,128)(2,1)S(1)}, bf16[32,864]{1,0:T(8,128)(2,1)}, u32[]{:S(2)}) copy-start(bf16[32,864]{1,0:T(8,128)(2,1)} %param.8) | copy-start | bytes 165892
  26.3 5.4 %copy-start.1 = (bf16[864,4096]{1,0:T(8,128)(2,1)S(1)}, bf16[864,4096]{1,0:T(8,128)(2,1)}, u32[]{:S(2)}) copy-start(bf16[864,4096]{1,0:T(8,128)(2,1)} %shard_map.93) | copy-start | bytes 21233668
  35.5 6.9 %copy-start.2 = (bf16[864,864]{1,0:T(8,128)(2,1)S(1)}, bf16[864,864]{1,0:T(8,128)(2,1)}, u32[]{:S(2)}) copy-start(bf16[864,864]{1,0:T(8,128)(2,1)} %get-tuple-element.12) | copy-start | bytes 4478980
  40.3 5.0 %collective-permute-start.10 = (f32[32,896]{1,0:T(8,128)S(1)}, f32[32,896]{1,0:T(8,128)S(1)}, u32[]{:S(2)}, u32[]{:S(2)}) collective-permute-start(f32[32,896]{1,0:T(8,128)S(1)} %pad_maximum_fusion.2), channel_id=1, source_target_pairs={{0,8},{4,12},{8,0},{12,4},{16,24},{20,28},{24,16},{28,20},{1,9},{5... | collective-permute-start | bytes 344072 | tf_op jit(solution)/shard_map/ppermute | solution.py:39
  42.2 5.3 %collective-permute-start.11 = (f32[32,896]{1,0:T(8,128)S(1)}, f32[32,896]{1,0:T(8,128)S(1)}, u32[]{:S(2)}, u32[]{:S(2)}) collective-permute-start(f32[32,896]{1,0:T(8,128)S(1)} %pad_maximum_fusion.2), channel_id=1, source_target_pairs={{0,12},{4,8},{8,4},{12,0},{16,28},{20,24},{24,20},{28,16},{1,13},{... | collective-permute-start | bytes 344072 | tf_op jit(solution)/shard_map/ppermute | solution.py:40
  42.2 5.3 %collective-permute-start.9 = (f32[32,896]{1,0:T(8,128)S(1)}, f32[32,896]{1,0:T(8,128)S(1)}, u32[]{:S(2)}, u32[]{:S(2)}) collective-permute-start(f32[32,896]{1,0:T(8,128)S(1)} %pad_maximum_fusion.2), channel_id=1, source_target_pairs={{0,4},{4,0},{8,12},{12,8},{16,20},{20,16},{24,28},{28,24},{1,5},{5... | collective-permute-start | bytes 344072 | tf_op jit(solution)/shard_map/ppermute | solution.py:37
  43.6 7.8 %copy-start.3 = (f32[864,432]{0,1:T(8,128)}, f32[864,432]{0,1:T(8,128)S(1)}, u32[]{:S(2)}) copy-start(f32[864,432]{0,1:T(8,128)S(1)} %fusion.41) | copy-start | bytes 4478980
  47.6 5.2 %collective-permute-start.12 = (f32[32,896]{1,0:T(8,128)S(1)}, f32[32,896]{1,0:T(8,128)S(1)}, u32[]{:S(2)}, u32[]{:S(2)}) collective-permute-start(f32[32,896]{1,0:T(8,128)S(1)} %add_add_fusion.1), channel_id=1, source_target_pairs={{0,16},{4,20},{8,24},{12,28},{16,0},{20,4},{24,8},{28,12},{1,17},{... | collective-permute-start | bytes 344072 | tf_op jit(solution)/shard_map/ppermute | solution.py:37
  52.3 10.0 %collective-permute-start.2 = (bf16[432,432]{0,1:T(8,128)(2,1)}, bf16[432,432]{0,1:T(8,128)(2,1)}, u32[]{:S(2)}, u32[]{:S(2)}) collective-permute-start(bf16[432,432]{0,1:T(8,128)(2,1)} %slice.123), channel_id=1, source_target_pairs={{0,4},{4,0},{8,12},{12,8},{16,20},{20,16},{24,28},{28,24},{1,5},{5... | collective-permute-start | bytes 1119752 | tf_op jit(solution)/shard_map/ppermute | solution.py:224
  53.5 8.3 %collective-permute-start.13 = (f32[32,1,216]{2,1,0:T(1,128)S(1)}, f32[32,1,216]{2,1,0:T(1,128)S(1)}, u32[]{:S(2)}, u32[]{:S(2)}) collective-permute-start(f32[32,1,216]{2,1,0:T(1,128)S(1)} %get-tuple-element.28), channel_id=1, source_target_pairs={{0,1},{1,0},{2,3},{3,2},{4,5},{5,4},{6,7},{7,6},{8,9},{9,8},{10,11... | collective-permute-start | bytes 82952 | tf_op jit(solution)/shard_map/ppermute | solution.py:77
  54.8 7.0 %collective-permute-start.14 = (f32[32,1,216]{2,1,0:T(1,128)S(1)}, f32[32,1,216]{2,1,0:T(1,128)S(1)}, u32[]{:S(2)}, u32[]{:S(2)}) collective-permute-start(f32[32,1,216]{2,1,0:T(1,128)S(1)} %get-tuple-element.27), channel_id=1, source_target_pairs={{0,2},{1,3},{2,0},{3,1},{4,6},{5,7},{6,4},{7,5},{8,10},{9,11},{10,... | collective-permute-start | bytes 82952 | tf_op jit(solution)/shard_map/ppermute | solution.py:77
  56.5 4.2 %copy-start.5 = (bf16[4,8,32,128]{3,1,2,0:T(8,128)(2,1)S(1)}, bf16[4,8,32,128]{3,1,2,0:T(8,128)(2,1)}, u32[]{:S(2)}) copy-start(bf16[4,8,32,128]{3,1,2,0:T(8,128)(2,1)} %fusion.10) | copy-start | bytes 786436
  56.5 5.7 %collective-permute-start.15 = (f32[32,1,216]{2,1,0:T(1,128)S(1)}, f32[32,1,216]{2,1,0:T(1,128)S(1)}, u32[]{:S(2)}, u32[]{:S(2)}) collective-permute-start(f32[32,1,216]{2,1,0:T(1,128)S(1)} %get-tuple-element.26), channel_id=1, source_target_pairs={{0,3},{1,2},{2,1},{3,0},{4,7},{5,6},{6,5},{7,4},{8,11},{9,10},{10,... | collective-permute-start | bytes 82952 | tf_op jit(solution)/shard_map/ppermute | solution.py:77
  60.7 1.6 %copy-start.4 = (f32[864,432]{0,1:T(8,128)S(1)}, f32[864,432]{0,1:T(8,128)}, u32[]{:S(2)}) copy-start(f32[864,432]{0,1:T(8,128)} %copy-done.3) | copy-start | bytes 4478980
  61.6 1.9 %collective-permute-start.3 = (bf16[432,432]{0,1:T(8,128)(2,1)S(1)}, bf16[432,432]{0,1:T(8,128)(2,1)S(1)}, u32[]{:S(2)}, u32[]{:S(2)}) collective-permute-start(bf16[432,432]{0,1:T(8,128)(2,1)S(1)} %slice.122), channel_id=1, source_target_pairs={{0,4},{4,0},{8,12},{12,8},{16,20},{20,16},{24,28},{28,24},{1,5},{5... | collective-permute-start | bytes 1119752 | tf_op jit(solution)/shard_map/ppermute | solution.py:224
  63.4 1.9 %copy-start.9 = (f32[32,32]{1,0:T(8,128)S(1)}, f32[32,32]{1,0:T(8,128)}, u32[]{:S(2)}) copy-start(f32[32,32]{1,0:T(8,128)} %param.11) | copy-start | bytes 12292
  64.0 12.3 %collective-permute-start.4 = (bf16[216,864]{0,1:T(8,128)(2,1)S(1)}, bf16[216,864]{0,1:T(8,128)(2,1)S(1)}, u32[]{:S(2)}, u32[]{:S(2)}) collective-permute-start(bf16[216,864]{0,1:T(8,128)(2,1)S(1)} %fusion.13), channel_id=1, source_target_pairs={{0,8},{4,12},{8,0},{12,4},{16,24},{20,28},{24,16},{28,20},{1,9},{5... | collective-permute-start | bytes 1119752 | tf_op jit(solution)/shard_map/ppermute | solution.py:231
  66.2 12.1 %collective-permute-start.17 = (f32[32,896]{1,0:T(8,128)S(1)}, f32[32,896]{1,0:T(8,128)S(1)}, u32[]{:S(2)}, u32[]{:S(2)}) collective-permute-start(f32[32,896]{1,0:T(8,128)S(1)} %pad_maximum_fusion.3), channel_id=1, source_target_pairs={{0,2},{1,3},{2,0},{3,1},{4,6},{5,7},{6,4},{7,5},{8,10},{9,11},{10,... | collective-permute-start | bytes 344072 | tf_op jit(solution)/shard_map/ppermute | solution.py:39
  68.2 10.2 %collective-permute-start.18 = (f32[32,896]{1,0:T(8,128)S(1)}, f32[32,896]{1,0:T(8,128)S(1)}, u32[]{:S(2)}, u32[]{:S(2)}) collective-permute-start(f32[32,896]{1,0:T(8,128)S(1)} %pad_maximum_fusion.3), channel_id=1, source_target_pairs={{0,3},{1,2},{2,1},{3,0},{4,7},{5,6},{6,5},{7,4},{8,11},{9,10},{10,... | collective-permute-start | bytes 344072 | tf_op jit(solution)/shard_map/ppermute | solution.py:40
  69.1 9.2 %collective-permute-start.16 = (f32[32,896]{1,0:T(8,128)S(1)}, f32[32,896]{1,0:T(8,128)S(1)}, u32[]{:S(2)}, u32[]{:S(2)}) collective-permute-start(f32[32,896]{1,0:T(8,128)S(1)} %pad_maximum_fusion.3), channel_id=1, source_target_pairs={{0,1},{1,0},{2,3},{3,2},{4,5},{5,4},{6,7},{7,6},{8,9},{9,8},{10,11... | collective-permute-start | bytes 344072 | tf_op jit(solution)/shard_map/ppermute | solution.py:37
  76.6 6.7 %collective-permute-start.5 = (bf16[108,864]{0,1:T(8,128)(2,1)S(1)}, bf16[108,864]{0,1:T(8,128)(2,1)S(1)}, u32[]{:S(2)}, u32[]{:S(2)}) collective-permute-start(bf16[108,864]{0,1:T(8,128)(2,1)S(1)} %slice.124), channel_id=1, source_target_pairs={{0,16},{4,20},{8,24},{12,28},{16,0},{20,4},{24,8},{28,12},{1,17},{... | collective-permute-start | bytes 559880 | tf_op jit(solution)/shard_map/ppermute | solution.py:231
  78.5 6.7 %copy-start.7 = (f32[32,896]{1,0:T(8,128)}, f32[32,896]{1,0:T(8,128)S(1)}, u32[]{:S(2)}) copy-start(f32[32,896]{1,0:T(8,128)S(1)} %add_add_fusion) | copy-start | bytes 344068
  85.3 6.5 %collective-permute-start.8 = (bf16[108,1,216]{0,2,1:T(8,128)(2,1)S(1)}, bf16[108,1,216]{0,2,1:T(8,128)(2,1)S(1)}, u32[]{:S(2)}, u32[]{:S(2)}) collective-permute-start(bf16[108,1,216]{0,2,1:T(8,128)(2,1)S(1)} %bitcast.76), channel_id=1, source_target_pairs={{0,3},{1,2},{2,1},{3,0},{4,7},{5,6},{6,5},{7,4},{8,11},{9,10},{10,... | collective-permute-start | bytes 139976 | tf_op jit(solution)/shard_map/ppermute | solution.py:77
  87.9 5.3 %collective-permute-start.7 = (bf16[108,1,216]{0,2,1:T(8,128)(2,1)S(1)}, bf16[108,1,216]{0,2,1:T(8,128)(2,1)S(1)}, u32[]{:S(2)}, u32[]{:S(2)}) collective-permute-start(bf16[108,1,216]{0,2,1:T(8,128)(2,1)S(1)} %bitcast.77), channel_id=1, source_target_pairs={{0,2},{1,3},{2,0},{3,1},{4,6},{5,7},{6,4},{7,5},{8,10},{9,11},{10,... | collective-permute-start | bytes 139976 | tf_op jit(solution)/shard_map/ppermute | solution.py:77
  88.1 5.1 %collective-permute-start.6 = (bf16[108,1,216]{0,2,1:T(8,128)(2,1)S(1)}, bf16[108,1,216]{0,2,1:T(8,128)(2,1)S(1)}, u32[]{:S(2)}, u32[]{:S(2)}) collective-permute-start(bf16[108,1,216]{0,2,1:T(8,128)(2,1)S(1)} %bitcast.78), channel_id=1, source_target_pairs={{0,1},{1,0},{2,3},{3,2},{4,5},{5,4},{6,7},{7,6},{8,9},{9,8},{10,11... | collective-permute-start | bytes 139976 | tf_op jit(solution)/shard_map/ppermute | solution.py:77

commit v22 on v16

--- a/solution.py
+++ b/solution.py
@@ -109,10 +109,10 @@
     shifted = jnp.stack([slab[:, :, :, dx : dx + x_cells] for dx in range(3)])
 
     def body(src_ref, out_ref):
-        dz = pl.program_id(0)
-        for dy in range(3):
-            for dx in range(3):
-                row = (dy * 3 + dx) * channels
+        for tap in range(27):
+            dz, dy, dx = tap // 9, (tap // 3) % 3, tap % 3
+            if True:
+                row = tap * channels
                 for z in range(planes):
                     for y in range(y_cells):
                         out_ref[pl.ds(row, channels), pl.ds((z * y_cells + y) * x_cells, x_cells)] = (
@@ -121,9 +121,9 @@
 
     return pl.pallas_call(
         body,
-        grid=(3,),
-        in_specs=[pl.BlockSpec(shifted.shape, lambda dz: (0, 0, 0, 0, 0))],
-        out_specs=pl.BlockSpec((9 * channels, cells), lambda dz: (dz, 0)),
+        grid=(1,),
+        in_specs=[pl.BlockSpec(shifted.shape, lambda i: (0, 0, 0, 0, 0))],
+        out_specs=pl.BlockSpec((27 * channels, cells), lambda i: (0, 0)),
         out_shape=jax.ShapeDtypeStruct((27 * channels, cells), slab.dtype),
     )(shifted)
 

time: 85.5 us -> 86.2 us (level)
  no operation moved by 1% of the time
where the time goes in v22:
time: 86.2 us; the launch traced here: 85.8 us
  starting transfers between devices  26.3 us (31%)
  matrix products  22.3 us (26%)
  waiting for transfers between devices  11.2 us (13%)
  other arithmetic  10.1 us (12%)
  local copies, waits for them, and re-layouts  9.36 us (11%)
  Pallas kernels  5.55 us (6%)
  between operations  0.98 us (1%)
    ppermute x6, starting transfers between devices, quad_scatter(): lax.ppermute(pick(digit ^ k).astype(wire), axis, partner(axis, k * low))  9.02 us
    dot_general x1, matrix products, on_device(): lax.dot_general(weighted, patches_t, contract_cells, preferred_element_ty...  7.49 us
    ppermute x1, starting transfers between devices, padded_2(): lax.ppermute(tail, axis, [(i, (i + 1) % count) for i in range(ends)])  6.21 us
    ppermute x3, waiting for transfers between devices, on_device(): lax.ppermute(a_orig[half:].astype(jnp.bfloat16), 'dp', partner('dp', step))  5.76 us
    pallas_call x1, Pallas kernels, patch_matrix(): pl.pallas_call(body, grid=(1,), in_specs=[pl.BlockSpec(shifted.shape, lam...  5.55 us
    dot_general x1, matrix products, on_device(): lax.dot_general(grad_flat, patches_t, contract_cells, preferred_element_t...  5.26 us
    dot_general x1, matrix products, on_device(): forward = jnp.dot(kernel_perm, patches_t, preferred_element_type=f32)  4.32 us
    ppermute x2, starting transfers between devices, butterfly_sum(): pair = lax.ppermute(x, axis, partner(axis, high))  3.66 us
  transfers between devices with their start and end apart: 18, of which 7 were waited for; matrix products, arithmetic and copies ran while one was open for 31% of the time, Pallas kernels for 0%

profile of v22, /device:TPU:0, one launch (start us, length us, event | category | flops | bytes accessed | tf_op | source)
XLA Modules:
  0.0 85.8 jit_solution(16197071684349581106)
XLA Ops:
  0.7 1.1 %copy.30 = bf16[1,32,2,16,128]{4,1,3,2,0:T(8,128)(2,1)S(1)} copy(bf16[1,32,2,16,128]{4,3,2,1,0:T(8,128)(2,1)} %param.6) | data formatting | bytes 524288 | tf_op args[0]
  2.5 1.3 %collective-permute-start.1 = (bf16[1,32,1,16,128]{4,1,3,2,0:T(8,128)(2,1)}, bf16[1,32,1,16,128]{4,1,3,2,0:T(8,128)(2,1)}, u32[]{:S(2)}, u32[]{:S(2)}) collective-permute-start(bf16[1,32,1,16,128]{4,1,3,2,0:T(8,128)(2,1)} %get-tuple-element.25), channel_id=1, source_target_pairs={{1,0},{2,1},{3,2},{5,4},{6,5},{7,6},{9,8},{10,9},{11,10},{13,12},{... | collective-permute-start | bytes 393224 | tf_op jit(solution)/shard_map/ppermute | solution.py:20
  3.8 6.2 %collective-permute-start = (bf16[1,32,1,16,128]{4,1,3,2,0:T(8,128)(2,1)}, bf16[1,32,1,16,128]{4,1,3,2,0:T(8,128)(2,1)}, u32[]{:S(2)}, u32[]{:S(2)}) collective-permute-start(bf16[1,32,1,16,128]{4,1,3,2,0:T(8,128)(2,1)} %get-tuple-element.24), channel_id=1, source_target_pairs={{0,1},{1,2},{2,3},{4,5},{5,6},{6,7},{8,9},{9,10},{10,11},{12,13},{... | collective-permute-start | bytes 393224 | tf_op jit(solution)/shard_map/ppermute | solution.py:18
  10.1 3.4 %convert_reduce_fusion = f32[4096]{0:T(1024)S(1)} fusion(s32[1024]{0:T(1024)} %bitcast.78), kind=kLoop, calls=%fused_computation | loop fusion | flops 12578816 | bytes 20480 | tf_op jit(solution)/shard_map/reduce_sum | solution.py:201
  13.4 1.7 %fusion.2 = (bf16[864,864]{1,0:T(8,128)(2,1)S(1)}, bf16[864,864]{1,0:T(8,128)(2,1)}) fusion(s32[864]{0:T(1024)S(1)} %fusion.24, s32[864]{0:T(1024)S(1)} %fusion.27), kind=kLoop, calls=%fused_computation.9 | loop fusion | flops 2985984 | bytes 2992896 | tf_op jit(solution)/shard_map/convert_element_type | solution.py:135
  16.5 1.3 %convolution_bitcast_fusion.1 = f32[32,32]{1,0:T(8,128)S(1)} fusion(bf16[32,2,16,128]{3,2,1,0:T(8,128)(2,1)} %bitcast.72), kind=kOutput, calls=%fused_computation.17 | convolution fusion | flops 8388608 | bytes 266240 | tf_op jit(solution)/shard_map/dot_general | solution.py:183
  17.8 1.0 %maximum_bitcast_fusion = bf16[32,4,16,128]{3,0,2,1:T(8,128)(2,1)S(1)} fusion(bf16[1,32,1,16,128]{4,1,3,2,0:T(8,128)(2,1)} %collective-permute-done.1, bf16[1,32,2,16,128]{4,1,3,2,0:T(8,128)(2,1)S(1)} %copy.30, bf16[1,32,1,16,128]{4,1,3,2,0:T(8,128)(2,1)} %collective-permute-done), kind=kLoop, calls=%fused_computation.23 | loop fusion | flops 524288 | bytes 1048576 | tf_op jit(solution)/shard_map/squeeze | solution.py:176
  19.7 1.5 %pad_maximum_fusion.src_ref = bf16[3,4,18,32,128]{4,3,2,1,0:T(8,128)(2,1)} fusion(bf16[1,4,18,32,128]{4,3,2,1,0:T(8,128)(2,1)S(1)} %get-tuple-element.19, bf16[1,4,18,32,128]{4,3,2,1,0:T(8,128)(2,1)S(1)} %get-tuple-element.20, bf16[1,4,18,32,128]{4,3,2,1,0:T(8,128)(2,1)S(1)} %get-tuple-element.18), kind=kLoop, calls=%fused_computation.11 | loop fusion | flops 1769472 | bytes 3538944 | tf_op jit(solution)/shard_map/stack | solution.py:109
  21.2 5.5 %shard_map.93 = bf16[864,4096]{1,0:T(8,128)(2,1)} custom-call(bf16[3,4,18,32,128]{4,3,2,1,0:T(8,128)(2,1)} %pad_maximum_fusion.src_ref), custom_call_target="tpu_custom_call" | custom-call | tf_op jit(solution)/shard_map/pallas_call | solution.py:122
  26.7 5.3 %convolution_bitcast_fusion = f32[32,864]{1,0:T(8,128)S(1)} fusion(bf16[864,4096]{1,0:T(8,128)(2,1)} %shard_map.93, bf16[32,4096]{1,0:T(8,128)(2,1)S(1)} %reshape_squeeze.3), kind=kOutput, calls=%fused_computation.16 | convolution fusion | flops 226492416 | bytes 7450624 | tf_op jit(solution)/shard_map/dot_general | solution.py:182
  32.1 2.0 %collective-permute-start.9 = (f32[32,896]{1,0:T(8,128)S(1)}, f32[32,896]{1,0:T(8,128)S(1)}, u32[]{:S(2)}, u32[]{:S(2)}) collective-permute-start(f32[32,896]{1,0:T(8,128)S(1)} %pad_maximum_fusion.1), channel_id=1, source_target_pairs={{0,8},{4,12},{8,0},{12,4},{16,24},{20,28},{24,16},{28,20},{1,9},{5... | collective-permute-start | bytes 344072 | tf_op jit(solution)/shard_map/ppermute | solution.py:39
  34.2 7.5 %multiply_convert_fusion.2 = bf16[864,864]{1,0:T(8,128)(2,1)S(1)} fusion(bf16[864,4096]{1,0:T(8,128)(2,1)S(1)} %copy-done.1, f32[4096]{0:T(1024)S(1)} %convert_reduce_fusion), kind=kOutput, calls=%fused_computation.6 | convolution fusion | flops 6127405056 | bytes 8587264 | tf_op jit(solution)/shard_map/dot_general | solution.py:206
  41.8 2.0 %collective-permute-start.11 = (f32[32,896]{1,0:T(8,128)S(1)}, f32[32,896]{1,0:T(8,128)S(1)}, u32[]{:S(2)}, u32[]{:S(2)}) collective-permute-start(f32[32,896]{1,0:T(8,128)S(1)} %add_add_fusion.1), channel_id=1, source_target_pairs={{0,16},{4,20},{8,24},{12,28},{16,0},{20,4},{24,8},{28,12},{1,17},{... | collective-permute-start | bytes 344072 | tf_op jit(solution)/shard_map/ppermute | solution.py:37
  43.8 2.2 %fusion.32 = f32[864,864]{1,0:T(8,128)S(1)} fusion(bf16[864,864]{1,0:T(8,128)(2,1)S(1)} %copy-done.4, bf16[864,864]{1,0:T(8,128)(2,1)S(1)} %multiply_convert_fusion.2), kind=kOutput, calls=%fused_computation.81 | convolution fusion | flops 1289945088 | bytes 5971968 | tf_op jit(solution)/shard_map/dot_general | solution.py:214
  46.0 1.1 %slice.87 = bf16[432,864]{1,0:T(8,128)(2,1)} slice(f32[864,864]{1,0:T(8,128)S(1)} %fusion.32), slice={[432:864], [0:864]} | slice | bytes 1492992 | tf_op jit(solution)/shard_map/slice | solution.py:221
  48.7 1.0 %collective-permute-start.12 = (f32[32,1,216]{2,1,0:T(1,128)S(1)}, f32[32,1,216]{2,1,0:T(1,128)S(1)}, u32[]{:S(2)}, u32[]{:S(2)}) collective-permute-start(f32[32,1,216]{2,1,0:T(1,128)S(1)} %get-tuple-element.28), channel_id=1, source_target_pairs={{0,1},{1,0},{2,3},{3,2},{4,5},{5,4},{6,7},{7,6},{8,9},{9,8},{10,11... | collective-permute-start | bytes 82952 | tf_op jit(solution)/shard_map/ppermute | solution.py:77
  49.7 1.7 %collective-permute-start.13 = (f32[32,1,216]{2,1,0:T(1,128)S(1)}, f32[32,1,216]{2,1,0:T(1,128)S(1)}, u32[]{:S(2)}, u32[]{:S(2)}) collective-permute-start(f32[32,1,216]{2,1,0:T(1,128)S(1)} %get-tuple-element.27), channel_id=1, source_target_pairs={{0,2},{1,3},{2,0},{3,1},{4,6},{5,7},{6,4},{7,5},{8,10},{9,11},{10,... | collective-permute-start | bytes 82952 | tf_op jit(solution)/shard_map/ppermute | solution.py:77
  51.4 1.7 %collective-permute-start.14 = (f32[32,1,216]{2,1,0:T(1,128)S(1)}, f32[32,1,216]{2,1,0:T(1,128)S(1)}, u32[]{:S(2)}, u32[]{:S(2)}) collective-permute-start(f32[32,1,216]{2,1,0:T(1,128)S(1)} %get-tuple-element.26), channel_id=1, source_target_pairs={{0,3},{1,2},{2,1},{3,0},{4,7},{5,6},{6,5},{7,4},{8,11},{9,10},{10,... | collective-permute-start | bytes 82952 | tf_op jit(solution)/shard_map/ppermute | solution.py:77
  53.1 4.3 %fusion.4 = bf16[4,8,32,128]{3,1,2,0:T(8,128)(2,1)S(1)} fusion(bf16[32,864]{1,0:T(8,128)(2,1)S(1)} %reshape.136, bf16[864,4096]{1,0:T(8,128)(2,1)} %shard_map.93), kind=kOutput, calls=%fused_computation.15 | convolution fusion | flops 226623488 | bytes 7395328 | tf_op jit(solution)/shard_map/dot_general | solution.py:216
  58.4 1.3 %convert_add_fusion = f32[432,864]{1,0:T(8,128)S(1)} fusion(bf16[432,864]{1,0:T(8,128)(2,1)} %collective-permute-done.2, f32[864,864]{1,0:T(8,128)S(1)} %copy-done.3), kind=kLoop, calls=%fused_computation.13 | loop fusion | flops 746496 | bytes 3732480 | tf_op jit(solution)/shard_map/add | solution.py:222
  59.8 1.6 %collective-permute-start.3 = (bf16[216,864]{1,0:T(8,128)(2,1)S(1)}, bf16[216,864]{1,0:T(8,128)(2,1)S(1)}, u32[]{:S(2)}, u32[]{:S(2)}) collective-permute-start(bf16[216,864]{1,0:T(8,128)(2,1)S(1)} %slice.88), channel_id=1, source_target_pairs={{0,8},{4,12},{8,0},{12,4},{16,24},{20,28},{24,16},{28,20},{1,9},{5... | collective-permute-start | bytes 1119752 | tf_op jit(solution)/shard_map/ppermute | solution.py:221
  62.2 1.7 %collective-permute-start.16 = (f32[32,896]{1,0:T(8,128)S(1)}, f32[32,896]{1,0:T(8,128)S(1)}, u32[]{:S(2)}, u32[]{:S(2)}) collective-permute-start(f32[32,896]{1,0:T(8,128)S(1)} %pad_maximum_fusion.2), channel_id=1, source_target_pairs={{0,2},{1,3},{2,0},{3,1},{4,6},{5,7},{6,4},{7,5},{8,10},{9,11},{10,... | collective-permute-start | bytes 344072 | tf_op jit(solution)/shard_map/ppermute | solution.py:39
  63.9 1.1 %collective-permute-start.17 = (f32[32,896]{1,0:T(8,128)S(1)}, f32[32,896]{1,0:T(8,128)S(1)}, u32[]{:S(2)}, u32[]{:S(2)}) collective-permute-start(f32[32,896]{1,0:T(8,128)S(1)} %pad_maximum_fusion.2), channel_id=1, source_target_pairs={{0,3},{1,2},{2,1},{3,0},{4,7},{5,6},{6,5},{7,4},{8,11},{9,10},{10,... | collective-permute-start | bytes 344072 | tf_op jit(solution)/shard_map/ppermute | solution.py:40
  65.0 0.7 collective-permute-start.15
  65.7 3.9 %collective-permute-done.3 = bf16[216,864]{1,0:T(8,128)(2,1)S(1)} collective-permute-done((bf16[216,864]{1,0:T(8,128)(2,1)S(1)}, bf16[216,864]{1,0:T(8,128)(2,1)S(1)}, u32[]{:S(2)}, u32[]{:S(2)}) %collective-permute-start.3) | collective-permute-done | bytes 373280 | tf_op jit(solution)/shard_map/ppermute | solution.py:221
  70.3 2.5 %collective-permute-done.16 = f32[32,896]{1,0:T(8,128)S(1)} collective-permute-done((f32[32,896]{1,0:T(8,128)S(1)}, f32[32,896]{1,0:T(8,128)S(1)}, u32[]{:S(2)}, u32[]{:S(2)}) %collective-permute-start.16) | collective-permute-done | bytes 114720 | tf_op jit(solution)/shard_map/ppermute | solution.py:39
  73.7 1.8 %collective-permute-done.4 = bf16[108,864]{1,0:T(8,128)(2,1)S(1)} collective-permute-done((bf16[108,864]{1,0:T(8,128)(2,1)S(1)}, bf16[108,864]{1,0:T(8,128)(2,1)S(1)}, u32[]{:S(2)}, u32[]{:S(2)}) %collective-permute-start.4) | collective-permute-done | bytes 186656 | tf_op jit(solution)/shard_map/ppermute | solution.py:221
  75.5 1.1 %fusion.5 = f32[108,864]{1,0:T(8,128)S(1)} fusion(bf16[864,864]{1,0:T(8,128)(2,1)S(1)} %get-tuple-element.16, f32[216,864]{1,0:T(8,128)S(1)} %slice_add_fusion, bf16[108,864]{1,0:T(8,128)(2,1)S(1)} %collective-permute-done.4), kind=kOutput, calls=%fused_computation.26 | convolution fusion | flops 483916032 | bytes 2523648 | tf_op jit(solution)/shard_map/dot_general | solution.py:224
  77.4 2.4 %collective-permute-start.7 = (bf16[108,1,216]{0,2,1:T(8,128)(2,1)S(1)}, bf16[108,1,216]{0,2,1:T(8,128)(2,1)S(1)}, u32[]{:S(2)}, u32[]{:S(2)}) collective-permute-start(bf16[108,1,216]{0,2,1:T(8,128)(2,1)S(1)} %bitcast.75), channel_id=1, source_target_pairs={{0,3},{1,2},{2,1},{3,0},{4,7},{5,6},{6,5},{7,4},{8,11},{9,10},{10,... | collective-permute-start | bytes 139976 | tf_op jit(solution)/shard_map/ppermute | solution.py:77
  80.2 2.0 %collective-permute-start.5 = (bf16[108,1,216]{0,2,1:T(8,128)(2,1)S(1)}, bf16[108,1,216]{0,2,1:T(8,128)(2,1)S(1)}, u32[]{:S(2)}, u32[]{:S(2)}) collective-permute-start(bf16[108,1,216]{0,2,1:T(8,128)(2,1)S(1)} %bitcast.77), channel_id=1, source_target_pairs={{0,1},{1,0},{2,3},{3,2},{4,5},{5,4},{6,7},{7,6},{8,9},{9,8},{10,11... | collective-permute-start | bytes 139976 | tf_op jit(solution)/shard_map/ppermute | solution.py:77
  82.5 1.0 %collective-permute-done.7 = bf16[108,1,216]{0,2,1:T(8,128)(2,1)S(1)} collective-permute-done((bf16[108,1,216]{0,2,1:T(8,128)(2,1)S(1)}, bf16[108,1,216]{0,2,1:T(8,128)(2,1)S(1)}, u32[]{:S(2)}, u32[]{:S(2)}) %collective-permute-start.7) | collective-permute-done | bytes 46688 | tf_op jit(solution)/shard_map/ppermute | solution.py:77
  83.4 1.7 %collective-permute-done.6 = bf16[108,1,216]{0,2,1:T(8,128)(2,1)S(1)} collective-permute-done((bf16[108,1,216]{0,2,1:T(8,128)(2,1)S(1)}, bf16[108,1,216]{0,2,1:T(8,128)(2,1)S(1)}, u32[]{:S(2)}, u32[]{:S(2)}) %collective-permute-start.6) | collective-permute-done | bytes 46688 | tf_op jit(solution)/shard_map/ppermute | solution.py:77
  (71 shorter events, 10.2 us)
Async XLA Ops:
  0.6 60.9 %copy-start = (f32[216,864]{1,0:T(8,128)S(1)}, f32[216,864]{1,0:T(8,128)}, u32[]{:S(2)}) copy-start(f32[216,864]{1,0:T(8,128)} %param.10) | copy-start | bytes 2239492
  0.6 14.5 %copy-start.5 = (bf16[1,32,2,16,128]{4,3,2,1,0:T(8,128)(2,1)S(1)}, bf16[1,32,2,16,128]{4,3,2,1,0:T(8,128)(2,1)}, u32[]{:S(2)}) copy-start(bf16[1,32,2,16,128]{4,3,2,1,0:T(8,128)(2,1)} %param.7) | copy-start | bytes 786436
  0.7 14.6 %copy-start.7 = (bf16[32,864]{1,0:T(8,128)(2,1)S(1)}, bf16[32,864]{1,0:T(8,128)(2,1)}, u32[]{:S(2)}) copy-start(bf16[32,864]{1,0:T(8,128)(2,1)} %param.8) | copy-start | bytes 165892
  2.5 15.3 %collective-permute-start.1 = (bf16[1,32,1,16,128]{4,1,3,2,0:T(8,128)(2,1)}, bf16[1,32,1,16,128]{4,1,3,2,0:T(8,128)(2,1)}, u32[]{:S(2)}, u32[]{:S(2)}) collective-permute-start(bf16[1,32,1,16,128]{4,1,3,2,0:T(8,128)(2,1)} %get-tuple-element.25), channel_id=1, source_target_pairs={{1,0},{2,1},{3,2},{5,4},{6,5},{7,6},{9,8},{10,9},{11,10},{13,12},{... | collective-permute-start | bytes 393224 | tf_op jit(solution)/shard_map/ppermute | solution.py:20
  3.8 14.0 %collective-permute-start = (bf16[1,32,1,16,128]{4,1,3,2,0:T(8,128)(2,1)}, bf16[1,32,1,16,128]{4,1,3,2,0:T(8,128)(2,1)}, u32[]{:S(2)}, u32[]{:S(2)}) collective-permute-start(bf16[1,32,1,16,128]{4,1,3,2,0:T(8,128)(2,1)} %get-tuple-element.24), channel_id=1, source_target_pairs={{0,1},{1,2},{2,3},{4,5},{5,6},{6,7},{8,9},{9,10},{10,11},{12,13},{... | collective-permute-start | bytes 393224 | tf_op jit(solution)/shard_map/ppermute | solution.py:18
  26.7 7.5 %copy-start.1 = (bf16[864,4096]{1,0:T(8,128)(2,1)S(1)}, bf16[864,4096]{1,0:T(8,128)(2,1)}, u32[]{:S(2)}) copy-start(bf16[864,4096]{1,0:T(8,128)(2,1)} %shard_map.93) | copy-start | bytes 21233668
  32.1 11.8 %copy-start.4 = (bf16[864,864]{1,0:T(8,128)(2,1)S(1)}, bf16[864,864]{1,0:T(8,128)(2,1)}, u32[]{:S(2)}) copy-start(bf16[864,864]{1,0:T(8,128)(2,1)} %get-tuple-element.12) | copy-start | bytes 4478980
  32.1 9.7 %collective-permute-start.9 = (f32[32,896]{1,0:T(8,128)S(1)}, f32[32,896]{1,0:T(8,128)S(1)}, u32[]{:S(2)}, u32[]{:S(2)}) collective-permute-start(f32[32,896]{1,0:T(8,128)S(1)} %pad_maximum_fusion.1), channel_id=1, source_target_pairs={{0,8},{4,12},{8,0},{12,4},{16,24},{20,28},{24,16},{28,20},{1,9},{5... | collective-permute-start | bytes 344072 | tf_op jit(solution)/shard_map/ppermute | solution.py:39
  34.0 7.7 %collective-permute-start.10 = (f32[32,896]{1,0:T(8,128)S(1)}, f32[32,896]{1,0:T(8,128)S(1)}, u32[]{:S(2)}, u32[]{:S(2)}) collective-permute-start(f32[32,896]{1,0:T(8,128)S(1)} %pad_maximum_fusion.1), channel_id=1, source_target_pairs={{0,12},{4,8},{8,4},{12,0},{16,28},{20,24},{24,20},{28,16},{1,13},{... | collective-permute-start | bytes 344072 | tf_op jit(solution)/shard_map/ppermute | solution.py:40
  34.0 7.7 %collective-permute-start.8 = (f32[32,896]{1,0:T(8,128)S(1)}, f32[32,896]{1,0:T(8,128)S(1)}, u32[]{:S(2)}, u32[]{:S(2)}) collective-permute-start(f32[32,896]{1,0:T(8,128)S(1)} %pad_maximum_fusion.1), channel_id=1, source_target_pairs={{0,4},{4,0},{8,12},{12,8},{16,20},{20,16},{24,28},{28,24},{1,5},{5... | collective-permute-start | bytes 344072 | tf_op jit(solution)/shard_map/ppermute | solution.py:37
  41.8 5.4 %collective-permute-start.11 = (f32[32,896]{1,0:T(8,128)S(1)}, f32[32,896]{1,0:T(8,128)S(1)}, u32[]{:S(2)}, u32[]{:S(2)}) collective-permute-start(f32[32,896]{1,0:T(8,128)S(1)} %add_add_fusion.1), channel_id=1, source_target_pairs={{0,16},{4,20},{8,24},{12,28},{16,0},{20,4},{24,8},{28,12},{1,17},{... | collective-permute-start | bytes 344072 | tf_op jit(solution)/shard_map/ppermute | solution.py:37
  46.0 1.9 %copy-start.2 = (f32[864,864]{1,0:T(8,128)}, f32[864,864]{1,0:T(8,128)S(1)}, u32[]{:S(2)}) copy-start(f32[864,864]{1,0:T(8,128)S(1)} %fusion.32) | copy-start | bytes 8957956
  47.1 11.3 %collective-permute-start.2 = (bf16[432,864]{1,0:T(8,128)(2,1)}, bf16[432,864]{1,0:T(8,128)(2,1)}, u32[]{:S(2)}, u32[]{:S(2)}) collective-permute-start(bf16[432,864]{1,0:T(8,128)(2,1)} %slice.87), channel_id=1, source_target_pairs={{0,4},{4,0},{8,12},{12,8},{16,20},{20,16},{24,28},{28,24},{1,5},{5... | collective-permute-start | bytes 2239496 | tf_op jit(solution)/shard_map/ppermute | solution.py:221
  48.7 9.6 %collective-permute-start.12 = (f32[32,1,216]{2,1,0:T(1,128)S(1)}, f32[32,1,216]{2,1,0:T(1,128)S(1)}, u32[]{:S(2)}, u32[]{:S(2)}) collective-permute-start(f32[32,1,216]{2,1,0:T(1,128)S(1)} %get-tuple-element.28), channel_id=1, source_target_pairs={{0,1},{1,0},{2,3},{3,2},{4,5},{5,4},{6,7},{7,6},{8,9},{9,8},{10,11... | collective-permute-start | bytes 82952 | tf_op jit(solution)/shard_map/ppermute | solution.py:77
  49.7 8.6 %collective-permute-start.13 = (f32[32,1,216]{2,1,0:T(1,128)S(1)}, f32[32,1,216]{2,1,0:T(1,128)S(1)}, u32[]{:S(2)}, u32[]{:S(2)}) collective-permute-start(f32[32,1,216]{2,1,0:T(1,128)S(1)} %get-tuple-element.27), channel_id=1, source_target_pairs={{0,2},{1,3},{2,0},{3,1},{4,6},{5,7},{6,4},{7,5},{8,10},{9,11},{10,... | collective-permute-start | bytes 82952 | tf_op jit(solution)/shard_map/ppermute | solution.py:77
  51.4 7.0 %copy-start.3 = (f32[864,864]{1,0:T(8,128)S(1)}, f32[864,864]{1,0:T(8,128)}, u32[]{:S(2)}) copy-start(f32[864,864]{1,0:T(8,128)} %copy-done.2) | copy-start | bytes 8957956
  51.4 6.9 %collective-permute-start.14 = (f32[32,1,216]{2,1,0:T(1,128)S(1)}, f32[32,1,216]{2,1,0:T(1,128)S(1)}, u32[]{:S(2)}, u32[]{:S(2)}) collective-permute-start(f32[32,1,216]{2,1,0:T(1,128)S(1)} %get-tuple-element.26), channel_id=1, source_target_pairs={{0,3},{1,2},{2,1},{3,0},{4,7},{5,6},{6,5},{7,4},{8,11},{9,10},{10,... | collective-permute-start | bytes 82952 | tf_op jit(solution)/shard_map/ppermute | solution.py:77
  57.5 3.9 %copy-start.8 = (f32[32,32]{1,0:T(8,128)S(1)}, f32[32,32]{1,0:T(8,128)}, u32[]{:S(2)}) copy-start(f32[32,32]{1,0:T(8,128)} %param.11) | copy-start | bytes 12292
  59.8 9.8 %collective-permute-start.3 = (bf16[216,864]{1,0:T(8,128)(2,1)S(1)}, bf16[216,864]{1,0:T(8,128)(2,1)S(1)}, u32[]{:S(2)}, u32[]{:S(2)}) collective-permute-start(bf16[216,864]{1,0:T(8,128)(2,1)S(1)} %slice.88), channel_id=1, source_target_pairs={{0,8},{4,12},{8,0},{12,4},{16,24},{20,28},{24,16},{28,20},{1,9},{5... | collective-permute-start | bytes 1119752 | tf_op jit(solution)/shard_map/ppermute | solution.py:221
  62.2 10.6 %collective-permute-start.16 = (f32[32,896]{1,0:T(8,128)S(1)}, f32[32,896]{1,0:T(8,128)S(1)}, u32[]{:S(2)}, u32[]{:S(2)}) collective-permute-start(f32[32,896]{1,0:T(8,128)S(1)} %pad_maximum_fusion.2), channel_id=1, source_target_pairs={{0,2},{1,3},{2,0},{3,1},{4,6},{5,7},{6,4},{7,5},{8,10},{9,11},{10,... | collective-permute-start | bytes 344072 | tf_op jit(solution)/shard_map/ppermute | solution.py:39
  63.9 8.9 %collective-permute-start.17 = (f32[32,896]{1,0:T(8,128)S(1)}, f32[32,896]{1,0:T(8,128)S(1)}, u32[]{:S(2)}, u32[]{:S(2)}) collective-permute-start(f32[32,896]{1,0:T(8,128)S(1)} %pad_maximum_fusion.2), channel_id=1, source_target_pairs={{0,3},{1,2},{2,1},{3,0},{4,7},{5,6},{6,5},{7,4},{8,11},{9,10},{10,... | collective-permute-start | bytes 344072 | tf_op jit(solution)/shard_map/ppermute | solution.py:40
  65.0 8.0 %collective-permute-start.15 = (f32[32,896]{1,0:T(8,128)S(1)}, f32[32,896]{1,0:T(8,128)S(1)}, u32[]{:S(2)}, u32[]{:S(2)}) collective-permute-start(f32[32,896]{1,0:T(8,128)S(1)} %pad_maximum_fusion.2), channel_id=1, source_target_pairs={{0,1},{1,0},{2,3},{3,2},{4,5},{5,4},{6,7},{7,6},{8,9},{9,8},{10,11... | collective-permute-start | bytes 344072 | tf_op jit(solution)/shard_map/ppermute | solution.py:37
  69.7 5.8 %collective-permute-start.4 = (bf16[108,864]{1,0:T(8,128)(2,1)S(1)}, bf16[108,864]{1,0:T(8,128)(2,1)S(1)}, u32[]{:S(2)}, u32[]{:S(2)}) collective-permute-start(bf16[108,864]{1,0:T(8,128)(2,1)S(1)} %slice.89), channel_id=1, source_target_pairs={{0,16},{4,20},{8,24},{12,28},{16,0},{20,4},{24,8},{28,12},{1,17},{... | collective-permute-start | bytes 559880 | tf_op jit(solution)/shard_map/ppermute | solution.py:221
  73.0 12.8 %copy-start.6 = (f32[32,896]{1,0:T(8,128)}, f32[32,896]{1,0:T(8,128)S(1)}, u32[]{:S(2)}) copy-start(f32[32,896]{1,0:T(8,128)S(1)} %add_add_fusion) | copy-start | bytes 344068
  77.4 6.0 %collective-permute-start.7 = (bf16[108,1,216]{0,2,1:T(8,128)(2,1)S(1)}, bf16[108,1,216]{0,2,1:T(8,128)(2,1)S(1)}, u32[]{:S(2)}, u32[]{:S(2)}) collective-permute-start(bf16[108,1,216]{0,2,1:T(8,128)(2,1)S(1)} %bitcast.75), channel_id=1, source_target_pairs={{0,3},{1,2},{2,1},{3,0},{4,7},{5,6},{6,5},{7,4},{8,11},{9,10},{10,... | collective-permute-start | bytes 139976 | tf_op jit(solution)/shard_map/ppermute | solution.py:77
  80.0 5.1 %collective-permute-start.6 = (bf16[108,1,216]{0,2,1:T(8,128)(2,1)S(1)}, bf16[108,1,216]{0,2,1:T(8,128)(2,1)S(1)}, u32[]{:S(2)}, u32[]{:S(2)}) collective-permute-start(bf16[108,1,216]{0,2,1:T(8,128)(2,1)S(1)} %bitcast.76), channel_id=1, source_target_pairs={{0,2},{1,3},{2,0},{3,1},{4,6},{5,7},{6,4},{7,5},{8,10},{9,11},{10,... | collective-permute-start | bytes 139976 | tf_op jit(solution)/shard_map/ppermute | solution.py:77
  80.2 4.9 %collective-permute-start.5 = (bf16[108,1,216]{0,2,1:T(8,128)(2,1)S(1)}, bf16[108,1,216]{0,2,1:T(8,128)(2,1)S(1)}, u32[]{:S(2)}, u32[]{:S(2)}) collective-permute-start(bf16[108,1,216]{0,2,1:T(8,128)(2,1)S(1)} %bitcast.77), channel_id=1, source_target_pairs={{0,1},{1,0},{2,3},{3,2},{4,5},{5,4},{6,7},{7,6},{8,9},{9,8},{10,11... | collective-permute-start | bytes 139976 | tf_op jit(solution)/shard_map/ppermute | solution.py:77
